TPU v7x, 512 devices: a whole 4x8x8 slice. The times are simulated.
512 devices in a mesh: sec: 2 (over core), atoms: 32 (over z_lo, y), batch: 8 (over z_hi, x).
Axes of the slice: x: 4, y: 8, z: 8 (z_hi: 2, z_lo: 4; z = z_hi * 4 + z_lo), core: 2. Of those that a mesh axis runs over, the one named last changes fastest.
Arguments:
- atoms_in: bfloat16 [8, 16384, 1024], P('batch', 'atoms', 'sec'), may hold values from -6 to 6
- tile_ids: int32 [8, 2, 512], P('batch', None, 'atoms'), may hold values from -1 to 127, as said below
- tile_vals: bfloat16 [8, 512, 128, 128], P('batch', 'atoms'), may hold values from -0.26367188 to 0.26367188
- seq_lens: int32 [8], P('batch'), may hold values from 8193 to 16384, as said below
- pair_labels: int32 [8, 16384], P('batch', 'atoms'), may hold values from 0 to 255
- peak_embed: bfloat16 [8, 256, 256], P('batch', 'sec'), may hold values from -6 to 6
- norm_gain: bfloat16 [1024], P('sec'), may hold values from 0.099609375 to 1.8984375
- w_query: bfloat16 [1024, 512], P(None, 'sec'), may hold values from -0.1875 to 0.1875
- w_key: bfloat16 [1024, 512], P(None, 'sec'), may hold values from -0.1875 to 0.1875
- w_value: bfloat16 [1024, 512], P(None, 'sec'), may hold values from -0.1875 to 0.1875
- w_out: bfloat16 [512, 1024], P('sec'), may hold values from -0.25 to 0.25
- w_proj: bfloat16 [1024, 256], P('sec'), may hold values from -0.1875 to 0.1875
Outputs:
- hidden_two: bfloat16 [8, 16384, 1024], P('batch', 'atoms', 'sec')
- seq_loss: float32 [8], P('batch')
- proj_grad: float32 [8, 1024, 256], P('batch', 'sec')
Inputs may be any that keep to these rules, and one draw needn't show every extreme that they name: `tile_ids`: each index of atoms owns 16 consecutive slots and the row blocks 4 i to 4 (i + 1) - 1; its first 4 slots hold the diagonal tiles of its row blocks; live slots come first and padded slots have both ids -1; every live tile's row block is one of its owner's and its column block lies within 2 blocks of it; in every sequence some index of atoms has all 16 slots live. `seq_lens`: at least one sequence has all 16384 atoms live.
All inputs are finite; a program needn't handle non-finite values.
Results may differ from a plain program's by a relative error of at most 0.013.
Values may be sent and summed in bfloat16 or wider, within the bound.
No kernel may reach another device: no remote copies, remote signals or barrier semaphores. Data moves between devices by JAX's collectives and lax.ppermute only.
A program may use at most 64 MiB of HBM per device.

v0:
```python
import math

import jax
import jax.numpy as jnp
from jax import lax
from jax.sharding import PartitionSpec as P

D = 1024
HEADS = 8
HEAD_DIM = 64
PEAKS = 256


EPSILON = 1e-06
HIGHEST = lax.Precision.HIGHEST


def extended(x, sides, width):
    for axis, dim in sides:
        peers, length = (lax.axis_size(axis), x.shape[dim])
        up = [(i, (i + 1) % peers) for i in range(peers - 1)]
        down = [(j, i) for i, j in up]
        last = lax.slice_in_dim(x, length - width, length, axis=dim)
        leading = lax.slice_in_dim(x, 0, width, axis=dim)
        before = lax.ppermute(last, axis, up)
        after = lax.ppermute(leading, axis, down)
        x = jnp.concatenate([before, x, after], axis=dim)
    return x


def feature_map(values):
    return jax.nn.elu(values) + 1.0


def message_pass(atom_rows, tile_pair, tile_block):
    tile_size = tile_block.shape[-1]
    local_rows, half_width = atom_rows.shape
    block_count = local_rows // tile_size
    reach_blocks = max(block_count // 2, 1)
    padded = extended(atom_rows, (("atoms", 0),), reach_blocks * tile_size)
    blocks = padded.reshape(block_count + 2 * reach_blocks, tile_size, half_width)
    first_block = lax.axis_index("atoms") * block_count
    row_ids = tile_pair[0]
    col_ids = tile_pair[1]
    live_tiles = row_ids >= 0
    col_local = jnp.where(live_tiles, col_ids - first_block + reach_blocks, 0)
    row_local = jnp.where(live_tiles, row_ids - first_block, -1)
    panels = jnp.take(blocks, col_local, axis=0)
    products = jnp.einsum("tij,tjf->tif", tile_block, panels, preferred_element_type=jnp.float32)
    selector = (row_local[None, :] == jnp.arange(block_count, dtype=jnp.int32)[:, None]).astype(
        jnp.float32
    )
    summed = jnp.einsum("bt,tif->bif", selector, products, precision=HIGHEST)
    return summed.reshape(local_rows, half_width).astype(jnp.bfloat16)


def key_summary(key_rows, value_rows, atom_mask, head_count):
    count_rows = key_rows.shape[0]
    feat_keys = (
        feature_map(key_rows.astype(jnp.float32)).reshape(count_rows, head_count, -1)
        * atom_mask[:, None, None]
    )
    value_f = value_rows.astype(jnp.float32).reshape(count_rows, head_count, -1)
    outer_state = jnp.einsum("nhd,nhe->hde", feat_keys, value_f, precision=HIGHEST)
    return (outer_state, jnp.sum(feat_keys, axis=0))


def read_summary(query_rows, outer_state, key_total, head_count):
    count_rows = query_rows.shape[0]
    feat_query = feature_map(query_rows.astype(jnp.float32)).reshape(count_rows, head_count, -1)
    numerator = jnp.einsum("nhd,hde->nhe", feat_query, outer_state, precision=HIGHEST)
    denominator = jnp.einsum("nhd,hd->nh", feat_query, key_total, precision=HIGHEST)
    return (numerator / denominator[..., None]).reshape(count_rows, -1)


def contrast(unit_rows, peak_rows, label_part, mask_part, peak_start):
    logit_scale = 2.0 / math.sqrt(unit_rows.shape[-1])
    peak_f = peak_rows.astype(jnp.float32)
    logits = logit_scale * jnp.dot(unit_rows, peak_f.T, precision=HIGHEST)
    peak_index = peak_start + jnp.arange(peak_rows.shape[0], dtype=jnp.int32)
    target = (label_part[:, None] == peak_index[None, :]).astype(jnp.float32)
    sign_rows = 2.0 * target - 1.0
    loss_part = jnp.sum(mask_part[:, None] * jax.nn.softplus(-sign_rows * logits)) / PEAKS
    slopes = mask_part[:, None] * (jax.nn.sigmoid(logits) - target) * (1.0 / math.sqrt(PEAKS))
    unit_grad = logit_scale * jnp.dot(slopes, peak_f, precision=HIGHEST)
    return (loss_part, unit_grad)


def embed_backward(unit_rows, unit_grad, embed_scale):
    inner_mean = jnp.mean(unit_grad * unit_rows, axis=-1, keepdims=True)
    return (embed_scale * (unit_grad - unit_rows * inner_mean)).astype(jnp.bfloat16)


def shards(
    atoms_in,
    tile_ids,
    tile_vals,
    seq_lens,
    pair_labels,
    peak_embed,
    norm_gain,
    w_query,
    w_key,
    w_value,
    w_out,
    w_proj,
):
    atom_rows = atoms_in[0]
    local_rows = atom_rows.shape[0]
    gathered = message_pass(atom_rows, tile_ids[0], tile_vals[0])
    hidden_one = (atom_rows.astype(jnp.float32) + gathered.astype(jnp.float32)).astype(jnp.bfloat16)
    atom_base = lax.axis_index("atoms") * local_rows
    length_one = seq_lens[0]
    label_row = pair_labels[0]
    peak_part = peak_embed[0]
    hidden_f = hidden_one.astype(jnp.float32)
    square_sum = lax.psum(jnp.sum(hidden_f * hidden_f, axis=-1), "sec")
    row_scale = lax.rsqrt(square_sum[:, None] / D + EPSILON)
    normed = (hidden_f * row_scale * norm_gain.astype(jnp.float32)).astype(jnp.bfloat16)
    head_cols = w_query.shape[1]
    piece_rows = lax.all_gather(normed, "sec", axis=1, tiled=True)
    query_f, key_f, value_f = tuple(
        (
            jnp.dot(piece_rows, weight, preferred_element_type=jnp.float32)
            for weight in (w_query, w_key, w_value)
        )
    )
    head_count = head_cols // HEAD_DIM
    atom_mask = (atom_base + jnp.arange(local_rows, dtype=jnp.int32) < length_one).astype(
        jnp.float32
    )
    outer_state, key_total = key_summary(
        key_f.astype(jnp.bfloat16), value_f.astype(jnp.bfloat16), atom_mask, head_count
    )
    outer_state, key_total = lax.psum((outer_state, key_total), "atoms")
    attended = read_summary(query_f.astype(jnp.bfloat16), outer_state, key_total, head_count)
    out_sum = lax.psum(jnp.sum(attended * attended, axis=-1), "sec")
    attended_n = (attended * lax.rsqrt(out_sum[:, None] / (HEADS * HEAD_DIM) + EPSILON)).astype(
        jnp.bfloat16
    )
    branch_full = jnp.dot(attended_n, w_out, preferred_element_type=jnp.float32)
    branch = lax.psum_scatter(branch_full, "sec", scatter_dimension=1, tiled=True)
    hidden_two = (hidden_f + branch).astype(jnp.bfloat16)
    embedded = lax.psum(jnp.dot(hidden_two, w_proj, preferred_element_type=jnp.float32), "sec")
    embed_scale = lax.rsqrt(jnp.mean(embedded * embedded, axis=-1, keepdims=True) + EPSILON)
    unit_rows = embedded * embed_scale
    peak_start = lax.axis_index("sec") * peak_part.shape[0]
    loss_part, unit_grad = contrast(unit_rows, peak_part, label_row, atom_mask, peak_start)
    unit_grad = lax.psum(unit_grad, "sec")
    embed_grad = embed_backward(unit_rows, unit_grad, embed_scale)
    proj_part = jnp.einsum("nd,ne->de", hidden_two, embed_grad, preferred_element_type=jnp.float32)
    loss_total = lax.psum(loss_part, ("sec", "atoms")) / (local_rows * lax.axis_size("atoms"))
    proj_total = lax.psum(proj_part, "atoms")
    return (hidden_two[None], loss_total.reshape(1), proj_total[None])


def solution(mesh):
    return jax.shard_map(
        shards,
        mesh=mesh,
        in_specs=(
            P("batch", "atoms", "sec"),
            P("batch", None, "atoms"),
            P("batch", "atoms", None, None),
            P("batch"),
            P("batch", "atoms"),
            P("batch", "sec", None),
            P("sec"),
            P(None, "sec"),
            P(None, "sec"),
            P(None, "sec"),
            P("sec", None),
            P("sec", None),
        ),
        out_specs=(P("batch", "atoms", "sec"), P("batch"), P("batch", "sec", None)),
        check_vma=False,
    )
```

profile of v0, /device:TPU:6, one launch (start us, length us, event | category | flops | bytes accessed | tf_op | source)
XLA Modules:
  0.0 773.8 jit_solution(17922998423100423061)
XLA Ops:
  7.2 1.1 slice_bitcast_fusion.1
  8.3 3.5 collective-permute-start
  11.8 1.3 collective-permute-start.1
  15.3 2.1 collective-permute-done
  17.4 4.1 collective-permute-done.1
  22.6 2.0 gather_fusion
  24.6 4.4 fusion.2
  29.0 5.5 copy.16
  34.5 3.7 fusion.8
  39.5 2.6 psum.56
  43.9 21.4 %all-gather.2.cloned.1.call-done = bf16[512,1024]{1,0:T(8,128)(2,1)} async-done(((bf16[512,512]{1,0:T(8,128)(2,1)}), bf16[512,1024]{1,0:T(8,128)(2,1)}) %all-gather.2.cloned.1.call-update) | async-done | bytes 1048592 | tf_op jit(solution)/shard_map/all_gather | solution.py:121
  65.3 1.7 convolution_convert_fusion.1
  67.0 2.1 multiply_reduce_fusion.3
  69.1 1.1 fusion.26
  70.3 80.4 %psum.58 = f32[4,64]{1,0:T(4,128)S(1)} all-reduce(f32[4,64]{1,0:T(4,128)S(1)} %reduce_sum.58), channel_id=1, replica_groups=mesh['sec'=2,'atoms'=32,'batch'=8] {'atoms'}, use_global_device_ids=true, to_apply=%region_4.5 | all-reduce | flops 256 | bytes 2048 | tf_op jit(solution)/shard_map/psum | solution.py:135
  150.7 1.7 fusion.23
  152.8 196.9 %all-reduce.5.cloned.1.call-done = f32[4,64,64]{1,2,0:T(8,128)} async-done(((f32[4,64,64]{1,2,0:T(8,128)}), f32[4,64,64]{1,2,0:T(8,128)}) %all-reduce.5.cloned.1.call-update) | async-done | bytes 65552 | tf_op jit(solution)/shard_map/psum | solution.py:135
  349.8 1.5 multiply_reduce_fusion.2
  351.3 2.5 psum.59
  353.8 1.8 fusion.64
  355.7 14.7 %reduce-scatter.2.cloned.1.call-done = f32[512,512]{1,0:T(8,128)} async-done(((f32[512,1024]{1,0:T(8,128)}), f32[512,512]{1,0:T(8,128)}) %reduce-scatter.2.cloned.1.call-update) | async-done | bytes 1048592 | tf_op jit(solution)/shard_map/reduce_scatter | solution.py:142
  370.5 1.4 fusion.17
  373.1 37.2 %all-reduce.7.cloned.1.call-done = f32[512,256]{1,0:T(8,128)} async-done(((f32[512,256]{1,0:T(8,128)}), f32[512,256]{1,0:T(8,128)}) %all-reduce.7.cloned.1.call-update) | async-done | bytes 524304 | tf_op jit(solution)/shard_map/psum | solution.py:144
  410.3 1.3 multiply_reduce_fusion.1
  411.6 2.2 fusion.37
  413.7 1.3 convolution_multiply_fusion
  415.1 36.6 %all-reduce.9.cloned.1.call-done = f32[512,256]{1,0:T(8,128)} async-done(((f32[512,256]{1,0:T(8,128)}), f32[512,256]{1,0:T(8,128)}) %all-reduce.9.cloned.1.call-update) | async-done | bytes 524304 | tf_op jit(solution)/shard_map/psum | solution.py:149
  451.6 1.3 multiply_reduce_fusion
  452.9 2.3 convolution_bitcast_fusion
  455.9 141.1 %psum.61 = f32[]{:T(128)} all-reduce(f32[]{:T(128)S(6)} %div.42), channel_id=1, replica_groups=mesh['sec'=2,'atoms'=32,'batch'=8] {'sec','atoms'}, use_global_device_ids=true, to_apply=%region_11.12 | all-reduce | flops 1 | bytes 8 | tf_op jit(solution)/shard_map/psum | solution.py:152
  597.7 166.3 %all-reduce.11.cloned.1.call-done = f32[1,512,256]{2,1,0:T(8,128)} async-done(((f32[1,512,256]{2,1,0:T(8,128)}), f32[1,512,256]{2,1,0:T(8,128)}) %all-reduce.11.cloned.1.call-update) | async-done | bytes 524304 | tf_op jit(solution)/shard_map/psum | solution.py:153
  763.9 1.9 copy.26
  (54 shorter events, 7.5 us)
Async XLA Ops:
  7.2 17.5 %copy-start = (bf16[1,16,128,128]{3,2,1,0:T(8,128)(2,1)S(1)}, bf16[1,16,128,128]{3,2,1,0:T(8,128)(2,1)}, u32[]{:S(2)}) copy-start(bf16[1,16,128,128]{3,2,1,0:T(8,128)(2,1)} %param.14) | copy-start | bytes 1572868
  7.2 58.1 %all-gather.2.cloned.1.call-start = ((), (), s32[]{:S(2)}) async-start(), calls=%async_computation.1 | async-start | bytes 1572864 | tf_op jit(solution)/shard_map/all_gather | solution.py:121
  8.3 9.0 %collective-permute-start = (bf16[256,512]{1,0:T(8,128)(2,1)S(1)}, bf16[256,512]{1,0:T(8,128)(2,1)S(1)}, u32[]{:S(2)}, u32[]{:S(2)}) collective-permute-start(bf16[256,512]{1,0:T(8,128)(2,1)S(1)} %get-tuple-element.7), channel_id=1, source_target_pairs={{0,8},{8,16},{16,24},{24,32},{32,40},{40,48},{48,56},{56,64},{64,7... | collective-permute-start | bytes 786440 | tf_op jit(solution)/shard_map/ppermute | solution.py:25
  11.8 9.7 %collective-permute-start.1 = (bf16[256,512]{1,0:T(8,128)(2,1)S(1)}, bf16[256,512]{1,0:T(8,128)(2,1)S(1)}, u32[]{:S(2)}, u32[]{:S(2)}) collective-permute-start(bf16[256,512]{1,0:T(8,128)(2,1)S(1)} %get-tuple-element.8), channel_id=1, source_target_pairs={{8,0},{16,8},{24,16},{32,24},{40,32},{48,40},{56,48},{64,56},{72,6... | collective-permute-start | bytes 786440 | tf_op jit(solution)/shard_map/ppermute | solution.py:26
  38.3 1.0 copy-start.1
  39.3 26.0 %copy-start.5 = (bf16[1024,256]{1,0:T(8,128)(2,1)S(1)}, bf16[1024,256]{1,0:T(8,128)(2,1)}, u32[]{:S(2)}) copy-start(bf16[1024,256]{1,0:T(8,128)(2,1)} %param.21) | copy-start | bytes 1572868
  39.5 27.4 %copy-start.8 = (bf16[1024,256]{1,0:T(8,128)(2,1)S(1)}, bf16[1024,256]{1,0:T(8,128)(2,1)}, u32[]{:S(2)}) copy-start(bf16[1024,256]{1,0:T(8,128)(2,1)} %param.20) | copy-start | bytes 1572868
  43.2 306.6 %all-reduce.5.cloned.1.call-start = ((), (), s32[]{:S(2)}) async-start(), calls=%async_computation.2 | async-start | bytes 262144 | tf_op jit(solution)/shard_map/psum | solution.py:135
  67.0 83.8 %copy-start.4 = (bf16[512,1024]{1,0:T(8,128)(2,1)S(1)}, bf16[512,1024]{1,0:T(8,128)(2,1)}, u32[]{:S(2)}) copy-start(bf16[512,1024]{1,0:T(8,128)(2,1)} %all-gather.2.cloned.1.call-done) | copy-start | bytes 3145732
  70.2 300.3 %reduce-scatter.2.cloned.1.call-start = ((), (), s32[]{:S(2)}) async-start(), calls=%async_computation.3 | async-start | bytes 3145728 | tf_op jit(solution)/shard_map/reduce_scatter | solution.py:142
  152.4 201.4 %copy-start.6 = (bf16[256,1024]{1,0:T(8,128)(2,1)S(1)}, bf16[256,1024]{1,0:T(8,128)(2,1)}, u32[]{:S(2)}) copy-start(bf16[256,1024]{1,0:T(8,128)(2,1)} %param.22) | copy-start | bytes 1572868
  355.6 16.2 %copy-start.7 = (bf16[512,256]{1,0:T(8,128)(2,1)S(1)}, bf16[512,256]{1,0:T(8,128)(2,1)}, u32[]{:S(2)}) copy-start(bf16[512,256]{1,0:T(8,128)(2,1)} %param.23) | copy-start | bytes 786436
  355.7 55.9 %copy-start.9 = (bf16[1,128,256]{2,1,0:T(8,128)(2,1)S(1)}, bf16[1,128,256]{2,1,0:T(8,128)(2,1)}, u32[]{:S(2)}) copy-start(bf16[1,128,256]{2,1,0:T(8,128)(2,1)} %param.17) | copy-start | bytes 196612
  355.7 55.9 %copy-start.10 = (s32[1,512]{1,0:T(1,128)S(1)}, s32[1,512]{1,0:T(1,128)}, u32[]{:S(2)}) copy-start(s32[1,512]{1,0:T(1,128)} %param.16) | copy-start | bytes 6148
  355.7 54.6 %all-reduce.7.cloned.1.call-start = ((), (), s32[]{:S(2)}) async-start(), calls=%async_computation.4 | async-start | bytes 1048576 | tf_op jit(solution)/shard_map/psum | solution.py:144
  371.9 81.1 %copy-start.3 = (bf16[512,512]{1,0:T(8,128)(2,1)}, bf16[512,512]{1,0:T(8,128)(2,1)S(1)}, u32[]{:S(2)}) copy-start(bf16[512,512]{1,0:T(8,128)(2,1)S(1)} %fusion.17) | copy-start | bytes 1572868
  373.0 78.6 %all-reduce.9.cloned.1.call-start = ((), (), s32[]{:S(2)}) async-start(), calls=%async_computation.5 | async-start | bytes 1048576 | tf_op jit(solution)/shard_map/psum | solution.py:149
  410.3 41.4 %copy-start.2 = (f32[512,256]{1,0:T(8,128)S(1)}, f32[512,256]{1,0:T(8,128)}, u32[]{:S(2)}) copy-start(f32[512,256]{1,0:T(8,128)} %all-reduce.7.cloned.1.call-done) | copy-start | bytes 1572868
  415.0 348.9 %all-reduce.11.cloned.1.call-start = ((), (), s32[]{:S(2)}) async-start(), calls=%async_computation.6 | async-start | bytes 1048576 | tf_op jit(solution)/shard_map/psum | solution.py:153
Sparse Core Ops, SparseCore 0:
  43.3 21.9 all-gather.1
  70.3 279.3 all-reduce.4
  355.8 14.6 reduce-scatter.1
  373.8 36.4 all-reduce.6
  415.1 36.4 all-reduce.8
  455.4 308.4 all-reduce.10
where the time goes:
time: 775 us; the launch traced here: 774 us
  waiting for transfers between devices  479 us (62%)
  blocking collectives  227 us (29%)
  matrix products  25.2 us (3%)
  between operations  17.4 us (2%)
  local copies, waits for them, and re-layouts  11.7 us (2%)
  other arithmetic  8.46 us (1%)
    psum x1, waiting for transfers between devices, shards(): outer_state, key_total = lax.psum((outer_state, key_total), 'atoms')  197 us
    psum x1, waiting for transfers between devices, shards(): proj_total = lax.psum(proj_part, 'atoms')  166 us
    psum x1, blocking collectives, shards(): lax.psum(loss_part, ('sec', 'atoms'))  141 us
    psum x1, blocking collectives, shards(): outer_state, key_total = lax.psum((outer_state, key_total), 'atoms')  80.4 us
    psum x1, waiting for transfers between devices, shards(): lax.psum(jnp.dot(hidden_two, w_proj, preferred_element_type=jnp.float32),...  37.2 us
    psum x1, waiting for transfers between devices, shards(): unit_grad = lax.psum(unit_grad, 'sec')  36.6 us
    all_gather x1, waiting for transfers between devices, shards(): piece_rows = lax.all_gather(normed, 'sec', axis=1, tiled=True)  21.4 us
  transfers between devices with their start and end apart: 8, of which 8 were waited for; matrix products, arithmetic and copies ran while one was open for 1% of the time, Pallas kernels for 0%

commit v1 on v0

--- a/solution.py
+++ b/solution.py
@@ -25,6 +25,26 @@
         before = lax.ppermute(last, axis, up)
         after = lax.ppermute(leading, axis, down)
         x = jnp.concatenate([before, x, after], axis=dim)
+    return x
+
+
+def swap_sec(x):
+    return lax.ppermute(x, "sec", [(0, 1), (1, 0)])
+
+
+def sum_sec(x):
+    return x + swap_sec(x)
+
+
+def sum_atoms(x):
+    peers = lax.axis_size("atoms")
+    if peers & (peers - 1):
+        return lax.psum(x, "atoms")
+    stride = 1
+    while stride < peers:
+        pairs = [(i, i ^ stride) for i in range(peers)]
+        x = x + lax.ppermute(x, "atoms", pairs)
+        stride *= 2
     return x
 
 
@@ -118,13 +138,16 @@
     row_scale = lax.rsqrt(square_sum[:, None] / D + EPSILON)
     normed = (hidden_f * row_scale * norm_gain.astype(jnp.float32)).astype(jnp.bfloat16)
     head_cols = w_query.shape[1]
-    piece_rows = lax.all_gather(normed, "sec", axis=1, tiled=True)
-    query_f, key_f, value_f = tuple(
-        (
-            jnp.dot(piece_rows, weight, preferred_element_type=jnp.float32)
-            for weight in (w_query, w_key, w_value)
-        )
-    )
+    sec = lax.axis_index("sec")
+    width = normed.shape[1]
+    other_rows = swap_sec(normed)
+
+    def project(weight):
+        halves = weight.reshape(2, width, weight.shape[1])
+        mine = jnp.dot(normed, halves[sec], preferred_element_type=jnp.float32)
+        return mine + jnp.dot(other_rows, halves[1 - sec], preferred_element_type=jnp.float32)
+
+    query_f, key_f, value_f = tuple((project(weight) for weight in (w_query, w_key, w_value)))
     head_count = head_cols // HEAD_DIM
     atom_mask = (atom_base + jnp.arange(local_rows, dtype=jnp.int32) < length_one).astype(
         jnp.float32
@@ -132,25 +155,31 @@
     outer_state, key_total = key_summary(
         key_f.astype(jnp.bfloat16), value_f.astype(jnp.bfloat16), atom_mask, head_count
     )
-    outer_state, key_total = lax.psum((outer_state, key_total), "atoms")
+    packed = sum_atoms(jnp.concatenate([outer_state, key_total[:, None, :]], axis=1))
+    outer_state, key_total = packed[:, :HEAD_DIM, :], packed[:, HEAD_DIM, :]
     attended = read_summary(query_f.astype(jnp.bfloat16), outer_state, key_total, head_count)
     out_sum = lax.psum(jnp.sum(attended * attended, axis=-1), "sec")
     attended_n = (attended * lax.rsqrt(out_sum[:, None] / (HEADS * HEAD_DIM) + EPSILON)).astype(
         jnp.bfloat16
     )
-    branch_full = jnp.dot(attended_n, w_out, preferred_element_type=jnp.float32)
-    branch = lax.psum_scatter(branch_full, "sec", scatter_dimension=1, tiled=True)
+    out_cols = w_out.reshape(w_out.shape[0], 2, width)
+    sent = jnp.dot(attended_n, out_cols[:, 1 - sec, :], preferred_element_type=jnp.float32)
+    kept = jnp.dot(attended_n, out_cols[:, sec, :], preferred_element_type=jnp.float32)
+    branch = kept + swap_sec(sent)
     hidden_two = (hidden_f + branch).astype(jnp.bfloat16)
-    embedded = lax.psum(jnp.dot(hidden_two, w_proj, preferred_element_type=jnp.float32), "sec")
+    embedded = sum_sec(jnp.dot(hidden_two, w_proj, preferred_element_type=jnp.float32))
     embed_scale = lax.rsqrt(jnp.mean(embedded * embedded, axis=-1, keepdims=True) + EPSILON)
     unit_rows = embedded * embed_scale
-    peak_start = lax.axis_index("sec") * peak_part.shape[0]
+    peak_start = sec * peak_part.shape[0]
     loss_part, unit_grad = contrast(unit_rows, peak_part, label_row, atom_mask, peak_start)
-    unit_grad = lax.psum(unit_grad, "sec")
+    unit_grad = sum_sec(unit_grad)
     embed_grad = embed_backward(unit_rows, unit_grad, embed_scale)
     proj_part = jnp.einsum("nd,ne->de", hidden_two, embed_grad, preferred_element_type=jnp.float32)
-    loss_total = lax.psum(loss_part, ("sec", "atoms")) / (local_rows * lax.axis_size("atoms"))
-    proj_total = lax.psum(proj_part, "atoms")
+    loss_pair = sum_sec(loss_part)
+    loss_rows = jnp.zeros((8, proj_part.shape[1]), jnp.float32).at[0, 0].set(loss_pair)
+    packed = sum_atoms(jnp.concatenate([proj_part, loss_rows], axis=0))
+    proj_total = packed[: proj_part.shape[0]]
+    loss_total = packed[proj_part.shape[0], 0] / (local_rows * lax.axis_size("atoms"))
     return (hidden_two[None], loss_total.reshape(1), proj_total[None])
 
 

time: 775 us -> 242 us (0.31)
  waiting for transfers between devices: 479 us -> 134 us
  blocking collectives: 227 us -> 4.93 us
  starting transfers between devices: 5.04 us -> 60.9 us
  between operations: 17.4 us -> 4.89 us
    psum x4 -> x0, waiting for transfers between devices: 437 us -> none  [the longest x1 197 us: shards(): outer_state, key_total = lax.psum((outer_state, key_total), 'atoms')]
    psum x2 -> x0, blocking collectives: 221 us -> none  [the longest x1 141 us: shards(): lax.psum(loss_part, ('sec', 'atoms'))]
    ppermute x0 -> x15, waiting for transfers between devices: none -> 129 us  [the longest x10 125 us: sum_atoms(): x = x + lax.ppermute(x, 'atoms', pairs)]
    ppermute x0 -> x15, starting transfers between devices: none -> 56.1 us  [the longest x10 44.7 us: sum_atoms(): x = x + lax.ppermute(x, 'atoms', pairs)]
    all_gather x1 -> x0, waiting for transfers between devices: 21.4 us -> none  [shards(): piece_rows = lax.all_gather(normed, 'sec', axis=1, tiled=True)]
    reduce_scatter x1 -> x0, waiting for transfers between devices: 14.7 us -> none  [shards(): lax.psum_scatter(branch_full, 'sec', scatter_dimension=1, tiled=True)]
  transfers between devices with their start and end apart: 8 -> 17, of which waited for: 8 -> 14; matrix products, arithmetic and copies ran while one was open for 1% -> 3% of each run, Pallas kernels for 0% -> 0%
where the time goes in v1:
time: 242 us; the launch traced here: 241 us
  waiting for transfers between devices  134 us (55%)
  starting transfers between devices  60.9 us (25%)
  matrix products  18.4 us (8%)
  local copies, waits for them, and re-layouts  12.5 us (5%)
  other arithmetic  4.98 us (2%)
  blocking collectives  4.93 us (2%)
  between operations  4.89 us (2%)
    ppermute x10, waiting for transfers between devices, sum_atoms(): x = x + lax.ppermute(x, 'atoms', pairs)  125 us
    ppermute x10, starting transfers between devices, sum_atoms(): x = x + lax.ppermute(x, 'atoms', pairs)  44.7 us
    ppermute x5, starting transfers between devices, swap_sec(): return lax.ppermute(x, 'sec', [(0, 1), (1, 0)])  11.4 us
    dot_general x1, local copies, waits for them, and re-layouts, message_pass(): jnp.einsum('tij,tjf->tif', tile_block, panels, preferred_element_type=jnp...  5.5 us
  transfers between devices with their start and end apart: 17, of which 14 were waited for; matrix products, arithmetic and copies ran while one was open for 3% of the time, Pallas kernels for 0%

profile of v1, /device:TPU:6, one launch (start us, length us, event | category | flops | bytes accessed | tf_op | source)
XLA Modules:
  0.0 241.0 jit_solution(11074566278863684161)
XLA Ops:
  1.8 3.5 %collective-permute-start = (bf16[256,512]{1,0:T(8,128)(2,1)S(1)}, bf16[256,512]{1,0:T(8,128)(2,1)S(1)}, u32[]{:S(2)}, u32[]{:S(2)}) collective-permute-start(bf16[256,512]{1,0:T(8,128)(2,1)S(1)} %get-tuple-element.23), channel_id=1, source_target_pairs={{0,8},{8,16},{16,24},{24,32},{32,40},{40,48},{48,56},{56,64},{64,7... | collective-permute-start | bytes 786440 | tf_op jit(solution)/shard_map/ppermute | solution.py:25
  10.8 4.1 %collective-permute-done.1 = bf16[256,512]{1,0:T(8,128)(2,1)S(1)} collective-permute-done((bf16[256,512]{1,0:T(8,128)(2,1)S(1)}, bf16[256,512]{1,0:T(8,128)(2,1)S(1)}, u32[]{:S(2)}, u32[]{:S(2)}) %collective-permute-start.1) | collective-permute-done | bytes 262176 | tf_op jit(solution)/shard_map/ppermute | solution.py:26
  16.0 2.0 gather_fusion
  18.1 4.4 %convolution_bitcast_fusion = f32[16,128,512]{1,2,0:T(8,128)} fusion(bf16[16,128,512]{2,1,0:T(8,128)(2,1)} %gather_fusion, pred[16]{0:T(512)(128)(4,1)S(1)} %get-tuple-element.21, bf16[1,16,128,128]{3,2,1,0:T(8,128)(2,1)S(1)} %copy-done), kind=kOutput, calls=%fused_computation.1 | convolution fusion | flops 269484032 | bytes 6815760 | tf_op jit(solution)/shard_map/tij,tjf->tif/dot_general | solution.py:69
  22.5 5.5 %copy.26 = f32[16,128,512]{2,0,1:T(8,128)} copy(f32[16,128,512]{1,2,0:T(8,128)} %convolution_bitcast_fusion) | data formatting | bytes 8388608 | tf_op jit(solution)/shard_map/tij,tjf->tif/dot_general | solution.py:69
  28.0 3.7 %fusion.2 = f32[4,128,512]{2,0,1:T(4,128)S(1)} fusion(f32[16,128,512]{2,0,1:T(8,128)} %copy.26, s32[16]{0:T(128)S(1)} %fusion.83), kind=kOutput, calls=%fused_computation.13 | convolution fusion | flops 50856000 | bytes 5242944 | tf_op jit(solution)/shard_map/bt,tif->bif/dot_general | solution.py:73
  33.0 2.5 %psum.14 = f32[512]{0:T(512)S(1)} all-reduce(f32[512]{0:T(512)S(1)} %get-tuple-element.19), channel_id=1, replica_groups=mesh['sec'=2,'atoms'=32,'batch'=8] {'sec'}, use_global_device_ids=true, to_apply=%region_1.2 | all-reduce | flops 512 | bytes 4096 | tf_op jit(solution)/shard_map/psum | solution.py:137
  35.6 2.1 collective-permute-start.2
  43.3 3.6 %collective-permute-start.3 = (f32[4,65,64]{1,2,0:T(8,128)S(1)}, f32[4,65,64]{1,2,0:T(8,128)S(1)}, u32[]{:S(2)}, u32[]{:S(2)}) collective-permute-start(f32[4,65,64]{1,2,0:T(8,128)S(1)} %pad_maximum_fusion.1), channel_id=1, source_target_pairs={{0,8},{8,0},{16,24},{24,16},{32,40},{40,32},{48,56},{56,48},{64,72... | collective-permute-start | bytes 199688 | tf_op jit(solution)/shard_map/ppermute | solution.py:46
  47.0 4.2 %collective-permute-done.3 = f32[4,65,64]{1,2,0:T(8,128)S(1)} collective-permute-done((f32[4,65,64]{1,2,0:T(8,128)S(1)}, f32[4,65,64]{1,2,0:T(8,128)S(1)}, u32[]{:S(2)}, u32[]{:S(2)}) %collective-permute-start.3) | collective-permute-done | bytes 66592 | tf_op jit(solution)/shard_map/ppermute | solution.py:46
  51.2 6.8 %collective-permute-start.4 = (f32[4,65,64]{1,2,0:T(8,128)S(1)}, f32[4,65,64]{1,2,0:T(8,128)S(1)}, u32[]{:S(2)}, u32[]{:S(2)}) collective-permute-start(f32[4,65,64]{1,2,0:T(8,128)S(1)} %fusion.108), channel_id=1, source_target_pairs={{0,16},{8,24},{16,0},{24,8},{32,48},{40,56},{48,32},{56,40},{64,80... | collective-permute-start | bytes 199688 | tf_op jit(solution)/shard_map/ppermute | solution.py:46
  58.0 6.2 %collective-permute-done.4 = f32[4,65,64]{1,2,0:T(8,128)S(1)} collective-permute-done((f32[4,65,64]{1,2,0:T(8,128)S(1)}, f32[4,65,64]{1,2,0:T(8,128)S(1)}, u32[]{:S(2)}, u32[]{:S(2)}) %collective-permute-start.4) | collective-permute-done | bytes 66592 | tf_op jit(solution)/shard_map/ppermute | solution.py:46
  64.2 4.8 %collective-permute-start.5 = (f32[4,65,64]{1,2,0:T(8,128)S(1)}, f32[4,65,64]{1,2,0:T(8,128)S(1)}, u32[]{:S(2)}, u32[]{:S(2)}) collective-permute-start(f32[4,65,64]{1,2,0:T(8,128)S(1)} %add.180), channel_id=1, source_target_pairs={{0,32},{8,40},{16,48},{24,56},{32,0},{40,8},{48,16},{56,24},{64,96... | collective-permute-start | bytes 199688 | tf_op jit(solution)/shard_map/ppermute | solution.py:46
  69.3 7.8 %collective-permute-done.5 = f32[4,65,64]{1,2,0:T(8,128)S(1)} collective-permute-done((f32[4,65,64]{1,2,0:T(8,128)S(1)}, f32[4,65,64]{1,2,0:T(8,128)S(1)}, u32[]{:S(2)}, u32[]{:S(2)}) %collective-permute-start.5) | collective-permute-done | bytes 66592 | tf_op jit(solution)/shard_map/ppermute | solution.py:46
  77.1 4.2 %collective-permute-start.6 = (f32[4,65,64]{1,2,0:T(8,128)S(1)}, f32[4,65,64]{1,2,0:T(8,128)S(1)}, u32[]{:S(2)}, u32[]{:S(2)}) collective-permute-start(f32[4,65,64]{1,2,0:T(8,128)S(1)} %add.181), channel_id=1, source_target_pairs={{0,64},{8,72},{16,80},{24,88},{32,96},{40,104},{48,112},{56,120},{... | collective-permute-start | bytes 199688 | tf_op jit(solution)/shard_map/ppermute | solution.py:46
  84.4 7.1 %collective-permute-start.7 = (f32[4,65,64]{1,2,0:T(8,128)S(1)}, f32[4,65,64]{1,2,0:T(8,128)S(1)}, u32[]{:S(2)}, u32[]{:S(2)}) collective-permute-start(f32[4,65,64]{1,2,0:T(8,128)S(1)} %add.182), channel_id=1, source_target_pairs={{0,128},{8,136},{16,144},{24,152},{32,160},{40,168},{48,176},{56,1... | collective-permute-start | bytes 199688 | tf_op jit(solution)/shard_map/ppermute | solution.py:46
  92.0 5.4 %collective-permute-done.7 = f32[4,65,64]{1,2,0:T(8,128)S(1)} collective-permute-done((f32[4,65,64]{1,2,0:T(8,128)S(1)}, f32[4,65,64]{1,2,0:T(8,128)S(1)}, u32[]{:S(2)}, u32[]{:S(2)}) %collective-permute-start.7) | collective-permute-done | bytes 66592 | tf_op jit(solution)/shard_map/ppermute | solution.py:46
  98.6 2.5 %psum.15 = f32[512]{0:T(512)S(1)} all-reduce(f32[512]{0:T(512)S(1)} %get-tuple-element.27), channel_id=1, replica_groups=mesh['sec'=2,'atoms'=32,'batch'=8] {'sec'}, use_global_device_ids=true, to_apply=%region_4.5 | all-reduce | flops 512 | bytes 4096 | tf_op jit(solution)/shard_map/psum | solution.py:161
  101.5 2.1 collective-permute-start.8
  103.6 2.5 %collective-permute-done.8 = f32[512,512]{1,0:T(8,128)S(1)} collective-permute-done((f32[512,512]{1,0:T(8,128)S(1)}, f32[512,512]{1,0:T(8,128)S(1)}, u32[]{:S(2)}, u32[]{:S(2)}) %collective-permute-start.8) | collective-permute-done | bytes 1048608 | tf_op jit(solution)/shard_map/ppermute | solution.py:32
  106.8 2.1 collective-permute-start.9
  112.7 2.1 collective-permute-start.10
  115.4 3.0 %collective-permute-start.11 = (f32[]{:T(128)}, f32[]{:T(128)}, u32[]{:S(2)}, u32[]{:S(2)}) collective-permute-start(f32[]{:T(128)} %div.44), channel_id=1, source_target_pairs={{0,256},{256,0},{1,257},{257,1},{2,258},{258,2},{3,259},{259,3},{4... | collective-permute-start | bytes 20 | tf_op jit(solution)/shard_map/ppermute | solution.py:32
  121.6 14.2 %collective-permute-done.12 = f32[520,256]{1,0:T(8,128)S(1)} collective-permute-done((f32[520,256]{1,0:T(8,128)S(1)}, f32[520,256]{1,0:T(8,128)S(1)}, u32[]{:S(2)}, u32[]{:S(2)}) %collective-permute-start.12) | collective-permute-done | bytes 532512 | tf_op jit(solution)/shard_map/ppermute | solution.py:46
  136.0 3.6 %collective-permute-start.13 = (f32[520,256]{1,0:T(8,128)S(1)}, f32[520,256]{1,0:T(8,128)S(1)}, u32[]{:S(2)}, u32[]{:S(2)}) collective-permute-start(f32[520,256]{1,0:T(8,128)S(1)} %fusion.88), channel_id=1, source_target_pairs={{0,16},{8,24},{16,0},{24,8},{32,48},{40,56},{48,32},{56,40},{64,80... | collective-permute-start | bytes 1597448 | tf_op jit(solution)/shard_map/ppermute | solution.py:46
  139.6 24.1 %collective-permute-done.13 = f32[520,256]{1,0:T(8,128)S(1)} collective-permute-done((f32[520,256]{1,0:T(8,128)S(1)}, f32[520,256]{1,0:T(8,128)S(1)}, u32[]{:S(2)}, u32[]{:S(2)}) %collective-permute-start.13) | collective-permute-done | bytes 532512 | tf_op jit(solution)/shard_map/ppermute | solution.py:46
  163.7 4.7 %collective-permute-start.14 = (f32[520,256]{1,0:T(8,128)S(1)}, f32[520,256]{1,0:T(8,128)S(1)}, u32[]{:S(2)}, u32[]{:S(2)}) collective-permute-start(f32[520,256]{1,0:T(8,128)S(1)} %add.198), channel_id=1, source_target_pairs={{0,32},{8,40},{16,48},{24,56},{32,0},{40,8},{48,16},{56,24},{64,96... | collective-permute-start | bytes 1597448 | tf_op jit(solution)/shard_map/ppermute | solution.py:46
  168.4 25.3 %collective-permute-done.14 = f32[520,256]{1,0:T(8,128)S(1)} collective-permute-done((f32[520,256]{1,0:T(8,128)S(1)}, f32[520,256]{1,0:T(8,128)S(1)}, u32[]{:S(2)}, u32[]{:S(2)}) %collective-permute-start.14) | collective-permute-done | bytes 532512 | tf_op jit(solution)/shard_map/ppermute | solution.py:46
  193.8 3.2 %collective-permute-start.15 = (f32[520,256]{1,0:T(8,128)S(1)}, f32[520,256]{1,0:T(8,128)S(1)}, u32[]{:S(2)}, u32[]{:S(2)}) collective-permute-start(f32[520,256]{1,0:T(8,128)S(1)} %add.199), channel_id=1, source_target_pairs={{0,64},{8,72},{16,80},{24,88},{32,96},{40,104},{48,112},{56,120},{... | collective-permute-start | bytes 1597448 | tf_op jit(solution)/shard_map/ppermute | solution.py:46
  197.0 12.7 %collective-permute-done.15 = f32[520,256]{1,0:T(8,128)S(1)} collective-permute-done((f32[520,256]{1,0:T(8,128)S(1)}, f32[520,256]{1,0:T(8,128)S(1)}, u32[]{:S(2)}, u32[]{:S(2)}) %collective-permute-start.15) | collective-permute-done | bytes 532512 | tf_op jit(solution)/shard_map/ppermute | solution.py:46
  209.8 4.8 %collective-permute-start.16 = (f32[520,256]{1,0:T(8,128)S(1)}, f32[520,256]{1,0:T(8,128)S(1)}, u32[]{:S(2)}, u32[]{:S(2)}) collective-permute-start(f32[520,256]{1,0:T(8,128)S(1)} %add.200), channel_id=1, source_target_pairs={{0,128},{8,136},{16,144},{24,152},{32,160},{40,168},{48,176},{56,1... | collective-permute-start | bytes 1597448 | tf_op jit(solution)/shard_map/ppermute | solution.py:46
  214.6 23.1 %collective-permute-done.16 = f32[520,256]{1,0:T(8,128)S(1)} collective-permute-done((f32[520,256]{1,0:T(8,128)S(1)}, f32[520,256]{1,0:T(8,128)S(1)}, u32[]{:S(2)}, u32[]{:S(2)}) %collective-permute-start.16) | collective-permute-done | bytes 532512 | tf_op jit(solution)/shard_map/ppermute | solution.py:46
  (87 shorter events, 28.2 us)
Async XLA Ops:
  0.6 17.4 %copy-start = (bf16[1,16,128,128]{3,2,1,0:T(8,128)(2,1)S(1)}, bf16[1,16,128,128]{3,2,1,0:T(8,128)(2,1)}, u32[]{:S(2)}) copy-start(bf16[1,16,128,128]{3,2,1,0:T(8,128)(2,1)} %param.16) | copy-start | bytes 1572868
  1.8 9.0 %collective-permute-start = (bf16[256,512]{1,0:T(8,128)(2,1)S(1)}, bf16[256,512]{1,0:T(8,128)(2,1)S(1)}, u32[]{:S(2)}, u32[]{:S(2)}) collective-permute-start(bf16[256,512]{1,0:T(8,128)(2,1)S(1)} %get-tuple-element.23), channel_id=1, source_target_pairs={{0,8},{8,16},{16,24},{24,32},{32,40},{40,48},{48,56},{56,64},{64,7... | collective-permute-start | bytes 786440 | tf_op jit(solution)/shard_map/ppermute | solution.py:25
  5.3 9.7 %collective-permute-start.1 = (bf16[256,512]{1,0:T(8,128)(2,1)S(1)}, bf16[256,512]{1,0:T(8,128)(2,1)S(1)}, u32[]{:S(2)}, u32[]{:S(2)}) collective-permute-start(bf16[256,512]{1,0:T(8,128)(2,1)S(1)} %get-tuple-element.24), channel_id=1, source_target_pairs={{8,0},{16,8},{24,16},{32,24},{40,32},{48,40},{56,48},{64,56},{72,6... | collective-permute-start | bytes 786440 | tf_op jit(solution)/shard_map/ppermute | solution.py:26
  31.7 1.0 copy-start.1
  35.4 3.9 %copy-start.5 = (bf16[1024,256]{1,0:T(8,128)(2,1)S(1)}, bf16[1024,256]{1,0:T(8,128)(2,1)}, u32[]{:S(2)}) copy-start(bf16[1024,256]{1,0:T(8,128)(2,1)} %param.23) | copy-start | bytes 1572868
  35.6 4.0 %collective-permute-start.2 = (bf16[512,512]{1,0:T(8,128)(2,1)S(1)}, bf16[512,512]{1,0:T(8,128)(2,1)S(1)}, u32[]{:S(2)}, u32[]{:S(2)}) collective-permute-start(bf16[512,512]{1,0:T(8,128)(2,1)S(1)} %fusion.12), channel_id=1, source_target_pairs={{0,256},{256,0},{1,257},{257,1},{2,258},{258,2},{3,259},{259,3},{4... | collective-permute-start | bytes 1572872 | tf_op jit(solution)/shard_map/ppermute | solution.py:32
  37.7 2.8 %copy-start.10 = (bf16[1024,256]{1,0:T(8,128)(2,1)S(1)}, bf16[1024,256]{1,0:T(8,128)(2,1)}, u32[]{:S(2)}) copy-start(bf16[1024,256]{1,0:T(8,128)(2,1)} %param.22) | copy-start | bytes 1572868
  37.9 3.4 %copy-start.6 = (bf16[1024,256]{1,0:T(8,128)(2,1)S(1)}, bf16[1024,256]{1,0:T(8,128)(2,1)}, u32[]{:S(2)}) copy-start(bf16[1024,256]{1,0:T(8,128)(2,1)} %param.23) | copy-start | bytes 1572868
  39.7 0.8 copy-start.3
  42.7 26.3 %copy-start.7 = (bf16[256,1024]{1,0:T(8,128)(2,1)S(1)}, bf16[256,1024]{1,0:T(8,128)(2,1)}, u32[]{:S(2)}) copy-start(bf16[256,1024]{1,0:T(8,128)(2,1)} %param.24) | copy-start | bytes 1572868
  43.3 48.2 %copy-start.4 = (bf16[512,512]{1,0:T(8,128)(2,1)S(1)}, bf16[512,512]{1,0:T(8,128)(2,1)}, u32[]{:S(2)}) copy-start(bf16[512,512]{1,0:T(8,128)(2,1)} %copy-done.3) | copy-start | bytes 1572868
  43.3 7.8 %collective-permute-start.3 = (f32[4,65,64]{1,2,0:T(8,128)S(1)}, f32[4,65,64]{1,2,0:T(8,128)S(1)}, u32[]{:S(2)}, u32[]{:S(2)}) collective-permute-start(f32[4,65,64]{1,2,0:T(8,128)S(1)} %pad_maximum_fusion.1), channel_id=1, source_target_pairs={{0,8},{8,0},{16,24},{24,16},{32,40},{40,32},{48,56},{56,48},{64,72... | collective-permute-start | bytes 199688 | tf_op jit(solution)/shard_map/ppermute | solution.py:46
  51.2 13.0 %collective-permute-start.4 = (f32[4,65,64]{1,2,0:T(8,128)S(1)}, f32[4,65,64]{1,2,0:T(8,128)S(1)}, u32[]{:S(2)}, u32[]{:S(2)}) collective-permute-start(f32[4,65,64]{1,2,0:T(8,128)S(1)} %fusion.108), channel_id=1, source_target_pairs={{0,16},{8,24},{16,0},{24,8},{32,48},{40,56},{48,32},{56,40},{64,80... | collective-permute-start | bytes 199688 | tf_op jit(solution)/shard_map/ppermute | solution.py:46
  64.2 12.9 %collective-permute-start.5 = (f32[4,65,64]{1,2,0:T(8,128)S(1)}, f32[4,65,64]{1,2,0:T(8,128)S(1)}, u32[]{:S(2)}, u32[]{:S(2)}) collective-permute-start(f32[4,65,64]{1,2,0:T(8,128)S(1)} %add.180), channel_id=1, source_target_pairs={{0,32},{8,40},{16,48},{24,56},{32,0},{40,8},{48,16},{56,24},{64,96... | collective-permute-start | bytes 199688 | tf_op jit(solution)/shard_map/ppermute | solution.py:46
  69.3 22.2 %copy-start.8 = (bf16[1024,256]{1,0:T(8,128)(2,1)S(1)}, bf16[1024,256]{1,0:T(8,128)(2,1)}, u32[]{:S(2)}) copy-start(bf16[1024,256]{1,0:T(8,128)(2,1)} %param.21) | copy-start | bytes 1572868
  77.1 7.2 %collective-permute-start.6 = (f32[4,65,64]{1,2,0:T(8,128)S(1)}, f32[4,65,64]{1,2,0:T(8,128)S(1)}, u32[]{:S(2)}, u32[]{:S(2)}) collective-permute-start(f32[4,65,64]{1,2,0:T(8,128)S(1)} %add.181), channel_id=1, source_target_pairs={{0,64},{8,72},{16,80},{24,88},{32,96},{40,104},{48,112},{56,120},{... | collective-permute-start | bytes 199688 | tf_op jit(solution)/shard_map/ppermute | solution.py:46
  84.4 13.0 %collective-permute-start.7 = (f32[4,65,64]{1,2,0:T(8,128)S(1)}, f32[4,65,64]{1,2,0:T(8,128)S(1)}, u32[]{:S(2)}, u32[]{:S(2)}) collective-permute-start(f32[4,65,64]{1,2,0:T(8,128)S(1)} %add.182), channel_id=1, source_target_pairs={{0,128},{8,136},{16,144},{24,152},{32,160},{40,168},{48,176},{56,1... | collective-permute-start | bytes 199688 | tf_op jit(solution)/shard_map/ppermute | solution.py:46
  101.2 5.3 %copy-start.9 = (bf16[512,256]{1,0:T(8,128)(2,1)S(1)}, bf16[512,256]{1,0:T(8,128)(2,1)}, u32[]{:S(2)}) copy-start(bf16[512,256]{1,0:T(8,128)(2,1)} %param.25) | copy-start | bytes 786436
  101.5 4.6 %collective-permute-start.8 = (f32[512,512]{1,0:T(8,128)S(1)}, f32[512,512]{1,0:T(8,128)S(1)}, u32[]{:S(2)}, u32[]{:S(2)}) collective-permute-start(f32[512,512]{1,0:T(8,128)S(1)} %fusion.35), channel_id=1, source_target_pairs={{0,256},{256,0},{1,257},{257,1},{2,258},{258,2},{3,259},{259,3},{4... | collective-permute-start | bytes 3145736 | tf_op jit(solution)/shard_map/ppermute | solution.py:32
  106.4 12.9 %copy-start.2 = (bf16[512,512]{1,0:T(8,128)(2,1)}, bf16[512,512]{1,0:T(8,128)(2,1)S(1)}, u32[]{:S(2)}) copy-start(bf16[512,512]{1,0:T(8,128)(2,1)S(1)} %fusion.3) | copy-start | bytes 1572868
  106.5 4.3 %copy-start.11 = (bf16[1,128,256]{2,1,0:T(8,128)(2,1)S(1)}, bf16[1,128,256]{2,1,0:T(8,128)(2,1)}, u32[]{:S(2)}) copy-start(bf16[1,128,256]{2,1,0:T(8,128)(2,1)} %param.19) | copy-start | bytes 196612
  106.5 4.3 %copy-start.12 = (s32[1,512]{1,0:T(1,128)S(1)}, s32[1,512]{1,0:T(1,128)}, u32[]{:S(2)}) copy-start(s32[1,512]{1,0:T(1,128)} %param.18) | copy-start | bytes 6148
  106.8 3.8 %collective-permute-start.9 = (f32[512,256]{0,1:T(8,128)S(1)}, f32[512,256]{0,1:T(8,128)S(1)}, u32[]{:S(2)}, u32[]{:S(2)}) collective-permute-start(f32[512,256]{0,1:T(8,128)S(1)} %fusion.91), channel_id=1, source_target_pairs={{0,256},{256,0},{1,257},{257,1},{2,258},{258,2},{3,259},{259,3},{4... | collective-permute-start | bytes 1572872 | tf_op jit(solution)/shard_map/ppermute | solution.py:32
  112.7 6.4 %collective-permute-start.10 = (f32[512,256]{0,1:T(8,128)S(1)}, f32[512,256]{0,1:T(8,128)S(1)}, u32[]{:S(2)}, u32[]{:S(2)}) collective-permute-start(f32[512,256]{0,1:T(8,128)S(1)} %convolution_multiply_fusion), channel_id=1, source_target_pairs={{0,256},{256,0},{1,257},{257,1},{2,258},{258,2},{3,259},{259,3},{4... | collective-permute-start | bytes 1572872 | tf_op jit(solution)/shard_map/ppermute | solution.py:32
  115.4 3.1 %collective-permute-start.11 = (f32[]{:T(128)}, f32[]{:T(128)}, u32[]{:S(2)}, u32[]{:S(2)}) collective-permute-start(f32[]{:T(128)} %div.44), channel_id=1, source_target_pairs={{0,256},{256,0},{1,257},{257,1},{2,258},{258,2},{3,259},{259,3},{4... | collective-permute-start | bytes 20 | tf_op jit(solution)/shard_map/ppermute | solution.py:32
  119.7 16.2 %collective-permute-start.12 = (f32[520,256]{1,0:T(8,128)S(1)}, f32[520,256]{1,0:T(8,128)S(1)}, u32[]{:S(2)}, u32[]{:S(2)}) collective-permute-start(f32[520,256]{1,0:T(8,128)S(1)} %select_maximum_fusion), channel_id=1, source_target_pairs={{0,8},{8,0},{16,24},{24,16},{32,40},{40,32},{48,56},{56,48},{64,72... | collective-permute-start | bytes 1597448 | tf_op jit(solution)/shard_map/ppermute | solution.py:46
  136.0 27.7 %collective-permute-start.13 = (f32[520,256]{1,0:T(8,128)S(1)}, f32[520,256]{1,0:T(8,128)S(1)}, u32[]{:S(2)}, u32[]{:S(2)}) collective-permute-start(f32[520,256]{1,0:T(8,128)S(1)} %fusion.88), channel_id=1, source_target_pairs={{0,16},{8,24},{16,0},{24,8},{32,48},{40,56},{48,32},{56,40},{64,80... | collective-permute-start | bytes 1597448 | tf_op jit(solution)/shard_map/ppermute | solution.py:46
  163.7 30.0 %collective-permute-start.14 = (f32[520,256]{1,0:T(8,128)S(1)}, f32[520,256]{1,0:T(8,128)S(1)}, u32[]{:S(2)}, u32[]{:S(2)}) collective-permute-start(f32[520,256]{1,0:T(8,128)S(1)} %add.198), channel_id=1, source_target_pairs={{0,32},{8,40},{16,48},{24,56},{32,0},{40,8},{48,16},{56,24},{64,96... | collective-permute-start | bytes 1597448 | tf_op jit(solution)/shard_map/ppermute | solution.py:46
  193.8 15.9 %collective-permute-start.15 = (f32[520,256]{1,0:T(8,128)S(1)}, f32[520,256]{1,0:T(8,128)S(1)}, u32[]{:S(2)}, u32[]{:S(2)}) collective-permute-start(f32[520,256]{1,0:T(8,128)S(1)} %add.199), channel_id=1, source_target_pairs={{0,64},{8,72},{16,80},{24,88},{32,96},{40,104},{48,112},{56,120},{... | collective-permute-start | bytes 1597448 | tf_op jit(solution)/shard_map/ppermute | solution.py:46
  209.8 28.0 %collective-permute-start.16 = (f32[520,256]{1,0:T(8,128)S(1)}, f32[520,256]{1,0:T(8,128)S(1)}, u32[]{:S(2)}, u32[]{:S(2)}) collective-permute-start(f32[520,256]{1,0:T(8,128)S(1)} %add.200), channel_id=1, source_target_pairs={{0,128},{8,136},{16,144},{24,152},{32,160},{40,168},{48,176},{56,1... | collective-permute-start | bytes 1597448 | tf_op jit(solution)/shard_map/ppermute | solution.py:46

commit v2 on v1

--- a/solution.py
+++ b/solution.py
@@ -36,16 +36,25 @@
     return x + swap_sec(x)
 
 
+def butterfly(x, strides):
+    peers = lax.axis_size("atoms")
+    for stride in strides:
+        pairs = [(i, i ^ stride) for i in range(peers)]
+        x = x + lax.ppermute(x, "atoms", pairs)
+    return x
+
+
 def sum_atoms(x):
     peers = lax.axis_size("atoms")
     if peers & (peers - 1):
         return lax.psum(x, "atoms")
-    stride = 1
-    while stride < peers:
-        pairs = [(i, i ^ stride) for i in range(peers)]
-        x = x + lax.ppermute(x, "atoms", pairs)
-        stride *= 2
-    return x
+    inner = min(peers, 8)
+    low = [1 << k for k in range(inner.bit_length() - 1)]
+    high = [inner << k for k in range((peers // inner).bit_length() - 1)]
+    half = (x.shape[0] // 2 + 7) // 8 * 8
+    first = butterfly(x[:half], low + high)
+    second = butterfly(x[half:], high + low)
+    return jnp.concatenate([first, second], axis=0)
 
 
 def feature_map(values):
@@ -66,11 +75,9 @@
     col_local = jnp.where(live_tiles, col_ids - first_block + reach_blocks, 0)
     row_local = jnp.where(live_tiles, row_ids - first_block, -1)
     panels = jnp.take(blocks, col_local, axis=0)
-    products = jnp.einsum("tij,tjf->tif", tile_block, panels, preferred_element_type=jnp.float32)
-    selector = (row_local[None, :] == jnp.arange(block_count, dtype=jnp.int32)[:, None]).astype(
-        jnp.float32
-    )
-    summed = jnp.einsum("bt,tif->bif", selector, products, precision=HIGHEST)
+    selector = row_local[None, :] == jnp.arange(block_count, dtype=jnp.int32)[:, None]
+    masked = jnp.where(selector[:, :, None, None], tile_block[None], jnp.zeros_like(tile_block[None]))
+    summed = jnp.einsum("btij,tjf->bif", masked, panels, preferred_element_type=jnp.float32)
     return summed.reshape(local_rows, half_width).astype(jnp.bfloat16)
 
 
@@ -155,7 +162,8 @@
     outer_state, key_total = key_summary(
         key_f.astype(jnp.bfloat16), value_f.astype(jnp.bfloat16), atom_mask, head_count
     )
-    packed = sum_atoms(jnp.concatenate([outer_state, key_total[:, None, :]], axis=1))
+    state_rows = jnp.concatenate([outer_state, key_total[:, None, :]], axis=1)
+    packed = sum_atoms(state_rows.reshape(-1, HEAD_DIM)).reshape(state_rows.shape)
     outer_state, key_total = packed[:, :HEAD_DIM, :], packed[:, HEAD_DIM, :]
     attended = read_summary(query_f.astype(jnp.bfloat16), outer_state, key_total, head_count)
     out_sum = lax.psum(jnp.sum(attended * attended, axis=-1), "sec")

time: 242 us -> 191 us (0.79)
  waiting for transfers between devices: 134 us -> 59 us
  starting transfers between devices: 60.9 us -> 95.3 us
  local copies, waits for them, and re-layouts: 12.5 us -> 5.58 us
  matrix products: 18.4 us -> 13.2 us
    ppermute x10 -> x20, waiting for transfers between devices: 125 us -> 46.5 us  [butterfly(): x = x + lax.ppermute(x, 'atoms', pairs)]
    ppermute x10 -> x20, starting transfers between devices: 44.7 us -> 79.5 us  [butterfly(): x = x + lax.ppermute(x, 'atoms', pairs)]
    dot_general x1 -> x0, local copies, waits for them, and re-layouts: 5.5 us -> none  [message_pass(): jnp.einsum('tij,tjf->tif', tile_block, panels, preferred_element_type=jnp...]
    dot_general x2 -> x1, matrix products: 8.13 us -> 2.99 us  [message_pass(): jnp.einsum('btij,tjf->bif', masked, panels, preferred_element_type=jnp.fl...]
    ppermute x5, waiting for transfers between devices: 4.18 us -> 6.95 us  [swap_sec(): return lax.ppermute(x, 'sec', [(0, 1), (1, 0)])]
  transfers between devices with their start and end apart: 17 -> 27, of which waited for: 14 -> 17; matrix products, arithmetic and copies ran while one was open for 3% -> 4% of each run, Pallas kernels for 0% -> 0%
where the time goes in v2:
time: 191 us; the launch traced here: 189 us
  starting transfers between devices  95.3 us (50%)
  waiting for transfers between devices  59 us (31%)
  matrix products  13.2 us (7%)
  other arithmetic  5.8 us (3%)
  local copies, waits for them, and re-layouts  5.58 us (3%)
  between operations  5.11 us (3%)
  blocking collectives  4.93 us (3%)
    ppermute x20, starting transfers between devices, butterfly(): x = x + lax.ppermute(x, 'atoms', pairs)  79.5 us
    ppermute x20, waiting for transfers between devices, butterfly(): x = x + lax.ppermute(x, 'atoms', pairs)  46.5 us
    ppermute x5, starting transfers between devices, swap_sec(): return lax.ppermute(x, 'sec', [(0, 1), (1, 0)])  11 us
    ppermute x5, waiting for transfers between devices, swap_sec(): return lax.ppermute(x, 'sec', [(0, 1), (1, 0)])  6.95 us
    ppermute x1, waiting for transfers between devices, extended(): after = lax.ppermute(leading, axis, down)  4.13 us
  transfers between devices with their start and end apart: 27, of which 17 were waited for; matrix products, arithmetic and copies ran while one was open for 4% of the time, Pallas kernels for 0%

profile of v2, /device:TPU:6, one launch (start us, length us, event | category | flops | bytes accessed | tf_op | source)
XLA Modules:
  0.0 189.0 jit_solution(11128795602440994384)
XLA Ops:
  1.8 3.5 %collective-permute-start = (bf16[256,512]{1,0:T(8,128)(2,1)S(1)}, bf16[256,512]{1,0:T(8,128)(2,1)S(1)}, u32[]{:S(2)}, u32[]{:S(2)}) collective-permute-start(bf16[256,512]{1,0:T(8,128)(2,1)S(1)} %get-tuple-element.23), channel_id=1, source_target_pairs={{0,8},{8,16},{16,24},{24,32},{32,40},{40,48},{48,56},{56,64},{64,7... | collective-permute-start | bytes 786440 | tf_op jit(solution)/shard_map/ppermute | solution.py:25
  10.8 4.1 %collective-permute-done.1 = bf16[256,512]{1,0:T(8,128)(2,1)S(1)} collective-permute-done((bf16[256,512]{1,0:T(8,128)(2,1)S(1)}, bf16[256,512]{1,0:T(8,128)(2,1)S(1)}, u32[]{:S(2)}, u32[]{:S(2)}) %collective-permute-start.1) | collective-permute-done | bytes 262176 | tf_op jit(solution)/shard_map/ppermute | solution.py:26
  18.1 3.0 %fusion.16 = f32[4,128,512]{2,1,0:T(8,128)S(1)} fusion(bf16[16,128,512]{2,1,0:T(8,128)(2,1)} %gather_fusion, pred[16]{0:T(512)(128)(4,1)S(1)} %get-tuple-element.21, pred[4,16]{1,0:T(4,128)(4,1)S(1)} %iota_compare_fusion, bf16[16,128,128]{2,1,0:T(8,128)(2,1)S(1)} %bitcast.152), kind=kOutput, calls=%fused_computation.17 | convolution fusion | flops 1076363264 | bytes 3670096 | tf_op jit(solution)/shard_map/btij,tjf->bif/dot_general | solution.py:80
  31.7 3.5 %collective-permute-start.3 = (f32[136,64]{0,1:T(8,128)S(1)}, f32[136,64]{0,1:T(8,128)S(1)}, u32[]{:S(2)}, u32[]{:S(2)}) collective-permute-start(f32[136,64]{0,1:T(8,128)S(1)} %slice.76), channel_id=1, source_target_pairs={{0,8},{8,0},{16,24},{24,16},{32,40},{40,32},{48,56},{56,48},{64,72... | collective-permute-start | bytes 104456 | tf_op jit(solution)/shard_map/ppermute | solution.py:43
  35.2 4.3 %collective-permute-start.8 = (f32[124,64]{0,1:T(8,128)S(1)}, f32[124,64]{0,1:T(8,128)S(1)}, u32[]{:S(2)}, u32[]{:S(2)}) collective-permute-start(f32[124,64]{0,1:T(8,128)S(1)} %slice.77), channel_id=1, source_target_pairs={{0,64},{8,72},{16,80},{24,88},{32,96},{40,104},{48,112},{56,120},{... | collective-permute-start | bytes 95240 | tf_op jit(solution)/shard_map/ppermute | solution.py:43
  39.5 6.9 %collective-permute-start.4 = (f32[136,64]{0,1:T(8,128)S(1)}, f32[136,64]{0,1:T(8,128)S(1)}, u32[]{:S(2)}, u32[]{:S(2)}) collective-permute-start(f32[136,64]{0,1:T(8,128)S(1)} %slice_add_fusion.1), channel_id=1, source_target_pairs={{0,16},{8,24},{16,0},{24,8},{32,48},{40,56},{48,32},{56,40},{64,80... | collective-permute-start | bytes 104456 | tf_op jit(solution)/shard_map/ppermute | solution.py:43
  46.5 6.1 %collective-permute-start.9 = (f32[124,64]{0,1:T(8,128)S(1)}, f32[124,64]{0,1:T(8,128)S(1)}, u32[]{:S(2)}, u32[]{:S(2)}) collective-permute-start(f32[124,64]{0,1:T(8,128)S(1)} %slice_add_fusion), channel_id=1, source_target_pairs={{0,128},{8,136},{16,144},{24,152},{32,160},{40,168},{48,176},{56,1... | collective-permute-start | bytes 95240 | tf_op jit(solution)/shard_map/ppermute | solution.py:43
  52.6 2.8 %collective-permute-start.5 = (f32[136,64]{0,1:T(8,128)S(1)}, f32[136,64]{0,1:T(8,128)S(1)}, u32[]{:S(2)}, u32[]{:S(2)}) collective-permute-start(f32[136,64]{0,1:T(8,128)S(1)} %add.210), channel_id=1, source_target_pairs={{0,32},{8,40},{16,48},{24,56},{32,0},{40,8},{48,16},{56,24},{64,96... | collective-permute-start | bytes 104456 | tf_op jit(solution)/shard_map/ppermute | solution.py:43
  55.4 3.7 %collective-permute-start.10 = (f32[124,64]{0,1:T(8,128)S(1)}, f32[124,64]{0,1:T(8,128)S(1)}, u32[]{:S(2)}, u32[]{:S(2)}) collective-permute-start(f32[124,64]{0,1:T(8,128)S(1)} %add.215), channel_id=1, source_target_pairs={{0,8},{8,0},{16,24},{24,16},{32,40},{40,32},{48,56},{56,48},{64,72... | collective-permute-start | bytes 95240 | tf_op jit(solution)/shard_map/ppermute | solution.py:43
  61.3 3.5 %collective-permute-start.11 = (f32[124,64]{0,1:T(8,128)S(1)}, f32[124,64]{0,1:T(8,128)S(1)}, u32[]{:S(2)}, u32[]{:S(2)}) collective-permute-start(f32[124,64]{0,1:T(8,128)S(1)} %add.216), channel_id=1, source_target_pairs={{0,16},{8,24},{16,0},{24,8},{32,48},{40,56},{48,32},{56,40},{64,80... | collective-permute-start | bytes 95240 | tf_op jit(solution)/shard_map/ppermute | solution.py:43
  64.8 3.0 %collective-permute-start.6 = (f32[136,64]{0,1:T(8,128)S(1)}, f32[136,64]{0,1:T(8,128)S(1)}, u32[]{:S(2)}, u32[]{:S(2)}) collective-permute-start(f32[136,64]{0,1:T(8,128)S(1)} %add.211), channel_id=1, source_target_pairs={{0,64},{8,72},{16,80},{24,88},{32,96},{40,104},{48,112},{56,120},{... | collective-permute-start | bytes 104456 | tf_op jit(solution)/shard_map/ppermute | solution.py:43
  69.2 6.2 %collective-permute-start.12 = (f32[124,64]{0,1:T(8,128)S(1)}, f32[124,64]{0,1:T(8,128)S(1)}, u32[]{:S(2)}, u32[]{:S(2)}) collective-permute-start(f32[124,64]{0,1:T(8,128)S(1)} %add.217), channel_id=1, source_target_pairs={{0,32},{8,40},{16,48},{24,56},{32,0},{40,8},{48,16},{56,24},{64,96... | collective-permute-start | bytes 95240 | tf_op jit(solution)/shard_map/ppermute | solution.py:43
  75.4 3.7 %collective-permute-start.7 = (f32[136,64]{0,1:T(8,128)S(1)}, f32[136,64]{0,1:T(8,128)S(1)}, u32[]{:S(2)}, u32[]{:S(2)}) collective-permute-start(f32[136,64]{0,1:T(8,128)S(1)} %add.212), channel_id=1, source_target_pairs={{0,128},{8,136},{16,144},{24,152},{32,160},{40,168},{48,176},{56,1... | collective-permute-start | bytes 104456 | tf_op jit(solution)/shard_map/ppermute | solution.py:43
  80.6 2.5 %collective-permute-done.7 = f32[136,64]{0,1:T(8,128)S(1)} collective-permute-done((f32[136,64]{0,1:T(8,128)S(1)}, f32[136,64]{0,1:T(8,128)S(1)}, u32[]{:S(2)}, u32[]{:S(2)}) %collective-permute-start.7) | collective-permute-done | bytes 34848 | tf_op jit(solution)/shard_map/ppermute | solution.py:43
  84.6 2.5 %psum.15 = f32[512]{0:T(512)S(1)} all-reduce(f32[512]{0:T(512)S(1)} %get-tuple-element.27), channel_id=1, replica_groups=mesh['sec'=2,'atoms'=32,'batch'=8] {'sec'}, use_global_device_ids=true, to_apply=%region_4.5 | all-reduce | flops 512 | bytes 4096 | tf_op jit(solution)/shard_map/psum | solution.py:169
  89.6 2.5 %collective-permute-done.13 = f32[512,512]{1,0:T(8,128)S(1)} collective-permute-done((f32[512,512]{1,0:T(8,128)S(1)}, f32[512,512]{1,0:T(8,128)S(1)}, u32[]{:S(2)}, u32[]{:S(2)}) %collective-permute-start.13) | collective-permute-done | bytes 1048608 | tf_op jit(solution)/shard_map/ppermute | solution.py:32
  103.1 2.8 %collective-permute-start.22 = (f32[264,256]{1,0:T(8,128)S(1)}, f32[264,256]{1,0:T(8,128)S(1)}, u32[]{:S(2)}, u32[]{:S(2)}) collective-permute-start(f32[264,256]{1,0:T(8,128)S(1)} %slice.81), channel_id=1, source_target_pairs={{0,8},{8,0},{16,24},{24,16},{32,40},{40,32},{48,56},{56,48},{64,72... | collective-permute-start | bytes 811016 | tf_op jit(solution)/shard_map/ppermute | solution.py:43
  106.5 2.7 %collective-permute-start.16 = (f32[]{:T(128)}, f32[]{:T(128)}, u32[]{:S(2)}, u32[]{:S(2)}) collective-permute-start(f32[]{:T(128)} %div.44), channel_id=1, source_target_pairs={{0,256},{256,0},{1,257},{257,1},{2,258},{258,2},{3,259},{259,3},{4... | collective-permute-start | bytes 20 | tf_op jit(solution)/shard_map/ppermute | solution.py:32
  113.5 2.9 %collective-permute-start.23 = (f32[264,256]{1,0:T(8,128)S(1)}, f32[264,256]{1,0:T(8,128)S(1)}, u32[]{:S(2)}, u32[]{:S(2)}) collective-permute-start(f32[264,256]{1,0:T(8,128)S(1)} %slice_add_fusion.2), channel_id=1, source_target_pairs={{0,16},{8,24},{16,0},{24,8},{32,48},{40,56},{48,32},{56,40},{64,80... | collective-permute-start | bytes 811016 | tf_op jit(solution)/shard_map/ppermute | solution.py:43
  116.5 4.1 %collective-permute-done.17 = f32[256,256]{1,0:T(8,128)S(1)} collective-permute-done((f32[256,256]{1,0:T(8,128)S(1)}, f32[256,256]{1,0:T(8,128)S(1)}, u32[]{:S(2)}, u32[]{:S(2)}) %collective-permute-start.17) | collective-permute-done | bytes 262176 | tf_op jit(solution)/shard_map/ppermute | solution.py:43
  120.5 4.1 %collective-permute-start.18 = (f32[256,256]{1,0:T(8,128)S(1)}, f32[256,256]{1,0:T(8,128)S(1)}, u32[]{:S(2)}, u32[]{:S(2)}) collective-permute-start(f32[256,256]{1,0:T(8,128)S(1)} %fusion.124), channel_id=1, source_target_pairs={{0,128},{8,136},{16,144},{24,152},{32,160},{40,168},{48,176},{56,1... | collective-permute-start | bytes 786440 | tf_op jit(solution)/shard_map/ppermute | solution.py:43
  124.7 5.2 %collective-permute-done.23 = f32[264,256]{1,0:T(8,128)S(1)} collective-permute-done((f32[264,256]{1,0:T(8,128)S(1)}, f32[264,256]{1,0:T(8,128)S(1)}, u32[]{:S(2)}, u32[]{:S(2)}) %collective-permute-start.23) | collective-permute-done | bytes 270368 | tf_op jit(solution)/shard_map/ppermute | solution.py:43
  129.9 3.7 %collective-permute-start.24 = (f32[264,256]{1,0:T(8,128)S(1)}, f32[264,256]{1,0:T(8,128)S(1)}, u32[]{:S(2)}, u32[]{:S(2)}) collective-permute-start(f32[264,256]{1,0:T(8,128)S(1)} %add.238), channel_id=1, source_target_pairs={{0,32},{8,40},{16,48},{24,56},{32,0},{40,8},{48,16},{56,24},{64,96... | collective-permute-start | bytes 811016 | tf_op jit(solution)/shard_map/ppermute | solution.py:43
  133.5 2.8 %collective-permute-done.18 = f32[256,256]{1,0:T(8,128)S(1)} collective-permute-done((f32[256,256]{1,0:T(8,128)S(1)}, f32[256,256]{1,0:T(8,128)S(1)}, u32[]{:S(2)}, u32[]{:S(2)}) %collective-permute-start.18) | collective-permute-done | bytes 262176 | tf_op jit(solution)/shard_map/ppermute | solution.py:43
  136.4 3.2 %collective-permute-start.19 = (f32[256,256]{1,0:T(8,128)S(1)}, f32[256,256]{1,0:T(8,128)S(1)}, u32[]{:S(2)}, u32[]{:S(2)}) collective-permute-start(f32[256,256]{1,0:T(8,128)S(1)} %add.233), channel_id=1, source_target_pairs={{0,8},{8,0},{16,24},{24,16},{32,40},{40,32},{48,56},{56,48},{64,72... | collective-permute-start | bytes 786440 | tf_op jit(solution)/shard_map/ppermute | solution.py:43
  139.7 8.2 %collective-permute-done.24 = f32[264,256]{1,0:T(8,128)S(1)} collective-permute-done((f32[264,256]{1,0:T(8,128)S(1)}, f32[264,256]{1,0:T(8,128)S(1)}, u32[]{:S(2)}, u32[]{:S(2)}) %collective-permute-start.24) | collective-permute-done | bytes 270368 | tf_op jit(solution)/shard_map/ppermute | solution.py:43
  147.9 3.2 %collective-permute-start.25 = (f32[264,256]{1,0:T(8,128)S(1)}, f32[264,256]{1,0:T(8,128)S(1)}, u32[]{:S(2)}, u32[]{:S(2)}) collective-permute-start(f32[264,256]{1,0:T(8,128)S(1)} %add.239), channel_id=1, source_target_pairs={{0,64},{8,72},{16,80},{24,88},{32,96},{40,104},{48,112},{56,120},{... | collective-permute-start | bytes 811016 | tf_op jit(solution)/shard_map/ppermute | solution.py:43
  151.3 4.3 %collective-permute-start.20 = (f32[256,256]{1,0:T(8,128)S(1)}, f32[256,256]{1,0:T(8,128)S(1)}, u32[]{:S(2)}, u32[]{:S(2)}) collective-permute-start(f32[256,256]{1,0:T(8,128)S(1)} %add.234), channel_id=1, source_target_pairs={{0,16},{8,24},{16,0},{24,8},{32,48},{40,56},{48,32},{56,40},{64,80... | collective-permute-start | bytes 786440 | tf_op jit(solution)/shard_map/ppermute | solution.py:43
  158.1 4.4 %collective-permute-start.26 = (f32[264,256]{1,0:T(8,128)S(1)}, f32[264,256]{1,0:T(8,128)S(1)}, u32[]{:S(2)}, u32[]{:S(2)}) collective-permute-start(f32[264,256]{1,0:T(8,128)S(1)} %add.240), channel_id=1, source_target_pairs={{0,128},{8,136},{16,144},{24,152},{32,160},{40,168},{48,176},{56,1... | collective-permute-start | bytes 811016 | tf_op jit(solution)/shard_map/ppermute | solution.py:43
  162.4 5.1 %collective-permute-done.20 = f32[256,256]{1,0:T(8,128)S(1)} collective-permute-done((f32[256,256]{1,0:T(8,128)S(1)}, f32[256,256]{1,0:T(8,128)S(1)}, u32[]{:S(2)}, u32[]{:S(2)}) %collective-permute-start.20) | collective-permute-done | bytes 262176 | tf_op jit(solution)/shard_map/ppermute | solution.py:43
  167.6 4.9 %collective-permute-start.21 = (f32[256,256]{1,0:T(8,128)S(1)}, f32[256,256]{1,0:T(8,128)S(1)}, u32[]{:S(2)}, u32[]{:S(2)}) collective-permute-start(f32[256,256]{1,0:T(8,128)S(1)} %add.235), channel_id=1, source_target_pairs={{0,32},{8,40},{16,48},{24,56},{32,0},{40,8},{48,16},{56,24},{64,96... | collective-permute-start | bytes 786440 | tf_op jit(solution)/shard_map/ppermute | solution.py:43
  172.4 13.3 %collective-permute-done.21 = f32[256,256]{1,0:T(8,128)S(1)} collective-permute-done((f32[256,256]{1,0:T(8,128)S(1)}, f32[256,256]{1,0:T(8,128)S(1)}, u32[]{:S(2)}, u32[]{:S(2)}) %collective-permute-start.21) | collective-permute-done | bytes 262176 | tf_op jit(solution)/shard_map/ppermute | solution.py:43
  (121 shorter events, 47.2 us)
Async XLA Ops:
  0.6 25.6 %copy-start = (bf16[1024,256]{1,0:T(8,128)(2,1)S(1)}, bf16[1024,256]{1,0:T(8,128)(2,1)}, u32[]{:S(2)}) copy-start(bf16[1024,256]{1,0:T(8,128)(2,1)} %param.22) | copy-start | bytes 1572868
  1.8 9.0 %collective-permute-start = (bf16[256,512]{1,0:T(8,128)(2,1)S(1)}, bf16[256,512]{1,0:T(8,128)(2,1)S(1)}, u32[]{:S(2)}, u32[]{:S(2)}) collective-permute-start(bf16[256,512]{1,0:T(8,128)(2,1)S(1)} %get-tuple-element.23), channel_id=1, source_target_pairs={{0,8},{8,16},{16,24},{24,32},{32,40},{40,48},{48,56},{56,64},{64,7... | collective-permute-start | bytes 786440 | tf_op jit(solution)/shard_map/ppermute | solution.py:25
  5.3 9.7 %collective-permute-start.1 = (bf16[256,512]{1,0:T(8,128)(2,1)S(1)}, bf16[256,512]{1,0:T(8,128)(2,1)S(1)}, u32[]{:S(2)}, u32[]{:S(2)}) collective-permute-start(bf16[256,512]{1,0:T(8,128)(2,1)S(1)} %get-tuple-element.24), channel_id=1, source_target_pairs={{8,0},{16,8},{24,16},{32,24},{40,32},{48,40},{56,48},{64,56},{72,6... | collective-permute-start | bytes 786440 | tf_op jit(solution)/shard_map/ppermute | solution.py:26
  24.0 3.8 %collective-permute-start.2 = (bf16[512,512]{1,0:T(8,128)(2,1)S(1)}, bf16[512,512]{1,0:T(8,128)(2,1)S(1)}, u32[]{:S(2)}, u32[]{:S(2)}) collective-permute-start(bf16[512,512]{1,0:T(8,128)(2,1)S(1)} %fusion.30), channel_id=1, source_target_pairs={{0,256},{256,0},{1,257},{257,1},{2,258},{258,2},{3,259},{259,3},{4... | collective-permute-start | bytes 1572872 | tf_op jit(solution)/shard_map/ppermute | solution.py:32
  30.8 28.3 %copy-start.7 = (bf16[256,1024]{1,0:T(8,128)(2,1)S(1)}, bf16[256,1024]{1,0:T(8,128)(2,1)}, u32[]{:S(2)}) copy-start(bf16[256,1024]{1,0:T(8,128)(2,1)} %param.24) | copy-start | bytes 1572868
  31.4 47.7 %copy-start.4 = (bf16[512,512]{1,0:T(8,128)(2,1)S(1)}, bf16[512,512]{1,0:T(8,128)(2,1)}, u32[]{:S(2)}) copy-start(bf16[512,512]{1,0:T(8,128)(2,1)} %copy-done.3) | copy-start | bytes 1572868
  31.7 7.8 %collective-permute-start.3 = (f32[136,64]{0,1:T(8,128)S(1)}, f32[136,64]{0,1:T(8,128)S(1)}, u32[]{:S(2)}, u32[]{:S(2)}) collective-permute-start(f32[136,64]{0,1:T(8,128)S(1)} %slice.76), channel_id=1, source_target_pairs={{0,8},{8,0},{16,24},{24,16},{32,40},{40,32},{48,56},{56,48},{64,72... | collective-permute-start | bytes 104456 | tf_op jit(solution)/shard_map/ppermute | solution.py:43
  35.2 11.3 %collective-permute-start.8 = (f32[124,64]{0,1:T(8,128)S(1)}, f32[124,64]{0,1:T(8,128)S(1)}, u32[]{:S(2)}, u32[]{:S(2)}) collective-permute-start(f32[124,64]{0,1:T(8,128)S(1)} %slice.77), channel_id=1, source_target_pairs={{0,64},{8,72},{16,80},{24,88},{32,96},{40,104},{48,112},{56,120},{... | collective-permute-start | bytes 95240 | tf_op jit(solution)/shard_map/ppermute | solution.py:43
  39.5 13.1 %collective-permute-start.4 = (f32[136,64]{0,1:T(8,128)S(1)}, f32[136,64]{0,1:T(8,128)S(1)}, u32[]{:S(2)}, u32[]{:S(2)}) collective-permute-start(f32[136,64]{0,1:T(8,128)S(1)} %slice_add_fusion.1), channel_id=1, source_target_pairs={{0,16},{8,24},{16,0},{24,8},{32,48},{40,56},{48,32},{56,40},{64,80... | collective-permute-start | bytes 104456 | tf_op jit(solution)/shard_map/ppermute | solution.py:43
  46.5 8.9 %collective-permute-start.9 = (f32[124,64]{0,1:T(8,128)S(1)}, f32[124,64]{0,1:T(8,128)S(1)}, u32[]{:S(2)}, u32[]{:S(2)}) collective-permute-start(f32[124,64]{0,1:T(8,128)S(1)} %slice_add_fusion), channel_id=1, source_target_pairs={{0,128},{8,136},{16,144},{24,152},{32,160},{40,168},{48,176},{56,1... | collective-permute-start | bytes 95240 | tf_op jit(solution)/shard_map/ppermute | solution.py:43
  52.6 12.1 %collective-permute-start.5 = (f32[136,64]{0,1:T(8,128)S(1)}, f32[136,64]{0,1:T(8,128)S(1)}, u32[]{:S(2)}, u32[]{:S(2)}) collective-permute-start(f32[136,64]{0,1:T(8,128)S(1)} %add.210), channel_id=1, source_target_pairs={{0,32},{8,40},{16,48},{24,56},{32,0},{40,8},{48,16},{56,24},{64,96... | collective-permute-start | bytes 104456 | tf_op jit(solution)/shard_map/ppermute | solution.py:43
  55.4 5.8 %collective-permute-start.10 = (f32[124,64]{0,1:T(8,128)S(1)}, f32[124,64]{0,1:T(8,128)S(1)}, u32[]{:S(2)}, u32[]{:S(2)}) collective-permute-start(f32[124,64]{0,1:T(8,128)S(1)} %add.215), channel_id=1, source_target_pairs={{0,8},{8,0},{16,24},{24,16},{32,40},{40,32},{48,56},{56,48},{64,72... | collective-permute-start | bytes 95240 | tf_op jit(solution)/shard_map/ppermute | solution.py:43
  61.3 7.9 %collective-permute-start.11 = (f32[124,64]{0,1:T(8,128)S(1)}, f32[124,64]{0,1:T(8,128)S(1)}, u32[]{:S(2)}, u32[]{:S(2)}) collective-permute-start(f32[124,64]{0,1:T(8,128)S(1)} %add.216), channel_id=1, source_target_pairs={{0,16},{8,24},{16,0},{24,8},{32,48},{40,56},{48,32},{56,40},{64,80... | collective-permute-start | bytes 95240 | tf_op jit(solution)/shard_map/ppermute | solution.py:43
  64.8 10.6 %collective-permute-start.6 = (f32[136,64]{0,1:T(8,128)S(1)}, f32[136,64]{0,1:T(8,128)S(1)}, u32[]{:S(2)}, u32[]{:S(2)}) collective-permute-start(f32[136,64]{0,1:T(8,128)S(1)} %add.211), channel_id=1, source_target_pairs={{0,64},{8,72},{16,80},{24,88},{32,96},{40,104},{48,112},{56,120},{... | collective-permute-start | bytes 104456 | tf_op jit(solution)/shard_map/ppermute | solution.py:43
  69.2 11.4 %collective-permute-start.12 = (f32[124,64]{0,1:T(8,128)S(1)}, f32[124,64]{0,1:T(8,128)S(1)}, u32[]{:S(2)}, u32[]{:S(2)}) collective-permute-start(f32[124,64]{0,1:T(8,128)S(1)} %add.217), channel_id=1, source_target_pairs={{0,32},{8,40},{16,48},{24,56},{32,0},{40,8},{48,16},{56,24},{64,96... | collective-permute-start | bytes 95240 | tf_op jit(solution)/shard_map/ppermute | solution.py:43
  75.4 7.7 %collective-permute-start.7 = (f32[136,64]{0,1:T(8,128)S(1)}, f32[136,64]{0,1:T(8,128)S(1)}, u32[]{:S(2)}, u32[]{:S(2)}) collective-permute-start(f32[136,64]{0,1:T(8,128)S(1)} %add.212), channel_id=1, source_target_pairs={{0,128},{8,136},{16,144},{24,152},{32,160},{40,168},{48,176},{56,1... | collective-permute-start | bytes 104456 | tf_op jit(solution)/shard_map/ppermute | solution.py:43
  87.1 5.3 %copy-start.8 = (bf16[512,256]{1,0:T(8,128)(2,1)S(1)}, bf16[512,256]{1,0:T(8,128)(2,1)}, u32[]{:S(2)}) copy-start(bf16[512,256]{1,0:T(8,128)(2,1)} %param.25) | copy-start | bytes 786436
  87.5 4.6 %collective-permute-start.13 = (f32[512,512]{1,0:T(8,128)S(1)}, f32[512,512]{1,0:T(8,128)S(1)}, u32[]{:S(2)}, u32[]{:S(2)}) collective-permute-start(f32[512,512]{1,0:T(8,128)S(1)} %fusion.55), channel_id=1, source_target_pairs={{0,256},{256,0},{1,257},{257,1},{2,258},{258,2},{3,259},{259,3},{4... | collective-permute-start | bytes 3145736 | tf_op jit(solution)/shard_map/ppermute | solution.py:32
  92.4 10.2 %copy-start.2 = (bf16[512,512]{1,0:T(8,128)(2,1)}, bf16[512,512]{1,0:T(8,128)(2,1)S(1)}, u32[]{:S(2)}) copy-start(bf16[512,512]{1,0:T(8,128)(2,1)S(1)} %fusion.21) | copy-start | bytes 1572868
  92.8 3.8 %collective-permute-start.14 = (f32[512,256]{0,1:T(8,128)S(1)}, f32[512,256]{0,1:T(8,128)S(1)}, u32[]{:S(2)}, u32[]{:S(2)}) collective-permute-start(f32[512,256]{0,1:T(8,128)S(1)} %fusion.108), channel_id=1, source_target_pairs={{0,256},{256,0},{1,257},{257,1},{2,258},{258,2},{3,259},{259,3},{4... | collective-permute-start | bytes 1572872 | tf_op jit(solution)/shard_map/ppermute | solution.py:32
  98.6 3.8 %collective-permute-start.15 = (f32[512,256]{0,1:T(8,128)S(1)}, f32[512,256]{0,1:T(8,128)S(1)}, u32[]{:S(2)}, u32[]{:S(2)}) collective-permute-start(f32[512,256]{0,1:T(8,128)S(1)} %convolution_multiply_fusion), channel_id=1, source_target_pairs={{0,256},{256,0},{1,257},{257,1},{2,258},{258,2},{3,259},{259,3},{4... | collective-permute-start | bytes 1572872 | tf_op jit(solution)/shard_map/ppermute | solution.py:32
  103.1 10.4 %collective-permute-start.22 = (f32[264,256]{1,0:T(8,128)S(1)}, f32[264,256]{1,0:T(8,128)S(1)}, u32[]{:S(2)}, u32[]{:S(2)}) collective-permute-start(f32[264,256]{1,0:T(8,128)S(1)} %slice.81), channel_id=1, source_target_pairs={{0,8},{8,0},{16,24},{24,16},{32,40},{40,32},{48,56},{56,48},{64,72... | collective-permute-start | bytes 811016 | tf_op jit(solution)/shard_map/ppermute | solution.py:43
  106.5 3.0 %collective-permute-start.16 = (f32[]{:T(128)}, f32[]{:T(128)}, u32[]{:S(2)}, u32[]{:S(2)}) collective-permute-start(f32[]{:T(128)} %div.44), channel_id=1, source_target_pairs={{0,256},{256,0},{1,257},{257,1},{2,258},{258,2},{3,259},{259,3},{4... | collective-permute-start | bytes 20 | tf_op jit(solution)/shard_map/ppermute | solution.py:32
  110.2 10.3 %collective-permute-start.17 = (f32[256,256]{1,0:T(8,128)S(1)}, f32[256,256]{1,0:T(8,128)S(1)}, u32[]{:S(2)}, u32[]{:S(2)}) collective-permute-start(f32[256,256]{1,0:T(8,128)S(1)} %pad_maximum_fusion.2), channel_id=1, source_target_pairs={{0,64},{8,72},{16,80},{24,88},{32,96},{40,104},{48,112},{56,120},{... | collective-permute-start | bytes 786440 | tf_op jit(solution)/shard_map/ppermute | solution.py:43
  113.5 16.3 %collective-permute-start.23 = (f32[264,256]{1,0:T(8,128)S(1)}, f32[264,256]{1,0:T(8,128)S(1)}, u32[]{:S(2)}, u32[]{:S(2)}) collective-permute-start(f32[264,256]{1,0:T(8,128)S(1)} %slice_add_fusion.2), channel_id=1, source_target_pairs={{0,16},{8,24},{16,0},{24,8},{32,48},{40,56},{48,32},{56,40},{64,80... | collective-permute-start | bytes 811016 | tf_op jit(solution)/shard_map/ppermute | solution.py:43
  120.5 15.8 %collective-permute-start.18 = (f32[256,256]{1,0:T(8,128)S(1)}, f32[256,256]{1,0:T(8,128)S(1)}, u32[]{:S(2)}, u32[]{:S(2)}) collective-permute-start(f32[256,256]{1,0:T(8,128)S(1)} %fusion.124), channel_id=1, source_target_pairs={{0,128},{8,136},{16,144},{24,152},{32,160},{40,168},{48,176},{56,1... | collective-permute-start | bytes 786440 | tf_op jit(solution)/shard_map/ppermute | solution.py:43
  129.9 18.0 %collective-permute-start.24 = (f32[264,256]{1,0:T(8,128)S(1)}, f32[264,256]{1,0:T(8,128)S(1)}, u32[]{:S(2)}, u32[]{:S(2)}) collective-permute-start(f32[264,256]{1,0:T(8,128)S(1)} %add.238), channel_id=1, source_target_pairs={{0,32},{8,40},{16,48},{24,56},{32,0},{40,8},{48,16},{56,24},{64,96... | collective-permute-start | bytes 811016 | tf_op jit(solution)/shard_map/ppermute | solution.py:43
  136.4 14.8 %collective-permute-start.19 = (f32[256,256]{1,0:T(8,128)S(1)}, f32[256,256]{1,0:T(8,128)S(1)}, u32[]{:S(2)}, u32[]{:S(2)}) collective-permute-start(f32[256,256]{1,0:T(8,128)S(1)} %add.233), channel_id=1, source_target_pairs={{0,8},{8,0},{16,24},{24,16},{32,40},{40,32},{48,56},{56,48},{64,72... | collective-permute-start | bytes 786440 | tf_op jit(solution)/shard_map/ppermute | solution.py:43
  147.9 10.1 %collective-permute-start.25 = (f32[264,256]{1,0:T(8,128)S(1)}, f32[264,256]{1,0:T(8,128)S(1)}, u32[]{:S(2)}, u32[]{:S(2)}) collective-permute-start(f32[264,256]{1,0:T(8,128)S(1)} %add.239), channel_id=1, source_target_pairs={{0,64},{8,72},{16,80},{24,88},{32,96},{40,104},{48,112},{56,120},{... | collective-permute-start | bytes 811016 | tf_op jit(solution)/shard_map/ppermute | solution.py:43
  151.3 16.3 %collective-permute-start.20 = (f32[256,256]{1,0:T(8,128)S(1)}, f32[256,256]{1,0:T(8,128)S(1)}, u32[]{:S(2)}, u32[]{:S(2)}) collective-permute-start(f32[256,256]{1,0:T(8,128)S(1)} %add.234), channel_id=1, source_target_pairs={{0,16},{8,24},{16,0},{24,8},{32,48},{40,56},{48,32},{56,40},{64,80... | collective-permute-start | bytes 786440 | tf_op jit(solution)/shard_map/ppermute | solution.py:43
  158.1 28.9 %collective-permute-start.26 = (f32[264,256]{1,0:T(8,128)S(1)}, f32[264,256]{1,0:T(8,128)S(1)}, u32[]{:S(2)}, u32[]{:S(2)}) collective-permute-start(f32[264,256]{1,0:T(8,128)S(1)} %add.240), channel_id=1, source_target_pairs={{0,128},{8,136},{16,144},{24,152},{32,160},{40,168},{48,176},{56,1... | collective-permute-start | bytes 811016 | tf_op jit(solution)/shard_map/ppermute | solution.py:43
  167.6 18.2 %collective-permute-start.21 = (f32[256,256]{1,0:T(8,128)S(1)}, f32[256,256]{1,0:T(8,128)S(1)}, u32[]{:S(2)}, u32[]{:S(2)}) collective-permute-start(f32[256,256]{1,0:T(8,128)S(1)} %add.235), channel_id=1, source_target_pairs={{0,32},{8,40},{16,48},{24,56},{32,0},{40,8},{48,16},{56,24},{64,96... | collective-permute-start | bytes 786440 | tf_op jit(solution)/shard_map/ppermute | solution.py:43
  (7 other events, 20.5 us)

commit v3 on v2

--- a/solution.py
+++ b/solution.py
@@ -36,25 +36,16 @@
     return x + swap_sec(x)
 
 
-def butterfly(x, strides):
-    peers = lax.axis_size("atoms")
-    for stride in strides:
-        pairs = [(i, i ^ stride) for i in range(peers)]
-        x = x + lax.ppermute(x, "atoms", pairs)
-    return x
-
-
 def sum_atoms(x):
     peers = lax.axis_size("atoms")
-    if peers & (peers - 1):
-        return lax.psum(x, "atoms")
-    inner = min(peers, 8)
-    low = [1 << k for k in range(inner.bit_length() - 1)]
-    high = [inner << k for k in range((peers // inner).bit_length() - 1)]
-    half = (x.shape[0] // 2 + 7) // 8 * 8
-    first = butterfly(x[:half], low + high)
-    second = butterfly(x[half:], high + low)
-    return jnp.concatenate([first, second], axis=0)
+    flat = x.reshape(-1)
+    chunk = -(-flat.shape[0] // (peers * 128)) * 128
+    flat = jnp.pad(flat, (0, chunk * peers - flat.shape[0]))
+    pieces = flat.reshape(peers, chunk // 128, 128)
+    arrived = lax.all_to_all(pieces, "atoms", 0, 0, tiled=True)
+    owned = jnp.sum(arrived, axis=0, keepdims=True)
+    spread = lax.all_to_all(jnp.broadcast_to(owned, pieces.shape), "atoms", 0, 0, tiled=True)
+    return spread.reshape(-1)[: x.size].reshape(x.shape)
 
 
 def feature_map(values):
@@ -163,7 +154,7 @@
         key_f.astype(jnp.bfloat16), value_f.astype(jnp.bfloat16), atom_mask, head_count
     )
     state_rows = jnp.concatenate([outer_state, key_total[:, None, :]], axis=1)
-    packed = sum_atoms(state_rows.reshape(-1, HEAD_DIM)).reshape(state_rows.shape)
+    packed = sum_atoms(state_rows)
     outer_state, key_total = packed[:, :HEAD_DIM, :], packed[:, HEAD_DIM, :]
     attended = read_summary(query_f.astype(jnp.bfloat16), outer_state, key_total, head_count)
     out_sum = lax.psum(jnp.sum(attended * attended, axis=-1), "sec")
@@ -184,10 +175,9 @@
     embed_grad = embed_backward(unit_rows, unit_grad, embed_scale)
     proj_part = jnp.einsum("nd,ne->de", hidden_two, embed_grad, preferred_element_type=jnp.float32)
     loss_pair = sum_sec(loss_part)
-    loss_rows = jnp.zeros((8, proj_part.shape[1]), jnp.float32).at[0, 0].set(loss_pair)
-    packed = sum_atoms(jnp.concatenate([proj_part, loss_rows], axis=0))
-    proj_total = packed[: proj_part.shape[0]]
-    loss_total = packed[proj_part.shape[0], 0] / (local_rows * lax.axis_size("atoms"))
+    packed = sum_atoms(jnp.concatenate([proj_part.reshape(-1), loss_pair.reshape(1)]))
+    proj_total = packed[: proj_part.size].reshape(proj_part.shape)
+    loss_total = packed[proj_part.size] / (local_rows * lax.axis_size("atoms"))
     return (hidden_two[None], loss_total.reshape(1), proj_total[None])
 
 

time: 191 us -> 147 us (0.77)
  starting transfers between devices: 95.3 us -> 33.2 us
  blocking collectives: 4.93 us -> 54.3 us
  waiting for transfers between devices: 59 us -> 27.2 us
  local copies, waits for them, and re-layouts: 5.58 us -> 9.79 us
  other arithmetic: 5.8 us -> 3.48 us
    ppermute x20 -> x0, starting transfers between devices: 79.5 us -> none  [butterfly(): x = x + lax.ppermute(x, 'atoms', pairs)]
    all_to_all x0 -> x2, blocking collectives: none -> 49.4 us  [the longest x1 25.7 us: sum_atoms(): lax.all_to_all(jnp.broadcast_to(owned, pieces.shape), 'atoms', 0, 0, tile...]
    ppermute x20 -> x0, waiting for transfers between devices: 46.5 us -> none  [butterfly(): x = x + lax.ppermute(x, 'atoms', pairs)]
    all_to_all x0 -> x2, waiting for transfers between devices: none -> 18.7 us  [the longest x1 9.57 us: sum_atoms(): arrived = lax.all_to_all(pieces, 'atoms', 0, 0, tiled=True)]
    all_to_all x0 -> x2, starting transfers between devices: none -> 16.9 us  [the longest x1 13.1 us: sum_atoms(): arrived = lax.all_to_all(pieces, 'atoms', 0, 0, tiled=True)]
    unnamed x25 -> x26, local copies, waits for them, and re-layouts: 1.06 us -> 3.17 us
    ppermute x5, waiting for transfers between devices: 6.95 us -> 4.96 us  [swap_sec(): return lax.ppermute(x, 'sec', [(0, 1), (1, 0)])]
  transfers between devices with their start and end apart: 27 -> 9, of which waited for: 17 -> 6; matrix products, arithmetic and copies ran while one was open for 4% -> 5% of each run, Pallas kernels for 0% -> 0%
where the time goes in v3:
time: 147 us; the launch traced here: 146 us
  blocking collectives  54.3 us (37%)
  starting transfers between devices  33.2 us (23%)
  waiting for transfers between devices  27.2 us (19%)
  matrix products  13.2 us (9%)
  local copies, waits for them, and re-layouts  9.79 us (7%)
  between operations  4.8 us (3%)
  other arithmetic  3.48 us (2%)
    all_to_all x1, blocking collectives, sum_atoms(): lax.all_to_all(jnp.broadcast_to(owned, pieces.shape), 'atoms', 0, 0, tile...  25.7 us
    all_to_all x1, blocking collectives, sum_atoms(): arrived = lax.all_to_all(pieces, 'atoms', 0, 0, tiled=True)  23.8 us
    all_to_all x1, starting transfers between devices, sum_atoms(): arrived = lax.all_to_all(pieces, 'atoms', 0, 0, tiled=True)  13.1 us
    ppermute x5, starting transfers between devices, swap_sec(): return lax.ppermute(x, 'sec', [(0, 1), (1, 0)])  11.5 us
    all_to_all x1, waiting for transfers between devices, sum_atoms(): arrived = lax.all_to_all(pieces, 'atoms', 0, 0, tiled=True)  9.57 us
    all_to_all x1, waiting for transfers between devices, sum_atoms(): lax.all_to_all(jnp.broadcast_to(owned, pieces.shape), 'atoms', 0, 0, tile...  9.14 us
    ppermute x5, waiting for transfers between devices, swap_sec(): return lax.ppermute(x, 'sec', [(0, 1), (1, 0)])  4.96 us
    all_to_all x1, starting transfers between devices, sum_atoms(): lax.all_to_all(jnp.broadcast_to(owned, pieces.shape), 'atoms', 0, 0, tile...  3.84 us
  transfers between devices with their start and end apart: 9, of which 6 were waited for; matrix products, arithmetic and copies ran while one was open for 5% of the time, Pallas kernels for 0%

profile of v3, /device:TPU:6, one launch (start us, length us, event | category | flops | bytes accessed | tf_op | source)
XLA Modules:
  0.0 146.0 jit_solution(1153561001030671897)
XLA Ops:
  0.7 1.2 slice_bitcast_fusion.1
  1.8 3.5 %collective-permute-start = (bf16[256,512]{1,0:T(8,128)(2,1)S(1)}, bf16[256,512]{1,0:T(8,128)(2,1)S(1)}, u32[]{:S(2)}, u32[]{:S(2)}) collective-permute-start(bf16[256,512]{1,0:T(8,128)(2,1)S(1)} %get-tuple-element.11), channel_id=1, source_target_pairs={{0,8},{8,16},{16,24},{24,32},{32,40},{40,48},{48,56},{56,64},{64,7... | collective-permute-start | bytes 786440 | tf_op jit(solution)/shard_map/ppermute | solution.py:25
  5.3 1.3 collective-permute-start.1
  6.6 0.8 compare_and_fusion
  7.4 0.7 fusion.99
  8.7 0.7 convert_element_type.130
  9.4 2.0 %copy.21 = bf16[256,1024]{0,1:T(8,128)(2,1)} copy(bf16[256,1024]{1,0:T(8,128)(2,1)} %param.22) | data formatting | bytes 1048576 | tf_op args[10]
  11.5 3.5 %collective-permute-done.1 = bf16[256,512]{1,0:T(8,128)(2,1)S(1)} collective-permute-done((bf16[256,512]{1,0:T(8,128)(2,1)S(1)}, bf16[256,512]{1,0:T(8,128)(2,1)S(1)}, u32[]{:S(2)}, u32[]{:S(2)}) %collective-permute-start.1) | collective-permute-done | bytes 262176 | tf_op jit(solution)/shard_map/ppermute | solution.py:26
  15.1 2.0 %gather_fusion = bf16[16,128,512]{2,1,0:T(8,128)(2,1)} fusion(bf16[8,128,512]{2,1,0:T(8,128)(2,1)S(1)} %bitcast.129, s32[1024]{0:T(1024)S(1)} %pad_clamp_fusion), kind=kCustom, calls=%fused_computation | custom fusion | bytes 4194368 | tf_op jit(solution)/shard_map/jit(_take)/gather | solution.py:68
  17.1 2.9 %fusion.16 = f32[4,128,512]{2,1,0:T(8,128)S(1)} fusion(bf16[16,128,512]{2,1,0:T(8,128)(2,1)} %gather_fusion, pred[16]{0:T(512)(128)(4,1)S(1)} %get-tuple-element.9, pred[4,16]{1,0:T(4,128)(4,1)S(1)} %iota_compare_fusion.1, bf16[16,128,128]{2,1,0:T(8,128)(2,1)S(1)} %bitcast.147), kind=kOutput, calls=%fused_computation.17 | convolution fusion | flops 1076363264 | bytes 3670096 | tf_op jit(solution)/shard_map/btij,tjf->bif/dot_general | solution.py:71
  20.2 2.5 %psum.14 = f32[512]{0:T(512)S(1)} all-reduce(f32[512]{0:T(512)S(1)} %get-tuple-element.7), channel_id=1, replica_groups=mesh['sec'=2,'atoms'=32,'batch'=8] {'sec'}, use_global_device_ids=true, to_apply=%region_1.2 | all-reduce | flops 512 | bytes 4096 | tf_op jit(solution)/shard_map/psum | solution.py:135
  22.9 2.1 %collective-permute-start.2 = (bf16[512,512]{1,0:T(8,128)(2,1)S(1)}, bf16[512,512]{1,0:T(8,128)(2,1)S(1)}, u32[]{:S(2)}, u32[]{:S(2)}) collective-permute-start(bf16[512,512]{1,0:T(8,128)(2,1)S(1)} %fusion.30), channel_id=1, source_target_pairs={{0,256},{256,0},{1,257},{257,1},{2,258},{258,2},{3,259},{259,3},{4... | collective-permute-start | bytes 1572872 | tf_op jit(solution)/shard_map/ppermute | solution.py:32
  26.0 0.8 collective-permute-done.2
  26.7 0.8 copy-done.3
  28.4 1.4 fusion.25
  31.2 13.1 %all-to-all-start = ((f32[32,5,128]{2,1,0:T(8,128)}), f32[32,5,128]{2,1,0:T(8,128)S(1)}, u32[]{:S(2)}, u32[]{:S(2)}) async-start(f32[32,5,128]{2,1,0:T(8,128)} %reshape.271), calls=%async_computation | async-start | bytes 262144 | tf_op jit(solution)/shard_map/all_to_all | solution.py:45
  44.4 1.3 fusion.57
  45.7 9.6 %all-to-all-done = f32[32,5,128]{2,1,0:T(8,128)S(1)} async-done(((f32[32,5,128]{2,1,0:T(8,128)}), f32[32,5,128]{2,1,0:T(8,128)S(1)}, u32[]{:S(2)}, u32[]{:S(2)}) %all-to-all-start) | async-done | bytes 81952 | tf_op jit(solution)/shard_map/all_to_all | solution.py:45
  55.9 3.8 %all-to-all-start.1 = ((f32[32,5,128]{2,1,0:T(8,128)}), f32[32,5,128]{2,1,0:T(8,128)S(1)}, u32[]{:S(2)}, u32[]{:S(2)}) async-start(f32[32,5,128]{2,1,0:T(8,128)} %broadcast_in_dim.85), calls=%async_computation.1 | async-start | bytes 262144 | tf_op jit(solution)/shard_map/all_to_all | solution.py:47
  59.8 1.5 %fusion.40 = f32[512,256]{0,1:T(8,128)S(1)} fusion(f32[512,256]{0,1:T(8,128)S(1)} %fusion.57, bf16[512,512]{1,0:T(8,128)(2,1)S(1)} %copy-done.4, bf16[2,512,256]{2,1,0:T(8,128)(2,1)} %bitcast.145, s32[]{:T(128)S(6)} %select_n.95), kind=kOutput, calls=%fused_computation.51 | convolution fusion | flops 135135232 | bytes 1835012 | tf_op jit(solution)/shard_map/dot_general | solution.py:146
  61.3 9.1 %all-to-all-done.1 = f32[32,5,128]{2,1,0:T(8,128)S(1)} async-done(((f32[32,5,128]{2,1,0:T(8,128)}), f32[32,5,128]{2,1,0:T(8,128)S(1)}, u32[]{:S(2)}, u32[]{:S(2)}) %all-to-all-start.1) | async-done | bytes 81952 | tf_op jit(solution)/shard_map/all_to_all | solution.py:47
  71.6 2.5 %psum.15 = f32[512]{0:T(512)S(1)} all-reduce(f32[512]{0:T(512)S(1)} %get-tuple-element.15), channel_id=1, replica_groups=mesh['sec'=2,'atoms'=32,'batch'=8] {'sec'}, use_global_device_ids=true, to_apply=%region_5.6 | all-reduce | flops 512 | bytes 4096 | tf_op jit(solution)/shard_map/psum | solution.py:160
  74.5 2.1 %collective-permute-start.3 = (f32[512,512]{1,0:T(8,128)S(1)}, f32[512,512]{1,0:T(8,128)S(1)}, u32[]{:S(2)}, u32[]{:S(2)}) collective-permute-start(f32[512,512]{1,0:T(8,128)S(1)} %fusion.53), channel_id=1, source_target_pairs={{0,256},{256,0},{1,257},{257,1},{2,258},{258,2},{3,259},{259,3},{4... | collective-permute-start | bytes 3145736 | tf_op jit(solution)/shard_map/ppermute | solution.py:32
  76.5 2.5 %collective-permute-done.3 = f32[512,512]{1,0:T(8,128)S(1)} collective-permute-done((f32[512,512]{1,0:T(8,128)S(1)}, f32[512,512]{1,0:T(8,128)S(1)}, u32[]{:S(2)}, u32[]{:S(2)}) %collective-permute-start.3) | collective-permute-done | bytes 1048608 | tf_op jit(solution)/shard_map/ppermute | solution.py:32
  79.8 2.1 %collective-permute-start.4 = (f32[512,256]{0,1:T(8,128)S(1)}, f32[512,256]{0,1:T(8,128)S(1)}, u32[]{:S(2)}, u32[]{:S(2)}) collective-permute-start(f32[512,256]{0,1:T(8,128)S(1)} %fusion.106), channel_id=1, source_target_pairs={{0,256},{256,0},{1,257},{257,1},{2,258},{258,2},{3,259},{259,3},{4... | collective-permute-start | bytes 1572872 | tf_op jit(solution)/shard_map/ppermute | solution.py:32
  81.9 1.7 %collective-permute-done.4 = f32[512,256]{0,1:T(8,128)S(1)} collective-permute-done((f32[512,256]{0,1:T(8,128)S(1)}, f32[512,256]{0,1:T(8,128)S(1)}, u32[]{:S(2)}, u32[]{:S(2)}) %collective-permute-start.4) | collective-permute-done | bytes 524320 | tf_op jit(solution)/shard_map/ppermute | solution.py:32
  83.7 1.3 fusion.52
  85.6 2.1 %collective-permute-start.5 = (f32[512,256]{0,1:T(8,128)S(1)}, f32[512,256]{0,1:T(8,128)S(1)}, u32[]{:S(2)}, u32[]{:S(2)}) collective-permute-start(f32[512,256]{0,1:T(8,128)S(1)} %convolution_multiply_fusion), channel_id=1, source_target_pairs={{0,256},{256,0},{1,257},{257,1},{2,258},{258,2},{3,259},{259,3},{4... | collective-permute-start | bytes 1572872 | tf_op jit(solution)/shard_map/ppermute | solution.py:32
  88.3 3.2 %collective-permute-start.6 = (f32[]{:T(128)}, f32[]{:T(128)}, u32[]{:S(2)}, u32[]{:S(2)}) collective-permute-start(f32[]{:T(128)} %div.44), channel_id=1, source_target_pairs={{0,256},{256,0},{1,257},{257,1},{2,258},{258,2},{3,259},{259,3},{4... | collective-permute-start | bytes 20 | tf_op jit(solution)/shard_map/ppermute | solution.py:32
  93.1 23.8 %all_to_all.20 = f32[32,33,128]{2,1,0:T(8,128)S(1)} all-to-all(f32[32,33,128]{2,1,0:T(8,128)S(1)} %reshape.278), channel_id=1, replica_groups=mesh['sec'=2,'atoms'=32,'batch'=8] {'atoms'}, dimensions={0} | all-to-all | bytes 1081344 | tf_op jit(solution)/shard_map/all_to_all | solution.py:45
  117.0 25.7 %all_to_all.21 = f32[32,33,128]{2,1,0:T(8,128)S(1)} all-to-all(f32[32,33,128]{2,1,0:T(8,128)S(1)} %broadcast_in_dim.87), channel_id=1, replica_groups=mesh['sec'=2,'atoms'=32,'batch'=8] {'atoms'}, dimensions={0} | all-to-all | bytes 1081344 | tf_op jit(solution)/shard_map/all_to_all | solution.py:47
  143.3 0.9 broadcast_in_dim_reshape.3
  (72 shorter events, 9.0 us)
Async XLA Ops:
  0.6 24.6 %copy-start = (bf16[1024,256]{1,0:T(8,128)(2,1)S(1)}, bf16[1024,256]{1,0:T(8,128)(2,1)}, u32[]{:S(2)}) copy-start(bf16[1024,256]{1,0:T(8,128)(2,1)} %param.20) | copy-start | bytes 1572868
  0.6 14.3 %copy-start.1 = (bf16[1,512,512]{2,1,0:T(8,128)(2,1)S(1)}, bf16[1,512,512]{2,1,0:T(8,128)(2,1)}, u32[]{:S(2)}) copy-start(bf16[1,512,512]{2,1,0:T(8,128)(2,1)} %param.12) | copy-start | bytes 1572868
  1.8 9.7 %collective-permute-start = (bf16[256,512]{1,0:T(8,128)(2,1)S(1)}, bf16[256,512]{1,0:T(8,128)(2,1)S(1)}, u32[]{:S(2)}, u32[]{:S(2)}) collective-permute-start(bf16[256,512]{1,0:T(8,128)(2,1)S(1)} %get-tuple-element.11), channel_id=1, source_target_pairs={{0,8},{8,16},{16,24},{24,32},{32,40},{40,48},{48,56},{56,64},{64,7... | collective-permute-start | bytes 786440 | tf_op jit(solution)/shard_map/ppermute | solution.py:25
  5.3 9.7 %collective-permute-start.1 = (bf16[256,512]{1,0:T(8,128)(2,1)S(1)}, bf16[256,512]{1,0:T(8,128)(2,1)S(1)}, u32[]{:S(2)}, u32[]{:S(2)}) collective-permute-start(bf16[256,512]{1,0:T(8,128)(2,1)S(1)} %get-tuple-element.12), channel_id=1, source_target_pairs={{8,0},{16,8},{24,16},{32,24},{40,32},{48,40},{56,48},{64,56},{72,6... | collective-permute-start | bytes 786440 | tf_op jit(solution)/shard_map/ppermute | solution.py:26
  15.0 2.0 %copy-start.9 = (bf16[1,16,128,128]{3,2,1,0:T(8,128)(2,1)S(1)}, bf16[1,16,128,128]{3,2,1,0:T(8,128)(2,1)}, u32[]{:S(2)}) copy-start(bf16[1,16,128,128]{3,2,1,0:T(8,128)(2,1)} %param.14) | copy-start | bytes 1572868
  22.7 2.9 %copy-start.6 = (bf16[1024,256]{1,0:T(8,128)(2,1)S(1)}, bf16[1024,256]{1,0:T(8,128)(2,1)}, u32[]{:S(2)}) copy-start(bf16[1024,256]{1,0:T(8,128)(2,1)} %param.21) | copy-start | bytes 1572868
  22.9 3.8 %collective-permute-start.2 = (bf16[512,512]{1,0:T(8,128)(2,1)S(1)}, bf16[512,512]{1,0:T(8,128)(2,1)S(1)}, u32[]{:S(2)}, u32[]{:S(2)}) collective-permute-start(bf16[512,512]{1,0:T(8,128)(2,1)S(1)} %fusion.30), channel_id=1, source_target_pairs={{0,256},{256,0},{1,257},{257,1},{2,258},{258,2},{3,259},{259,3},{4... | collective-permute-start | bytes 1572872 | tf_op jit(solution)/shard_map/ppermute | solution.py:32
  25.2 3.2 %copy-start.7 = (bf16[1024,256]{1,0:T(8,128)(2,1)S(1)}, bf16[1024,256]{1,0:T(8,128)(2,1)}, u32[]{:S(2)}) copy-start(bf16[1024,256]{1,0:T(8,128)(2,1)} %param.21) | copy-start | bytes 1572868
  26.7 0.8 copy-start.3
  29.8 30.0 %copy-start.4 = (bf16[512,512]{1,0:T(8,128)(2,1)S(1)}, bf16[512,512]{1,0:T(8,128)(2,1)}, u32[]{:S(2)}) copy-start(bf16[512,512]{1,0:T(8,128)(2,1)} %copy-done.3) | copy-start | bytes 1572868
  31.2 24.0 %all-to-all-start = ((f32[32,5,128]{2,1,0:T(8,128)}), f32[32,5,128]{2,1,0:T(8,128)S(1)}, u32[]{:S(2)}, u32[]{:S(2)}) async-start(f32[32,5,128]{2,1,0:T(8,128)} %reshape.271), calls=%async_computation | async-start | bytes 262144 | tf_op jit(solution)/shard_map/all_to_all | solution.py:45
  55.9 14.5 %all-to-all-start.1 = ((f32[32,5,128]{2,1,0:T(8,128)}), f32[32,5,128]{2,1,0:T(8,128)S(1)}, u32[]{:S(2)}, u32[]{:S(2)}) async-start(f32[32,5,128]{2,1,0:T(8,128)} %broadcast_in_dim.85), calls=%async_computation.1 | async-start | bytes 262144 | tf_op jit(solution)/shard_map/all_to_all | solution.py:47
  61.3 12.8 %copy-start.5 = (bf16[256,1024]{0,1:T(8,128)(2,1)S(1)}, bf16[256,1024]{0,1:T(8,128)(2,1)}, u32[]{:S(2)}) copy-start(bf16[256,1024]{0,1:T(8,128)(2,1)} %copy.21) | copy-start | bytes 1572868
  74.1 5.3 %copy-start.8 = (bf16[512,256]{1,0:T(8,128)(2,1)S(1)}, bf16[512,256]{1,0:T(8,128)(2,1)}, u32[]{:S(2)}) copy-start(bf16[512,256]{1,0:T(8,128)(2,1)} %param.23) | copy-start | bytes 786436
  74.5 4.6 %collective-permute-start.3 = (f32[512,512]{1,0:T(8,128)S(1)}, f32[512,512]{1,0:T(8,128)S(1)}, u32[]{:S(2)}, u32[]{:S(2)}) collective-permute-start(f32[512,512]{1,0:T(8,128)S(1)} %fusion.53), channel_id=1, source_target_pairs={{0,256},{256,0},{1,257},{257,1},{2,258},{258,2},{3,259},{259,3},{4... | collective-permute-start | bytes 3145736 | tf_op jit(solution)/shard_map/ppermute | solution.py:32
  79.4 13.0 %copy-start.2 = (bf16[512,512]{1,0:T(8,128)(2,1)}, bf16[512,512]{1,0:T(8,128)(2,1)S(1)}, u32[]{:S(2)}) copy-start(bf16[512,512]{1,0:T(8,128)(2,1)S(1)} %fusion.21) | copy-start | bytes 1572868
  79.4 4.3 %copy-start.10 = (bf16[1,128,256]{2,1,0:T(8,128)(2,1)S(1)}, bf16[1,128,256]{2,1,0:T(8,128)(2,1)}, u32[]{:S(2)}) copy-start(bf16[1,128,256]{2,1,0:T(8,128)(2,1)} %param.17) | copy-start | bytes 196612
  79.4 4.3 %copy-start.11 = (s32[1,512]{1,0:T(1,128)S(1)}, s32[1,512]{1,0:T(1,128)}, u32[]{:S(2)}) copy-start(s32[1,512]{1,0:T(1,128)} %param.16) | copy-start | bytes 6148
  79.8 3.8 %collective-permute-start.4 = (f32[512,256]{0,1:T(8,128)S(1)}, f32[512,256]{0,1:T(8,128)S(1)}, u32[]{:S(2)}, u32[]{:S(2)}) collective-permute-start(f32[512,256]{0,1:T(8,128)S(1)} %fusion.106), channel_id=1, source_target_pairs={{0,256},{256,0},{1,257},{257,1},{2,258},{258,2},{3,259},{259,3},{4... | collective-permute-start | bytes 1572872 | tf_op jit(solution)/shard_map/ppermute | solution.py:32
  85.6 6.6 %collective-permute-start.5 = (f32[512,256]{0,1:T(8,128)S(1)}, f32[512,256]{0,1:T(8,128)S(1)}, u32[]{:S(2)}, u32[]{:S(2)}) collective-permute-start(f32[512,256]{0,1:T(8,128)S(1)} %convolution_multiply_fusion), channel_id=1, source_target_pairs={{0,256},{256,0},{1,257},{257,1},{2,258},{258,2},{3,259},{259,3},{4... | collective-permute-start | bytes 1572872 | tf_op jit(solution)/shard_map/ppermute | solution.py:32
  88.3 3.2 %collective-permute-start.6 = (f32[]{:T(128)}, f32[]{:T(128)}, u32[]{:S(2)}, u32[]{:S(2)}) collective-permute-start(f32[]{:T(128)} %div.44), channel_id=1, source_target_pairs={{0,256},{256,0},{1,257},{257,1},{2,258},{258,2},{3,259},{259,3},{4... | collective-permute-start | bytes 20 | tf_op jit(solution)/shard_map/ppermute | solution.py:32

commit v4 on v3

--- a/solution.py
+++ b/solution.py
@@ -30,6 +30,12 @@
 
 def swap_sec(x):
     return lax.ppermute(x, "sec", [(0, 1), (1, 0)])
+
+
+def join_sec(mine, other, sec, axis):
+    first = jnp.where(sec == 0, mine, other)
+    second = jnp.where(sec == 0, other, mine)
+    return jnp.concatenate([first, second], axis=axis)
 
 
 def sum_sec(x):
@@ -139,6 +145,9 @@
     sec = lax.axis_index("sec")
     width = normed.shape[1]
     other_rows = swap_sec(normed)
+    peak_all = join_sec(peak_part, swap_sec(peak_part), sec, 0)
+    out_cols = w_out.reshape(w_out.shape[0], 2, width)
+    out_rows = join_sec(out_cols[:, sec, :], swap_sec(out_cols[:, 1 - sec, :]), sec, 0)
 
     def project(weight):
         halves = weight.reshape(2, width, weight.shape[1])
@@ -157,25 +166,20 @@
     packed = sum_atoms(state_rows)
     outer_state, key_total = packed[:, :HEAD_DIM, :], packed[:, HEAD_DIM, :]
     attended = read_summary(query_f.astype(jnp.bfloat16), outer_state, key_total, head_count)
-    out_sum = lax.psum(jnp.sum(attended * attended, axis=-1), "sec")
-    attended_n = (attended * lax.rsqrt(out_sum[:, None] / (HEADS * HEAD_DIM) + EPSILON)).astype(
+    attended_all = join_sec(attended, swap_sec(attended), sec, 1)
+    out_sum = jnp.sum(attended_all * attended_all, axis=-1)
+    attended_n = (attended_all * lax.rsqrt(out_sum[:, None] / (HEADS * HEAD_DIM) + EPSILON)).astype(
         jnp.bfloat16
     )
-    out_cols = w_out.reshape(w_out.shape[0], 2, width)
-    sent = jnp.dot(attended_n, out_cols[:, 1 - sec, :], preferred_element_type=jnp.float32)
-    kept = jnp.dot(attended_n, out_cols[:, sec, :], preferred_element_type=jnp.float32)
-    branch = kept + swap_sec(sent)
+    branch = jnp.dot(attended_n, out_rows, preferred_element_type=jnp.float32)
     hidden_two = (hidden_f + branch).astype(jnp.bfloat16)
     embedded = sum_sec(jnp.dot(hidden_two, w_proj, preferred_element_type=jnp.float32))
     embed_scale = lax.rsqrt(jnp.mean(embedded * embedded, axis=-1, keepdims=True) + EPSILON)
     unit_rows = embedded * embed_scale
-    peak_start = sec * peak_part.shape[0]
-    loss_part, unit_grad = contrast(unit_rows, peak_part, label_row, atom_mask, peak_start)
-    unit_grad = sum_sec(unit_grad)
+    loss_part, unit_grad = contrast(unit_rows, peak_all, label_row, atom_mask, 0)
     embed_grad = embed_backward(unit_rows, unit_grad, embed_scale)
     proj_part = jnp.einsum("nd,ne->de", hidden_two, embed_grad, preferred_element_type=jnp.float32)
-    loss_pair = sum_sec(loss_part)
-    packed = sum_atoms(jnp.concatenate([proj_part.reshape(-1), loss_pair.reshape(1)]))
+    packed = sum_atoms(jnp.concatenate([proj_part.reshape(-1), loss_part.reshape(1)]))
     proj_total = packed[: proj_part.size].reshape(proj_part.shape)
     loss_total = packed[proj_part.size] / (local_rows * lax.axis_size("atoms"))
     return (hidden_two[None], loss_total.reshape(1), proj_total[None])

time: 147 us -> 141 us (0.959)
  blocking collectives: 54.3 us -> 51.7 us
  waiting for transfers between devices: 27.2 us -> 25 us
    psum x1 -> x0, blocking collectives: 2.47 us -> none  [shards(): out_sum = lax.psum(jnp.sum(attended * attended, axis=-1), 'sec')]
    ppermute x5, waiting for transfers between devices: 4.96 us -> 2.87 us  [swap_sec(): return lax.ppermute(x, 'sec', [(0, 1), (1, 0)])]
  transfers between devices with their start and end apart: 9 -> 9, of which waited for: 6 -> 6; matrix products, arithmetic and copies ran while one was open for 5% -> 6% of each run, Pallas kernels for 0% -> 0%
where the time goes in v4:
time: 141 us
  blocking collectives  51.7 us (37%)
  starting transfers between devices  32.5 us (23%)
  waiting for transfers between devices  25 us (18%)
  matrix products  13.3 us (9%)
  local copies, waits for them, and re-layouts  10.5 us (7%)
  between operations  4.18 us (3%)
  other arithmetic  3.51 us (2%)
    all_to_all x1, blocking collectives, sum_atoms(): lax.all_to_all(jnp.broadcast_to(owned, pieces.shape), 'atoms', 0, 0, tile...  25.5 us
    all_to_all x1, blocking collectives, sum_atoms(): arrived = lax.all_to_all(pieces, 'atoms', 0, 0, tiled=True)  23.8 us
    all_to_all x1, starting transfers between devices, sum_atoms(): arrived = lax.all_to_all(pieces, 'atoms', 0, 0, tiled=True)  13.1 us
    ppermute x5, starting transfers between devices, swap_sec(): return lax.ppermute(x, 'sec', [(0, 1), (1, 0)])  10.7 us
    all_to_all x1, waiting for transfers between devices, sum_atoms(): arrived = lax.all_to_all(pieces, 'atoms', 0, 0, tiled=True)  9.59 us
    all_to_all x1, waiting for transfers between devices, sum_atoms(): lax.all_to_all(jnp.broadcast_to(owned, pieces.shape), 'atoms', 0, 0, tile...  9.09 us
    all_to_all x1, starting transfers between devices, sum_atoms(): lax.all_to_all(jnp.broadcast_to(owned, pieces.shape), 'atoms', 0, 0, tile...  3.84 us
    dot_general x3, matrix products, project(): jnp.dot(other_rows, halves[1 - sec], preferred_element_type=jnp.float32)  3.54 us
  transfers between devices with their start and end apart: 9, of which 6 were waited for; matrix products, arithmetic and copies ran while one was open for 6% of the time, Pallas kernels for 0%

profile of v4, /device:TPU:6, one launch (start us, length us, event | category | flops | bytes accessed | tf_op | source)
XLA Modules:
  0.0 140.7 jit_solution(14058247962040386680)
XLA Ops:
  0.7 1.2 slice_bitcast_fusion.1
  1.8 3.5 %collective-permute-start = (bf16[256,512]{1,0:T(8,128)(2,1)S(1)}, bf16[256,512]{1,0:T(8,128)(2,1)S(1)}, u32[]{:S(2)}, u32[]{:S(2)}) collective-permute-start(bf16[256,512]{1,0:T(8,128)(2,1)S(1)} %get-tuple-element.15), channel_id=1, source_target_pairs={{0,8},{8,16},{16,24},{24,32},{32,40},{40,48},{48,56},{56,64},{64,7... | collective-permute-start | bytes 786440 | tf_op jit(solution)/shard_map/ppermute | solution.py:25
  5.3 1.3 collective-permute-start.1
  6.6 0.8 compare_and_fusion
  7.4 0.7 fusion.90
  8.7 0.7 convert_element_type.126
  9.4 2.0 %copy.23 = bf16[256,1024]{0,1:T(8,128)(2,1)} copy(bf16[256,1024]{1,0:T(8,128)(2,1)} %param.22) | data formatting | bytes 1048576 | tf_op args[10]
  11.5 3.5 %collective-permute-done.1 = bf16[256,512]{1,0:T(8,128)(2,1)S(1)} collective-permute-done((bf16[256,512]{1,0:T(8,128)(2,1)S(1)}, bf16[256,512]{1,0:T(8,128)(2,1)S(1)}, u32[]{:S(2)}, u32[]{:S(2)}) %collective-permute-start.1) | collective-permute-done | bytes 262176 | tf_op jit(solution)/shard_map/ppermute | solution.py:26
  15.1 2.0 %gather_fusion = bf16[16,128,512]{2,1,0:T(8,128)(2,1)} fusion(bf16[8,128,512]{2,1,0:T(8,128)(2,1)S(1)} %bitcast.121, s32[1024]{0:T(1024)S(1)} %pad_clamp_fusion), kind=kCustom, calls=%fused_computation | custom fusion | bytes 4194368 | tf_op jit(solution)/shard_map/jit(_take)/gather | solution.py:74
  17.1 2.9 %fusion.16 = f32[4,128,512]{2,1,0:T(8,128)S(1)} fusion(bf16[16,128,512]{2,1,0:T(8,128)(2,1)} %gather_fusion, pred[16]{0:T(512)(128)(4,1)S(1)} %get-tuple-element.7, pred[4,16]{1,0:T(4,128)(4,1)S(1)} %iota_compare_fusion.3, bf16[16,128,128]{2,1,0:T(8,128)(2,1)S(1)} %bitcast.139), kind=kOutput, calls=%fused_computation.17 | convolution fusion | flops 1076363264 | bytes 3670096 | tf_op jit(solution)/shard_map/btij,tjf->bif/dot_general | solution.py:77
  20.2 2.5 %psum.7 = f32[512]{0:T(512)S(1)} all-reduce(f32[512]{0:T(512)S(1)} %get-tuple-element.5), channel_id=1, replica_groups=mesh['sec'=2,'atoms'=32,'batch'=8] {'sec'}, use_global_device_ids=true, to_apply=%region_1.2 | all-reduce | flops 512 | bytes 4096 | tf_op jit(solution)/shard_map/psum | solution.py:141
  22.9 2.1 %collective-permute-start.2 = (bf16[512,512]{1,0:T(8,128)(2,1)S(1)}, bf16[512,512]{1,0:T(8,128)(2,1)S(1)}, u32[]{:S(2)}, u32[]{:S(2)}) collective-permute-start(bf16[512,512]{1,0:T(8,128)(2,1)S(1)} %fusion.30), channel_id=1, source_target_pairs={{0,256},{256,0},{1,257},{257,1},{2,258},{258,2},{3,259},{259,3},{4... | collective-permute-start | bytes 1572872 | tf_op jit(solution)/shard_map/ppermute | solution.py:32
  25.9 0.8 collective-permute-done.2
  26.7 0.8 copy-done.4
  28.4 1.4 fusion.25
  31.2 13.1 %all-to-all-start = ((f32[32,5,128]{2,1,0:T(8,128)}), f32[32,5,128]{2,1,0:T(8,128)S(1)}, u32[]{:S(2)}, u32[]{:S(2)}) async-start(f32[32,5,128]{2,1,0:T(8,128)} %reshape.262), calls=%async_computation | async-start | bytes 262144 | tf_op jit(solution)/shard_map/all_to_all | solution.py:51
  44.4 1.3 fusion.59
  45.7 9.6 %all-to-all-done = f32[32,5,128]{2,1,0:T(8,128)S(1)} async-done(((f32[32,5,128]{2,1,0:T(8,128)}), f32[32,5,128]{2,1,0:T(8,128)S(1)}, u32[]{:S(2)}, u32[]{:S(2)}) %all-to-all-start) | async-done | bytes 81952 | tf_op jit(solution)/shard_map/all_to_all | solution.py:51
  56.0 3.8 %all-to-all-start.1 = ((f32[32,5,128]{2,1,0:T(8,128)}), f32[32,5,128]{2,1,0:T(8,128)S(1)}, u32[]{:S(2)}, u32[]{:S(2)}) async-start(f32[32,5,128]{2,1,0:T(8,128)} %broadcast_in_dim.85), calls=%async_computation.1 | async-start | bytes 262144 | tf_op jit(solution)/shard_map/all_to_all | solution.py:53
  59.8 1.5 %fusion.42 = f32[512,256]{0,1:T(8,128)S(1)} fusion(f32[512,256]{0,1:T(8,128)S(1)} %fusion.59, bf16[512,512]{1,0:T(8,128)(2,1)S(1)} %copy-done.5, bf16[2,512,256]{2,1,0:T(8,128)(2,1)} %bitcast.135, s32[]{:T(128)S(6)} %select_n.132), kind=kOutput, calls=%fused_computation.55 | convolution fusion | flops 135135232 | bytes 1835012 | tf_op jit(solution)/shard_map/dot_general | solution.py:155
  61.4 9.1 %all-to-all-done.1 = f32[32,5,128]{2,1,0:T(8,128)S(1)} async-done(((f32[32,5,128]{2,1,0:T(8,128)}), f32[32,5,128]{2,1,0:T(8,128)S(1)}, u32[]{:S(2)}, u32[]{:S(2)}) %all-to-all-start.1) | async-done | bytes 81952 | tf_op jit(solution)/shard_map/all_to_all | solution.py:53
  71.6 1.9 %collective-permute-start.3 = (f32[512,256]{0,1:T(8,128)S(1)}, f32[512,256]{0,1:T(8,128)S(1)}, u32[]{:S(2)}, u32[]{:S(2)}) collective-permute-start(f32[512,256]{0,1:T(8,128)S(1)} %bitcast.130), channel_id=1, source_target_pairs={{0,256},{256,0},{1,257},{257,1},{2,258},{258,2},{3,259},{259,3},{4... | collective-permute-start | bytes 1572872 | tf_op jit(solution)/shard_map/ppermute | solution.py:32
  73.7 2.4 %collective-permute-start.4 = (bf16[256,512]{1,0:T(8,128)(2,1)S(1)}, bf16[256,512]{1,0:T(8,128)(2,1)S(1)}, u32[]{:S(2)}, u32[]{:S(2)}) collective-permute-start(bf16[256,512]{1,0:T(8,128)(2,1)S(1)} %bitcast.136), channel_id=1, source_target_pairs={{0,256},{256,0},{1,257},{257,1},{2,258},{258,2},{3,259},{259,3},{4... | collective-permute-start | bytes 786440 | tf_op jit(solution)/shard_map/ppermute | solution.py:32
  76.3 1.0 collective-permute-done.4
  78.8 2.3 %collective-permute-start.5 = (f32[512,256]{0,1:T(8,128)S(1)}, f32[512,256]{0,1:T(8,128)S(1)}, u32[]{:S(2)}, u32[]{:S(2)}) collective-permute-start(f32[512,256]{0,1:T(8,128)S(1)} %fusion.101), channel_id=1, source_target_pairs={{0,256},{256,0},{1,257},{257,1},{2,258},{258,2},{3,259},{259,3},{4... | collective-permute-start | bytes 1572872 | tf_op jit(solution)/shard_map/ppermute | solution.py:32
  81.1 2.0 %collective-permute-start.6 = (bf16[128,256]{1,0:T(8,128)(2,1)S(1)}, bf16[128,256]{1,0:T(8,128)(2,1)S(1)}, u32[]{:S(2)}, u32[]{:S(2)}) collective-permute-start(bf16[128,256]{1,0:T(8,128)(2,1)S(1)} %bitcast.137), channel_id=1, source_target_pairs={{0,256},{256,0},{1,257},{257,1},{2,258},{258,2},{3,259},{259,3},{4... | collective-permute-start | bytes 196616 | tf_op jit(solution)/shard_map/ppermute | solution.py:32
  83.1 1.1 collective-permute-done.6
  84.4 1.5 %fusion.38 = (f32[]{:T(128)}, f32[512,256]{0,1:T(8,128)S(1)}) fusion(s32[512]{0:T(512)S(1)} %bitcast.140, f32[512]{0:T(512)S(1)} %fusion.89, bf16[128,256]{1,0:T(8,128)(2,1)S(1)} %get-tuple-element.18, bf16[128,256]{1,0:T(8,128)(2,1)S(1)} %get-tuple-element.17, f32[512,256]{0,1:T(8,128)S(1)} %get-tuple-element.4, f32[512]{0:T(512)S(1)} %add_rsqrt_fusion), kind=kOutput, calls=%fused_computation.51 | convolution fusion | flops 404881408 | bytes 1185796 | tf_op jit(solution)/shard_map/dot_general | solution.py:103
  85.8 0.7 multiply_reduce_fusion.1
  88.0 23.8 %all_to_all.20 = f32[32,33,128]{2,1,0:T(8,128)S(1)} all-to-all(f32[32,33,128]{2,1,0:T(8,128)S(1)} %reshape.270), channel_id=1, replica_groups=mesh['sec'=2,'atoms'=32,'batch'=8] {'atoms'}, dimensions={0} | all-to-all | bytes 1081344 | tf_op jit(solution)/shard_map/all_to_all | solution.py:51
  111.8 25.5 %all_to_all.21 = f32[32,33,128]{2,1,0:T(8,128)S(1)} all-to-all(f32[32,33,128]{2,1,0:T(8,128)S(1)} %broadcast_in_dim.87), channel_id=1, replica_groups=mesh['sec'=2,'atoms'=32,'batch'=8] {'atoms'}, dimensions={0} | all-to-all | bytes 1081344 | tf_op jit(solution)/shard_map/all_to_all | solution.py:53
  137.9 0.9 broadcast_in_dim_reshape.3
  (74 shorter events, 8.9 us)
Async XLA Ops:
  0.6 24.6 %copy-start = (bf16[1024,256]{1,0:T(8,128)(2,1)S(1)}, bf16[1024,256]{1,0:T(8,128)(2,1)}, u32[]{:S(2)}) copy-start(bf16[1024,256]{1,0:T(8,128)(2,1)} %param.20) | copy-start | bytes 1572868
  0.6 14.3 %copy-start.1 = (bf16[1,512,512]{2,1,0:T(8,128)(2,1)S(1)}, bf16[1,512,512]{2,1,0:T(8,128)(2,1)}, u32[]{:S(2)}) copy-start(bf16[1,512,512]{2,1,0:T(8,128)(2,1)} %param.12) | copy-start | bytes 1572868
  1.8 9.7 %collective-permute-start = (bf16[256,512]{1,0:T(8,128)(2,1)S(1)}, bf16[256,512]{1,0:T(8,128)(2,1)S(1)}, u32[]{:S(2)}, u32[]{:S(2)}) collective-permute-start(bf16[256,512]{1,0:T(8,128)(2,1)S(1)} %get-tuple-element.15), channel_id=1, source_target_pairs={{0,8},{8,16},{16,24},{24,32},{32,40},{40,48},{48,56},{56,64},{64,7... | collective-permute-start | bytes 786440 | tf_op jit(solution)/shard_map/ppermute | solution.py:25
  5.3 9.7 %collective-permute-start.1 = (bf16[256,512]{1,0:T(8,128)(2,1)S(1)}, bf16[256,512]{1,0:T(8,128)(2,1)S(1)}, u32[]{:S(2)}, u32[]{:S(2)}) collective-permute-start(bf16[256,512]{1,0:T(8,128)(2,1)S(1)} %get-tuple-element.16), channel_id=1, source_target_pairs={{8,0},{16,8},{24,16},{32,24},{40,32},{48,40},{56,48},{64,56},{72,6... | collective-permute-start | bytes 786440 | tf_op jit(solution)/shard_map/ppermute | solution.py:26
  15.0 2.0 %copy-start.10 = (bf16[1,16,128,128]{3,2,1,0:T(8,128)(2,1)S(1)}, bf16[1,16,128,128]{3,2,1,0:T(8,128)(2,1)}, u32[]{:S(2)}) copy-start(bf16[1,16,128,128]{3,2,1,0:T(8,128)(2,1)} %param.14) | copy-start | bytes 1572868
  22.7 2.9 %copy-start.6 = (bf16[1024,256]{1,0:T(8,128)(2,1)S(1)}, bf16[1024,256]{1,0:T(8,128)(2,1)}, u32[]{:S(2)}) copy-start(bf16[1024,256]{1,0:T(8,128)(2,1)} %param.21) | copy-start | bytes 1572868
  22.9 3.8 %collective-permute-start.2 = (bf16[512,512]{1,0:T(8,128)(2,1)S(1)}, bf16[512,512]{1,0:T(8,128)(2,1)S(1)}, u32[]{:S(2)}, u32[]{:S(2)}) collective-permute-start(bf16[512,512]{1,0:T(8,128)(2,1)S(1)} %fusion.30), channel_id=1, source_target_pairs={{0,256},{256,0},{1,257},{257,1},{2,258},{258,2},{3,259},{259,3},{4... | collective-permute-start | bytes 1572872 | tf_op jit(solution)/shard_map/ppermute | solution.py:32
  25.2 3.2 %copy-start.7 = (bf16[1024,256]{1,0:T(8,128)(2,1)S(1)}, bf16[1024,256]{1,0:T(8,128)(2,1)}, u32[]{:S(2)}) copy-start(bf16[1024,256]{1,0:T(8,128)(2,1)} %param.21) | copy-start | bytes 1572868
  26.7 0.8 copy-start.4
  29.8 30.1 %copy-start.5 = (bf16[512,512]{1,0:T(8,128)(2,1)S(1)}, bf16[512,512]{1,0:T(8,128)(2,1)}, u32[]{:S(2)}) copy-start(bf16[512,512]{1,0:T(8,128)(2,1)} %copy-done.4) | copy-start | bytes 1572868
  31.2 24.0 %all-to-all-start = ((f32[32,5,128]{2,1,0:T(8,128)}), f32[32,5,128]{2,1,0:T(8,128)S(1)}, u32[]{:S(2)}, u32[]{:S(2)}) async-start(f32[32,5,128]{2,1,0:T(8,128)} %reshape.262), calls=%async_computation | async-start | bytes 262144 | tf_op jit(solution)/shard_map/all_to_all | solution.py:51
  56.0 14.5 %all-to-all-start.1 = ((f32[32,5,128]{2,1,0:T(8,128)}), f32[32,5,128]{2,1,0:T(8,128)S(1)}, u32[]{:S(2)}, u32[]{:S(2)}) async-start(f32[32,5,128]{2,1,0:T(8,128)} %broadcast_in_dim.85), calls=%async_computation.1 | async-start | bytes 262144 | tf_op jit(solution)/shard_map/all_to_all | solution.py:53
  59.8 13.7 %copy-start.2 = (bf16[256,1024]{0,1:T(8,128)(2,1)S(1)}, bf16[256,1024]{0,1:T(8,128)(2,1)}, u32[]{:S(2)}) copy-start(bf16[256,1024]{0,1:T(8,128)(2,1)} %copy.23) | copy-start | bytes 1572868
  71.6 5.7 %collective-permute-start.3 = (f32[512,256]{0,1:T(8,128)S(1)}, f32[512,256]{0,1:T(8,128)S(1)}, u32[]{:S(2)}, u32[]{:S(2)}) collective-permute-start(f32[512,256]{0,1:T(8,128)S(1)} %bitcast.130), channel_id=1, source_target_pairs={{0,256},{256,0},{1,257},{257,1},{2,258},{258,2},{3,259},{259,3},{4... | collective-permute-start | bytes 1572872 | tf_op jit(solution)/shard_map/ppermute | solution.py:32
  73.7 3.6 %collective-permute-start.4 = (bf16[256,512]{1,0:T(8,128)(2,1)S(1)}, bf16[256,512]{1,0:T(8,128)(2,1)S(1)}, u32[]{:S(2)}, u32[]{:S(2)}) collective-permute-start(bf16[256,512]{1,0:T(8,128)(2,1)S(1)} %bitcast.136), channel_id=1, source_target_pairs={{0,256},{256,0},{1,257},{257,1},{2,258},{258,2},{3,259},{259,3},{4... | collective-permute-start | bytes 786440 | tf_op jit(solution)/shard_map/ppermute | solution.py:32
  77.5 1.0 copy-start.8
  77.6 3.5 %copy-start.9 = (bf16[1,128,256]{2,1,0:T(8,128)(2,1)S(1)}, bf16[1,128,256]{2,1,0:T(8,128)(2,1)}, u32[]{:S(2)}) copy-start(bf16[1,128,256]{2,1,0:T(8,128)(2,1)} %param.17) | copy-start | bytes 196612
  78.4 8.1 %copy-start.3 = (bf16[512,512]{1,0:T(8,128)(2,1)}, bf16[512,512]{1,0:T(8,128)(2,1)S(1)}, u32[]{:S(2)}) copy-start(bf16[512,512]{1,0:T(8,128)(2,1)S(1)} %fusion.21) | copy-start | bytes 1572868
  78.4 6.0 %copy-start.11 = (s32[1,512]{1,0:T(1,128)S(1)}, s32[1,512]{1,0:T(1,128)}, u32[]{:S(2)}) copy-start(s32[1,512]{1,0:T(1,128)} %param.16) | copy-start | bytes 6148
  78.8 5.5 %collective-permute-start.5 = (f32[512,256]{0,1:T(8,128)S(1)}, f32[512,256]{0,1:T(8,128)S(1)}, u32[]{:S(2)}, u32[]{:S(2)}) collective-permute-start(f32[512,256]{0,1:T(8,128)S(1)} %fusion.101), channel_id=1, source_target_pairs={{0,256},{256,0},{1,257},{257,1},{2,258},{258,2},{3,259},{259,3},{4... | collective-permute-start | bytes 1572872 | tf_op jit(solution)/shard_map/ppermute | solution.py:32
  81.1 3.1 %collective-permute-start.6 = (bf16[128,256]{1,0:T(8,128)(2,1)S(1)}, bf16[128,256]{1,0:T(8,128)(2,1)S(1)}, u32[]{:S(2)}, u32[]{:S(2)}) collective-permute-start(bf16[128,256]{1,0:T(8,128)(2,1)S(1)} %bitcast.137), channel_id=1, source_target_pairs={{0,256},{256,0},{1,257},{257,1},{2,258},{258,2},{3,259},{259,3},{4... | collective-permute-start | bytes 196616 | tf_op jit(solution)/shard_map/ppermute | solution.py:32

commit v5 on v4

--- a/solution.py
+++ b/solution.py
@@ -36,10 +36,6 @@
     first = jnp.where(sec == 0, mine, other)
     second = jnp.where(sec == 0, other, mine)
     return jnp.concatenate([first, second], axis=axis)
-
-
-def sum_sec(x):
-    return x + swap_sec(x)
 
 
 def sum_atoms(x):
@@ -130,31 +126,29 @@
     w_proj,
 ):
     atom_rows = atoms_in[0]
-    local_rows = atom_rows.shape[0]
+    local_rows, width = atom_rows.shape
+    sec = lax.axis_index("sec")
+    peak_part = peak_embed[0]
+    partner = swap_sec((norm_gain, peak_part, w_out, w_proj))
+    gain_all, peak_all, out_all, proj_all = (
+        join_sec(mine, other, sec, 0)
+        for mine, other in zip((norm_gain, peak_part, w_out, w_proj), partner)
+    )
     gathered = message_pass(atom_rows, tile_ids[0], tile_vals[0])
     hidden_one = (atom_rows.astype(jnp.float32) + gathered.astype(jnp.float32)).astype(jnp.bfloat16)
+    hidden_f = join_sec(hidden_one, swap_sec(hidden_one), sec, 1).astype(jnp.float32)
     atom_base = lax.axis_index("atoms") * local_rows
     length_one = seq_lens[0]
     label_row = pair_labels[0]
-    peak_part = peak_embed[0]
-    hidden_f = hidden_one.astype(jnp.float32)
-    square_sum = lax.psum(jnp.sum(hidden_f * hidden_f, axis=-1), "sec")
-    row_scale = lax.rsqrt(square_sum[:, None] / D + EPSILON)
-    normed = (hidden_f * row_scale * norm_gain.astype(jnp.float32)).astype(jnp.bfloat16)
+    row_scale = lax.rsqrt(jnp.mean(hidden_f * hidden_f, axis=-1, keepdims=True) + EPSILON)
+    normed = (hidden_f * row_scale * gain_all.astype(jnp.float32)).astype(jnp.bfloat16)
     head_cols = w_query.shape[1]
-    sec = lax.axis_index("sec")
-    width = normed.shape[1]
-    other_rows = swap_sec(normed)
-    peak_all = join_sec(peak_part, swap_sec(peak_part), sec, 0)
-    out_cols = w_out.reshape(w_out.shape[0], 2, width)
-    out_rows = join_sec(out_cols[:, sec, :], swap_sec(out_cols[:, 1 - sec, :]), sec, 0)
-
-    def project(weight):
-        halves = weight.reshape(2, width, weight.shape[1])
-        mine = jnp.dot(normed, halves[sec], preferred_element_type=jnp.float32)
-        return mine + jnp.dot(other_rows, halves[1 - sec], preferred_element_type=jnp.float32)
-
-    query_f, key_f, value_f = tuple((project(weight) for weight in (w_query, w_key, w_value)))
+    query_f, key_f, value_f = tuple(
+        (
+            jnp.dot(normed, weight, preferred_element_type=jnp.float32)
+            for weight in (w_query, w_key, w_value)
+        )
+    )
     head_count = head_cols // HEAD_DIM
     atom_mask = (atom_base + jnp.arange(local_rows, dtype=jnp.int32) < length_one).astype(
         jnp.float32
@@ -167,17 +161,16 @@
     outer_state, key_total = packed[:, :HEAD_DIM, :], packed[:, HEAD_DIM, :]
     attended = read_summary(query_f.astype(jnp.bfloat16), outer_state, key_total, head_count)
     attended_all = join_sec(attended, swap_sec(attended), sec, 1)
-    out_sum = jnp.sum(attended_all * attended_all, axis=-1)
-    attended_n = (attended_all * lax.rsqrt(out_sum[:, None] / (HEADS * HEAD_DIM) + EPSILON)).astype(
-        jnp.bfloat16
-    )
-    branch = jnp.dot(attended_n, out_rows, preferred_element_type=jnp.float32)
-    hidden_two = (hidden_f + branch).astype(jnp.bfloat16)
-    embedded = sum_sec(jnp.dot(hidden_two, w_proj, preferred_element_type=jnp.float32))
+    out_scale = lax.rsqrt(jnp.mean(attended_all * attended_all, axis=-1, keepdims=True) + EPSILON)
+    attended_n = (attended_all * out_scale).astype(jnp.bfloat16)
+    branch = jnp.dot(attended_n, out_all, preferred_element_type=jnp.float32)
+    hidden_all = (hidden_f + branch).astype(jnp.bfloat16)
+    embedded = jnp.dot(hidden_all, proj_all, preferred_element_type=jnp.float32)
     embed_scale = lax.rsqrt(jnp.mean(embedded * embedded, axis=-1, keepdims=True) + EPSILON)
     unit_rows = embedded * embed_scale
     loss_part, unit_grad = contrast(unit_rows, peak_all, label_row, atom_mask, 0)
     embed_grad = embed_backward(unit_rows, unit_grad, embed_scale)
+    hidden_two = lax.dynamic_slice_in_dim(hidden_all, sec * width, width, axis=1)
     proj_part = jnp.einsum("nd,ne->de", hidden_two, embed_grad, preferred_element_type=jnp.float32)
     packed = sum_atoms(jnp.concatenate([proj_part.reshape(-1), loss_part.reshape(1)]))
     proj_total = packed[: proj_part.size].reshape(proj_part.shape)

time: 141 us -> 145 us (1.028)
  blocking collectives: 51.7 us -> 23.8 us
  waiting for transfers between devices: 25 us -> 46.1 us
  starting transfers between devices: 32.5 us -> 39 us
  other arithmetic: 3.51 us -> 7.32 us
    all_to_all x1 -> x0, blocking collectives: 25.5 us -> none  [sum_atoms(): lax.all_to_all(jnp.broadcast_to(owned, pieces.shape), 'atoms', 0, 0, tile...]
    all_to_all x1 -> x2, waiting for transfers between devices: 9.09 us -> 28.9 us  [sum_atoms(): lax.all_to_all(jnp.broadcast_to(owned, pieces.shape), 'atoms', 0, 0, tile...]
    all_to_all x1 -> x2, starting transfers between devices: 3.84 us -> 8.65 us  [sum_atoms(): lax.all_to_all(jnp.broadcast_to(owned, pieces.shape), 'atoms', 0, 0, tile...]
    select_n x3 -> x6, other arithmetic: 0.18 us -> 3.87 us  [join_sec(): first = jnp.where(sec == 0, mine, other)]
    unnamed x26 -> x17, local copies, waits for them, and re-layouts: 3.49 us -> 0.63 us
    ppermute x1, waiting for transfers between devices: 0.01 us -> 2.75 us  [extended(): before = lax.ppermute(last, axis, up)]
    psum x1 -> x0, blocking collectives: 2.46 us -> none  [shards(): square_sum = lax.psum(jnp.sum(hidden_f * hidden_f, axis=-1), 'sec')]
    ppermute x5 -> x6, waiting for transfers between devices: 2.87 us -> 0.71 us  [swap_sec(): return lax.ppermute(x, 'sec', [(0, 1), (1, 0)])]
  transfers between devices with their start and end apart: 9 -> 11, of which waited for: 6 -> 6; matrix products, arithmetic and copies ran while one was open for 6% -> 11% of each run, Pallas kernels for 0% -> 0%
where the time goes in v5:
time: 145 us; the launch traced here: 144 us
  waiting for transfers between devices  46.1 us (32%)
  starting transfers between devices  39 us (27%)
  blocking collectives  23.8 us (16%)
  matrix products  13.4 us (9%)
  local copies, waits for them, and re-layouts  10.2 us (7%)
  other arithmetic  7.32 us (5%)
  between operations  4.15 us (3%)
    all_to_all x2, waiting for transfers between devices, sum_atoms(): lax.all_to_all(jnp.broadcast_to(owned, pieces.shape), 'atoms', 0, 0, tile...  28.9 us
    all_to_all x1, blocking collectives, sum_atoms(): arrived = lax.all_to_all(pieces, 'atoms', 0, 0, tiled=True)  23.8 us
    all_to_all x1, starting transfers between devices, sum_atoms(): arrived = lax.all_to_all(pieces, 'atoms', 0, 0, tiled=True)  13.1 us
    ppermute x6, starting transfers between devices, swap_sec(): return lax.ppermute(x, 'sec', [(0, 1), (1, 0)])  12.5 us
    all_to_all x1, waiting for transfers between devices, sum_atoms(): arrived = lax.all_to_all(pieces, 'atoms', 0, 0, tiled=True)  9.59 us
    all_to_all x2, starting transfers between devices, sum_atoms(): lax.all_to_all(jnp.broadcast_to(owned, pieces.shape), 'atoms', 0, 0, tile...  8.65 us
    dot_general x3, matrix products, shards(): jnp.dot(normed, weight, preferred_element_type=jnp.float32)  4.31 us
    ppermute x1, waiting for transfers between devices, extended(): after = lax.ppermute(leading, axis, down)  4.13 us
  transfers between devices with their start and end apart: 11, of which 6 were waited for; matrix products, arithmetic and copies ran while one was open for 11% of the time, Pallas kernels for 0%

profile of v5, /device:TPU:6, one launch (start us, length us, event | category | flops | bytes accessed | tf_op | source)
XLA Modules:
  0.0 144.0 jit_solution(14159101707361651790)
XLA Ops:
  0.6 1.1 slice_bitcast_fusion.1
  1.8 3.5 %collective-permute-start = (bf16[256,512]{1,0:T(8,128)(2,1)S(1)}, bf16[256,512]{1,0:T(8,128)(2,1)S(1)}, u32[]{:S(2)}, u32[]{:S(2)}) collective-permute-start(bf16[256,512]{1,0:T(8,128)(2,1)S(1)} %get-tuple-element.13), channel_id=1, source_target_pairs={{0,8},{8,16},{16,24},{24,32},{32,40},{40,48},{48,56},{56,64},{64,7... | collective-permute-start | bytes 786440 | tf_op jit(solution)/shard_map/ppermute | solution.py:25
  5.3 1.3 collective-permute-start.1
  8.1 2.8 %collective-permute-done = bf16[256,512]{1,0:T(8,128)(2,1)S(1)} collective-permute-done((bf16[256,512]{1,0:T(8,128)(2,1)S(1)}, bf16[256,512]{1,0:T(8,128)(2,1)S(1)}, u32[]{:S(2)}, u32[]{:S(2)}) %collective-permute-start) | collective-permute-done | bytes 262176 | tf_op jit(solution)/shard_map/ppermute | solution.py:25
  10.8 4.1 %collective-permute-done.1 = bf16[256,512]{1,0:T(8,128)(2,1)S(1)} collective-permute-done((bf16[256,512]{1,0:T(8,128)(2,1)S(1)}, bf16[256,512]{1,0:T(8,128)(2,1)S(1)}, u32[]{:S(2)}, u32[]{:S(2)}) %collective-permute-start.1) | collective-permute-done | bytes 262176 | tf_op jit(solution)/shard_map/ppermute | solution.py:26
  14.9 1.1 pad_maximum_fusion
  16.1 2.0 %gather_fusion = bf16[16,128,512]{2,1,0:T(8,128)(2,1)} fusion(bf16[8,128,512]{2,1,0:T(8,128)(2,1)S(1)} %bitcast.69, s32[1024]{0:T(1024)S(1)} %pad_clamp_fusion), kind=kCustom, calls=%fused_computation | custom fusion | bytes 4194368 | tf_op jit(solution)/shard_map/jit(_take)/gather | solution.py:70
  18.1 3.0 %fusion.15 = bf16[4,128,512]{2,1,0:T(8,128)(2,1)S(1)} fusion(bf16[16,128,512]{2,1,0:T(8,128)(2,1)} %gather_fusion, pred[16]{0:T(512)(128)(4,1)S(1)} %get-tuple-element.3, pred[4,16]{1,0:T(4,128)(4,1)S(1)} %iota_compare_fusion.3, bf16[16,128,128]{2,1,0:T(8,128)(2,1)S(1)} %bitcast.78), kind=kOutput, calls=%fused_computation.20 | convolution fusion | flops 1076101120 | bytes 3145808 | tf_op jit(solution)/shard_map/btij,tjf->bif/dot_general | solution.py:73
  21.3 1.9 %collective-permute-start.2 = (bf16[512,512]{1,0:T(8,128)(2,1)S(1)}, bf16[512,512]{1,0:T(8,128)(2,1)}, u32[]{:S(2)}, u32[]{:S(2)}) collective-permute-start(bf16[512,512]{1,0:T(8,128)(2,1)S(1)} %fusion.26), channel_id=1, source_target_pairs={{0,256},{256,0},{1,257},{257,1},{2,258},{258,2},{3,259},{259,3},{4... | collective-permute-start | bytes 1572872 | tf_op jit(solution)/shard_map/ppermute | solution.py:32
  23.2 2.4 %collective-permute-start.3 = (bf16[512]{0:T(512)(128)(2,1)S(1)}, bf16[512]{0:T(512)(128)(2,1)S(1)}, u32[]{:S(2)}, u32[]{:S(2)}) collective-permute-start(bf16[512]{0:T(512)(128)(2,1)S(1)} %copy-done.5), channel_id=1, source_target_pairs={{0,256},{256,0},{1,257},{257,1},{2,258},{258,2},{3,259},{259,3},{4... | collective-permute-start | bytes 3080 | tf_op jit(solution)/shard_map/ppermute | solution.py:32
  25.6 1.9 %collective-permute-start.5 = (bf16[256,1024]{1,0:T(8,128)(2,1)S(1)}, bf16[256,1024]{1,0:T(8,128)(2,1)S(1)}, u32[]{:S(2)}, u32[]{:S(2)}) collective-permute-start(bf16[256,1024]{1,0:T(8,128)(2,1)S(1)} %copy-done.2), channel_id=1, source_target_pairs={{0,256},{256,0},{1,257},{257,1},{2,258},{258,2},{3,259},{259,3},{4... | collective-permute-start | bytes 1572872 | tf_op jit(solution)/shard_map/ppermute | solution.py:32
  27.6 2.4 %collective-permute-start.6 = (bf16[512,256]{1,0:T(8,128)(2,1)}, bf16[512,256]{1,0:T(8,128)(2,1)}, u32[]{:S(2)}, u32[]{:S(2)}) collective-permute-start(bf16[512,256]{1,0:T(8,128)(2,1)} %param.23), channel_id=1, source_target_pairs={{0,256},{256,0},{1,257},{257,1},{2,258},{258,2},{3,259},{259,3},{4... | collective-permute-start | bytes 786440 | tf_op jit(solution)/shard_map/ppermute | solution.py:32
  30.0 1.9 %collective-permute-start.7 = (bf16[128,256]{1,0:T(8,128)(2,1)}, bf16[128,256]{1,0:T(8,128)(2,1)}, u32[]{:S(2)}, u32[]{:S(2)}) collective-permute-start(bf16[128,256]{1,0:T(8,128)(2,1)} %bitcast.25), channel_id=1, source_target_pairs={{0,256},{256,0},{1,257},{257,1},{2,258},{258,2},{3,259},{259,3},{4... | collective-permute-start | bytes 196616 | tf_op jit(solution)/shard_map/ppermute | solution.py:32
  32.6 1.1 broadcast_select_fusion.3
  34.1 1.6 %convolution_convert_fusion.1 = bf16[512,256]{0,1:T(8,128)(2,1)S(1)} fusion(bf16[1024,256]{1,0:T(8,128)(2,1)} %param.21, f32[1024]{0:T(1024)S(1)} %maximum_convert_fusion, f32[512]{0:T(512)S(1)} %add_rsqrt_fusion.2, bf16[512,512]{1,0:T(8,128)(2,1)S(1)} %get-tuple-element.8, bf16[512,512]{1,0:T(8,128)(2,1)S(1)} %get-tuple-element.7), kind=kOutput, calls=%fused_computation.28 | convolution fusion | flops 272236544 | bytes 1841152 | tf_op jit(solution)/shard_map/dot_general | solution.py:148
  35.7 0.9 multiply_reduce_fusion.3
  38.3 13.1 %all-to-all-start = ((f32[32,5,128]{2,1,0:T(8,128)}), f32[32,5,128]{2,1,0:T(8,128)S(1)}, u32[]{:S(2)}, u32[]{:S(2)}) async-start(f32[32,5,128]{2,1,0:T(8,128)} %reshape.216), calls=%async_computation | async-start | bytes 262144 | tf_op jit(solution)/shard_map/all_to_all | solution.py:47
  51.4 1.5 %broadcast_select_fusion.9 = (bf16[128,256]{1,0:T(8,128)(2,1)}, bf16[128,256]{1,0:T(8,128)(2,1)}) fusion(bf16[128,256]{1,0:T(8,128)(2,1)} %collective-permute-done.7, pred[]{:T(512)S(6)} %eq.20, bf16[1,128,256]{2,1,0:T(8,128)(2,1)} %param.17), kind=kLoop, calls=%fused_computation.97 | loop fusion | flops 65536 | bytes 262145 | tf_op jit(solution)/shard_map/jit(_where)/select_n | solution.py:36
  52.9 9.6 %all-to-all-done = f32[32,5,128]{2,1,0:T(8,128)S(1)} async-done(((f32[32,5,128]{2,1,0:T(8,128)}), f32[32,5,128]{2,1,0:T(8,128)S(1)}, u32[]{:S(2)}, u32[]{:S(2)}) %all-to-all-start) | async-done | bytes 81952 | tf_op jit(solution)/shard_map/all_to_all | solution.py:47
  63.2 3.9 %all-to-all-start.1 = ((f32[32,5,128]{2,1,0:T(8,128)}), f32[32,5,128]{2,1,0:T(8,128)S(1)}, u32[]{:S(2)}, u32[]{:S(2)}) async-start(f32[32,5,128]{2,1,0:T(8,128)} %broadcast_in_dim.85), calls=%async_computation.1 | async-start | bytes 262144 | tf_op jit(solution)/shard_map/all_to_all | solution.py:49
  67.1 1.8 %fusion.35 = f32[512,256]{0,1:T(8,128)S(1)} fusion(bf16[1024,256]{1,0:T(8,128)(2,1)} %param.19, f32[1024]{0:T(1024)S(1)} %maximum_convert_fusion, f32[512]{0:T(512)S(1)} %add_rsqrt_fusion.2, bf16[512,512]{1,0:T(8,128)(2,1)S(1)} %get-tuple-element.8, bf16[512,512]{1,0:T(8,128)(2,1)S(1)} %get-tuple-element.7), kind=kOutput, calls=%fused_computation.51 | convolution fusion | flops 272891904 | bytes 2103296 | tf_op jit(solution)/shard_map/dot_general | solution.py:148
  68.9 8.9 %all-to-all-done.1 = f32[32,5,128]{2,1,0:T(8,128)S(1)} async-done(((f32[32,5,128]{2,1,0:T(8,128)}), f32[32,5,128]{2,1,0:T(8,128)S(1)}, u32[]{:S(2)}, u32[]{:S(2)}) %all-to-all-start.1) | async-done | bytes 81952 | tf_op jit(solution)/shard_map/all_to_all | solution.py:49
  78.3 1.4 fusion.20
  79.7 1.2 copy.23
  80.9 1.9 %collective-permute-start.4 = (f32[512,256]{1,0:T(8,128)S(1)}, f32[512,256]{1,0:T(8,128)S(1)}, u32[]{:S(2)}, u32[]{:S(2)}) collective-permute-start(f32[512,256]{1,0:T(8,128)S(1)} %copy.23), channel_id=1, source_target_pairs={{0,256},{256,0},{1,257},{257,1},{2,258},{258,2},{3,259},{259,3},{4... | collective-permute-start | bytes 1572872 | tf_op jit(solution)/shard_map/ppermute | solution.py:32
  82.9 1.1 broadcast_select_fusion.5
  86.6 1.5 %fusion.31 = (f32[]{:T(128)}, f32[512,256]{0,1:T(8,128)S(1)}) fusion(s32[512]{0:T(512)S(1)} %bitcast.79, f32[512]{0:T(512)S(1)} %fusion.63, bf16[128,256]{1,0:T(8,128)(2,1)S(1)} %copy-done.4, bf16[128,256]{1,0:T(8,128)(2,1)S(1)} %copy-done.3, f32[512,256]{0,1:T(8,128)S(1)} %get-tuple-element.22, f32[512]{0:T(512)S(1)} %add_rsqrt_fusion), kind=kOutput, calls=%fused_computation.47 | convolution fusion | flops 404881408 | bytes 1185796 | tf_op jit(solution)/shard_map/dot_general | solution.py:99
  90.2 23.8 %all_to_all.20 = f32[32,33,128]{2,1,0:T(8,128)S(1)} all-to-all(f32[32,33,128]{2,1,0:T(8,128)S(1)} %reshape.222), channel_id=1, replica_groups=mesh['sec'=2,'atoms'=32,'batch'=8] {'atoms'}, dimensions={0} | all-to-all | bytes 1081344 | tf_op jit(solution)/shard_map/all_to_all | solution.py:47
  114.1 0.9 broadcast_in_dim.87
  114.9 4.8 %all-to-all-start.3 = ((f32[32,33,128]{2,1,0:T(8,128)}), f32[32,33,128]{2,1,0:T(8,128)S(1)}, u32[]{:S(2)}, u32[]{:S(2)}) async-start(f32[32,33,128]{2,1,0:T(8,128)} %broadcast_in_dim.87), calls=%async_computation.3 | async-start | bytes 1310720 | tf_op jit(solution)/shard_map/all_to_all | solution.py:49
  120.6 20.1 %all-to-all-done.3 = f32[32,33,128]{2,1,0:T(8,128)S(1)} async-done(((f32[32,33,128]{2,1,0:T(8,128)}), f32[32,33,128]{2,1,0:T(8,128)S(1)}, u32[]{:S(2)}, u32[]{:S(2)}) %all-to-all-start.3) | async-done | bytes 540704 | tf_op jit(solution)/shard_map/all_to_all | solution.py:49
  141.2 0.9 broadcast_in_dim_reshape.3
  (64 shorter events, 10.4 us)
Async XLA Ops:
  0.6 35.1 %copy-start = (bf16[1024,256]{1,0:T(8,128)(2,1)S(1)}, bf16[1024,256]{1,0:T(8,128)(2,1)}, u32[]{:S(2)}) copy-start(bf16[1024,256]{1,0:T(8,128)(2,1)} %param.20) | copy-start | bytes 1572868
  1.8 9.0 %collective-permute-start = (bf16[256,512]{1,0:T(8,128)(2,1)S(1)}, bf16[256,512]{1,0:T(8,128)(2,1)S(1)}, u32[]{:S(2)}, u32[]{:S(2)}) collective-permute-start(bf16[256,512]{1,0:T(8,128)(2,1)S(1)} %get-tuple-element.13), channel_id=1, source_target_pairs={{0,8},{8,16},{16,24},{24,32},{32,40},{40,48},{48,56},{56,64},{64,7... | collective-permute-start | bytes 786440 | tf_op jit(solution)/shard_map/ppermute | solution.py:25
  5.3 9.7 %collective-permute-start.1 = (bf16[256,512]{1,0:T(8,128)(2,1)S(1)}, bf16[256,512]{1,0:T(8,128)(2,1)S(1)}, u32[]{:S(2)}, u32[]{:S(2)}) collective-permute-start(bf16[256,512]{1,0:T(8,128)(2,1)S(1)} %get-tuple-element.14), channel_id=1, source_target_pairs={{8,0},{16,8},{24,16},{32,24},{40,32},{48,40},{56,48},{64,56},{72,6... | collective-permute-start | bytes 786440 | tf_op jit(solution)/shard_map/ppermute | solution.py:26
  16.0 2.0 %copy-start.6 = (bf16[1,16,128,128]{3,2,1,0:T(8,128)(2,1)S(1)}, bf16[1,16,128,128]{3,2,1,0:T(8,128)(2,1)}, u32[]{:S(2)}) copy-start(bf16[1,16,128,128]{3,2,1,0:T(8,128)(2,1)} %param.14) | copy-start | bytes 1572868
  18.1 3.0 %copy-start.1 = (bf16[1,512,512]{2,1,0:T(8,128)(2,1)S(1)}, bf16[1,512,512]{2,1,0:T(8,128)(2,1)}, u32[]{:S(2)}) copy-start(bf16[1,512,512]{2,1,0:T(8,128)(2,1)} %param.12) | copy-start | bytes 1572868
  18.1 5.1 %copy-start.5 = (bf16[512]{0:T(512)(128)(2,1)S(1)}, bf16[512]{0:T(512)(128)(2,1)}, u32[]{:S(2)}) copy-start(bf16[512]{0:T(512)(128)(2,1)} %param.18) | copy-start | bytes 3076
  18.1 7.6 %copy-start.2 = (bf16[256,1024]{1,0:T(8,128)(2,1)S(1)}, bf16[256,1024]{1,0:T(8,128)(2,1)}, u32[]{:S(2)}) copy-start(bf16[256,1024]{1,0:T(8,128)(2,1)} %param.22) | copy-start | bytes 1572868
  21.3 11.4 %collective-permute-start.2 = (bf16[512,512]{1,0:T(8,128)(2,1)S(1)}, bf16[512,512]{1,0:T(8,128)(2,1)}, u32[]{:S(2)}, u32[]{:S(2)}) collective-permute-start(bf16[512,512]{1,0:T(8,128)(2,1)S(1)} %fusion.26), channel_id=1, source_target_pairs={{0,256},{256,0},{1,257},{257,1},{2,258},{258,2},{3,259},{259,3},{4... | collective-permute-start | bytes 1572872 | tf_op jit(solution)/shard_map/ppermute | solution.py:32
  23.2 9.4 %collective-permute-start.3 = (bf16[512]{0:T(512)(128)(2,1)S(1)}, bf16[512]{0:T(512)(128)(2,1)S(1)}, u32[]{:S(2)}, u32[]{:S(2)}) collective-permute-start(bf16[512]{0:T(512)(128)(2,1)S(1)} %copy-done.5), channel_id=1, source_target_pairs={{0,256},{256,0},{1,257},{257,1},{2,258},{258,2},{3,259},{259,3},{4... | collective-permute-start | bytes 3080 | tf_op jit(solution)/shard_map/ppermute | solution.py:32
  25.6 58.3 %collective-permute-start.5 = (bf16[256,1024]{1,0:T(8,128)(2,1)S(1)}, bf16[256,1024]{1,0:T(8,128)(2,1)S(1)}, u32[]{:S(2)}, u32[]{:S(2)}) collective-permute-start(bf16[256,1024]{1,0:T(8,128)(2,1)S(1)} %copy-done.2), channel_id=1, source_target_pairs={{0,256},{256,0},{1,257},{257,1},{2,258},{258,2},{3,259},{259,3},{4... | collective-permute-start | bytes 1572872 | tf_op jit(solution)/shard_map/ppermute | solution.py:32
  27.6 55.3 %collective-permute-start.6 = (bf16[512,256]{1,0:T(8,128)(2,1)}, bf16[512,256]{1,0:T(8,128)(2,1)}, u32[]{:S(2)}, u32[]{:S(2)}) collective-permute-start(bf16[512,256]{1,0:T(8,128)(2,1)} %param.23), channel_id=1, source_target_pairs={{0,256},{256,0},{1,257},{257,1},{2,258},{258,2},{3,259},{259,3},{4... | collective-permute-start | bytes 786440 | tf_op jit(solution)/shard_map/ppermute | solution.py:32
  30.0 21.4 %collective-permute-start.7 = (bf16[128,256]{1,0:T(8,128)(2,1)}, bf16[128,256]{1,0:T(8,128)(2,1)}, u32[]{:S(2)}, u32[]{:S(2)}) collective-permute-start(bf16[128,256]{1,0:T(8,128)(2,1)} %bitcast.25), channel_id=1, source_target_pairs={{0,256},{256,0},{1,257},{257,1},{2,258},{258,2},{3,259},{259,3},{4... | collective-permute-start | bytes 196616 | tf_op jit(solution)/shard_map/ppermute | solution.py:32
  38.3 24.2 %all-to-all-start = ((f32[32,5,128]{2,1,0:T(8,128)}), f32[32,5,128]{2,1,0:T(8,128)S(1)}, u32[]{:S(2)}, u32[]{:S(2)}) async-start(f32[32,5,128]{2,1,0:T(8,128)} %reshape.216), calls=%async_computation | async-start | bytes 262144 | tf_op jit(solution)/shard_map/all_to_all | solution.py:47
  63.2 14.5 %all-to-all-start.1 = ((f32[32,5,128]{2,1,0:T(8,128)}), f32[32,5,128]{2,1,0:T(8,128)S(1)}, u32[]{:S(2)}, u32[]{:S(2)}) async-start(f32[32,5,128]{2,1,0:T(8,128)} %broadcast_in_dim.85), calls=%async_computation.1 | async-start | bytes 262144 | tf_op jit(solution)/shard_map/all_to_all | solution.py:49
  80.9 3.8 %collective-permute-start.4 = (f32[512,256]{1,0:T(8,128)S(1)}, f32[512,256]{1,0:T(8,128)S(1)}, u32[]{:S(2)}, u32[]{:S(2)}) collective-permute-start(f32[512,256]{1,0:T(8,128)S(1)} %copy.23), channel_id=1, source_target_pairs={{0,256},{256,0},{1,257},{257,1},{2,258},{258,2},{3,259},{259,3},{4... | collective-permute-start | bytes 1572872 | tf_op jit(solution)/shard_map/ppermute | solution.py:32
  85.7 0.8 copy-start.3
  85.8 0.9 copy-start.4
  85.8 0.9 copy-start.7
  114.9 25.7 %all-to-all-start.3 = ((f32[32,33,128]{2,1,0:T(8,128)}), f32[32,33,128]{2,1,0:T(8,128)S(1)}, u32[]{:S(2)}, u32[]{:S(2)}) async-start(f32[32,33,128]{2,1,0:T(8,128)} %broadcast_in_dim.87), calls=%async_computation.3 | async-start | bytes 1310720 | tf_op jit(solution)/shard_map/all_to_all | solution.py:49

commit v6 on v5

--- a/solution.py
+++ b/solution.py
@@ -30,12 +30,6 @@
 
 def swap_sec(x):
     return lax.ppermute(x, "sec", [(0, 1), (1, 0)])
-
-
-def join_sec(mine, other, sec, axis):
-    first = jnp.where(sec == 0, mine, other)
-    second = jnp.where(sec == 0, other, mine)
-    return jnp.concatenate([first, second], axis=axis)
 
 
 def sum_atoms(x):
@@ -129,26 +123,36 @@
     local_rows, width = atom_rows.shape
     sec = lax.axis_index("sec")
     peak_part = peak_embed[0]
-    partner = swap_sec((norm_gain, peak_part, w_out, w_proj))
-    gain_all, peak_all, out_all, proj_all = (
-        join_sec(mine, other, sec, 0)
-        for mine, other in zip((norm_gain, peak_part, w_out, w_proj), partner)
+    statics = (norm_gain, peak_part, w_out, w_proj)
+    arrived = swap_sec(jnp.concatenate([piece.reshape(-1) for piece in statics]))
+    offsets = [0]
+    for piece in statics:
+        offsets.append(offsets[-1] + piece.size)
+    gain_other, peak_other, out_other, proj_other = (
+        arrived[start:stop].reshape(piece.shape)
+        for piece, start, stop in zip(statics, offsets[:-1], offsets[1:])
     )
     gathered = message_pass(atom_rows, tile_ids[0], tile_vals[0])
     hidden_one = (atom_rows.astype(jnp.float32) + gathered.astype(jnp.float32)).astype(jnp.bfloat16)
-    hidden_f = join_sec(hidden_one, swap_sec(hidden_one), sec, 1).astype(jnp.float32)
+    mine_f = hidden_one.astype(jnp.float32)
+    other_f = swap_sec(hidden_one).astype(jnp.float32)
     atom_base = lax.axis_index("atoms") * local_rows
     length_one = seq_lens[0]
     label_row = pair_labels[0]
-    row_scale = lax.rsqrt(jnp.mean(hidden_f * hidden_f, axis=-1, keepdims=True) + EPSILON)
-    normed = (hidden_f * row_scale * gain_all.astype(jnp.float32)).astype(jnp.bfloat16)
+    square_sum = jnp.sum(mine_f * mine_f, axis=-1, keepdims=True) + jnp.sum(
+        other_f * other_f, axis=-1, keepdims=True
+    )
+    row_scale = lax.rsqrt(square_sum / D + EPSILON)
+    normed_mine = (mine_f * row_scale * norm_gain.astype(jnp.float32)).astype(jnp.bfloat16)
+    normed_other = (other_f * row_scale * gain_other.astype(jnp.float32)).astype(jnp.bfloat16)
     head_cols = w_query.shape[1]
-    query_f, key_f, value_f = tuple(
-        (
-            jnp.dot(normed, weight, preferred_element_type=jnp.float32)
-            for weight in (w_query, w_key, w_value)
-        )
-    )
+
+    def project(weight):
+        halves = weight.reshape(2, width, weight.shape[1])
+        mine = jnp.dot(normed_mine, halves[sec], preferred_element_type=jnp.float32)
+        return mine + jnp.dot(normed_other, halves[1 - sec], preferred_element_type=jnp.float32)
+
+    query_f, key_f, value_f = tuple((project(weight) for weight in (w_query, w_key, w_value)))
     head_count = head_cols // HEAD_DIM
     atom_mask = (atom_base + jnp.arange(local_rows, dtype=jnp.int32) < length_one).astype(
         jnp.float32
@@ -160,17 +164,31 @@
     packed = sum_atoms(state_rows)
     outer_state, key_total = packed[:, :HEAD_DIM, :], packed[:, HEAD_DIM, :]
     attended = read_summary(query_f.astype(jnp.bfloat16), outer_state, key_total, head_count)
-    attended_all = join_sec(attended, swap_sec(attended), sec, 1)
-    out_scale = lax.rsqrt(jnp.mean(attended_all * attended_all, axis=-1, keepdims=True) + EPSILON)
-    attended_n = (attended_all * out_scale).astype(jnp.bfloat16)
-    branch = jnp.dot(attended_n, out_all, preferred_element_type=jnp.float32)
-    hidden_all = (hidden_f + branch).astype(jnp.bfloat16)
-    embedded = jnp.dot(hidden_all, proj_all, preferred_element_type=jnp.float32)
+    attended_other = swap_sec(attended)
+    out_sum = jnp.sum(attended * attended, axis=-1, keepdims=True) + jnp.sum(
+        attended_other * attended_other, axis=-1, keepdims=True
+    )
+    out_scale = lax.rsqrt(out_sum / (HEADS * HEAD_DIM) + EPSILON)
+    branch = jnp.dot(
+        (attended * out_scale).astype(jnp.bfloat16), w_out, preferred_element_type=jnp.float32
+    ) + jnp.dot(
+        (attended_other * out_scale).astype(jnp.bfloat16), out_other, preferred_element_type=jnp.float32
+    )
+    branch_cols = branch.reshape(local_rows, 2, width)
+    hidden_two = (mine_f + branch_cols[:, sec, :]).astype(jnp.bfloat16)
+    hidden_other = (other_f + branch_cols[:, 1 - sec, :]).astype(jnp.bfloat16)
+    embedded = jnp.dot(hidden_two, w_proj, preferred_element_type=jnp.float32) + jnp.dot(
+        hidden_other, proj_other, preferred_element_type=jnp.float32
+    )
     embed_scale = lax.rsqrt(jnp.mean(embedded * embedded, axis=-1, keepdims=True) + EPSILON)
     unit_rows = embedded * embed_scale
-    loss_part, unit_grad = contrast(unit_rows, peak_all, label_row, atom_mask, 0)
-    embed_grad = embed_backward(unit_rows, unit_grad, embed_scale)
-    hidden_two = lax.dynamic_slice_in_dim(hidden_all, sec * width, width, axis=1)
+    peak_count = peak_part.shape[0]
+    loss_mine, grad_mine = contrast(unit_rows, peak_part, label_row, atom_mask, sec * peak_count)
+    loss_other, grad_other = contrast(
+        unit_rows, peak_other, label_row, atom_mask, (1 - sec) * peak_count
+    )
+    loss_part = loss_mine + loss_other
+    embed_grad = embed_backward(unit_rows, grad_mine + grad_other, embed_scale)
     proj_part = jnp.einsum("nd,ne->de", hidden_two, embed_grad, preferred_element_type=jnp.float32)
     packed = sum_atoms(jnp.concatenate([proj_part.reshape(-1), loss_part.reshape(1)]))
     proj_total = packed[: proj_part.size].reshape(proj_part.shape)

time: 145 us -> 168 us (1.16)
  local copies, waits for them, and re-layouts: 10.2 us -> 32.4 us
  matrix products: 13.4 us -> 22.6 us
  waiting for transfers between devices: 46.1 us -> 40.1 us
  starting transfers between devices: 39 us -> 33.3 us
  blocking collectives: 23.8 us -> 25.5 us
    dot_general x5 -> x10, matrix products: 5.58 us -> 12.6 us  [the longest x3 4.8 us: project(): jnp.dot(normed_other, halves[1 - sec], preferred_element_type=jnp.float32)]
    ppermute x6 -> x3, starting transfers between devices: 12.5 us -> 6.4 us  [swap_sec(): return lax.ppermute(x, 'sec', [(0, 1), (1, 0)])]
    unnamed x17 -> x30, local copies, waits for them, and re-layouts: 0.63 us -> 6.54 us
    slice x0 -> x5, local copies, waits for them, and re-layouts: none -> 5.64 us  [shards(): arrived[start:stop].reshape(piece.shape)]
    dynamic_slice x0 -> x1, local copies, waits for them, and re-layouts: none -> 4.45 us  [shards(): hidden_other = (other_f + branch_cols[:, 1 - sec, :]).astype(jnp.bfloat16)]
    reshape x1 -> x2, local copies, waits for them, and re-layouts: 1.24 us -> 5.26 us  [the longest x1 3.99 us: shards(): branch_cols = branch.reshape(local_rows, 2, width)]
    select_n x6 -> x0, other arithmetic: 3.87 us -> none  [join_sec(): first = jnp.where(sec == 0, mine, other)]
    ppermute x1, waiting for transfers between devices: 2.75 us -> 0.01 us  [extended(): before = lax.ppermute(last, axis, up)]
  transfers between devices with their start and end apart: 11 -> 8, of which waited for: 6 -> 4; matrix products, arithmetic and copies ran while one was open for 11% -> 12% of each run, Pallas kernels for 0% -> 0%
where the time goes in v6:
time: 168 us; the launch traced here: 167 us
  waiting for transfers between devices  40.1 us (24%)
  starting transfers between devices  33.3 us (20%)
  local copies, waits for them, and re-layouts  32.4 us (19%)
  blocking collectives  25.5 us (15%)
  matrix products  22.6 us (13%)
  other arithmetic  8.26 us (5%)
  between operations  4.83 us (3%)
    all_to_all x2, waiting for transfers between devices, sum_atoms(): lax.all_to_all(jnp.broadcast_to(owned, pieces.shape), 'atoms', 0, 0, tile...  28.7 us
    all_to_all x1, blocking collectives, sum_atoms(): arrived = lax.all_to_all(pieces, 'atoms', 0, 0, tiled=True)  25.5 us
    all_to_all x1, starting transfers between devices, sum_atoms(): arrived = lax.all_to_all(pieces, 'atoms', 0, 0, tiled=True)  13.1 us
    all_to_all x2, starting transfers between devices, sum_atoms(): lax.all_to_all(jnp.broadcast_to(owned, pieces.shape), 'atoms', 0, 0, tile...  8.96 us
    all_to_all x1, waiting for transfers between devices, sum_atoms(): arrived = lax.all_to_all(pieces, 'atoms', 0, 0, tiled=True)  8.54 us
    unnamed x30, local copies, waits for them, and re-layouts  6.54 us
    ppermute x3, starting transfers between devices, swap_sec(): return lax.ppermute(x, 'sec', [(0, 1), (1, 0)])  6.4 us
    slice x5, local copies, waits for them, and re-layouts, shards(): arrived[start:stop].reshape(piece.shape)  5.64 us
  transfers between devices with their start and end apart: 8, of which 4 were waited for; matrix products, arithmetic and copies ran while one was open for 12% of the time, Pallas kernels for 0%

profile of v6, /device:TPU:6, one launch (start us, length us, event | category | flops | bytes accessed | tf_op | source)
XLA Modules:
  0.0 166.9 jit_solution(2831605891208640419)
XLA Ops:
  1.8 3.5 %collective-permute-start = (bf16[256,512]{1,0:T(8,128)(2,1)S(1)}, bf16[256,512]{1,0:T(8,128)(2,1)S(1)}, u32[]{:S(2)}, u32[]{:S(2)}) collective-permute-start(bf16[256,512]{1,0:T(8,128)(2,1)S(1)} %get-tuple-element.11), channel_id=1, source_target_pairs={{0,8},{8,16},{16,24},{24,32},{32,40},{40,48},{48,56},{56,64},{64,7... | collective-permute-start | bytes 786440 | tf_op jit(solution)/shard_map/ppermute | solution.py:25
  5.3 1.3 collective-permute-start.1
  10.1 1.9 %copy.26 = bf16[32,8,8,128]{3,1,2,0:T(8,128)(2,1)} copy(bf16[32,8,8,128]{3,2,1,0:T(8,128)(2,1)} %bitcast.141) | data formatting | bytes 1048576
  12.1 2.9 %collective-permute-done.1 = bf16[256,512]{1,0:T(8,128)(2,1)S(1)} collective-permute-done((bf16[256,512]{1,0:T(8,128)(2,1)S(1)}, bf16[256,512]{1,0:T(8,128)(2,1)S(1)}, u32[]{:S(2)}, u32[]{:S(2)}) %collective-permute-start.1) | collective-permute-done | bytes 262176 | tf_op jit(solution)/shard_map/ppermute | solution.py:26
  15.1 2.0 %gather_fusion = bf16[16,128,512]{2,1,0:T(8,128)(2,1)} fusion(bf16[8,128,512]{2,1,0:T(8,128)(2,1)S(1)} %bitcast.138, s32[1024]{0:T(1024)S(1)} %pad_clamp_fusion), kind=kCustom, calls=%fused_computation | custom fusion | bytes 4194368 | tf_op jit(solution)/shard_map/jit(_take)/gather | solution.py:64
  17.1 2.9 %fusion.16 = f32[4,128,512]{2,1,0:T(8,128)S(1)} fusion(bf16[16,128,512]{2,1,0:T(8,128)(2,1)} %gather_fusion, pred[16]{0:T(512)(128)(4,1)S(1)} %get-tuple-element.7, pred[4,16]{1,0:T(4,128)(4,1)S(1)} %iota_compare_fusion.1, bf16[16,128,128]{2,1,0:T(8,128)(2,1)S(1)} %bitcast.155), kind=kOutput, calls=%fused_computation.21 | convolution fusion | flops 1076363264 | bytes 3670096 | tf_op jit(solution)/shard_map/btij,tjf->bif/dot_general | solution.py:67
  20.3 1.9 %collective-permute-start.2 = (bf16[512,512]{1,0:T(8,128)(2,1)S(1)}, bf16[512,512]{1,0:T(8,128)(2,1)S(1)}, u32[]{:S(2)}, u32[]{:S(2)}) collective-permute-start(bf16[512,512]{1,0:T(8,128)(2,1)S(1)} %get-tuple-element.6), channel_id=1, source_target_pairs={{0,256},{256,0},{1,257},{257,1},{2,258},{258,2},{3,259},{259,3},{4... | collective-permute-start | bytes 1572872 | tf_op jit(solution)/shard_map/ppermute | solution.py:32
  23.3 2.4 %collective-permute-start.3 = (bf16[426496]{0:T(1024)(128)(2,1)}, bf16[426496]{0:T(1024)(128)(2,1)}, u32[]{:S(2)}, u32[]{:S(2)}) collective-permute-start(bf16[426496]{0:T(1024)(128)(2,1)} %pad_maximum_fusion.1), channel_id=1, source_target_pairs={{0,256},{256,0},{1,257},{257,1},{2,258},{258,2},{3,259},{259,3},{4... | collective-permute-start | bytes 2558984 | tf_op jit(solution)/shard_map/ppermute | solution.py:32
  29.8 1.4 multiply_reduce_fusion.4
  31.5 1.6 fusion.25
  33.1 1.5 fusion.48
  35.6 13.1 %all-to-all-start = ((f32[32,5,128]{2,1,0:T(8,128)}), f32[32,5,128]{2,1,0:T(8,128)S(1)}, u32[]{:S(2)}, u32[]{:S(2)}) async-start(f32[32,5,128]{2,1,0:T(8,128)} %reshape.322), calls=%async_computation | async-start | bytes 262144 | tf_op jit(solution)/shard_map/all_to_all | solution.py:41
  48.7 2.1 %fusion.73 = f32[512,256]{0,1:T(8,128)} fusion(bf16[512,512]{1,0:T(8,128)(2,1)S(1)} %fusion.43, bf16[2,512,256]{2,1,0:T(8,128)(2,1)} %bitcast.152, s32[]{:T(128)S(6)} %select_n.97), kind=kOutput, calls=%fused_computation.100 | convolution fusion | flops 134217728 | bytes 1310724 | tf_op jit(solution)/shard_map/dot_general | solution.py:152
  50.8 8.5 %all-to-all-done = f32[32,5,128]{2,1,0:T(8,128)S(1)} async-done(((f32[32,5,128]{2,1,0:T(8,128)}), f32[32,5,128]{2,1,0:T(8,128)S(1)}, u32[]{:S(2)}, u32[]{:S(2)}) %all-to-all-start) | async-done | bytes 81952 | tf_op jit(solution)/shard_map/all_to_all | solution.py:41
  60.0 3.9 %all-to-all-start.1 = ((f32[32,5,128]{2,1,0:T(8,128)}), f32[32,5,128]{2,1,0:T(8,128)S(1)}, u32[]{:S(2)}, u32[]{:S(2)}) async-start(f32[32,5,128]{2,1,0:T(8,128)} %broadcast_in_dim.89), calls=%async_computation.1 | async-start | bytes 262144 | tf_op jit(solution)/shard_map/all_to_all | solution.py:43
  63.9 1.8 %fusion.47 = f32[512,256]{0,1:T(8,128)S(1)} fusion(f32[512,256]{0,1:T(8,128)} %fusion.73, bf16[2,512,256]{2,1,0:T(8,128)(2,1)} %bitcast.153, s32[]{:T(128)S(6)} %select_n.98, bf16[512,512]{1,0:T(8,128)(2,1)S(1)} %collective-permute-done.2, f32[512]{0:T(512)S(1)} %slice_convert_fusion, f32[512]{0:T(512)S(1)} %add_rsqrt_fusion.2), kind=kOutput, calls=%fused_computation.64 | convolution fusion | flops 136183808 | bytes 1839108 | tf_op jit(solution)/shard_map/dot_general | solution.py:153
  65.7 8.8 %all-to-all-done.1 = f32[32,5,128]{2,1,0:T(8,128)S(1)} async-done(((f32[32,5,128]{2,1,0:T(8,128)}), f32[32,5,128]{2,1,0:T(8,128)S(1)}, u32[]{:S(2)}, u32[]{:S(2)}) %all-to-all-start.1) | async-done | bytes 81952 | tf_op jit(solution)/shard_map/all_to_all | solution.py:43
  75.0 1.4 multiply_reduce_fusion.3
  76.5 2.1 %collective-permute-start.4 = (f32[512,256]{0,1:T(8,128)}, f32[512,256]{0,1:T(8,128)S(1)}, u32[]{:S(2)}, u32[]{:S(2)}) collective-permute-start(f32[512,256]{0,1:T(8,128)} %bitcast.34), channel_id=1, source_target_pairs={{0,256},{256,0},{1,257},{257,1},{2,258},{258,2},{3,259},{259,3},{4... | collective-permute-start | bytes 1572872 | tf_op jit(solution)/shard_map/ppermute | solution.py:32
  79.5 2.0 %slice.94 = bf16[262144]{0:T(1024)(128)(2,1)} slice(bf16[426496]{0:T(1024)(128)(2,1)} %collective-permute-done.3), slice={[33280:295424]} | slice | bytes 1048576 | tf_op jit(solution)/shard_map/slice | solution.py:132
  81.5 1.3 reshape.327
  82.7 1.7 %slice.95 = bf16[131072]{0:T(1024)(128)(2,1)} slice(bf16[426496]{0:T(1024)(128)(2,1)} %collective-permute-done.3), slice={[295424:426496]} | slice | bytes 524288 | tf_op jit(solution)/shard_map/slice | solution.py:132
  85.6 1.7 fusion.67
  87.3 1.8 %convolution_add_fusion = f32[512,1024]{1,0:T(8,128)} fusion(f32[512,1024]{1,0:T(8,128)S(1)} %fusion.67, bf16[256,1024]{1,0:T(8,128)(2,1)S(1)} %reshape.327, f32[512,256]{0,1:T(8,128)S(1)} %collective-permute-done.4, f32[512]{0:T(512)S(1)} %add_rsqrt_fusion.1), kind=kOutput, calls=%fused_computation.11 | convolution fusion | flops 269221888 | bytes 5244928 | tf_op jit(solution)/shard_map/dot_general | solution.py:174
  89.1 4.0 %reshape.328 = f32[512,2,512]{2,1,0:T(2,128)} reshape(f32[512,1024]{1,0:T(8,128)} %convolution_add_fusion) | data formatting | bytes 4194304 | tf_op jit(solution)/shard_map/reshape | solution.py:177
  93.1 4.5 %constant_dynamic-slice_fusion = (f32[512,1,512]{2,1,0:T(1,128)S(1)}, f32[512,1,512]{2,1,0:T(1,128)S(1)}) fusion(f32[512,2,512]{2,1,0:T(2,128)} %reshape.328, s32[]{:T(128)S(6)} %select_n.98, s32[]{:T(128)S(6)} %select_n.97), kind=kLoop, calls=%fused_computation.156 | loop fusion | bytes 4194312 | tf_op jit(solution)/shard_map/dynamic_slice | solution.py:179
  100.2 1.5 fusion.71
  105.2 1.9 %select_maximum_fusion = f32[135168]{0:T(1024)} fusion(f32[1]{0:T(128)} %bitcast.37, f32[131072]{0:T(1024)} %bitcast.140), kind=kLoop, calls=%fused_computation.58 | loop fusion | flops 540672 | bytes 1064964 | tf_op jit(solution)/shard_map/concatenate | solution.py:193
  107.0 1.9 %reshape.331 = f32[32,33,128]{2,1,0:T(8,128)} reshape(f32[135168]{0:T(1024)} %select_maximum_fusion) | data formatting | bytes 1081344 | tf_op jit(solution)/shard_map/reshape | solution.py:40
  109.0 25.5 %all_to_all.20 = f32[32,33,128]{2,1,0:T(8,128)} all-to-all(f32[32,33,128]{2,1,0:T(8,128)} %reshape.331), channel_id=1, replica_groups=mesh['sec'=2,'atoms'=32,'batch'=8] {'atoms'}, dimensions={0} | all-to-all | bytes 1081344 | tf_op jit(solution)/shard_map/all_to_all | solution.py:41
  136.5 5.1 %all-to-all-start.3 = ((f32[32,33,128]{2,1,0:T(8,128)}), f32[32,33,128]{2,1,0:T(8,128)}, u32[]{:S(2)}, u32[]{:S(2)}) async-start(f32[32,33,128]{2,1,0:T(8,128)} %broadcast_in_dim.90), calls=%async_computation.3 | async-start | bytes 1310720 | tf_op jit(solution)/shard_map/all_to_all | solution.py:43
  142.7 19.8 %all-to-all-done.3 = f32[32,33,128]{2,1,0:T(8,128)} async-done(((f32[32,33,128]{2,1,0:T(8,128)}), f32[32,33,128]{2,1,0:T(8,128)}, u32[]{:S(2)}, u32[]{:S(2)}) %all-to-all-start.3) | async-done | bytes 540704 | tf_op jit(solution)/shard_map/all_to_all | solution.py:43
  (83 shorter events, 24.4 us)
Async XLA Ops:
  0.6 28.1 %copy-start = (bf16[1024,256]{1,0:T(8,128)(2,1)S(1)}, bf16[1024,256]{1,0:T(8,128)(2,1)}, u32[]{:S(2)}) copy-start(bf16[1024,256]{1,0:T(8,128)(2,1)} %param.20) | copy-start | bytes 1572868
  0.6 14.3 %copy-start.1 = (bf16[1,512,512]{2,1,0:T(8,128)(2,1)S(1)}, bf16[1,512,512]{2,1,0:T(8,128)(2,1)}, u32[]{:S(2)}) copy-start(bf16[1,512,512]{2,1,0:T(8,128)(2,1)} %param.12) | copy-start | bytes 1572868
  1.8 10.3 %collective-permute-start = (bf16[256,512]{1,0:T(8,128)(2,1)S(1)}, bf16[256,512]{1,0:T(8,128)(2,1)S(1)}, u32[]{:S(2)}, u32[]{:S(2)}) collective-permute-start(bf16[256,512]{1,0:T(8,128)(2,1)S(1)} %get-tuple-element.11), channel_id=1, source_target_pairs={{0,8},{8,16},{16,24},{24,32},{32,40},{40,48},{48,56},{56,64},{64,7... | collective-permute-start | bytes 786440 | tf_op jit(solution)/shard_map/ppermute | solution.py:25
  5.3 9.7 %collective-permute-start.1 = (bf16[256,512]{1,0:T(8,128)(2,1)S(1)}, bf16[256,512]{1,0:T(8,128)(2,1)S(1)}, u32[]{:S(2)}, u32[]{:S(2)}) collective-permute-start(bf16[256,512]{1,0:T(8,128)(2,1)S(1)} %get-tuple-element.12), channel_id=1, source_target_pairs={{8,0},{16,8},{24,16},{32,24},{40,32},{48,40},{56,48},{64,56},{72,6... | collective-permute-start | bytes 786440 | tf_op jit(solution)/shard_map/ppermute | solution.py:26
  15.0 2.0 %copy-start.11 = (bf16[1,16,128,128]{3,2,1,0:T(8,128)(2,1)S(1)}, bf16[1,16,128,128]{3,2,1,0:T(8,128)(2,1)}, u32[]{:S(2)}) copy-start(bf16[1,16,128,128]{3,2,1,0:T(8,128)(2,1)} %param.14) | copy-start | bytes 1572868
  20.0 2.2 %copy-start.6 = (bf16[32,8,8,128]{3,1,2,0:T(8,128)(2,1)S(1)}, bf16[32,8,8,128]{3,1,2,0:T(8,128)(2,1)}, u32[]{:S(2)}) copy-start(bf16[32,8,8,128]{3,1,2,0:T(8,128)(2,1)} %copy.26) | copy-start | bytes 1572868
  20.0 2.2 %copy-start.10 = (bf16[512]{0:T(512)(128)(2,1)S(1)}, bf16[512]{0:T(512)(128)(2,1)}, u32[]{:S(2)}) copy-start(bf16[512]{0:T(512)(128)(2,1)} %param.18) | copy-start | bytes 3076
  20.3 6.4 %copy-start.4 = (bf16[512,512]{1,0:T(8,128)(2,1)}, bf16[512,512]{1,0:T(8,128)(2,1)S(1)}, u32[]{:S(2)}) copy-start(bf16[512,512]{1,0:T(8,128)(2,1)S(1)} %get-tuple-element.6) | copy-start | bytes 1572868
  20.3 6.2 %collective-permute-start.2 = (bf16[512,512]{1,0:T(8,128)(2,1)S(1)}, bf16[512,512]{1,0:T(8,128)(2,1)S(1)}, u32[]{:S(2)}, u32[]{:S(2)}) collective-permute-start(bf16[512,512]{1,0:T(8,128)(2,1)S(1)} %get-tuple-element.6), channel_id=1, source_target_pairs={{0,256},{256,0},{1,257},{257,1},{2,258},{258,2},{3,259},{259,3},{4... | collective-permute-start | bytes 1572872 | tf_op jit(solution)/shard_map/ppermute | solution.py:32
  23.3 5.8 %collective-permute-start.3 = (bf16[426496]{0:T(1024)(128)(2,1)}, bf16[426496]{0:T(1024)(128)(2,1)}, u32[]{:S(2)}, u32[]{:S(2)}) collective-permute-start(bf16[426496]{0:T(1024)(128)(2,1)} %pad_maximum_fusion.1), channel_id=1, source_target_pairs={{0,256},{256,0},{1,257},{257,1},{2,258},{258,2},{3,259},{259,3},{4... | collective-permute-start | bytes 2558984 | tf_op jit(solution)/shard_map/ppermute | solution.py:32
  26.4 1.2 copy-start.8
  26.4 37.5 %copy-start.2 = (bf16[512,512]{1,0:T(8,128)(2,1)}, bf16[512,512]{1,0:T(8,128)(2,1)S(1)}, u32[]{:S(2)}) copy-start(bf16[512,512]{1,0:T(8,128)(2,1)S(1)} %collective-permute-done.2) | copy-start | bytes 1572868
  35.6 23.8 %all-to-all-start = ((f32[32,5,128]{2,1,0:T(8,128)}), f32[32,5,128]{2,1,0:T(8,128)S(1)}, u32[]{:S(2)}, u32[]{:S(2)}) async-start(f32[32,5,128]{2,1,0:T(8,128)} %reshape.322), calls=%async_computation | async-start | bytes 262144 | tf_op jit(solution)/shard_map/all_to_all | solution.py:41
  60.0 14.5 %all-to-all-start.1 = ((f32[32,5,128]{2,1,0:T(8,128)}), f32[32,5,128]{2,1,0:T(8,128)S(1)}, u32[]{:S(2)}, u32[]{:S(2)}) async-start(f32[32,5,128]{2,1,0:T(8,128)} %broadcast_in_dim.89), calls=%async_computation.1 | async-start | bytes 262144 | tf_op jit(solution)/shard_map/all_to_all | solution.py:43
  76.5 9.0 %collective-permute-start.4 = (f32[512,256]{0,1:T(8,128)}, f32[512,256]{0,1:T(8,128)S(1)}, u32[]{:S(2)}, u32[]{:S(2)}) collective-permute-start(f32[512,256]{0,1:T(8,128)} %bitcast.34), channel_id=1, source_target_pairs={{0,256},{256,0},{1,257},{257,1},{2,258},{258,2},{3,259},{259,3},{4... | collective-permute-start | bytes 1572872 | tf_op jit(solution)/shard_map/ppermute | solution.py:32
  93.1 4.5 %copy-start.5 = (bf16[512,512]{1,0:T(8,128)(2,1)S(1)}, bf16[512,512]{1,0:T(8,128)(2,1)}, u32[]{:S(2)}) copy-start(bf16[512,512]{1,0:T(8,128)(2,1)} %copy-done.4) | copy-start | bytes 1572868
  93.1 4.5 %copy-start.7 = (bf16[512,256]{1,0:T(8,128)(2,1)S(1)}, bf16[512,256]{1,0:T(8,128)(2,1)}, u32[]{:S(2)}) copy-start(bf16[512,256]{1,0:T(8,128)(2,1)} %param.23) | copy-start | bytes 786436
  97.5 1.0 copy-start.3
  97.5 1.4 copy-start.9
  97.9 1.7 copy-start.12
  136.5 26.0 %all-to-all-start.3 = ((f32[32,33,128]{2,1,0:T(8,128)}), f32[32,33,128]{2,1,0:T(8,128)}, u32[]{:S(2)}, u32[]{:S(2)}) async-start(f32[32,33,128]{2,1,0:T(8,128)} %broadcast_in_dim.90), calls=%async_computation.3 | async-start | bytes 1310720 | tf_op jit(solution)/shard_map/all_to_all | solution.py:43

commit v7 on v4

--- a/solution.py
+++ b/solution.py
@@ -42,7 +42,7 @@
     return x + swap_sec(x)
 
 
-def sum_atoms(x):
+def sum_atoms(x, exact=None):
     peers = lax.axis_size("atoms")
     flat = x.reshape(-1)
     chunk = -(-flat.shape[0] // (peers * 128)) * 128
@@ -50,8 +50,15 @@
     pieces = flat.reshape(peers, chunk // 128, 128)
     arrived = lax.all_to_all(pieces, "atoms", 0, 0, tiled=True)
     owned = jnp.sum(arrived, axis=0, keepdims=True)
+    if exact is not None:
+        owner, slot = divmod(exact, chunk)
+        rest = owned - owned.astype(jnp.bfloat16).astype(jnp.float32)
+        here = lax.axis_index("atoms") == owner
+        spare = (slot + 1) // 128, (slot + 1) % 128
+        kept = jnp.where(here, rest[0, slot // 128, slot % 128], owned[0, spare[0], spare[1]])
+        owned = owned.at[0, spare[0], spare[1]].set(kept).astype(jnp.bfloat16)
     spread = lax.all_to_all(jnp.broadcast_to(owned, pieces.shape), "atoms", 0, 0, tiled=True)
-    return spread.reshape(-1)[: x.size].reshape(x.shape)
+    return spread.reshape(-1)[: x.size].reshape(x.shape).astype(jnp.float32)
 
 
 def feature_map(values):
@@ -179,9 +186,12 @@
     loss_part, unit_grad = contrast(unit_rows, peak_all, label_row, atom_mask, 0)
     embed_grad = embed_backward(unit_rows, unit_grad, embed_scale)
     proj_part = jnp.einsum("nd,ne->de", hidden_two, embed_grad, preferred_element_type=jnp.float32)
-    packed = sum_atoms(jnp.concatenate([proj_part.reshape(-1), loss_part.reshape(1)]))
+    zero = jnp.zeros((1,), jnp.float32)
+    payload = jnp.concatenate([proj_part.reshape(-1), loss_part.reshape(1), zero])
+    packed = sum_atoms(payload, exact=proj_part.size)
     proj_total = packed[: proj_part.size].reshape(proj_part.shape)
-    loss_total = packed[proj_part.size] / (local_rows * lax.axis_size("atoms"))
+    loss_sum = packed[proj_part.size] + packed[proj_part.size + 1]
+    loss_total = loss_sum / (local_rows * lax.axis_size("atoms"))
     return (hidden_two[None], loss_total.reshape(1), proj_total[None])
 
 

time: 141 us -> 140 us (level)
  blocking collectives: 51.7 us -> 20.5 us
  waiting for transfers between devices: 25 us -> 45.8 us
  starting transfers between devices: 32.5 us -> 36.4 us
  between operations: 4.18 us -> 6.78 us
  local copies, waits for them, and re-layouts: 10.5 us -> 12.5 us
    all_to_all x1 -> x0, blocking collectives: 23.8 us -> none  [sum_atoms(): arrived = lax.all_to_all(pieces, 'atoms', 0, 0, tiled=True)]
    all_to_all x1 -> x2, waiting for transfers between devices: 9.59 us -> 30.3 us  [sum_atoms(): arrived = lax.all_to_all(pieces, 'atoms', 0, 0, tiled=True)]
    all_to_all x1, blocking collectives: 25.5 us -> 18 us  [sum_atoms(): lax.all_to_all(jnp.broadcast_to(owned, pieces.shape), 'atoms', 0, 0, tile...]
    all_to_all x1 -> x2, starting transfers between devices: 13.1 us -> 17 us  [sum_atoms(): arrived = lax.all_to_all(pieces, 'atoms', 0, 0, tiled=True)]
  transfers between devices with their start and end apart: 9 -> 10, of which waited for: 6 -> 7; matrix products, arithmetic and copies ran while one was open for 6% -> 6% of each run, Pallas kernels for 0% -> 0%
where the time goes in v7:
time: 140 us; the launch traced here: 139 us
  waiting for transfers between devices  45.8 us (33%)
  starting transfers between devices  36.4 us (26%)
  blocking collectives  20.5 us (15%)
  matrix products  13.3 us (10%)
  local copies, waits for them, and re-layouts  12.5 us (9%)
  between operations  6.78 us (5%)
  other arithmetic  3.52 us (3%)
    all_to_all x2, waiting for transfers between devices, sum_atoms(): arrived = lax.all_to_all(pieces, 'atoms', 0, 0, tiled=True)  30.3 us
    all_to_all x1, blocking collectives, sum_atoms(): lax.all_to_all(jnp.broadcast_to(owned, pieces.shape), 'atoms', 0, 0, tile...  18 us
    all_to_all x2, starting transfers between devices, sum_atoms(): arrived = lax.all_to_all(pieces, 'atoms', 0, 0, tiled=True)  17 us
    ppermute x5, starting transfers between devices, swap_sec(): return lax.ppermute(x, 'sec', [(0, 1), (1, 0)])  10.7 us
    all_to_all x1, waiting for transfers between devices, sum_atoms(): lax.all_to_all(jnp.broadcast_to(owned, pieces.shape), 'atoms', 0, 0, tile...  9.08 us
    all_to_all x1, starting transfers between devices, sum_atoms(): lax.all_to_all(jnp.broadcast_to(owned, pieces.shape), 'atoms', 0, 0, tile...  3.84 us
    dot_general x3, matrix products, project(): jnp.dot(other_rows, halves[1 - sec], preferred_element_type=jnp.float32)  3.55 us
    ppermute x1, starting transfers between devices, extended(): before = lax.ppermute(last, axis, up)  3.5 us
  transfers between devices with their start and end apart: 10, of which 7 were waited for; matrix products, arithmetic and copies ran while one was open for 6% of the time, Pallas kernels for 0%

profile of v7, /device:TPU:6, one launch (start us, length us, event | category | flops | bytes accessed | tf_op | source)
XLA Modules:
  0.0 138.6 jit_solution(12702023228944615396)
XLA Ops:
  0.7 1.2 slice_bitcast_fusion.1
  1.8 3.5 %collective-permute-start = (bf16[256,512]{1,0:T(8,128)(2,1)S(1)}, bf16[256,512]{1,0:T(8,128)(2,1)S(1)}, u32[]{:S(2)}, u32[]{:S(2)}) collective-permute-start(bf16[256,512]{1,0:T(8,128)(2,1)S(1)} %get-tuple-element.29), channel_id=1, source_target_pairs={{0,8},{8,16},{16,24},{24,32},{32,40},{40,48},{48,56},{56,64},{64,7... | collective-permute-start | bytes 786440 | tf_op jit(solution)/shard_map/ppermute | solution.py:25
  5.3 1.3 collective-permute-start.1
  6.6 0.8 compare_and_fusion
  9.4 2.0 %copy.23 = bf16[256,1024]{0,1:T(8,128)(2,1)} copy(bf16[256,1024]{1,0:T(8,128)(2,1)} %param.24) | data formatting | bytes 1048576 | tf_op args[10]
  11.5 3.5 %collective-permute-done.1 = bf16[256,512]{1,0:T(8,128)(2,1)S(1)} collective-permute-done((bf16[256,512]{1,0:T(8,128)(2,1)S(1)}, bf16[256,512]{1,0:T(8,128)(2,1)S(1)}, u32[]{:S(2)}, u32[]{:S(2)}) %collective-permute-start.1) | collective-permute-done | bytes 262176 | tf_op jit(solution)/shard_map/ppermute | solution.py:26
  15.1 2.0 %gather_fusion = bf16[16,128,512]{2,1,0:T(8,128)(2,1)} fusion(bf16[8,128,512]{2,1,0:T(8,128)(2,1)S(1)} %bitcast.127, s32[1024]{0:T(1024)S(1)} %pad_clamp_fusion), kind=kCustom, calls=%fused_computation | custom fusion | bytes 4194368 | tf_op jit(solution)/shard_map/jit(_take)/gather | solution.py:81
  17.1 2.9 %fusion.16 = f32[4,128,512]{2,1,0:T(8,128)S(1)} fusion(bf16[16,128,512]{2,1,0:T(8,128)(2,1)} %gather_fusion, pred[16]{0:T(512)(128)(4,1)S(1)} %get-tuple-element.19, pred[4,16]{1,0:T(4,128)(4,1)S(1)} %iota_compare_fusion.2, bf16[16,128,128]{2,1,0:T(8,128)(2,1)S(1)} %bitcast.147), kind=kOutput, calls=%fused_computation.17 | convolution fusion | flops 1076363264 | bytes 3670096 | tf_op jit(solution)/shard_map/btij,tjf->bif/dot_general | solution.py:84
  20.2 2.5 %psum.7 = f32[512]{0:T(512)S(1)} all-reduce(f32[512]{0:T(512)S(1)} %get-tuple-element.17), channel_id=1, replica_groups=mesh['sec'=2,'atoms'=32,'batch'=8] {'sec'}, use_global_device_ids=true, to_apply=%region_1.2 | all-reduce | flops 512 | bytes 4096 | tf_op jit(solution)/shard_map/psum | solution.py:148
  22.9 2.1 %collective-permute-start.2 = (bf16[512,512]{1,0:T(8,128)(2,1)S(1)}, bf16[512,512]{1,0:T(8,128)(2,1)S(1)}, u32[]{:S(2)}, u32[]{:S(2)}) collective-permute-start(bf16[512,512]{1,0:T(8,128)(2,1)S(1)} %fusion.30), channel_id=1, source_target_pairs={{0,256},{256,0},{1,257},{257,1},{2,258},{258,2},{3,259},{259,3},{4... | collective-permute-start | bytes 1572872 | tf_op jit(solution)/shard_map/ppermute | solution.py:32
  25.9 0.8 collective-permute-done.2
  26.7 0.8 copy-done.4
  28.4 1.4 %fusion.25 = bf16[512,256]{0,1:T(8,128)(2,1)S(1)} fusion(f32[512,256]{0,1:T(8,128)S(1)} %fusion.62, bf16[512,512]{1,0:T(8,128)(2,1)} %copy-done.4, bf16[2,512,256]{2,1,0:T(8,128)(2,1)S(1)} %bitcast.139, s32[]{:T(128)S(6)} %select_n.136), kind=kOutput, calls=%fused_computation.29 | convolution fusion | flops 134479872 | bytes 1572868 | tf_op jit(solution)/shard_map/dot_general | solution.py:162
  31.2 13.1 %all-to-all-start = ((f32[32,5,128]{2,1,0:T(8,128)}), f32[32,5,128]{2,1,0:T(8,128)S(1)}, u32[]{:S(2)}, u32[]{:S(2)}) async-start(f32[32,5,128]{2,1,0:T(8,128)} %reshape.314), calls=%async_computation | async-start | bytes 262144 | tf_op jit(solution)/shard_map/all_to_all | solution.py:51
  44.3 1.3 fusion.59
  45.6 9.6 %all-to-all-done = f32[32,5,128]{2,1,0:T(8,128)S(1)} async-done(((f32[32,5,128]{2,1,0:T(8,128)}), f32[32,5,128]{2,1,0:T(8,128)S(1)}, u32[]{:S(2)}, u32[]{:S(2)}) %all-to-all-start) | async-done | bytes 81952 | tf_op jit(solution)/shard_map/all_to_all | solution.py:51
  55.9 3.8 %all-to-all-start.1 = ((f32[32,5,128]{2,1,0:T(8,128)}), f32[32,5,128]{2,1,0:T(8,128)S(1)}, u32[]{:S(2)}, u32[]{:S(2)}) async-start(f32[32,5,128]{2,1,0:T(8,128)} %broadcast_in_dim.89), calls=%async_computation.1 | async-start | bytes 262144 | tf_op jit(solution)/shard_map/all_to_all | solution.py:60
  59.8 1.5 %fusion.42 = f32[512,256]{0,1:T(8,128)S(1)} fusion(f32[512,256]{0,1:T(8,128)S(1)} %fusion.59, bf16[512,512]{1,0:T(8,128)(2,1)S(1)} %copy-done.5, bf16[2,512,256]{2,1,0:T(8,128)(2,1)} %bitcast.141, s32[]{:T(128)S(6)} %select_n.136), kind=kOutput, calls=%fused_computation.53 | convolution fusion | flops 135135232 | bytes 1835012 | tf_op jit(solution)/shard_map/dot_general | solution.py:162
  61.3 9.1 %all-to-all-done.1 = f32[32,5,128]{2,1,0:T(8,128)S(1)} async-done(((f32[32,5,128]{2,1,0:T(8,128)}), f32[32,5,128]{2,1,0:T(8,128)S(1)}, u32[]{:S(2)}, u32[]{:S(2)}) %all-to-all-start.1) | async-done | bytes 81952 | tf_op jit(solution)/shard_map/all_to_all | solution.py:60
  71.5 1.9 %collective-permute-start.3 = (f32[512,256]{0,1:T(8,128)S(1)}, f32[512,256]{0,1:T(8,128)S(1)}, u32[]{:S(2)}, u32[]{:S(2)}) collective-permute-start(f32[512,256]{0,1:T(8,128)S(1)} %bitcast.136), channel_id=1, source_target_pairs={{0,256},{256,0},{1,257},{257,1},{2,258},{258,2},{3,259},{259,3},{4... | collective-permute-start | bytes 1572872 | tf_op jit(solution)/shard_map/ppermute | solution.py:32
  73.6 2.4 %collective-permute-start.4 = (bf16[256,512]{1,0:T(8,128)(2,1)S(1)}, bf16[256,512]{1,0:T(8,128)(2,1)S(1)}, u32[]{:S(2)}, u32[]{:S(2)}) collective-permute-start(bf16[256,512]{1,0:T(8,128)(2,1)S(1)} %bitcast.142), channel_id=1, source_target_pairs={{0,256},{256,0},{1,257},{257,1},{2,258},{258,2},{3,259},{259,3},{4... | collective-permute-start | bytes 786440 | tf_op jit(solution)/shard_map/ppermute | solution.py:32
  76.2 1.0 collective-permute-done.4
  78.7 2.3 %collective-permute-start.5 = (f32[512,256]{0,1:T(8,128)S(1)}, f32[512,256]{0,1:T(8,128)S(1)}, u32[]{:S(2)}, u32[]{:S(2)}) collective-permute-start(f32[512,256]{0,1:T(8,128)S(1)} %fusion.103), channel_id=1, source_target_pairs={{0,256},{256,0},{1,257},{257,1},{2,258},{258,2},{3,259},{259,3},{4... | collective-permute-start | bytes 1572872 | tf_op jit(solution)/shard_map/ppermute | solution.py:32
  81.0 2.0 %collective-permute-start.6 = (bf16[128,256]{1,0:T(8,128)(2,1)S(1)}, bf16[128,256]{1,0:T(8,128)(2,1)S(1)}, u32[]{:S(2)}, u32[]{:S(2)}) collective-permute-start(bf16[128,256]{1,0:T(8,128)(2,1)S(1)} %bitcast.145), channel_id=1, source_target_pairs={{0,256},{256,0},{1,257},{257,1},{2,258},{258,2},{3,259},{259,3},{4... | collective-permute-start | bytes 196616 | tf_op jit(solution)/shard_map/ppermute | solution.py:32
  83.0 1.1 collective-permute-done.6
  84.3 1.5 %fusion.38 = (f32[]{:T(128)}, f32[512,256]{0,1:T(8,128)S(1)}) fusion(s32[512]{0:T(512)S(1)} %bitcast.148, f32[512]{0:T(512)S(1)} %fusion.89, bf16[128,256]{1,0:T(8,128)(2,1)S(1)} %get-tuple-element.32, bf16[128,256]{1,0:T(8,128)(2,1)S(1)} %get-tuple-element.31, f32[512,256]{0,1:T(8,128)S(1)} %get-tuple-element.16, f32[512]{0:T(512)S(1)} %add_rsqrt_fusion), kind=kOutput, calls=%fused_computation.49 | convolution fusion | flops 404881408 | bytes 1185796 | tf_op jit(solution)/shard_map/dot_general | solution.py:110
  85.8 0.7 multiply_reduce_fusion.1
  88.1 0.9 reshape.322
  89.0 3.9 %all-to-all-start.2 = ((f32[32,33,128]{2,1,0:T(8,128)}), f32[32,33,128]{2,1,0:T(8,128)S(1)}, u32[]{:S(2)}, u32[]{:S(2)}) async-start(f32[32,33,128]{2,1,0:T(8,128)} %reshape.322), calls=%async_computation.2 | async-start | bytes 1310720 | tf_op jit(solution)/shard_map/all_to_all | solution.py:51
  92.9 20.8 %all-to-all-done.2 = f32[32,33,128]{2,1,0:T(8,128)S(1)} async-done(((f32[32,33,128]{2,1,0:T(8,128)}), f32[32,33,128]{2,1,0:T(8,128)S(1)}, u32[]{:S(2)}, u32[]{:S(2)}) %all-to-all-start.2) | async-done | bytes 540704 | tf_op jit(solution)/shard_map/all_to_all | solution.py:51
  116.5 18.0 %all_to_all.20 = bf16[32,33,128]{2,1,0:T(8,128)(2,1)S(1)} all-to-all(bf16[32,33,128]{2,1,0:T(8,128)(2,1)S(1)} %broadcast_in_dim.93), channel_id=1, replica_groups=mesh['sec'=2,'atoms'=32,'batch'=8] {'atoms'}, dimensions={0} | all-to-all | bytes 540672 | tf_op jit(solution)/shard_map/all_to_all | solution.py:60
  135.3 0.9 broadcast_in_dim_reshape.3
  (80 shorter events, 11.4 us)
Async XLA Ops:
  0.6 24.5 %copy-start = (bf16[1024,256]{1,0:T(8,128)(2,1)S(1)}, bf16[1024,256]{1,0:T(8,128)(2,1)}, u32[]{:S(2)}) copy-start(bf16[1024,256]{1,0:T(8,128)(2,1)} %param.22) | copy-start | bytes 1572868
  0.6 14.3 %copy-start.1 = (bf16[1,512,512]{2,1,0:T(8,128)(2,1)S(1)}, bf16[1,512,512]{2,1,0:T(8,128)(2,1)}, u32[]{:S(2)}) copy-start(bf16[1,512,512]{2,1,0:T(8,128)(2,1)} %param.14) | copy-start | bytes 1572868
  1.8 9.7 %collective-permute-start = (bf16[256,512]{1,0:T(8,128)(2,1)S(1)}, bf16[256,512]{1,0:T(8,128)(2,1)S(1)}, u32[]{:S(2)}, u32[]{:S(2)}) collective-permute-start(bf16[256,512]{1,0:T(8,128)(2,1)S(1)} %get-tuple-element.29), channel_id=1, source_target_pairs={{0,8},{8,16},{16,24},{24,32},{32,40},{40,48},{48,56},{56,64},{64,7... | collective-permute-start | bytes 786440 | tf_op jit(solution)/shard_map/ppermute | solution.py:25
  5.3 9.7 %collective-permute-start.1 = (bf16[256,512]{1,0:T(8,128)(2,1)S(1)}, bf16[256,512]{1,0:T(8,128)(2,1)S(1)}, u32[]{:S(2)}, u32[]{:S(2)}) collective-permute-start(bf16[256,512]{1,0:T(8,128)(2,1)S(1)} %get-tuple-element.30), channel_id=1, source_target_pairs={{8,0},{16,8},{24,16},{32,24},{40,32},{48,40},{56,48},{64,56},{72,6... | collective-permute-start | bytes 786440 | tf_op jit(solution)/shard_map/ppermute | solution.py:26
  15.0 2.0 %copy-start.10 = (bf16[1,16,128,128]{3,2,1,0:T(8,128)(2,1)S(1)}, bf16[1,16,128,128]{3,2,1,0:T(8,128)(2,1)}, u32[]{:S(2)}) copy-start(bf16[1,16,128,128]{3,2,1,0:T(8,128)(2,1)} %param.16) | copy-start | bytes 1572868
  22.7 2.9 %copy-start.6 = (bf16[1024,256]{1,0:T(8,128)(2,1)S(1)}, bf16[1024,256]{1,0:T(8,128)(2,1)}, u32[]{:S(2)}) copy-start(bf16[1024,256]{1,0:T(8,128)(2,1)} %param.23) | copy-start | bytes 1572868
  22.9 3.8 %collective-permute-start.2 = (bf16[512,512]{1,0:T(8,128)(2,1)S(1)}, bf16[512,512]{1,0:T(8,128)(2,1)S(1)}, u32[]{:S(2)}, u32[]{:S(2)}) collective-permute-start(bf16[512,512]{1,0:T(8,128)(2,1)S(1)} %fusion.30), channel_id=1, source_target_pairs={{0,256},{256,0},{1,257},{257,1},{2,258},{258,2},{3,259},{259,3},{4... | collective-permute-start | bytes 1572872 | tf_op jit(solution)/shard_map/ppermute | solution.py:32
  25.2 3.2 %copy-start.7 = (bf16[1024,256]{1,0:T(8,128)(2,1)S(1)}, bf16[1024,256]{1,0:T(8,128)(2,1)}, u32[]{:S(2)}) copy-start(bf16[1024,256]{1,0:T(8,128)(2,1)} %param.23) | copy-start | bytes 1572868
  26.7 0.8 copy-start.4
  29.8 30.0 %copy-start.5 = (bf16[512,512]{1,0:T(8,128)(2,1)S(1)}, bf16[512,512]{1,0:T(8,128)(2,1)}, u32[]{:S(2)}) copy-start(bf16[512,512]{1,0:T(8,128)(2,1)} %copy-done.4) | copy-start | bytes 1572868
  31.2 24.0 %all-to-all-start = ((f32[32,5,128]{2,1,0:T(8,128)}), f32[32,5,128]{2,1,0:T(8,128)S(1)}, u32[]{:S(2)}, u32[]{:S(2)}) async-start(f32[32,5,128]{2,1,0:T(8,128)} %reshape.314), calls=%async_computation | async-start | bytes 262144 | tf_op jit(solution)/shard_map/all_to_all | solution.py:51
  55.9 14.5 %all-to-all-start.1 = ((f32[32,5,128]{2,1,0:T(8,128)}), f32[32,5,128]{2,1,0:T(8,128)S(1)}, u32[]{:S(2)}, u32[]{:S(2)}) async-start(f32[32,5,128]{2,1,0:T(8,128)} %broadcast_in_dim.89), calls=%async_computation.1 | async-start | bytes 262144 | tf_op jit(solution)/shard_map/all_to_all | solution.py:60
  59.7 13.7 %copy-start.2 = (bf16[256,1024]{0,1:T(8,128)(2,1)S(1)}, bf16[256,1024]{0,1:T(8,128)(2,1)}, u32[]{:S(2)}) copy-start(bf16[256,1024]{0,1:T(8,128)(2,1)} %copy.23) | copy-start | bytes 1572868
  71.5 5.7 %collective-permute-start.3 = (f32[512,256]{0,1:T(8,128)S(1)}, f32[512,256]{0,1:T(8,128)S(1)}, u32[]{:S(2)}, u32[]{:S(2)}) collective-permute-start(f32[512,256]{0,1:T(8,128)S(1)} %bitcast.136), channel_id=1, source_target_pairs={{0,256},{256,0},{1,257},{257,1},{2,258},{258,2},{3,259},{259,3},{4... | collective-permute-start | bytes 1572872 | tf_op jit(solution)/shard_map/ppermute | solution.py:32
  73.6 3.6 %collective-permute-start.4 = (bf16[256,512]{1,0:T(8,128)(2,1)S(1)}, bf16[256,512]{1,0:T(8,128)(2,1)S(1)}, u32[]{:S(2)}, u32[]{:S(2)}) collective-permute-start(bf16[256,512]{1,0:T(8,128)(2,1)S(1)} %bitcast.142), channel_id=1, source_target_pairs={{0,256},{256,0},{1,257},{257,1},{2,258},{258,2},{3,259},{259,3},{4... | collective-permute-start | bytes 786440 | tf_op jit(solution)/shard_map/ppermute | solution.py:32
  77.4 1.0 copy-start.8
  77.5 3.5 %copy-start.9 = (bf16[1,128,256]{2,1,0:T(8,128)(2,1)S(1)}, bf16[1,128,256]{2,1,0:T(8,128)(2,1)}, u32[]{:S(2)}) copy-start(bf16[1,128,256]{2,1,0:T(8,128)(2,1)} %param.19) | copy-start | bytes 196612
  78.3 8.1 %copy-start.3 = (bf16[512,512]{1,0:T(8,128)(2,1)}, bf16[512,512]{1,0:T(8,128)(2,1)S(1)}, u32[]{:S(2)}) copy-start(bf16[512,512]{1,0:T(8,128)(2,1)S(1)} %fusion.21) | copy-start | bytes 1572868
  78.3 6.0 %copy-start.11 = (s32[1,512]{1,0:T(1,128)S(1)}, s32[1,512]{1,0:T(1,128)}, u32[]{:S(2)}) copy-start(s32[1,512]{1,0:T(1,128)} %param.18) | copy-start | bytes 6148
  78.7 5.5 %collective-permute-start.5 = (f32[512,256]{0,1:T(8,128)S(1)}, f32[512,256]{0,1:T(8,128)S(1)}, u32[]{:S(2)}, u32[]{:S(2)}) collective-permute-start(f32[512,256]{0,1:T(8,128)S(1)} %fusion.103), channel_id=1, source_target_pairs={{0,256},{256,0},{1,257},{257,1},{2,258},{258,2},{3,259},{259,3},{4... | collective-permute-start | bytes 1572872 | tf_op jit(solution)/shard_map/ppermute | solution.py:32
  81.0 3.1 %collective-permute-start.6 = (bf16[128,256]{1,0:T(8,128)(2,1)S(1)}, bf16[128,256]{1,0:T(8,128)(2,1)S(1)}, u32[]{:S(2)}, u32[]{:S(2)}) collective-permute-start(bf16[128,256]{1,0:T(8,128)(2,1)S(1)} %bitcast.145), channel_id=1, source_target_pairs={{0,256},{256,0},{1,257},{257,1},{2,258},{258,2},{3,259},{259,3},{4... | collective-permute-start | bytes 196616 | tf_op jit(solution)/shard_map/ppermute | solution.py:32
  89.0 24.7 %all-to-all-start.2 = ((f32[32,33,128]{2,1,0:T(8,128)}), f32[32,33,128]{2,1,0:T(8,128)S(1)}, u32[]{:S(2)}, u32[]{:S(2)}) async-start(f32[32,33,128]{2,1,0:T(8,128)} %reshape.322), calls=%async_computation.2 | async-start | bytes 1310720 | tf_op jit(solution)/shard_map/all_to_all | solution.py:51

commit v8 on v7

--- a/solution.py
+++ b/solution.py
@@ -42,13 +42,15 @@
     return x + swap_sec(x)
 
 
-def sum_atoms(x, exact=None):
+def sum_atoms(x, exact=None, riders=None):
     peers = lax.axis_size("atoms")
     flat = x.reshape(-1)
     chunk = -(-flat.shape[0] // (peers * 128)) * 128
     flat = jnp.pad(flat, (0, chunk * peers - flat.shape[0]))
     pieces = flat.reshape(peers, chunk // 128, 128)
     arrived = lax.all_to_all(pieces, "atoms", 0, 0, tiled=True)
+    if riders is not None:
+        arrived, riders = lax.optimization_barrier((arrived, riders))
     owned = jnp.sum(arrived, axis=0, keepdims=True)
     if exact is not None:
         owner, slot = divmod(exact, chunk)
@@ -58,7 +60,8 @@
         kept = jnp.where(here, rest[0, slot // 128, slot % 128], owned[0, spare[0], spare[1]])
         owned = owned.at[0, spare[0], spare[1]].set(kept).astype(jnp.bfloat16)
     spread = lax.all_to_all(jnp.broadcast_to(owned, pieces.shape), "atoms", 0, 0, tiled=True)
-    return spread.reshape(-1)[: x.size].reshape(x.shape).astype(jnp.float32)
+    total = spread.reshape(-1)[: x.size].reshape(x.shape).astype(jnp.float32)
+    return total if riders is None else (total, riders)
 
 
 def feature_map(values):
@@ -152,9 +155,8 @@
     sec = lax.axis_index("sec")
     width = normed.shape[1]
     other_rows = swap_sec(normed)
-    peak_all = join_sec(peak_part, swap_sec(peak_part), sec, 0)
     out_cols = w_out.reshape(w_out.shape[0], 2, width)
-    out_rows = join_sec(out_cols[:, sec, :], swap_sec(out_cols[:, 1 - sec, :]), sec, 0)
+    partner = (swap_sec(peak_part), swap_sec(out_cols[:, 1 - sec, :]))
 
     def project(weight):
         halves = weight.reshape(2, width, weight.shape[1])
@@ -170,7 +172,9 @@
         key_f.astype(jnp.bfloat16), value_f.astype(jnp.bfloat16), atom_mask, head_count
     )
     state_rows = jnp.concatenate([outer_state, key_total[:, None, :]], axis=1)
-    packed = sum_atoms(state_rows)
+    packed, partner = sum_atoms(state_rows, riders=partner)
+    peak_all = join_sec(peak_part, partner[0], sec, 0)
+    out_rows = join_sec(out_cols[:, sec, :], partner[1], sec, 0)
     outer_state, key_total = packed[:, :HEAD_DIM, :], packed[:, HEAD_DIM, :]
     attended = read_summary(query_f.astype(jnp.bfloat16), outer_state, key_total, head_count)
     attended_all = join_sec(attended, swap_sec(attended), sec, 1)

time: 140 us -> 138 us (0.986)
  matrix products: 13.3 us -> 11.4 us
    ppermute x1, waiting for transfers between devices: 3.49 us -> 1.09 us  [extended(): after = lax.ppermute(leading, axis, down)]
    select_n x3, other arithmetic: 0.18 us -> 1.97 us  [join_sec(): first = jnp.where(sec == 0, mine, other)]
    unnamed x26 -> x28, local copies, waits for them, and re-layouts: 3.49 us -> 2.7 us
  transfers between devices with their start and end apart: 10 -> 10, of which waited for: 7 -> 7; matrix products, arithmetic and copies ran while one was open for 6% -> 11% of each run, Pallas kernels for 0% -> 0%
where the time goes in v8:
time: 138 us; the launch traced here: 136 us
  waiting for transfers between devices  44.8 us (32%)
  starting transfers between devices  37 us (27%)
  blocking collectives  20.5 us (15%)
  local copies, waits for them, and re-layouts  12.4 us (9%)
  matrix products  11.4 us (8%)
  between operations  6.85 us (5%)
  other arithmetic  3.22 us (2%)
    all_to_all x2, waiting for transfers between devices, sum_atoms(): arrived = lax.all_to_all(pieces, 'atoms', 0, 0, tiled=True)  31.2 us
    all_to_all x2, starting transfers between devices, sum_atoms(): arrived = lax.all_to_all(pieces, 'atoms', 0, 0, tiled=True)  18 us
    all_to_all x1, blocking collectives, sum_atoms(): lax.all_to_all(jnp.broadcast_to(owned, pieces.shape), 'atoms', 0, 0, tile...  18 us
    ppermute x5, starting transfers between devices, swap_sec(): return lax.ppermute(x, 'sec', [(0, 1), (1, 0)])  10.4 us
    all_to_all x1, waiting for transfers between devices, sum_atoms(): lax.all_to_all(jnp.broadcast_to(owned, pieces.shape), 'atoms', 0, 0, tile...  10.1 us
    all_to_all x1, starting transfers between devices, sum_atoms(): lax.all_to_all(jnp.broadcast_to(owned, pieces.shape), 'atoms', 0, 0, tile...  3.86 us
    ppermute x1, starting transfers between devices, extended(): before = lax.ppermute(last, axis, up)  3.5 us
    dot_general x1, matrix products, message_pass(): jnp.einsum('btij,tjf->bif', masked, panels, preferred_element_type=jnp.fl...  2.92 us
  transfers between devices with their start and end apart: 10, of which 7 were waited for; matrix products, arithmetic and copies ran while one was open for 11% of the time, Pallas kernels for 0%

profile of v8, /device:TPU:6, one launch (start us, length us, event | category | flops | bytes accessed | tf_op | source)
XLA Modules:
  0.0 136.1 jit_solution(7593182744413839390)
XLA Ops:
  0.7 1.1 slice_bitcast_fusion.1
  1.8 3.5 %collective-permute-start = (bf16[256,512]{1,0:T(8,128)(2,1)S(1)}, bf16[256,512]{1,0:T(8,128)(2,1)S(1)}, u32[]{:S(2)}, u32[]{:S(2)}) collective-permute-start(bf16[256,512]{1,0:T(8,128)(2,1)S(1)} %get-tuple-element.35), channel_id=1, source_target_pairs={{0,8},{8,16},{16,24},{24,32},{32,40},{40,48},{48,56},{56,64},{64,7... | collective-permute-start | bytes 786440 | tf_op jit(solution)/shard_map/ppermute | solution.py:25
  5.3 1.3 collective-permute-start.1
  6.6 1.2 copy.22
  7.9 0.8 copy.23
  8.8 1.9 %collective-permute-start.4 = (bf16[256,512]{1,0:T(8,128)(2,1)}, bf16[256,512]{1,0:T(8,128)(2,1)}, u32[]{:S(2)}, u32[]{:S(2)}) collective-permute-start(bf16[256,512]{1,0:T(8,128)(2,1)} %bitcast.26), channel_id=1, source_target_pairs={{0,256},{256,0},{1,257},{257,1},{2,258},{258,2},{3,259},{259,3},{4... | collective-permute-start | bytes 786440 | tf_op jit(solution)/shard_map/ppermute | solution.py:32
  10.7 2.4 %collective-permute-start.3 = (bf16[128,256]{1,0:T(8,128)(2,1)}, bf16[128,256]{1,0:T(8,128)(2,1)}, u32[]{:S(2)}, u32[]{:S(2)}) collective-permute-start(bf16[128,256]{1,0:T(8,128)(2,1)} %bitcast.24), channel_id=1, source_target_pairs={{0,256},{256,0},{1,257},{257,1},{2,258},{258,2},{3,259},{259,3},{4... | collective-permute-start | bytes 196616 | tf_op jit(solution)/shard_map/ppermute | solution.py:32
  13.9 1.1 collective-permute-done.1
  15.1 2.0 %gather_fusion = bf16[16,128,512]{2,1,0:T(8,128)(2,1)} fusion(bf16[8,128,512]{2,1,0:T(8,128)(2,1)S(1)} %bitcast.127, s32[1024]{0:T(1024)S(1)} %pad_clamp_fusion), kind=kCustom, calls=%fused_computation | custom fusion | bytes 4194368 | tf_op jit(solution)/shard_map/jit(_take)/gather | solution.py:84
  17.1 2.9 %fusion.16 = f32[4,128,512]{2,1,0:T(8,128)S(1)} fusion(bf16[16,128,512]{2,1,0:T(8,128)(2,1)} %gather_fusion, pred[16]{0:T(512)(128)(4,1)S(1)} %get-tuple-element.25, pred[4,16]{1,0:T(4,128)(4,1)S(1)} %iota_compare_fusion.2, bf16[16,128,128]{2,1,0:T(8,128)(2,1)S(1)} %bitcast.145), kind=kOutput, calls=%fused_computation.17 | convolution fusion | flops 1076363264 | bytes 3670096 | tf_op jit(solution)/shard_map/btij,tjf->bif/dot_general | solution.py:87
  20.3 2.5 %psum.7 = f32[512]{0:T(512)S(1)} all-reduce(f32[512]{0:T(512)S(1)} %get-tuple-element.23), channel_id=1, replica_groups=mesh['sec'=2,'atoms'=32,'batch'=8] {'sec'}, use_global_device_ids=true, to_apply=%region_1.2 | all-reduce | flops 512 | bytes 4096 | tf_op jit(solution)/shard_map/psum | solution.py:151
  22.9 2.1 %collective-permute-start.2 = (bf16[512,512]{1,0:T(8,128)(2,1)S(1)}, bf16[512,512]{1,0:T(8,128)(2,1)S(1)}, u32[]{:S(2)}, u32[]{:S(2)}) collective-permute-start(bf16[512,512]{1,0:T(8,128)(2,1)S(1)} %fusion.30), channel_id=1, source_target_pairs={{0,256},{256,0},{1,257},{257,1},{2,258},{258,2},{3,259},{259,3},{4... | collective-permute-start | bytes 1572872 | tf_op jit(solution)/shard_map/ppermute | solution.py:32
  26.0 0.8 collective-permute-done.2
  26.7 0.8 copy-done.3
  28.4 1.4 %fusion.25 = bf16[512,256]{0,1:T(8,128)(2,1)S(1)} fusion(f32[512,256]{0,1:T(8,128)S(1)} %fusion.62, bf16[512,512]{1,0:T(8,128)(2,1)} %copy-done.3, bf16[2,512,256]{2,1,0:T(8,128)(2,1)S(1)} %bitcast.139, s32[]{:T(128)S(6)} %select_n.136), kind=kOutput, calls=%fused_computation.29 | convolution fusion | flops 134479872 | bytes 1572868 | tf_op jit(solution)/shard_map/dot_general | solution.py:164
  31.3 14.1 %all-to-all-start = ((f32[32,5,128]{2,1,0:T(8,128)}), f32[32,5,128]{2,1,0:T(8,128)S(1)}, u32[]{:S(2)}, u32[]{:S(2)}) async-start(f32[32,5,128]{2,1,0:T(8,128)} %reshape.314), calls=%async_computation | async-start | bytes 262144 | tf_op jit(solution)/shard_map/all_to_all | solution.py:51
  45.8 10.5 %all-to-all-done = f32[32,5,128]{2,1,0:T(8,128)S(1)} async-done(((f32[32,5,128]{2,1,0:T(8,128)}), f32[32,5,128]{2,1,0:T(8,128)S(1)}, u32[]{:S(2)}, u32[]{:S(2)}) %all-to-all-start) | async-done | bytes 81952 | tf_op jit(solution)/shard_map/all_to_all | solution.py:51
  57.0 3.9 %all-to-all-start.1 = ((f32[32,5,128]{2,1,0:T(8,128)}), f32[32,5,128]{2,1,0:T(8,128)S(1)}, u32[]{:S(2)}, u32[]{:S(2)}) async-start(f32[32,5,128]{2,1,0:T(8,128)} %broadcast_in_dim.89), calls=%async_computation.1 | async-start | bytes 262144 | tf_op jit(solution)/shard_map/all_to_all | solution.py:62
  61.4 10.1 %all-to-all-done.1 = f32[32,5,128]{2,1,0:T(8,128)S(1)} async-done(((f32[32,5,128]{2,1,0:T(8,128)}), f32[32,5,128]{2,1,0:T(8,128)S(1)}, u32[]{:S(2)}, u32[]{:S(2)}) %all-to-all-start.1) | async-done | bytes 81952 | tf_op jit(solution)/shard_map/all_to_all | solution.py:62
  72.6 1.9 %collective-permute-start.5 = (f32[512,256]{0,1:T(8,128)S(1)}, f32[512,256]{0,1:T(8,128)S(1)}, u32[]{:S(2)}, u32[]{:S(2)}) collective-permute-start(f32[512,256]{0,1:T(8,128)S(1)} %bitcast.136), channel_id=1, source_target_pairs={{0,256},{256,0},{1,257},{257,1},{2,258},{258,2},{3,259},{259,3},{4... | collective-permute-start | bytes 1572872 | tf_op jit(solution)/shard_map/ppermute | solution.py:32
  74.7 1.0 bitcast_select_fusion.1
  75.7 0.7 collective-permute-done.5
  77.8 2.0 %collective-permute-start.6 = (f32[512,256]{0,1:T(8,128)S(1)}, f32[512,256]{0,1:T(8,128)S(1)}, u32[]{:S(2)}, u32[]{:S(2)}) collective-permute-start(f32[512,256]{0,1:T(8,128)S(1)} %fusion.103), channel_id=1, source_target_pairs={{0,256},{256,0},{1,257},{257,1},{2,258},{258,2},{3,259},{259,3},{4... | collective-permute-start | bytes 1572872 | tf_op jit(solution)/shard_map/ppermute | solution.py:32
  79.9 0.9 broadcast_select_fusion.3
  80.8 0.9 collective-permute-done.6
  81.8 1.5 %fusion.38 = (f32[]{:T(128)}, f32[512,256]{0,1:T(8,128)S(1)}) fusion(s32[512]{0:T(512)S(1)} %bitcast.146, f32[512]{0:T(512)S(1)} %fusion.89, bf16[128,256]{1,0:T(8,128)(2,1)S(1)} %get-tuple-element.38, bf16[128,256]{1,0:T(8,128)(2,1)S(1)} %get-tuple-element.37, f32[512,256]{0,1:T(8,128)S(1)} %get-tuple-element.22, f32[512]{0:T(512)S(1)} %add_rsqrt_fusion), kind=kOutput, calls=%fused_computation.49 | convolution fusion | flops 404881408 | bytes 1185796 | tf_op jit(solution)/shard_map/dot_general | solution.py:113
  83.3 0.7 multiply_reduce_fusion.1
  85.6 0.9 reshape.322
  86.5 3.9 %all-to-all-start.2 = ((f32[32,33,128]{2,1,0:T(8,128)}), f32[32,33,128]{2,1,0:T(8,128)S(1)}, u32[]{:S(2)}, u32[]{:S(2)}) async-start(f32[32,33,128]{2,1,0:T(8,128)} %reshape.322), calls=%async_computation.2 | async-start | bytes 1310720 | tf_op jit(solution)/shard_map/all_to_all | solution.py:51
  90.4 20.8 %all-to-all-done.2 = f32[32,33,128]{2,1,0:T(8,128)S(1)} async-done(((f32[32,33,128]{2,1,0:T(8,128)}), f32[32,33,128]{2,1,0:T(8,128)S(1)}, u32[]{:S(2)}, u32[]{:S(2)}) %all-to-all-start.2) | async-done | bytes 540704 | tf_op jit(solution)/shard_map/all_to_all | solution.py:51
  114.0 18.0 %all_to_all.20 = bf16[32,33,128]{2,1,0:T(8,128)(2,1)S(1)} all-to-all(bf16[32,33,128]{2,1,0:T(8,128)(2,1)S(1)} %broadcast_in_dim.93), channel_id=1, replica_groups=mesh['sec'=2,'atoms'=32,'batch'=8] {'atoms'}, dimensions={0} | all-to-all | bytes 540672 | tf_op jit(solution)/shard_map/all_to_all | solution.py:62
  132.8 0.9 broadcast_in_dim_reshape.3
  (82 shorter events, 10.8 us)
Async XLA Ops:
  0.6 24.6 %copy-start = (bf16[1024,256]{1,0:T(8,128)(2,1)S(1)}, bf16[1024,256]{1,0:T(8,128)(2,1)}, u32[]{:S(2)}) copy-start(bf16[1024,256]{1,0:T(8,128)(2,1)} %param.22) | copy-start | bytes 1572868
  0.6 14.3 %copy-start.1 = (bf16[1,512,512]{2,1,0:T(8,128)(2,1)S(1)}, bf16[1,512,512]{2,1,0:T(8,128)(2,1)}, u32[]{:S(2)}) copy-start(bf16[1,512,512]{2,1,0:T(8,128)(2,1)} %param.14) | copy-start | bytes 1572868
  0.7 12.5 %copy-start.10 = (s32[1,2,16]{2,1,0:T(2,128)S(1)}, s32[1,2,16]{2,1,0:T(2,128)}, u32[]{:S(2)}) copy-start(s32[1,2,16]{2,1,0:T(2,128)} %param.15) | copy-start | bytes 388
  0.7 13.2 %copy-start.9 = (bf16[512]{0:T(512)(128)(2,1)S(1)}, bf16[512]{0:T(512)(128)(2,1)}, u32[]{:S(2)}) copy-start(bf16[512]{0:T(512)(128)(2,1)} %param.20) | copy-start | bytes 3076
  1.8 12.1 %collective-permute-start = (bf16[256,512]{1,0:T(8,128)(2,1)S(1)}, bf16[256,512]{1,0:T(8,128)(2,1)S(1)}, u32[]{:S(2)}, u32[]{:S(2)}) collective-permute-start(bf16[256,512]{1,0:T(8,128)(2,1)S(1)} %get-tuple-element.35), channel_id=1, source_target_pairs={{0,8},{8,16},{16,24},{24,32},{32,40},{40,48},{48,56},{56,64},{64,7... | collective-permute-start | bytes 786440 | tf_op jit(solution)/shard_map/ppermute | solution.py:25
  5.3 9.7 %collective-permute-start.1 = (bf16[256,512]{1,0:T(8,128)(2,1)S(1)}, bf16[256,512]{1,0:T(8,128)(2,1)S(1)}, u32[]{:S(2)}, u32[]{:S(2)}) collective-permute-start(bf16[256,512]{1,0:T(8,128)(2,1)S(1)} %get-tuple-element.36), channel_id=1, source_target_pairs={{8,0},{16,8},{24,16},{32,24},{40,32},{48,40},{56,48},{64,56},{72,6... | collective-permute-start | bytes 786440 | tf_op jit(solution)/shard_map/ppermute | solution.py:26
  8.8 37.0 %collective-permute-start.4 = (bf16[256,512]{1,0:T(8,128)(2,1)}, bf16[256,512]{1,0:T(8,128)(2,1)}, u32[]{:S(2)}, u32[]{:S(2)}) collective-permute-start(bf16[256,512]{1,0:T(8,128)(2,1)} %bitcast.26), channel_id=1, source_target_pairs={{0,256},{256,0},{1,257},{257,1},{2,258},{258,2},{3,259},{259,3},{4... | collective-permute-start | bytes 786440 | tf_op jit(solution)/shard_map/ppermute | solution.py:32
  10.7 35.1 %collective-permute-start.3 = (bf16[128,256]{1,0:T(8,128)(2,1)}, bf16[128,256]{1,0:T(8,128)(2,1)}, u32[]{:S(2)}, u32[]{:S(2)}) collective-permute-start(bf16[128,256]{1,0:T(8,128)(2,1)} %bitcast.24), channel_id=1, source_target_pairs={{0,256},{256,0},{1,257},{257,1},{2,258},{258,2},{3,259},{259,3},{4... | collective-permute-start | bytes 196616 | tf_op jit(solution)/shard_map/ppermute | solution.py:32
  15.1 2.0 %copy-start.11 = (bf16[1,16,128,128]{3,2,1,0:T(8,128)(2,1)S(1)}, bf16[1,16,128,128]{3,2,1,0:T(8,128)(2,1)}, u32[]{:S(2)}) copy-start(bf16[1,16,128,128]{3,2,1,0:T(8,128)(2,1)} %param.16) | copy-start | bytes 1572868
  22.7 2.9 %copy-start.5 = (bf16[1024,256]{1,0:T(8,128)(2,1)S(1)}, bf16[1024,256]{1,0:T(8,128)(2,1)}, u32[]{:S(2)}) copy-start(bf16[1024,256]{1,0:T(8,128)(2,1)} %param.23) | copy-start | bytes 1572868
  22.9 3.8 %collective-permute-start.2 = (bf16[512,512]{1,0:T(8,128)(2,1)S(1)}, bf16[512,512]{1,0:T(8,128)(2,1)S(1)}, u32[]{:S(2)}, u32[]{:S(2)}) collective-permute-start(bf16[512,512]{1,0:T(8,128)(2,1)S(1)} %fusion.30), channel_id=1, source_target_pairs={{0,256},{256,0},{1,257},{257,1},{2,258},{258,2},{3,259},{259,3},{4... | collective-permute-start | bytes 1572872 | tf_op jit(solution)/shard_map/ppermute | solution.py:32
  25.2 3.2 %copy-start.6 = (bf16[1024,256]{1,0:T(8,128)(2,1)S(1)}, bf16[1024,256]{1,0:T(8,128)(2,1)}, u32[]{:S(2)}) copy-start(bf16[1024,256]{1,0:T(8,128)(2,1)} %param.23) | copy-start | bytes 1572868
  26.7 0.8 copy-start.3
  29.8 15.6 %copy-start.7 = (bf16[1024,256]{1,0:T(8,128)(2,1)S(1)}, bf16[1024,256]{1,0:T(8,128)(2,1)}, u32[]{:S(2)}) copy-start(bf16[1024,256]{1,0:T(8,128)(2,1)} %param.21) | copy-start | bytes 1572868
  29.8 31.1 %copy-start.4 = (bf16[512,512]{1,0:T(8,128)(2,1)S(1)}, bf16[512,512]{1,0:T(8,128)(2,1)}, u32[]{:S(2)}) copy-start(bf16[512,512]{1,0:T(8,128)(2,1)} %copy-done.3) | copy-start | bytes 1572868
  31.3 25.0 %all-to-all-start = ((f32[32,5,128]{2,1,0:T(8,128)}), f32[32,5,128]{2,1,0:T(8,128)S(1)}, u32[]{:S(2)}, u32[]{:S(2)}) async-start(f32[32,5,128]{2,1,0:T(8,128)} %reshape.314), calls=%async_computation | async-start | bytes 262144 | tf_op jit(solution)/shard_map/all_to_all | solution.py:51
  57.0 14.5 %all-to-all-start.1 = ((f32[32,5,128]{2,1,0:T(8,128)}), f32[32,5,128]{2,1,0:T(8,128)S(1)}, u32[]{:S(2)}, u32[]{:S(2)}) async-start(f32[32,5,128]{2,1,0:T(8,128)} %broadcast_in_dim.89), calls=%async_computation.1 | async-start | bytes 262144 | tf_op jit(solution)/shard_map/all_to_all | solution.py:62
  72.6 3.8 %collective-permute-start.5 = (f32[512,256]{0,1:T(8,128)S(1)}, f32[512,256]{0,1:T(8,128)S(1)}, u32[]{:S(2)}, u32[]{:S(2)}) collective-permute-start(f32[512,256]{0,1:T(8,128)S(1)} %bitcast.136), channel_id=1, source_target_pairs={{0,256},{256,0},{1,257},{257,1},{2,258},{258,2},{3,259},{259,3},{4... | collective-permute-start | bytes 1572872 | tf_op jit(solution)/shard_map/ppermute | solution.py:32
  76.5 1.0 copy-start.8
  77.5 6.5 %copy-start.2 = (bf16[512,512]{1,0:T(8,128)(2,1)}, bf16[512,512]{1,0:T(8,128)(2,1)S(1)}, u32[]{:S(2)}) copy-start(bf16[512,512]{1,0:T(8,128)(2,1)S(1)} %fusion.21) | copy-start | bytes 1572868
  77.5 4.3 %copy-start.12 = (s32[1,512]{1,0:T(1,128)S(1)}, s32[1,512]{1,0:T(1,128)}, u32[]{:S(2)}) copy-start(s32[1,512]{1,0:T(1,128)} %param.18) | copy-start | bytes 6148
  77.8 3.8 %collective-permute-start.6 = (f32[512,256]{0,1:T(8,128)S(1)}, f32[512,256]{0,1:T(8,128)S(1)}, u32[]{:S(2)}, u32[]{:S(2)}) collective-permute-start(f32[512,256]{0,1:T(8,128)S(1)} %fusion.103), channel_id=1, source_target_pairs={{0,256},{256,0},{1,257},{257,1},{2,258},{258,2},{3,259},{259,3},{4... | collective-permute-start | bytes 1572872 | tf_op jit(solution)/shard_map/ppermute | solution.py:32
  86.5 24.7 %all-to-all-start.2 = ((f32[32,33,128]{2,1,0:T(8,128)}), f32[32,33,128]{2,1,0:T(8,128)S(1)}, u32[]{:S(2)}, u32[]{:S(2)}) async-start(f32[32,33,128]{2,1,0:T(8,128)} %reshape.322), calls=%async_computation.2 | async-start | bytes 1310720 | tf_op jit(solution)/shard_map/all_to_all | solution.py:51

commit v9 on v8

--- a/solution.py
+++ b/solution.py
@@ -36,10 +36,6 @@
     first = jnp.where(sec == 0, mine, other)
     second = jnp.where(sec == 0, other, mine)
     return jnp.concatenate([first, second], axis=axis)
-
-
-def sum_sec(x):
-    return x + swap_sec(x)
 
 
 def sum_atoms(x, exact=None, riders=None):
@@ -140,28 +136,32 @@
     w_proj,
 ):
     atom_rows = atoms_in[0]
-    local_rows = atom_rows.shape[0]
+    local_rows, width = atom_rows.shape
+    sec = lax.axis_index("sec")
+    peak_part = peak_embed[0]
+    peak_count, embed_width = peak_part.shape
+    early = swap_sec(jnp.concatenate([peak_part, norm_gain.reshape(-1, embed_width)], axis=0))
+    peak_other, gain_other = early[:peak_count], early[peak_count:].reshape(-1)
+    partner = (swap_sec(w_out), swap_sec(w_proj))
     gathered = message_pass(atom_rows, tile_ids[0], tile_vals[0])
     hidden_one = (atom_rows.astype(jnp.float32) + gathered.astype(jnp.float32)).astype(jnp.bfloat16)
+    mine_f = hidden_one.astype(jnp.float32)
+    other_f = swap_sec(hidden_one).astype(jnp.float32)
     atom_base = lax.axis_index("atoms") * local_rows
     length_one = seq_lens[0]
     label_row = pair_labels[0]
-    peak_part = peak_embed[0]
-    hidden_f = hidden_one.astype(jnp.float32)
-    square_sum = lax.psum(jnp.sum(hidden_f * hidden_f, axis=-1), "sec")
-    row_scale = lax.rsqrt(square_sum[:, None] / D + EPSILON)
-    normed = (hidden_f * row_scale * norm_gain.astype(jnp.float32)).astype(jnp.bfloat16)
+    square_sum = jnp.sum(mine_f * mine_f, axis=-1, keepdims=True) + jnp.sum(
+        other_f * other_f, axis=-1, keepdims=True
+    )
+    row_scale = lax.rsqrt(square_sum / D + EPSILON)
+    normed_mine = (mine_f * row_scale * norm_gain.astype(jnp.float32)).astype(jnp.bfloat16)
+    normed_other = (other_f * row_scale * gain_other.astype(jnp.float32)).astype(jnp.bfloat16)
     head_cols = w_query.shape[1]
-    sec = lax.axis_index("sec")
-    width = normed.shape[1]
-    other_rows = swap_sec(normed)
-    out_cols = w_out.reshape(w_out.shape[0], 2, width)
-    partner = (swap_sec(peak_part), swap_sec(out_cols[:, 1 - sec, :]))
 
     def project(weight):
         halves = weight.reshape(2, width, weight.shape[1])
-        mine = jnp.dot(normed, halves[sec], preferred_element_type=jnp.float32)
-        return mine + jnp.dot(other_rows, halves[1 - sec], preferred_element_type=jnp.float32)
+        mine = jnp.dot(normed_mine, halves[sec], preferred_element_type=jnp.float32)
+        return mine + jnp.dot(normed_other, halves[1 - sec], preferred_element_type=jnp.float32)
 
     query_f, key_f, value_f = tuple((project(weight) for weight in (w_query, w_key, w_value)))
     head_count = head_cols // HEAD_DIM
@@ -173,20 +173,32 @@
     )
     state_rows = jnp.concatenate([outer_state, key_total[:, None, :]], axis=1)
     packed, partner = sum_atoms(state_rows, riders=partner)
-    peak_all = join_sec(peak_part, partner[0], sec, 0)
-    out_rows = join_sec(out_cols[:, sec, :], partner[1], sec, 0)
+    out_other, proj_other = partner
     outer_state, key_total = packed[:, :HEAD_DIM, :], packed[:, HEAD_DIM, :]
     attended = read_summary(query_f.astype(jnp.bfloat16), outer_state, key_total, head_count)
-    attended_all = join_sec(attended, swap_sec(attended), sec, 1)
-    out_sum = jnp.sum(attended_all * attended_all, axis=-1)
-    attended_n = (attended_all * lax.rsqrt(out_sum[:, None] / (HEADS * HEAD_DIM) + EPSILON)).astype(
-        jnp.bfloat16
-    )
-    branch = jnp.dot(attended_n, out_rows, preferred_element_type=jnp.float32)
-    hidden_two = (hidden_f + branch).astype(jnp.bfloat16)
-    embedded = sum_sec(jnp.dot(hidden_two, w_proj, preferred_element_type=jnp.float32))
+    attended_other = swap_sec(attended)
+    out_sum = jnp.sum(attended * attended, axis=-1, keepdims=True) + jnp.sum(
+        attended_other * attended_other, axis=-1, keepdims=True
+    )
+    out_scale = lax.rsqrt(out_sum / (HEADS * HEAD_DIM) + EPSILON)
+    normed_att = (attended * out_scale).astype(jnp.bfloat16)
+    normed_att_other = (attended_other * out_scale).astype(jnp.bfloat16)
+    out_mine = w_out.reshape(w_out.shape[0], 2, width)
+    out_other = out_other.reshape(out_mine.shape)
+
+    def branch_for(half):
+        return jnp.dot(normed_att, out_mine[:, half, :], preferred_element_type=jnp.float32) + jnp.dot(
+            normed_att_other, out_other[:, half, :], preferred_element_type=jnp.float32
+        )
+
+    hidden_two = (mine_f + branch_for(sec)).astype(jnp.bfloat16)
+    hidden_other = (other_f + branch_for(1 - sec)).astype(jnp.bfloat16)
+    embedded = jnp.dot(hidden_two, w_proj, preferred_element_type=jnp.float32) + jnp.dot(
+        hidden_other, proj_other, preferred_element_type=jnp.float32
+    )
     embed_scale = lax.rsqrt(jnp.mean(embedded * embedded, axis=-1, keepdims=True) + EPSILON)
     unit_rows = embedded * embed_scale
+    peak_all = join_sec(peak_part, peak_other, sec, 0)
     loss_part, unit_grad = contrast(unit_rows, peak_all, label_row, atom_mask, 0)
     embed_grad = embed_backward(unit_rows, unit_grad, embed_scale)
     proj_part = jnp.einsum("nd,ne->de", hidden_two, embed_grad, preferred_element_type=jnp.float32)

time: 138 us -> 147 us (1.065)
  matrix products: 11.4 us -> 19.7 us
  waiting for transfers between devices: 44.8 us -> 47.8 us
  other arithmetic: 3.22 us -> 5.82 us
  blocking collectives: 20.5 us -> 18 us
    dot_general x7 -> x10, matrix products: 4.09 us -> 10.4 us  [the longest x3 2.79 us: project(): jnp.dot(normed_other, halves[1 - sec], preferred_element_type=jnp.float32)]
    ppermute x1, waiting for transfers between devices: 1.09 us -> 4.13 us  [extended(): after = lax.ppermute(leading, axis, down)]
    ppermute x1, waiting for transfers between devices: 0.01 us -> 2.75 us  [extended(): before = lax.ppermute(last, axis, up)]
    psum x1 -> x0, blocking collectives: 2.46 us -> none  [shards(): square_sum = lax.psum(jnp.sum(hidden_f * hidden_f, axis=-1), 'sec')]
    ppermute x5, waiting for transfers between devices: 2.35 us -> 0.84 us  [swap_sec(): return lax.ppermute(x, 'sec', [(0, 1), (1, 0)])]
  transfers between devices with their start and end apart: 10 -> 10, of which waited for: 7 -> 6; matrix products, arithmetic and copies ran while one was open for 11% -> 9% of each run, Pallas kernels for 0% -> 0%
where the time goes in v9:
time: 147 us; the launch traced here: 146 us
  waiting for transfers between devices  47.8 us (33%)
  starting transfers between devices  36.4 us (25%)
  matrix products  19.7 us (13%)
  blocking collectives  18 us (12%)
  local copies, waits for them, and re-layouts  11.1 us (8%)
  between operations  6.85 us (5%)
  other arithmetic  5.82 us (4%)
    all_to_all x2, waiting for transfers between devices, sum_atoms(): arrived = lax.all_to_all(pieces, 'atoms', 0, 0, tiled=True)  30.1 us
    all_to_all x1, blocking collectives, sum_atoms(): lax.all_to_all(jnp.broadcast_to(owned, pieces.shape), 'atoms', 0, 0, tile...  18 us
    all_to_all x2, starting transfers between devices, sum_atoms(): arrived = lax.all_to_all(pieces, 'atoms', 0, 0, tiled=True)  17 us
    ppermute x5, starting transfers between devices, swap_sec(): return lax.ppermute(x, 'sec', [(0, 1), (1, 0)])  10.7 us
    all_to_all x1, waiting for transfers between devices, sum_atoms(): lax.all_to_all(jnp.broadcast_to(owned, pieces.shape), 'atoms', 0, 0, tile...  9.99 us
    ppermute x1, waiting for transfers between devices, extended(): after = lax.ppermute(leading, axis, down)  4.13 us
    all_to_all x1, starting transfers between devices, sum_atoms(): lax.all_to_all(jnp.broadcast_to(owned, pieces.shape), 'atoms', 0, 0, tile...  3.85 us
    ppermute x1, starting transfers between devices, extended(): before = lax.ppermute(last, axis, up)  3.5 us
  transfers between devices with their start and end apart: 10, of which 6 were waited for; matrix products, arithmetic and copies ran while one was open for 9% of the time, Pallas kernels for 0%

profile of v9, /device:TPU:6, one launch (start us, length us, event | category | flops | bytes accessed | tf_op | source)
XLA Modules:
  0.0 145.6 jit_solution(13347224909147028596)
XLA Ops:
  0.6 1.1 slice_bitcast_fusion.1
  1.8 3.5 %collective-permute-start = (bf16[256,512]{1,0:T(8,128)(2,1)S(1)}, bf16[256,512]{1,0:T(8,128)(2,1)S(1)}, u32[]{:S(2)}, u32[]{:S(2)}) collective-permute-start(bf16[256,512]{1,0:T(8,128)(2,1)S(1)} %get-tuple-element.27), channel_id=1, source_target_pairs={{0,8},{8,16},{16,24},{24,32},{32,40},{40,48},{48,56},{56,64},{64,7... | collective-permute-start | bytes 786440 | tf_op jit(solution)/shard_map/ppermute | solution.py:25
  5.3 1.3 collective-permute-start.1
  8.1 2.8 %collective-permute-done = bf16[256,512]{1,0:T(8,128)(2,1)S(1)} collective-permute-done((bf16[256,512]{1,0:T(8,128)(2,1)S(1)}, bf16[256,512]{1,0:T(8,128)(2,1)S(1)}, u32[]{:S(2)}, u32[]{:S(2)}) %collective-permute-start) | collective-permute-done | bytes 262176 | tf_op jit(solution)/shard_map/ppermute | solution.py:25
  10.8 4.1 %collective-permute-done.1 = bf16[256,512]{1,0:T(8,128)(2,1)S(1)} collective-permute-done((bf16[256,512]{1,0:T(8,128)(2,1)S(1)}, bf16[256,512]{1,0:T(8,128)(2,1)S(1)}, u32[]{:S(2)}, u32[]{:S(2)}) %collective-permute-start.1) | collective-permute-done | bytes 262176 | tf_op jit(solution)/shard_map/ppermute | solution.py:26
  14.9 1.1 pad_maximum_fusion
  16.1 2.0 %gather_fusion = bf16[16,128,512]{2,1,0:T(8,128)(2,1)} fusion(bf16[8,128,512]{2,1,0:T(8,128)(2,1)S(1)} %bitcast.145, s32[1024]{0:T(1024)S(1)} %pad_clamp_fusion), kind=kCustom, calls=%fused_computation | custom fusion | bytes 4194368 | tf_op jit(solution)/shard_map/jit(_take)/gather | solution.py:80
  18.1 3.0 %fusion.17 = f32[4,128,512]{2,1,0:T(8,128)S(1)} fusion(bf16[16,128,512]{2,1,0:T(8,128)(2,1)} %gather_fusion, pred[16]{0:T(512)(128)(4,1)S(1)} %get-tuple-element.23, pred[4,16]{1,0:T(4,128)(4,1)S(1)} %iota_compare_fusion.2, bf16[16,128,128]{2,1,0:T(8,128)(2,1)S(1)} %bitcast.170), kind=kOutput, calls=%fused_computation.21 | convolution fusion | flops 1076363264 | bytes 3670096 | tf_op jit(solution)/shard_map/btij,tjf->bif/dot_general | solution.py:83
  21.4 1.9 %collective-permute-start.2 = (bf16[512,512]{1,0:T(8,128)(2,1)S(1)}, bf16[512,512]{1,0:T(8,128)(2,1)S(1)}, u32[]{:S(2)}, u32[]{:S(2)}) collective-permute-start(bf16[512,512]{1,0:T(8,128)(2,1)S(1)} %get-tuple-element.22), channel_id=1, source_target_pairs={{0,256},{256,0},{1,257},{257,1},{2,258},{258,2},{3,259},{259,3},{4... | collective-permute-start | bytes 1572872 | tf_op jit(solution)/shard_map/ppermute | solution.py:32
  23.3 2.4 %collective-permute-start.3 = (bf16[130,256]{1,0:T(8,128)(2,1)S(1)}, bf16[130,256]{1,0:T(8,128)(2,1)}, u32[]{:S(2)}, u32[]{:S(2)}) collective-permute-start(bf16[130,256]{1,0:T(8,128)(2,1)S(1)} %pad_maximum_fusion.5), channel_id=1, source_target_pairs={{0,256},{256,0},{1,257},{257,1},{2,258},{258,2},{3,259},{259,3},{4... | collective-permute-start | bytes 199688 | tf_op jit(solution)/shard_map/ppermute | solution.py:32
  25.7 2.0 %copy.22 = bf16[256,1024]{0,1:T(8,128)(2,1)} copy(bf16[256,1024]{1,0:T(8,128)(2,1)} %param.24) | data formatting | bytes 1048576 | tf_op args[10]
  27.8 1.9 %collective-permute-start.4 = (bf16[256,1024]{0,1:T(8,128)(2,1)}, bf16[256,1024]{0,1:T(8,128)(2,1)}, u32[]{:S(2)}, u32[]{:S(2)}) collective-permute-start(bf16[256,1024]{0,1:T(8,128)(2,1)} %copy.22), channel_id=1, source_target_pairs={{0,256},{256,0},{1,257},{257,1},{2,258},{258,2},{3,259},{259,3},{4... | collective-permute-start | bytes 1572872 | tf_op jit(solution)/shard_map/ppermute | solution.py:32
  29.7 2.4 %collective-permute-start.5 = (bf16[512,256]{1,0:T(8,128)(2,1)S(1)}, bf16[512,256]{1,0:T(8,128)(2,1)}, u32[]{:S(2)}, u32[]{:S(2)}) collective-permute-start(bf16[512,256]{1,0:T(8,128)(2,1)S(1)} %copy-done.8), channel_id=1, source_target_pairs={{0,256},{256,0},{1,257},{257,1},{2,258},{258,2},{3,259},{259,3},{4... | collective-permute-start | bytes 786440 | tf_op jit(solution)/shard_map/ppermute | solution.py:32
  36.3 1.4 fusion.29
  39.3 13.1 %all-to-all-start = ((f32[32,5,128]{2,1,0:T(8,128)}), f32[32,5,128]{2,1,0:T(8,128)S(1)}, u32[]{:S(2)}, u32[]{:S(2)}) async-start(f32[32,5,128]{2,1,0:T(8,128)} %reshape.361), calls=%async_computation | async-start | bytes 262144 | tf_op jit(solution)/shard_map/all_to_all | solution.py:47
  52.4 1.3 fusion.67
  53.7 9.3 %all-to-all-done = f32[32,5,128]{2,1,0:T(8,128)S(1)} async-done(((f32[32,5,128]{2,1,0:T(8,128)}), f32[32,5,128]{2,1,0:T(8,128)S(1)}, u32[]{:S(2)}, u32[]{:S(2)}) %all-to-all-start) | async-done | bytes 81952 | tf_op jit(solution)/shard_map/all_to_all | solution.py:47
  63.7 3.8 %all-to-all-start.1 = ((f32[32,5,128]{2,1,0:T(8,128)}), f32[32,5,128]{2,1,0:T(8,128)S(1)}, u32[]{:S(2)}, u32[]{:S(2)}) async-start(f32[32,5,128]{2,1,0:T(8,128)} %broadcast_in_dim.92), calls=%async_computation.1 | async-start | bytes 262144 | tf_op jit(solution)/shard_map/all_to_all | solution.py:58
  68.2 10.0 %all-to-all-done.1 = f32[32,5,128]{2,1,0:T(8,128)S(1)} async-done(((f32[32,5,128]{2,1,0:T(8,128)}), f32[32,5,128]{2,1,0:T(8,128)S(1)}, u32[]{:S(2)}, u32[]{:S(2)}) %all-to-all-start.1) | async-done | bytes 81952 | tf_op jit(solution)/shard_map/all_to_all | solution.py:58
  79.3 2.1 %collective-permute-start.6 = (f32[512,256]{0,1:T(8,128)S(1)}, f32[512,256]{0,1:T(8,128)S(1)}, u32[]{:S(2)}, u32[]{:S(2)}) collective-permute-start(f32[512,256]{0,1:T(8,128)S(1)} %bitcast.156), channel_id=1, source_target_pairs={{0,256},{256,0},{1,257},{257,1},{2,258},{258,2},{3,259},{259,3},{4... | collective-permute-start | bytes 1572872 | tf_op jit(solution)/shard_map/ppermute | solution.py:32
  81.5 0.9 broadcast_select_fusion.1
  82.3 0.8 collective-permute-done.6
  83.7 1.3 fusion.61
  85.0 1.3 fusion.22
  86.4 1.1 fusion.124
  87.5 2.6 %multiply_reduce_fusion.1 = (f32[512]{0:T(512)S(1)}, f32[512,256]{0,1:T(8,128)}) fusion(f32[512,256]{0,1:T(8,128)} %fusion.124, bf16[512,256]{1,0:T(8,128)(2,1)} %collective-permute-done.5, f32[512,512]{1,0:T(8,128)S(1)} %fusion.61, bf16[512,512]{1,0:T(8,128)(2,1)S(1)} %collective-permute-done.2, bf16[256,2,512]{0,2,1:T(8,128)(2,1)} %bitcast.39, ...), kind=kOutput, calls=%fused_computation.70 | convolution fusion | flops 270138880 | bytes 3674116 | tf_op jit(solution)/shard_map/dot_general | solution.py:196
  90.1 2.6 %fusion.43 = (f32[]{:T(128)}, f32[512,256]{0,1:T(8,128)S(1)}) fusion(s32[512]{0:T(512)S(1)} %bitcast.171, f32[512]{0:T(512)S(1)} %fusion.107, bf16[128,256]{1,0:T(8,128)(2,1)S(1)} %get-tuple-element.30, bf16[128,256]{1,0:T(8,128)(2,1)S(1)} %get-tuple-element.29, f32[512,256]{0,1:T(8,128)} %get-tuple-element.38, f32[512]{0:T(512)S(1)} %add_rsqrt_fusion), kind=kOutput, calls=%fused_computation.54 | convolution fusion | flops 404881408 | bytes 1185796 | tf_op jit(solution)/shard_map/dot_general | solution.py:109
  95.1 0.9 reshape.370
  96.0 3.9 %all-to-all-start.2 = ((f32[32,33,128]{2,1,0:T(8,128)}), f32[32,33,128]{2,1,0:T(8,128)S(1)}, u32[]{:S(2)}, u32[]{:S(2)}) async-start(f32[32,33,128]{2,1,0:T(8,128)} %reshape.370), calls=%async_computation.2 | async-start | bytes 1310720 | tf_op jit(solution)/shard_map/all_to_all | solution.py:47
  99.9 20.8 %all-to-all-done.2 = f32[32,33,128]{2,1,0:T(8,128)S(1)} async-done(((f32[32,33,128]{2,1,0:T(8,128)}), f32[32,33,128]{2,1,0:T(8,128)S(1)}, u32[]{:S(2)}, u32[]{:S(2)}) %all-to-all-start.2) | async-done | bytes 540704 | tf_op jit(solution)/shard_map/all_to_all | solution.py:47
  123.4 18.0 %all_to_all.20 = bf16[32,33,128]{2,1,0:T(8,128)(2,1)S(1)} all-to-all(bf16[32,33,128]{2,1,0:T(8,128)(2,1)S(1)} %broadcast_in_dim.96), channel_id=1, replica_groups=mesh['sec'=2,'atoms'=32,'batch'=8] {'atoms'}, dimensions={0} | all-to-all | bytes 540672 | tf_op jit(solution)/shard_map/all_to_all | solution.py:58
  142.2 0.9 broadcast_in_dim_reshape.3
  (87 shorter events, 12.9 us)
Async XLA Ops:
  0.6 34.0 %copy-start = (bf16[1024,256]{1,0:T(8,128)(2,1)S(1)}, bf16[1024,256]{1,0:T(8,128)(2,1)}, u32[]{:S(2)}) copy-start(bf16[1024,256]{1,0:T(8,128)(2,1)} %param.22) | copy-start | bytes 1572868
  1.8 9.0 %collective-permute-start = (bf16[256,512]{1,0:T(8,128)(2,1)S(1)}, bf16[256,512]{1,0:T(8,128)(2,1)S(1)}, u32[]{:S(2)}, u32[]{:S(2)}) collective-permute-start(bf16[256,512]{1,0:T(8,128)(2,1)S(1)} %get-tuple-element.27), channel_id=1, source_target_pairs={{0,8},{8,16},{16,24},{24,32},{32,40},{40,48},{48,56},{56,64},{64,7... | collective-permute-start | bytes 786440 | tf_op jit(solution)/shard_map/ppermute | solution.py:25
  5.3 9.7 %collective-permute-start.1 = (bf16[256,512]{1,0:T(8,128)(2,1)S(1)}, bf16[256,512]{1,0:T(8,128)(2,1)S(1)}, u32[]{:S(2)}, u32[]{:S(2)}) collective-permute-start(bf16[256,512]{1,0:T(8,128)(2,1)S(1)} %get-tuple-element.28), channel_id=1, source_target_pairs={{8,0},{16,8},{24,16},{32,24},{40,32},{48,40},{56,48},{64,56},{72,6... | collective-permute-start | bytes 786440 | tf_op jit(solution)/shard_map/ppermute | solution.py:26
  16.0 2.0 %copy-start.13 = (bf16[1,16,128,128]{3,2,1,0:T(8,128)(2,1)S(1)}, bf16[1,16,128,128]{3,2,1,0:T(8,128)(2,1)}, u32[]{:S(2)}) copy-start(bf16[1,16,128,128]{3,2,1,0:T(8,128)(2,1)} %param.16) | copy-start | bytes 1572868
  18.1 3.0 %copy-start.1 = (bf16[1,512,512]{2,1,0:T(8,128)(2,1)S(1)}, bf16[1,512,512]{2,1,0:T(8,128)(2,1)}, u32[]{:S(2)}) copy-start(bf16[1,512,512]{2,1,0:T(8,128)(2,1)} %param.14) | copy-start | bytes 1572868
  21.1 2.2 %copy-start.12 = (bf16[512]{0:T(512)(128)(2,1)S(1)}, bf16[512]{0:T(512)(128)(2,1)}, u32[]{:S(2)}) copy-start(bf16[512]{0:T(512)(128)(2,1)} %param.20) | copy-start | bytes 3076
  21.1 2.2 %copy-start.10 = (bf16[1,128,256]{2,1,0:T(8,128)(2,1)S(1)}, bf16[1,128,256]{2,1,0:T(8,128)(2,1)}, u32[]{:S(2)}) copy-start(bf16[1,128,256]{2,1,0:T(8,128)(2,1)} %param.19) | copy-start | bytes 196612
  21.1 8.6 %copy-start.8 = (bf16[512,256]{1,0:T(8,128)(2,1)S(1)}, bf16[512,256]{1,0:T(8,128)(2,1)}, u32[]{:S(2)}) copy-start(bf16[512,256]{1,0:T(8,128)(2,1)} %param.25) | copy-start | bytes 786436
  21.3 13.1 %copy-start.3 = (bf16[512,512]{1,0:T(8,128)(2,1)}, bf16[512,512]{1,0:T(8,128)(2,1)S(1)}, u32[]{:S(2)}) copy-start(bf16[512,512]{1,0:T(8,128)(2,1)S(1)} %get-tuple-element.22) | copy-start | bytes 1572868
  21.4 12.9 %collective-permute-start.2 = (bf16[512,512]{1,0:T(8,128)(2,1)S(1)}, bf16[512,512]{1,0:T(8,128)(2,1)S(1)}, u32[]{:S(2)}, u32[]{:S(2)}) collective-permute-start(bf16[512,512]{1,0:T(8,128)(2,1)S(1)} %get-tuple-element.22), channel_id=1, source_target_pairs={{0,256},{256,0},{1,257},{257,1},{2,258},{258,2},{3,259},{259,3},{4... | collective-permute-start | bytes 1572872 | tf_op jit(solution)/shard_map/ppermute | solution.py:32
  23.3 10.2 %collective-permute-start.3 = (bf16[130,256]{1,0:T(8,128)(2,1)S(1)}, bf16[130,256]{1,0:T(8,128)(2,1)}, u32[]{:S(2)}, u32[]{:S(2)}) collective-permute-start(bf16[130,256]{1,0:T(8,128)(2,1)S(1)} %pad_maximum_fusion.5), channel_id=1, source_target_pairs={{0,256},{256,0},{1,257},{257,1},{2,258},{258,2},{3,259},{259,3},{4... | collective-permute-start | bytes 199688 | tf_op jit(solution)/shard_map/ppermute | solution.py:32
  27.8 25.9 %collective-permute-start.4 = (bf16[256,1024]{0,1:T(8,128)(2,1)}, bf16[256,1024]{0,1:T(8,128)(2,1)}, u32[]{:S(2)}, u32[]{:S(2)}) collective-permute-start(bf16[256,1024]{0,1:T(8,128)(2,1)} %copy.22), channel_id=1, source_target_pairs={{0,256},{256,0},{1,257},{257,1},{2,258},{258,2},{3,259},{259,3},{4... | collective-permute-start | bytes 1572872 | tf_op jit(solution)/shard_map/ppermute | solution.py:32
  29.7 23.9 %collective-permute-start.5 = (bf16[512,256]{1,0:T(8,128)(2,1)S(1)}, bf16[512,256]{1,0:T(8,128)(2,1)}, u32[]{:S(2)}, u32[]{:S(2)}) collective-permute-start(bf16[512,256]{1,0:T(8,128)(2,1)S(1)} %copy-done.8), channel_id=1, source_target_pairs={{0,256},{256,0},{1,257},{257,1},{2,258},{258,2},{3,259},{259,3},{4... | collective-permute-start | bytes 786440 | tf_op jit(solution)/shard_map/ppermute | solution.py:32
  33.5 1.5 %copy-start.7 = (bf16[1024,256]{1,0:T(8,128)(2,1)S(1)}, bf16[1024,256]{1,0:T(8,128)(2,1)}, u32[]{:S(2)}) copy-start(bf16[1024,256]{1,0:T(8,128)(2,1)} %param.23) | copy-start | bytes 1572868
  38.2 29.3 %copy-start.11 = (bf16[1024,256]{1,0:T(8,128)(2,1)S(1)}, bf16[1024,256]{1,0:T(8,128)(2,1)}, u32[]{:S(2)}) copy-start(bf16[1024,256]{1,0:T(8,128)(2,1)} %param.21) | copy-start | bytes 1572868
  39.3 23.7 %all-to-all-start = ((f32[32,5,128]{2,1,0:T(8,128)}), f32[32,5,128]{2,1,0:T(8,128)S(1)}, u32[]{:S(2)}, u32[]{:S(2)}) async-start(f32[32,5,128]{2,1,0:T(8,128)} %reshape.361), calls=%async_computation | async-start | bytes 262144 | tf_op jit(solution)/shard_map/all_to_all | solution.py:47
  63.7 14.5 %all-to-all-start.1 = ((f32[32,5,128]{2,1,0:T(8,128)}), f32[32,5,128]{2,1,0:T(8,128)S(1)}, u32[]{:S(2)}, u32[]{:S(2)}) async-start(f32[32,5,128]{2,1,0:T(8,128)} %broadcast_in_dim.92), calls=%async_computation.1 | async-start | bytes 262144 | tf_op jit(solution)/shard_map/all_to_all | solution.py:58
  78.3 5.0 %copy-start.6 = (bf16[256,1024]{0,1:T(8,128)(2,1)S(1)}, bf16[256,1024]{0,1:T(8,128)(2,1)}, u32[]{:S(2)}) copy-start(bf16[256,1024]{0,1:T(8,128)(2,1)} %copy.22) | copy-start | bytes 1572868
  79.3 3.8 %collective-permute-start.6 = (f32[512,256]{0,1:T(8,128)S(1)}, f32[512,256]{0,1:T(8,128)S(1)}, u32[]{:S(2)}, u32[]{:S(2)}) collective-permute-start(f32[512,256]{0,1:T(8,128)S(1)} %bitcast.156), channel_id=1, source_target_pairs={{0,256},{256,0},{1,257},{257,1},{2,258},{258,2},{3,259},{259,3},{4... | collective-permute-start | bytes 1572872 | tf_op jit(solution)/shard_map/ppermute | solution.py:32
  83.2 1.8 %copy-start.4 = (bf16[512,512]{1,0:T(8,128)(2,1)S(1)}, bf16[512,512]{1,0:T(8,128)(2,1)}, u32[]{:S(2)}) copy-start(bf16[512,512]{1,0:T(8,128)(2,1)} %copy-done.3) | copy-start | bytes 1572868
  83.6 2.7 %copy-start.9 = (bf16[512,256]{1,0:T(8,128)(2,1)S(1)}, bf16[512,256]{1,0:T(8,128)(2,1)}, u32[]{:S(2)}) copy-start(bf16[512,256]{1,0:T(8,128)(2,1)} %param.25) | copy-start | bytes 786436
  86.3 7.1 %copy-start.2 = (bf16[512,512]{1,0:T(8,128)(2,1)}, bf16[512,512]{1,0:T(8,128)(2,1)S(1)}, u32[]{:S(2)}) copy-start(bf16[512,512]{1,0:T(8,128)(2,1)S(1)} %fusion.22) | copy-start | bytes 1572868
  87.5 2.6 %copy-start.14 = (s32[1,512]{1,0:T(1,128)S(1)}, s32[1,512]{1,0:T(1,128)}, u32[]{:S(2)}) copy-start(s32[1,512]{1,0:T(1,128)} %param.18) | copy-start | bytes 6148
  90.1 2.6 %copy-start.5 = (f32[512,256]{0,1:T(8,128)S(1)}, f32[512,256]{0,1:T(8,128)}, u32[]{:S(2)}) copy-start(f32[512,256]{0,1:T(8,128)} %get-tuple-element.38) | copy-start | bytes 1572868
  96.0 24.7 %all-to-all-start.2 = ((f32[32,33,128]{2,1,0:T(8,128)}), f32[32,33,128]{2,1,0:T(8,128)S(1)}, u32[]{:S(2)}, u32[]{:S(2)}) async-start(f32[32,33,128]{2,1,0:T(8,128)} %reshape.370), calls=%async_computation.2 | async-start | bytes 1310720 | tf_op jit(solution)/shard_map/all_to_all | solution.py:47

commit v10 on v8

--- a/solution.py
+++ b/solution.py
@@ -141,22 +141,28 @@
 ):
     atom_rows = atoms_in[0]
     local_rows = atom_rows.shape[0]
+    sec = lax.axis_index("sec")
+    peak_part = peak_embed[0]
+    peak_count, embed_width = peak_part.shape
+    early = swap_sec(jnp.concatenate([peak_part, norm_gain.reshape(-1, embed_width)], axis=0))
+    peak_other, gain_other = early[:peak_count], early[peak_count:].reshape(-1)
     gathered = message_pass(atom_rows, tile_ids[0], tile_vals[0])
     hidden_one = (atom_rows.astype(jnp.float32) + gathered.astype(jnp.float32)).astype(jnp.bfloat16)
     atom_base = lax.axis_index("atoms") * local_rows
     length_one = seq_lens[0]
     label_row = pair_labels[0]
-    peak_part = peak_embed[0]
     hidden_f = hidden_one.astype(jnp.float32)
-    square_sum = lax.psum(jnp.sum(hidden_f * hidden_f, axis=-1), "sec")
-    row_scale = lax.rsqrt(square_sum[:, None] / D + EPSILON)
+    other_f = swap_sec(hidden_one).astype(jnp.float32)
+    square_sum = jnp.sum(hidden_f * hidden_f, axis=-1, keepdims=True) + jnp.sum(
+        other_f * other_f, axis=-1, keepdims=True
+    )
+    row_scale = lax.rsqrt(square_sum / D + EPSILON)
     normed = (hidden_f * row_scale * norm_gain.astype(jnp.float32)).astype(jnp.bfloat16)
+    other_rows = (other_f * row_scale * gain_other.astype(jnp.float32)).astype(jnp.bfloat16)
     head_cols = w_query.shape[1]
-    sec = lax.axis_index("sec")
     width = normed.shape[1]
-    other_rows = swap_sec(normed)
     out_cols = w_out.reshape(w_out.shape[0], 2, width)
-    partner = (swap_sec(peak_part), swap_sec(out_cols[:, 1 - sec, :]))
+    partner = swap_sec(out_cols[:, 1 - sec, :])
 
     def project(weight):
         halves = weight.reshape(2, width, weight.shape[1])
@@ -173,8 +179,8 @@
     )
     state_rows = jnp.concatenate([outer_state, key_total[:, None, :]], axis=1)
     packed, partner = sum_atoms(state_rows, riders=partner)
-    peak_all = join_sec(peak_part, partner[0], sec, 0)
-    out_rows = join_sec(out_cols[:, sec, :], partner[1], sec, 0)
+    peak_all = join_sec(peak_part, peak_other, sec, 0)
+    out_rows = join_sec(out_cols[:, sec, :], partner, sec, 0)
     outer_state, key_total = packed[:, :HEAD_DIM, :], packed[:, HEAD_DIM, :]
     attended = read_summary(query_f.astype(jnp.bfloat16), outer_state, key_total, head_count)
     attended_all = join_sec(attended, swap_sec(attended), sec, 1)

time: 138 us -> 146 us (1.058)
  other arithmetic: 3.22 us -> 7.06 us
  waiting for transfers between devices: 44.8 us -> 48.4 us
  matrix products: 11.4 us -> 14.6 us
  blocking collectives: 20.5 us -> 18 us
    ppermute x1, waiting for transfers between devices: 1.09 us -> 4.13 us  [extended(): after = lax.ppermute(leading, axis, down)]
    psum x1 -> x0, blocking collectives: 2.46 us -> none  [shards(): square_sum = lax.psum(jnp.sum(hidden_f * hidden_f, axis=-1), 'sec')]
    ppermute x1, waiting for transfers between devices: 0.01 us -> 2.06 us  [extended(): before = lax.ppermute(last, axis, up)]
    dynamic_slice x3, local copies, waits for them, and re-layouts: 1.03 us -> 2.67 us  [the longest x1 1.79 us: shards(): partner = swap_sec(out_cols[:, 1 - sec, :])]
where the time goes in v10:
time: 146 us; the launch traced here: 144 us
  waiting for transfers between devices  48.4 us (33%)
  starting transfers between devices  35.9 us (25%)
  blocking collectives  18 us (12%)
  matrix products  14.6 us (10%)
  local copies, waits for them, and re-layouts  13.6 us (9%)
  other arithmetic  7.06 us (5%)
  between operations  6.85 us (5%)
    all_to_all x2, waiting for transfers between devices, sum_atoms(): arrived = lax.all_to_all(pieces, 'atoms', 0, 0, tiled=True)  31.5 us
    all_to_all x1, blocking collectives, sum_atoms(): lax.all_to_all(jnp.broadcast_to(owned, pieces.shape), 'atoms', 0, 0, tile...  18 us
    all_to_all x2, starting transfers between devices, sum_atoms(): arrived = lax.all_to_all(pieces, 'atoms', 0, 0, tiled=True)  17 us
    ppermute x5, starting transfers between devices, swap_sec(): return lax.ppermute(x, 'sec', [(0, 1), (1, 0)])  10.2 us
    all_to_all x1, waiting for transfers between devices, sum_atoms(): lax.all_to_all(jnp.broadcast_to(owned, pieces.shape), 'atoms', 0, 0, tile...  9.08 us
    ppermute x1, waiting for transfers between devices, extended(): after = lax.ppermute(leading, axis, down)  4.13 us
    all_to_all x1, starting transfers between devices, sum_atoms(): lax.all_to_all(jnp.broadcast_to(owned, pieces.shape), 'atoms', 0, 0, tile...  3.86 us
    dot_general x3, matrix products, project(): jnp.dot(other_rows, halves[1 - sec], preferred_element_type=jnp.float32)  3.75 us
  transfers between devices with their start and end apart: 10, of which 7 were waited for; matrix products, arithmetic and copies ran while one was open for 11% of the time, Pallas kernels for 0%

profile of v10, /device:TPU:6, one launch (start us, length us, event | category | flops | bytes accessed | tf_op | source)
XLA Modules:
  0.0 144.4 jit_solution(6248468862597538339)
XLA Ops:
  0.6 1.1 slice_bitcast_fusion.1
  1.8 3.5 %collective-permute-start = (bf16[256,512]{1,0:T(8,128)(2,1)S(1)}, bf16[256,512]{1,0:T(8,128)(2,1)S(1)}, u32[]{:S(2)}, u32[]{:S(2)}) collective-permute-start(bf16[256,512]{1,0:T(8,128)(2,1)S(1)} %get-tuple-element.33), channel_id=1, source_target_pairs={{0,8},{8,16},{16,24},{24,32},{32,40},{40,48},{48,56},{56,64},{64,7... | collective-permute-start | bytes 786440 | tf_op jit(solution)/shard_map/ppermute | solution.py:25
  5.3 1.3 collective-permute-start.1
  8.7 2.1 %collective-permute-done = bf16[256,512]{1,0:T(8,128)(2,1)S(1)} collective-permute-done((bf16[256,512]{1,0:T(8,128)(2,1)S(1)}, bf16[256,512]{1,0:T(8,128)(2,1)S(1)}, u32[]{:S(2)}, u32[]{:S(2)}) %collective-permute-start) | collective-permute-done | bytes 262176 | tf_op jit(solution)/shard_map/ppermute | solution.py:25
  10.8 4.1 %collective-permute-done.1 = bf16[256,512]{1,0:T(8,128)(2,1)S(1)} collective-permute-done((bf16[256,512]{1,0:T(8,128)(2,1)S(1)}, bf16[256,512]{1,0:T(8,128)(2,1)S(1)}, u32[]{:S(2)}, u32[]{:S(2)}) %collective-permute-start.1) | collective-permute-done | bytes 262176 | tf_op jit(solution)/shard_map/ppermute | solution.py:26
  14.9 1.1 pad_maximum_fusion
  16.1 2.0 %gather_fusion = bf16[16,128,512]{2,1,0:T(8,128)(2,1)} fusion(bf16[8,128,512]{2,1,0:T(8,128)(2,1)S(1)} %bitcast.127, s32[1024]{0:T(1024)S(1)} %pad_clamp_fusion), kind=kCustom, calls=%fused_computation | custom fusion | bytes 4194368 | tf_op jit(solution)/shard_map/jit(_take)/gather | solution.py:84
  18.1 3.0 %fusion.16 = f32[4,128,512]{2,1,0:T(8,128)S(1)} fusion(bf16[16,128,512]{2,1,0:T(8,128)(2,1)} %gather_fusion, pred[16]{0:T(512)(128)(4,1)S(1)} %get-tuple-element.23, pred[4,16]{1,0:T(4,128)(4,1)S(1)} %iota_compare_fusion.2, bf16[16,128,128]{2,1,0:T(8,128)(2,1)S(1)} %bitcast.149), kind=kOutput, calls=%fused_computation.18 | convolution fusion | flops 1076363264 | bytes 3670096 | tf_op jit(solution)/shard_map/btij,tjf->bif/dot_general | solution.py:87
  21.1 0.9 fusion.28
  22.1 1.9 %collective-permute-start.2 = (bf16[512,512]{1,0:T(8,128)(2,1)}, bf16[512,512]{1,0:T(8,128)(2,1)S(1)}, u32[]{:S(2)}, u32[]{:S(2)}) collective-permute-start(bf16[512,512]{1,0:T(8,128)(2,1)} %get-tuple-element.22), channel_id=1, source_target_pairs={{0,256},{256,0},{1,257},{257,1},{2,258},{258,2},{3,259},{259,3},{4... | collective-permute-start | bytes 1572872 | tf_op jit(solution)/shard_map/ppermute | solution.py:32
  24.0 2.4 %collective-permute-start.3 = (bf16[130,256]{1,0:T(8,128)(2,1)S(1)}, bf16[130,256]{1,0:T(8,128)(2,1)}, u32[]{:S(2)}, u32[]{:S(2)}) collective-permute-start(bf16[130,256]{1,0:T(8,128)(2,1)S(1)} %pad_maximum_fusion.6), channel_id=1, source_target_pairs={{0,256},{256,0},{1,257},{257,1},{2,258},{258,2},{3,259},{259,3},{4... | collective-permute-start | bytes 199688 | tf_op jit(solution)/shard_map/ppermute | solution.py:32
  26.4 1.2 copy.22
  28.4 1.8 %copy.23 = bf16[256,1,512]{2,0,1:T(8,128)(2,1)} copy(bf16[256,1,512]{0,2,1:T(8,128)(2,1)} %get-tuple-element.32) | data formatting | bytes 524288 | tf_op jit(solution)/shard_map/dynamic_slice | solution.py:165
  30.2 1.9 %collective-permute-start.4 = (bf16[256,512]{1,0:T(8,128)(2,1)}, bf16[256,512]{1,0:T(8,128)(2,1)}, u32[]{:S(2)}, u32[]{:S(2)}) collective-permute-start(bf16[256,512]{1,0:T(8,128)(2,1)} %bitcast.26), channel_id=1, source_target_pairs={{0,256},{256,0},{1,257},{257,1},{2,258},{258,2},{3,259},{259,3},{4... | collective-permute-start | bytes 786440 | tf_op jit(solution)/shard_map/ppermute | solution.py:32
  34.3 1.3 fusion.63
  36.5 1.4 fusion.25
  39.4 13.1 %all-to-all-start = ((f32[32,5,128]{2,1,0:T(8,128)}), f32[32,5,128]{2,1,0:T(8,128)S(1)}, u32[]{:S(2)}, u32[]{:S(2)}) async-start(f32[32,5,128]{2,1,0:T(8,128)} %reshape.342), calls=%async_computation | async-start | bytes 262144 | tf_op jit(solution)/shard_map/all_to_all | solution.py:51
  52.9 10.8 %all-to-all-done = f32[32,5,128]{2,1,0:T(8,128)S(1)} async-done(((f32[32,5,128]{2,1,0:T(8,128)}), f32[32,5,128]{2,1,0:T(8,128)S(1)}, u32[]{:S(2)}, u32[]{:S(2)}) %all-to-all-start) | async-done | bytes 81952 | tf_op jit(solution)/shard_map/all_to_all | solution.py:51
  64.4 3.9 %all-to-all-start.1 = ((f32[32,5,128]{2,1,0:T(8,128)}), f32[32,5,128]{2,1,0:T(8,128)S(1)}, u32[]{:S(2)}, u32[]{:S(2)}) async-start(f32[32,5,128]{2,1,0:T(8,128)} %broadcast_in_dim.91), calls=%async_computation.1 | async-start | bytes 262144 | tf_op jit(solution)/shard_map/all_to_all | solution.py:62
  68.3 1.6 %fusion.43 = f32[512,256]{0,1:T(8,128)S(1)} fusion(f32[512,256]{0,1:T(8,128)S(1)} %fusion.60, bf16[2,512,256]{2,1,0:T(8,128)(2,1)} %bitcast.141, s32[]{:T(128)S(6)} %select_n.136, bf16[512,512]{1,0:T(8,128)(2,1)S(1)} %collective-permute-done.2, f32[512]{0:T(512)S(1)} %bitcast.147, f32[512]{0:T(512)S(1)} %add_rsqrt_fusion.2), kind=kOutput, calls=%fused_computation.55 | convolution fusion | flops 136183808 | bytes 1839108 | tf_op jit(solution)/shard_map/dot_general | solution.py:170
  69.9 9.1 %all-to-all-done.1 = f32[32,5,128]{2,1,0:T(8,128)S(1)} async-done(((f32[32,5,128]{2,1,0:T(8,128)}), f32[32,5,128]{2,1,0:T(8,128)S(1)}, u32[]{:S(2)}, u32[]{:S(2)}) %all-to-all-start.1) | async-done | bytes 81952 | tf_op jit(solution)/shard_map/all_to_all | solution.py:62
  80.1 1.9 %collective-permute-start.5 = (f32[512,256]{0,1:T(8,128)S(1)}, f32[512,256]{0,1:T(8,128)S(1)}, u32[]{:S(2)}, u32[]{:S(2)}) collective-permute-start(f32[512,256]{0,1:T(8,128)S(1)} %bitcast.134), channel_id=1, source_target_pairs={{0,256},{256,0},{1,257},{257,1},{2,258},{258,2},{3,259},{259,3},{4... | collective-permute-start | bytes 1572872 | tf_op jit(solution)/shard_map/ppermute | solution.py:32
  82.1 1.0 bitcast_select_fusion.1
  84.1 1.5 %fusion.21 = bf16[512,512]{1,0:T(8,128)(2,1)S(1)} fusion(bf16[512,512]{1,0:T(8,128)(2,1)} %get-tuple-element.22, f32[512,256]{0,1:T(8,128)S(1)} %get-tuple-element.26, f32[512,256]{0,1:T(8,128)S(1)} %get-tuple-element.25, bf16[256,512]{1,0:T(8,128)(2,1)S(1)} %get-tuple-element.30, bf16[256,512]{1,0:T(8,128)(2,1)S(1)} %get-tuple-element.29, ...), kind=kOutput, calls=%fused_computation.19 | convolution fusion | flops 271056896 | bytes 2623488 | tf_op jit(solution)/shard_map/dot_general | solution.py:191
  86.0 2.0 %collective-permute-start.6 = (f32[512,256]{0,1:T(8,128)S(1)}, f32[512,256]{0,1:T(8,128)S(1)}, u32[]{:S(2)}, u32[]{:S(2)}) collective-permute-start(f32[512,256]{0,1:T(8,128)S(1)} %fusion.107), channel_id=1, source_target_pairs={{0,256},{256,0},{1,257},{257,1},{2,258},{258,2},{3,259},{259,3},{4... | collective-permute-start | bytes 1572872 | tf_op jit(solution)/shard_map/ppermute | solution.py:32
  89.0 0.9 collective-permute-done.6
  90.0 1.5 %fusion.39 = (f32[]{:T(128)}, f32[512,256]{0,1:T(8,128)S(1)}) fusion(s32[512]{0:T(512)S(1)} %bitcast.150, f32[512]{0:T(512)S(1)} %fusion.90, bf16[128,256]{1,0:T(8,128)(2,1)S(1)} %get-tuple-element.36, bf16[128,256]{1,0:T(8,128)(2,1)S(1)} %get-tuple-element.35, f32[512,256]{0,1:T(8,128)S(1)} %get-tuple-element.20, f32[512]{0:T(512)S(1)} %add_rsqrt_fusion), kind=kOutput, calls=%fused_computation.51 | convolution fusion | flops 404881408 | bytes 1185796 | tf_op jit(solution)/shard_map/dot_general | solution.py:113
  93.8 0.9 reshape.350
  94.7 3.9 %all-to-all-start.2 = ((f32[32,33,128]{2,1,0:T(8,128)}), f32[32,33,128]{2,1,0:T(8,128)S(1)}, u32[]{:S(2)}, u32[]{:S(2)}) async-start(f32[32,33,128]{2,1,0:T(8,128)} %reshape.350), calls=%async_computation.2 | async-start | bytes 1310720 | tf_op jit(solution)/shard_map/all_to_all | solution.py:51
  98.6 20.8 %all-to-all-done.2 = f32[32,33,128]{2,1,0:T(8,128)S(1)} async-done(((f32[32,33,128]{2,1,0:T(8,128)}), f32[32,33,128]{2,1,0:T(8,128)S(1)}, u32[]{:S(2)}, u32[]{:S(2)}) %all-to-all-start.2) | async-done | bytes 540704 | tf_op jit(solution)/shard_map/all_to_all | solution.py:51
  122.2 18.0 %all_to_all.20 = bf16[32,33,128]{2,1,0:T(8,128)(2,1)S(1)} all-to-all(bf16[32,33,128]{2,1,0:T(8,128)(2,1)S(1)} %broadcast_in_dim.95), channel_id=1, replica_groups=mesh['sec'=2,'atoms'=32,'batch'=8] {'atoms'}, dimensions={0} | all-to-all | bytes 540672 | tf_op jit(solution)/shard_map/all_to_all | solution.py:62
  141.0 0.9 broadcast_in_dim_reshape.3
  (77 shorter events, 14.7 us)
Async XLA Ops:
  0.6 33.3 %copy-start = (bf16[1024,256]{1,0:T(8,128)(2,1)S(1)}, bf16[1024,256]{1,0:T(8,128)(2,1)}, u32[]{:S(2)}) copy-start(bf16[1024,256]{1,0:T(8,128)(2,1)} %param.22) | copy-start | bytes 1572868
  1.8 9.0 %collective-permute-start = (bf16[256,512]{1,0:T(8,128)(2,1)S(1)}, bf16[256,512]{1,0:T(8,128)(2,1)S(1)}, u32[]{:S(2)}, u32[]{:S(2)}) collective-permute-start(bf16[256,512]{1,0:T(8,128)(2,1)S(1)} %get-tuple-element.33), channel_id=1, source_target_pairs={{0,8},{8,16},{16,24},{24,32},{32,40},{40,48},{48,56},{56,64},{64,7... | collective-permute-start | bytes 786440 | tf_op jit(solution)/shard_map/ppermute | solution.py:25
  5.3 9.7 %collective-permute-start.1 = (bf16[256,512]{1,0:T(8,128)(2,1)S(1)}, bf16[256,512]{1,0:T(8,128)(2,1)S(1)}, u32[]{:S(2)}, u32[]{:S(2)}) collective-permute-start(bf16[256,512]{1,0:T(8,128)(2,1)S(1)} %get-tuple-element.34), channel_id=1, source_target_pairs={{8,0},{16,8},{24,16},{32,24},{40,32},{48,40},{56,48},{64,56},{72,6... | collective-permute-start | bytes 786440 | tf_op jit(solution)/shard_map/ppermute | solution.py:26
  16.0 2.0 %copy-start.7 = (bf16[1,16,128,128]{3,2,1,0:T(8,128)(2,1)S(1)}, bf16[1,16,128,128]{3,2,1,0:T(8,128)(2,1)}, u32[]{:S(2)}) copy-start(bf16[1,16,128,128]{3,2,1,0:T(8,128)(2,1)} %param.16) | copy-start | bytes 1572868
  18.1 3.0 %copy-start.1 = (bf16[1,512,512]{2,1,0:T(8,128)(2,1)S(1)}, bf16[1,512,512]{2,1,0:T(8,128)(2,1)}, u32[]{:S(2)}) copy-start(bf16[1,512,512]{2,1,0:T(8,128)(2,1)} %param.14) | copy-start | bytes 1572868
  21.1 2.9 %copy-start.4 = (bf16[1,128,256]{2,1,0:T(8,128)(2,1)S(1)}, bf16[1,128,256]{2,1,0:T(8,128)(2,1)}, u32[]{:S(2)}) copy-start(bf16[1,128,256]{2,1,0:T(8,128)(2,1)} %param.19) | copy-start | bytes 196612
  21.1 11.0 %copy-start.6 = (bf16[512]{0:T(512)(128)(2,1)S(1)}, bf16[512]{0:T(512)(128)(2,1)}, u32[]{:S(2)}) copy-start(bf16[512]{0:T(512)(128)(2,1)} %param.20) | copy-start | bytes 3076
  22.1 11.5 %collective-permute-start.2 = (bf16[512,512]{1,0:T(8,128)(2,1)}, bf16[512,512]{1,0:T(8,128)(2,1)S(1)}, u32[]{:S(2)}, u32[]{:S(2)}) collective-permute-start(bf16[512,512]{1,0:T(8,128)(2,1)} %get-tuple-element.22), channel_id=1, source_target_pairs={{0,256},{256,0},{1,257},{257,1},{2,258},{258,2},{3,259},{259,3},{4... | collective-permute-start | bytes 1572872 | tf_op jit(solution)/shard_map/ppermute | solution.py:32
  24.0 8.8 %collective-permute-start.3 = (bf16[130,256]{1,0:T(8,128)(2,1)S(1)}, bf16[130,256]{1,0:T(8,128)(2,1)}, u32[]{:S(2)}, u32[]{:S(2)}) collective-permute-start(bf16[130,256]{1,0:T(8,128)(2,1)S(1)} %pad_maximum_fusion.6), channel_id=1, source_target_pairs={{0,256},{256,0},{1,257},{257,1},{2,258},{258,2},{3,259},{259,3},{4... | collective-permute-start | bytes 199688 | tf_op jit(solution)/shard_map/ppermute | solution.py:32
  30.2 22.7 %collective-permute-start.4 = (bf16[256,512]{1,0:T(8,128)(2,1)}, bf16[256,512]{1,0:T(8,128)(2,1)}, u32[]{:S(2)}, u32[]{:S(2)}) collective-permute-start(bf16[256,512]{1,0:T(8,128)(2,1)} %bitcast.26), channel_id=1, source_target_pairs={{0,256},{256,0},{1,257},{257,1},{2,258},{258,2},{3,259},{259,3},{4... | collective-permute-start | bytes 786440 | tf_op jit(solution)/shard_map/ppermute | solution.py:32
  38.0 14.6 %copy-start.5 = (bf16[1024,256]{1,0:T(8,128)(2,1)S(1)}, bf16[1024,256]{1,0:T(8,128)(2,1)}, u32[]{:S(2)}) copy-start(bf16[1024,256]{1,0:T(8,128)(2,1)} %param.21) | copy-start | bytes 1572868
  39.4 24.3 %all-to-all-start = ((f32[32,5,128]{2,1,0:T(8,128)}), f32[32,5,128]{2,1,0:T(8,128)S(1)}, u32[]{:S(2)}, u32[]{:S(2)}) async-start(f32[32,5,128]{2,1,0:T(8,128)} %reshape.342), calls=%async_computation | async-start | bytes 262144 | tf_op jit(solution)/shard_map/all_to_all | solution.py:51
  64.4 14.5 %all-to-all-start.1 = ((f32[32,5,128]{2,1,0:T(8,128)}), f32[32,5,128]{2,1,0:T(8,128)S(1)}, u32[]{:S(2)}, u32[]{:S(2)}) async-start(f32[32,5,128]{2,1,0:T(8,128)} %broadcast_in_dim.91), calls=%async_computation.1 | async-start | bytes 262144 | tf_op jit(solution)/shard_map/all_to_all | solution.py:62
  80.1 3.8 %collective-permute-start.5 = (f32[512,256]{0,1:T(8,128)S(1)}, f32[512,256]{0,1:T(8,128)S(1)}, u32[]{:S(2)}, u32[]{:S(2)}) collective-permute-start(f32[512,256]{0,1:T(8,128)S(1)} %bitcast.134), channel_id=1, source_target_pairs={{0,256},{256,0},{1,257},{257,1},{2,258},{258,2},{3,259},{259,3},{4... | collective-permute-start | bytes 1572872 | tf_op jit(solution)/shard_map/ppermute | solution.py:32
  84.0 1.7 %copy-start.3 = (bf16[512,256]{1,0:T(8,128)(2,1)S(1)}, bf16[512,256]{1,0:T(8,128)(2,1)}, u32[]{:S(2)}) copy-start(bf16[512,256]{1,0:T(8,128)(2,1)} %param.25) | copy-start | bytes 786436
  85.7 6.5 %copy-start.2 = (bf16[512,512]{1,0:T(8,128)(2,1)}, bf16[512,512]{1,0:T(8,128)(2,1)S(1)}, u32[]{:S(2)}) copy-start(bf16[512,512]{1,0:T(8,128)(2,1)S(1)} %fusion.21) | copy-start | bytes 1572868
  85.7 4.3 %copy-start.8 = (s32[1,512]{1,0:T(1,128)S(1)}, s32[1,512]{1,0:T(1,128)}, u32[]{:S(2)}) copy-start(s32[1,512]{1,0:T(1,128)} %param.18) | copy-start | bytes 6148
  86.0 3.8 %collective-permute-start.6 = (f32[512,256]{0,1:T(8,128)S(1)}, f32[512,256]{0,1:T(8,128)S(1)}, u32[]{:S(2)}, u32[]{:S(2)}) collective-permute-start(f32[512,256]{0,1:T(8,128)S(1)} %fusion.107), channel_id=1, source_target_pairs={{0,256},{256,0},{1,257},{257,1},{2,258},{258,2},{3,259},{259,3},{4... | collective-permute-start | bytes 1572872 | tf_op jit(solution)/shard_map/ppermute | solution.py:32
  94.7 24.7 %all-to-all-start.2 = ((f32[32,33,128]{2,1,0:T(8,128)}), f32[32,33,128]{2,1,0:T(8,128)S(1)}, u32[]{:S(2)}, u32[]{:S(2)}) async-start(f32[32,33,128]{2,1,0:T(8,128)} %reshape.350), calls=%async_computation.2 | async-start | bytes 1310720 | tf_op jit(solution)/shard_map/all_to_all | solution.py:51

commit v11 on v8

--- a/solution.py
+++ b/solution.py
@@ -174,15 +174,18 @@
     state_rows = jnp.concatenate([outer_state, key_total[:, None, :]], axis=1)
     packed, partner = sum_atoms(state_rows, riders=partner)
     peak_all = join_sec(peak_part, partner[0], sec, 0)
-    out_rows = join_sec(out_cols[:, sec, :], partner[1], sec, 0)
     outer_state, key_total = packed[:, :HEAD_DIM, :], packed[:, HEAD_DIM, :]
     attended = read_summary(query_f.astype(jnp.bfloat16), outer_state, key_total, head_count)
-    attended_all = join_sec(attended, swap_sec(attended), sec, 1)
-    out_sum = jnp.sum(attended_all * attended_all, axis=-1)
-    attended_n = (attended_all * lax.rsqrt(out_sum[:, None] / (HEADS * HEAD_DIM) + EPSILON)).astype(
-        jnp.bfloat16
-    )
-    branch = jnp.dot(attended_n, out_rows, preferred_element_type=jnp.float32)
+    attended_other = swap_sec(attended)
+    out_sum = jnp.sum(attended * attended, axis=-1, keepdims=True) + jnp.sum(
+        attended_other * attended_other, axis=-1, keepdims=True
+    )
+    out_scale = lax.rsqrt(out_sum / (HEADS * HEAD_DIM) + EPSILON)
+    branch = jnp.dot(
+        (attended * out_scale).astype(jnp.bfloat16), out_cols[:, sec, :], preferred_element_type=jnp.float32
+    ) + jnp.dot(
+        (attended_other * out_scale).astype(jnp.bfloat16), partner[1], preferred_element_type=jnp.float32
+    )
     hidden_two = (hidden_f + branch).astype(jnp.bfloat16)
     embedded = sum_sec(jnp.dot(hidden_two, w_proj, preferred_element_type=jnp.float32))
     embed_scale = lax.rsqrt(jnp.mean(embedded * embedded, axis=-1, keepdims=True) + EPSILON)

time: 138 us -> 138 us (level)
  transfers between devices with their start and end apart: 10 -> 10, of which waited for: 7 -> 7; matrix products, arithmetic and copies ran while one was open for 11% -> 10% of each run, Pallas kernels for 0% -> 0%
where the time goes in v11:
time: 138 us; the launch traced here: 136 us
  waiting for transfers between devices  46 us (33%)
  starting transfers between devices  37 us (27%)
  blocking collectives  20.5 us (15%)
  local copies, waits for them, and re-layouts  12.2 us (9%)
  matrix products  11.7 us (8%)
  between operations  6.91 us (5%)
  other arithmetic  2.11 us (2%)
    all_to_all x2, waiting for transfers between devices, sum_atoms(): arrived = lax.all_to_all(pieces, 'atoms', 0, 0, tiled=True)  31.3 us
    all_to_all x2, starting transfers between devices, sum_atoms(): arrived = lax.all_to_all(pieces, 'atoms', 0, 0, tiled=True)  18 us
    all_to_all x1, blocking collectives, sum_atoms(): lax.all_to_all(jnp.broadcast_to(owned, pieces.shape), 'atoms', 0, 0, tile...  18 us
    ppermute x5, starting transfers between devices, swap_sec(): return lax.ppermute(x, 'sec', [(0, 1), (1, 0)])  10.4 us
    all_to_all x1, waiting for transfers between devices, sum_atoms(): lax.all_to_all(jnp.broadcast_to(owned, pieces.shape), 'atoms', 0, 0, tile...  10.1 us
    all_to_all x1, starting transfers between devices, sum_atoms(): lax.all_to_all(jnp.broadcast_to(owned, pieces.shape), 'atoms', 0, 0, tile...  3.86 us
    ppermute x5, waiting for transfers between devices, swap_sec(): return lax.ppermute(x, 'sec', [(0, 1), (1, 0)])  3.52 us
    ppermute x1, starting transfers between devices, extended(): before = lax.ppermute(last, axis, up)  3.5 us
  transfers between devices with their start and end apart: 10, of which 7 were waited for; matrix products, arithmetic and copies ran while one was open for 10% of the time, Pallas kernels for 0%

profile of v11, /device:TPU:6, one launch (start us, length us, event | category | flops | bytes accessed | tf_op | source)
XLA Modules:
  0.0 136.4 jit_solution(7461391623598156733)
XLA Ops:
  0.7 1.1 slice_bitcast_fusion.1
  1.8 3.5 %collective-permute-start = (bf16[256,512]{1,0:T(8,128)(2,1)S(1)}, bf16[256,512]{1,0:T(8,128)(2,1)S(1)}, u32[]{:S(2)}, u32[]{:S(2)}) collective-permute-start(bf16[256,512]{1,0:T(8,128)(2,1)S(1)} %get-tuple-element.29), channel_id=1, source_target_pairs={{0,8},{8,16},{16,24},{24,32},{32,40},{40,48},{48,56},{56,64},{64,7... | collective-permute-start | bytes 786440 | tf_op jit(solution)/shard_map/ppermute | solution.py:25
  5.3 1.3 collective-permute-start.1
  6.6 1.2 copy.22
  7.9 0.8 copy.23
  8.8 1.9 %collective-permute-start.4 = (bf16[256,512]{1,0:T(8,128)(2,1)}, bf16[256,512]{1,0:T(8,128)(2,1)S(1)}, u32[]{:S(2)}, u32[]{:S(2)}) collective-permute-start(bf16[256,512]{1,0:T(8,128)(2,1)} %bitcast.26), channel_id=1, source_target_pairs={{0,256},{256,0},{1,257},{257,1},{2,258},{258,2},{3,259},{259,3},{4... | collective-permute-start | bytes 786440 | tf_op jit(solution)/shard_map/ppermute | solution.py:32
  10.7 2.4 %collective-permute-start.3 = (bf16[128,256]{1,0:T(8,128)(2,1)}, bf16[128,256]{1,0:T(8,128)(2,1)}, u32[]{:S(2)}, u32[]{:S(2)}) collective-permute-start(bf16[128,256]{1,0:T(8,128)(2,1)} %bitcast.24), channel_id=1, source_target_pairs={{0,256},{256,0},{1,257},{257,1},{2,258},{258,2},{3,259},{259,3},{4... | collective-permute-start | bytes 196616 | tf_op jit(solution)/shard_map/ppermute | solution.py:32
  13.9 1.1 collective-permute-done.1
  15.1 2.0 %gather_fusion = bf16[16,128,512]{2,1,0:T(8,128)(2,1)} fusion(bf16[8,128,512]{2,1,0:T(8,128)(2,1)S(1)} %bitcast.129, s32[1024]{0:T(1024)S(1)} %pad_clamp_fusion), kind=kCustom, calls=%fused_computation | custom fusion | bytes 4194368 | tf_op jit(solution)/shard_map/jit(_take)/gather | solution.py:84
  17.1 3.1 %fusion.16 = f32[4,128,512]{2,1,0:T(8,128)S(1)} fusion(bf16[16,128,512]{2,1,0:T(8,128)(2,1)} %gather_fusion, pred[16]{0:T(512)(128)(4,1)S(1)} %get-tuple-element.25, pred[4,16]{1,0:T(4,128)(4,1)S(1)} %iota_compare_fusion.2, bf16[16,128,128]{2,1,0:T(8,128)(2,1)} %bitcast.149), kind=kOutput, calls=%fused_computation.18 | convolution fusion | flops 1076363264 | bytes 3670096 | tf_op jit(solution)/shard_map/btij,tjf->bif/dot_general | solution.py:87
  20.4 2.5 %psum.7 = f32[512]{0:T(512)S(1)} all-reduce(f32[512]{0:T(512)S(1)} %get-tuple-element.23), channel_id=1, replica_groups=mesh['sec'=2,'atoms'=32,'batch'=8] {'sec'}, use_global_device_ids=true, to_apply=%region_1.2 | all-reduce | flops 512 | bytes 4096 | tf_op jit(solution)/shard_map/psum | solution.py:151
  23.1 2.1 %collective-permute-start.2 = (bf16[512,512]{1,0:T(8,128)(2,1)S(1)}, bf16[512,512]{1,0:T(8,128)(2,1)S(1)}, u32[]{:S(2)}, u32[]{:S(2)}) collective-permute-start(bf16[512,512]{1,0:T(8,128)(2,1)S(1)} %fusion.30), channel_id=1, source_target_pairs={{0,256},{256,0},{1,257},{257,1},{2,258},{258,2},{3,259},{259,3},{4... | collective-permute-start | bytes 1572872 | tf_op jit(solution)/shard_map/ppermute | solution.py:32
  26.1 0.8 collective-permute-done.2
  26.9 0.8 copy-done.5
  28.5 1.4 %fusion.25 = bf16[512,256]{0,1:T(8,128)(2,1)S(1)} fusion(f32[512,256]{0,1:T(8,128)S(1)} %fusion.60, bf16[512,512]{1,0:T(8,128)(2,1)} %copy-done.5, bf16[2,512,256]{2,1,0:T(8,128)(2,1)S(1)} %bitcast.143, s32[]{:T(128)S(6)} %select_n.111), kind=kOutput, calls=%fused_computation.30 | convolution fusion | flops 134479872 | bytes 1572868 | tf_op jit(solution)/shard_map/dot_general | solution.py:164
  31.4 14.1 %all-to-all-start = ((f32[32,5,128]{2,1,0:T(8,128)}), f32[32,5,128]{2,1,0:T(8,128)S(1)}, u32[]{:S(2)}, u32[]{:S(2)}) async-start(f32[32,5,128]{2,1,0:T(8,128)} %reshape.324), calls=%async_computation | async-start | bytes 262144 | tf_op jit(solution)/shard_map/all_to_all | solution.py:51
  46.0 10.5 %all-to-all-done = f32[32,5,128]{2,1,0:T(8,128)S(1)} async-done(((f32[32,5,128]{2,1,0:T(8,128)}), f32[32,5,128]{2,1,0:T(8,128)S(1)}, u32[]{:S(2)}, u32[]{:S(2)}) %all-to-all-start) | async-done | bytes 81952 | tf_op jit(solution)/shard_map/all_to_all | solution.py:51
  57.2 3.9 %all-to-all-start.1 = ((f32[32,5,128]{2,1,0:T(8,128)}), f32[32,5,128]{2,1,0:T(8,128)S(1)}, u32[]{:S(2)}, u32[]{:S(2)}) async-start(f32[32,5,128]{2,1,0:T(8,128)} %broadcast_in_dim.90), calls=%async_computation.1 | async-start | bytes 262144 | tf_op jit(solution)/shard_map/all_to_all | solution.py:62
  61.6 10.1 %all-to-all-done.1 = f32[32,5,128]{2,1,0:T(8,128)S(1)} async-done(((f32[32,5,128]{2,1,0:T(8,128)}), f32[32,5,128]{2,1,0:T(8,128)S(1)}, u32[]{:S(2)}, u32[]{:S(2)}) %all-to-all-start.1) | async-done | bytes 81952 | tf_op jit(solution)/shard_map/all_to_all | solution.py:62
  72.1 0.7 multiply_reduce_fusion.3
  72.8 1.9 %collective-permute-start.5 = (f32[512,256]{0,1:T(8,128)S(1)}, f32[512,256]{0,1:T(8,128)S(1)}, u32[]{:S(2)}, u32[]{:S(2)}) collective-permute-start(f32[512,256]{0,1:T(8,128)S(1)} %bitcast.141), channel_id=1, source_target_pairs={{0,256},{256,0},{1,257},{257,1},{2,258},{258,2},{3,259},{259,3},{4... | collective-permute-start | bytes 1572872 | tf_op jit(solution)/shard_map/ppermute | solution.py:32
  74.7 1.9 %collective-permute-done.5 = f32[512,256]{0,1:T(8,128)S(1)} collective-permute-done((f32[512,256]{0,1:T(8,128)S(1)}, f32[512,256]{0,1:T(8,128)S(1)}, u32[]{:S(2)}, u32[]{:S(2)}) %collective-permute-start.5) | collective-permute-done | bytes 524320 | tf_op jit(solution)/shard_map/ppermute | solution.py:32
  78.1 2.0 %collective-permute-start.6 = (f32[512,256]{0,1:T(8,128)S(1)}, f32[512,256]{0,1:T(8,128)S(1)}, u32[]{:S(2)}, u32[]{:S(2)}) collective-permute-start(f32[512,256]{0,1:T(8,128)S(1)} %fusion.102), channel_id=1, source_target_pairs={{0,256},{256,0},{1,257},{257,1},{2,258},{258,2},{3,259},{259,3},{4... | collective-permute-start | bytes 1572872 | tf_op jit(solution)/shard_map/ppermute | solution.py:32
  80.1 0.9 broadcast_select_fusion.1
  81.0 0.9 collective-permute-done.6
  82.0 1.5 %fusion.38 = (f32[]{:T(128)}, f32[512,256]{0,1:T(8,128)S(1)}) fusion(s32[512]{0:T(512)S(1)} %bitcast.150, f32[512]{0:T(512)S(1)} %fusion.90, bf16[128,256]{1,0:T(8,128)(2,1)S(1)} %get-tuple-element.32, bf16[128,256]{1,0:T(8,128)(2,1)S(1)} %get-tuple-element.31, f32[512,256]{0,1:T(8,128)S(1)} %get-tuple-element.22, f32[512]{0:T(512)S(1)} %add_rsqrt_fusion), kind=kOutput, calls=%fused_computation.47 | convolution fusion | flops 404881408 | bytes 1185796 | tf_op jit(solution)/shard_map/dot_general | solution.py:113
  83.5 0.7 multiply_reduce_fusion
  85.9 0.9 reshape.332
  86.7 3.9 %all-to-all-start.2 = ((f32[32,33,128]{2,1,0:T(8,128)}), f32[32,33,128]{2,1,0:T(8,128)S(1)}, u32[]{:S(2)}, u32[]{:S(2)}) async-start(f32[32,33,128]{2,1,0:T(8,128)} %reshape.332), calls=%async_computation.2 | async-start | bytes 1310720 | tf_op jit(solution)/shard_map/all_to_all | solution.py:51
  90.7 20.8 %all-to-all-done.2 = f32[32,33,128]{2,1,0:T(8,128)S(1)} async-done(((f32[32,33,128]{2,1,0:T(8,128)}), f32[32,33,128]{2,1,0:T(8,128)S(1)}, u32[]{:S(2)}, u32[]{:S(2)}) %all-to-all-start.2) | async-done | bytes 540704 | tf_op jit(solution)/shard_map/all_to_all | solution.py:51
  114.2 18.0 %all_to_all.20 = bf16[32,33,128]{2,1,0:T(8,128)(2,1)S(1)} all-to-all(bf16[32,33,128]{2,1,0:T(8,128)(2,1)S(1)} %broadcast_in_dim.94), channel_id=1, replica_groups=mesh['sec'=2,'atoms'=32,'batch'=8] {'atoms'}, dimensions={0} | all-to-all | bytes 540672 | tf_op jit(solution)/shard_map/all_to_all | solution.py:62
  133.0 0.9 broadcast_in_dim_reshape.3
  (83 shorter events, 10.0 us)
Async XLA Ops:
  0.6 24.7 %copy-start = (bf16[1024,256]{1,0:T(8,128)(2,1)S(1)}, bf16[1024,256]{1,0:T(8,128)(2,1)}, u32[]{:S(2)}) copy-start(bf16[1024,256]{1,0:T(8,128)(2,1)} %param.22) | copy-start | bytes 1572868
  0.6 14.3 %copy-start.1 = (bf16[1,512,512]{2,1,0:T(8,128)(2,1)S(1)}, bf16[1,512,512]{2,1,0:T(8,128)(2,1)}, u32[]{:S(2)}) copy-start(bf16[1,512,512]{2,1,0:T(8,128)(2,1)} %param.14) | copy-start | bytes 1572868
  0.7 12.5 %copy-start.12 = (s32[1,2,16]{2,1,0:T(2,128)S(1)}, s32[1,2,16]{2,1,0:T(2,128)}, u32[]{:S(2)}) copy-start(s32[1,2,16]{2,1,0:T(2,128)} %param.15) | copy-start | bytes 388
  0.7 13.2 %copy-start.11 = (bf16[512]{0:T(512)(128)(2,1)S(1)}, bf16[512]{0:T(512)(128)(2,1)}, u32[]{:S(2)}) copy-start(bf16[512]{0:T(512)(128)(2,1)} %param.20) | copy-start | bytes 3076
  1.8 12.1 %collective-permute-start = (bf16[256,512]{1,0:T(8,128)(2,1)S(1)}, bf16[256,512]{1,0:T(8,128)(2,1)S(1)}, u32[]{:S(2)}, u32[]{:S(2)}) collective-permute-start(bf16[256,512]{1,0:T(8,128)(2,1)S(1)} %get-tuple-element.29), channel_id=1, source_target_pairs={{0,8},{8,16},{16,24},{24,32},{32,40},{40,48},{48,56},{56,64},{64,7... | collective-permute-start | bytes 786440 | tf_op jit(solution)/shard_map/ppermute | solution.py:25
  5.3 9.7 %collective-permute-start.1 = (bf16[256,512]{1,0:T(8,128)(2,1)S(1)}, bf16[256,512]{1,0:T(8,128)(2,1)S(1)}, u32[]{:S(2)}, u32[]{:S(2)}) collective-permute-start(bf16[256,512]{1,0:T(8,128)(2,1)S(1)} %get-tuple-element.30), channel_id=1, source_target_pairs={{8,0},{16,8},{24,16},{32,24},{40,32},{48,40},{56,48},{64,56},{72,6... | collective-permute-start | bytes 786440 | tf_op jit(solution)/shard_map/ppermute | solution.py:26
  7.9 7.1 %copy-start.3 = (bf16[256,1024]{0,1:T(8,128)(2,1)}, bf16[256,1024]{0,1:T(8,128)(2,1)S(1)}, u32[]{:S(2)}) copy-start(bf16[256,1024]{0,1:T(8,128)(2,1)S(1)} %copy.22) | copy-start | bytes 1572868
  8.8 37.2 %collective-permute-start.4 = (bf16[256,512]{1,0:T(8,128)(2,1)}, bf16[256,512]{1,0:T(8,128)(2,1)S(1)}, u32[]{:S(2)}, u32[]{:S(2)}) collective-permute-start(bf16[256,512]{1,0:T(8,128)(2,1)} %bitcast.26), channel_id=1, source_target_pairs={{0,256},{256,0},{1,257},{257,1},{2,258},{258,2},{3,259},{259,3},{4... | collective-permute-start | bytes 786440 | tf_op jit(solution)/shard_map/ppermute | solution.py:32
  10.7 35.2 %collective-permute-start.3 = (bf16[128,256]{1,0:T(8,128)(2,1)}, bf16[128,256]{1,0:T(8,128)(2,1)}, u32[]{:S(2)}, u32[]{:S(2)}) collective-permute-start(bf16[128,256]{1,0:T(8,128)(2,1)} %bitcast.24), channel_id=1, source_target_pairs={{0,256},{256,0},{1,257},{257,1},{2,258},{258,2},{3,259},{259,3},{4... | collective-permute-start | bytes 196616 | tf_op jit(solution)/shard_map/ppermute | solution.py:32
  22.9 2.9 %copy-start.7 = (bf16[1024,256]{1,0:T(8,128)(2,1)S(1)}, bf16[1024,256]{1,0:T(8,128)(2,1)}, u32[]{:S(2)}) copy-start(bf16[1024,256]{1,0:T(8,128)(2,1)} %param.23) | copy-start | bytes 1572868
  23.1 3.8 %collective-permute-start.2 = (bf16[512,512]{1,0:T(8,128)(2,1)S(1)}, bf16[512,512]{1,0:T(8,128)(2,1)S(1)}, u32[]{:S(2)}, u32[]{:S(2)}) collective-permute-start(bf16[512,512]{1,0:T(8,128)(2,1)S(1)} %fusion.30), channel_id=1, source_target_pairs={{0,256},{256,0},{1,257},{257,1},{2,258},{258,2},{3,259},{259,3},{4... | collective-permute-start | bytes 1572872 | tf_op jit(solution)/shard_map/ppermute | solution.py:32
  25.4 3.2 %copy-start.8 = (bf16[1024,256]{1,0:T(8,128)(2,1)S(1)}, bf16[1024,256]{1,0:T(8,128)(2,1)}, u32[]{:S(2)}) copy-start(bf16[1024,256]{1,0:T(8,128)(2,1)} %param.23) | copy-start | bytes 1572868
  26.9 0.8 copy-start.5
  29.9 15.6 %copy-start.9 = (bf16[1024,256]{1,0:T(8,128)(2,1)S(1)}, bf16[1024,256]{1,0:T(8,128)(2,1)}, u32[]{:S(2)}) copy-start(bf16[1024,256]{1,0:T(8,128)(2,1)} %param.21) | copy-start | bytes 1572868
  30.0 31.1 %copy-start.6 = (bf16[512,512]{1,0:T(8,128)(2,1)S(1)}, bf16[512,512]{1,0:T(8,128)(2,1)}, u32[]{:S(2)}) copy-start(bf16[512,512]{1,0:T(8,128)(2,1)} %copy-done.5) | copy-start | bytes 1572868
  31.4 25.0 %all-to-all-start = ((f32[32,5,128]{2,1,0:T(8,128)}), f32[32,5,128]{2,1,0:T(8,128)S(1)}, u32[]{:S(2)}, u32[]{:S(2)}) async-start(f32[32,5,128]{2,1,0:T(8,128)} %reshape.324), calls=%async_computation | async-start | bytes 262144 | tf_op jit(solution)/shard_map/all_to_all | solution.py:51
  57.2 14.5 %all-to-all-start.1 = ((f32[32,5,128]{2,1,0:T(8,128)}), f32[32,5,128]{2,1,0:T(8,128)S(1)}, u32[]{:S(2)}, u32[]{:S(2)}) async-start(f32[32,5,128]{2,1,0:T(8,128)} %broadcast_in_dim.90), calls=%async_computation.1 | async-start | bytes 262144 | tf_op jit(solution)/shard_map/all_to_all | solution.py:62
  61.6 15.2 %copy-start.4 = (bf16[256,1024]{0,1:T(8,128)(2,1)S(1)}, bf16[256,1024]{0,1:T(8,128)(2,1)}, u32[]{:S(2)}) copy-start(bf16[256,1024]{0,1:T(8,128)(2,1)} %copy-done.3) | copy-start | bytes 1572868
  72.8 3.8 %collective-permute-start.5 = (f32[512,256]{0,1:T(8,128)S(1)}, f32[512,256]{0,1:T(8,128)S(1)}, u32[]{:S(2)}, u32[]{:S(2)}) collective-permute-start(f32[512,256]{0,1:T(8,128)S(1)} %bitcast.141), channel_id=1, source_target_pairs={{0,256},{256,0},{1,257},{257,1},{2,258},{258,2},{3,259},{259,3},{4... | collective-permute-start | bytes 1572872 | tf_op jit(solution)/shard_map/ppermute | solution.py:32
  76.8 1.0 copy-start.10
  77.7 6.5 %copy-start.2 = (bf16[512,512]{1,0:T(8,128)(2,1)}, bf16[512,512]{1,0:T(8,128)(2,1)S(1)}, u32[]{:S(2)}) copy-start(bf16[512,512]{1,0:T(8,128)(2,1)S(1)} %fusion.21) | copy-start | bytes 1572868
  77.7 4.3 %copy-start.13 = (s32[1,512]{1,0:T(1,128)S(1)}, s32[1,512]{1,0:T(1,128)}, u32[]{:S(2)}) copy-start(s32[1,512]{1,0:T(1,128)} %param.18) | copy-start | bytes 6148
  78.1 3.8 %collective-permute-start.6 = (f32[512,256]{0,1:T(8,128)S(1)}, f32[512,256]{0,1:T(8,128)S(1)}, u32[]{:S(2)}, u32[]{:S(2)}) collective-permute-start(f32[512,256]{0,1:T(8,128)S(1)} %fusion.102), channel_id=1, source_target_pairs={{0,256},{256,0},{1,257},{257,1},{2,258},{258,2},{3,259},{259,3},{4... | collective-permute-start | bytes 1572872 | tf_op jit(solution)/shard_map/ppermute | solution.py:32
  86.7 24.7 %all-to-all-start.2 = ((f32[32,33,128]{2,1,0:T(8,128)}), f32[32,33,128]{2,1,0:T(8,128)S(1)}, u32[]{:S(2)}, u32[]{:S(2)}) async-start(f32[32,33,128]{2,1,0:T(8,128)} %reshape.332), calls=%async_computation.2 | async-start | bytes 1310720 | tf_op jit(solution)/shard_map/all_to_all | solution.py:51

commit v12 on v8

--- a/solution.py
+++ b/solution.py
@@ -57,8 +57,10 @@
         rest = owned - owned.astype(jnp.bfloat16).astype(jnp.float32)
         here = lax.axis_index("atoms") == owner
         spare = (slot + 1) // 128, (slot + 1) % 128
-        kept = jnp.where(here, rest[0, slot // 128, slot % 128], owned[0, spare[0], spare[1]])
-        owned = owned.at[0, spare[0], spare[1]].set(kept).astype(jnp.bfloat16)
+        row = lax.broadcasted_iota(jnp.int32, owned.shape, 1)
+        lane = lax.broadcasted_iota(jnp.int32, owned.shape, 2)
+        target = here & (row == spare[0]) & (lane == spare[1])
+        owned = jnp.where(target, rest[0, slot // 128, slot % 128], owned).astype(jnp.bfloat16)
     spread = lax.all_to_all(jnp.broadcast_to(owned, pieces.shape), "atoms", 0, 0, tiled=True)
     total = spread.reshape(-1)[: x.size].reshape(x.shape).astype(jnp.float32)
     return total if riders is None else (total, riders)

time: 138 us -> 137 us (level)
  no operation moved by 1% of the time
where the time goes in v12:
time: 137 us; the launch traced here: 135 us
  waiting for transfers between devices  44.8 us (33%)
  starting transfers between devices  37 us (27%)
  blocking collectives  20.5 us (15%)
  local copies, waits for them, and re-layouts  12.2 us (9%)
  matrix products  11.4 us (8%)
  between operations  6.19 us (5%)
  other arithmetic  3.3 us (2%)
    all_to_all x2, waiting for transfers between devices, sum_atoms(): arrived = lax.all_to_all(pieces, 'atoms', 0, 0, tiled=True)  31.2 us
    all_to_all x2, starting transfers between devices, sum_atoms(): arrived = lax.all_to_all(pieces, 'atoms', 0, 0, tiled=True)  18 us
    all_to_all x1, blocking collectives, sum_atoms(): lax.all_to_all(jnp.broadcast_to(owned, pieces.shape), 'atoms', 0, 0, tile...  18 us
    ppermute x5, starting transfers between devices, swap_sec(): return lax.ppermute(x, 'sec', [(0, 1), (1, 0)])  10.4 us
    all_to_all x1, waiting for transfers between devices, sum_atoms(): lax.all_to_all(jnp.broadcast_to(owned, pieces.shape), 'atoms', 0, 0, tile...  10.1 us
    all_to_all x1, starting transfers between devices, sum_atoms(): lax.all_to_all(jnp.broadcast_to(owned, pieces.shape), 'atoms', 0, 0, tile...  3.86 us
    ppermute x1, starting transfers between devices, extended(): before = lax.ppermute(last, axis, up)  3.5 us
    dot_general x1, matrix products, message_pass(): jnp.einsum('btij,tjf->bif', masked, panels, preferred_element_type=jnp.fl...  2.92 us
  transfers between devices with their start and end apart: 10, of which 7 were waited for; matrix products, arithmetic and copies ran while one was open for 11% of the time, Pallas kernels for 0%

profile of v12, /device:TPU:6, one launch (start us, length us, event | category | flops | bytes accessed | tf_op | source)
XLA Modules:
  0.0 135.3 jit_solution(6520356772559909925)
XLA Ops:
  0.7 1.1 slice_bitcast_fusion.1
  1.8 3.5 %collective-permute-start = (bf16[256,512]{1,0:T(8,128)(2,1)S(1)}, bf16[256,512]{1,0:T(8,128)(2,1)S(1)}, u32[]{:S(2)}, u32[]{:S(2)}) collective-permute-start(bf16[256,512]{1,0:T(8,128)(2,1)S(1)} %get-tuple-element.23), channel_id=1, source_target_pairs={{0,8},{8,16},{16,24},{24,32},{32,40},{40,48},{48,56},{56,64},{64,7... | collective-permute-start | bytes 786440 | tf_op jit(solution)/shard_map/ppermute | solution.py:25
  5.3 1.3 collective-permute-start.1
  6.6 1.2 copy.22
  7.9 0.8 copy.23
  8.8 1.9 %collective-permute-start.4 = (bf16[256,512]{1,0:T(8,128)(2,1)}, bf16[256,512]{1,0:T(8,128)(2,1)}, u32[]{:S(2)}, u32[]{:S(2)}) collective-permute-start(bf16[256,512]{1,0:T(8,128)(2,1)} %bitcast.26), channel_id=1, source_target_pairs={{0,256},{256,0},{1,257},{257,1},{2,258},{258,2},{3,259},{259,3},{4... | collective-permute-start | bytes 786440 | tf_op jit(solution)/shard_map/ppermute | solution.py:32
  10.7 2.4 %collective-permute-start.3 = (bf16[128,256]{1,0:T(8,128)(2,1)}, bf16[128,256]{1,0:T(8,128)(2,1)}, u32[]{:S(2)}, u32[]{:S(2)}) collective-permute-start(bf16[128,256]{1,0:T(8,128)(2,1)} %bitcast.24), channel_id=1, source_target_pairs={{0,256},{256,0},{1,257},{257,1},{2,258},{258,2},{3,259},{259,3},{4... | collective-permute-start | bytes 196616 | tf_op jit(solution)/shard_map/ppermute | solution.py:32
  13.9 1.1 collective-permute-done.1
  15.1 2.0 %gather_fusion = bf16[16,128,512]{2,1,0:T(8,128)(2,1)} fusion(bf16[8,128,512]{2,1,0:T(8,128)(2,1)S(1)} %bitcast.123, s32[1024]{0:T(1024)S(1)} %pad_clamp_fusion), kind=kCustom, calls=%fused_computation | custom fusion | bytes 4194368 | tf_op jit(solution)/shard_map/jit(_take)/gather | solution.py:86
  17.1 2.9 %fusion.16 = f32[4,128,512]{2,1,0:T(8,128)S(1)} fusion(bf16[16,128,512]{2,1,0:T(8,128)(2,1)} %gather_fusion, pred[16]{0:T(512)(128)(4,1)S(1)} %get-tuple-element.13, pred[4,16]{1,0:T(4,128)(4,1)S(1)} %iota_compare_fusion.2, bf16[16,128,128]{2,1,0:T(8,128)(2,1)S(1)} %bitcast.140), kind=kOutput, calls=%fused_computation.17 | convolution fusion | flops 1076363264 | bytes 3670096 | tf_op jit(solution)/shard_map/btij,tjf->bif/dot_general | solution.py:89
  20.2 2.5 %psum.7 = f32[512]{0:T(512)S(1)} all-reduce(f32[512]{0:T(512)S(1)} %get-tuple-element.11), channel_id=1, replica_groups=mesh['sec'=2,'atoms'=32,'batch'=8] {'sec'}, use_global_device_ids=true, to_apply=%region_1.2 | all-reduce | flops 512 | bytes 4096 | tf_op jit(solution)/shard_map/psum | solution.py:153
  22.9 2.1 %collective-permute-start.2 = (bf16[512,512]{1,0:T(8,128)(2,1)S(1)}, bf16[512,512]{1,0:T(8,128)(2,1)S(1)}, u32[]{:S(2)}, u32[]{:S(2)}) collective-permute-start(bf16[512,512]{1,0:T(8,128)(2,1)S(1)} %fusion.30), channel_id=1, source_target_pairs={{0,256},{256,0},{1,257},{257,1},{2,258},{258,2},{3,259},{259,3},{4... | collective-permute-start | bytes 1572872 | tf_op jit(solution)/shard_map/ppermute | solution.py:32
  26.0 0.8 collective-permute-done.2
  26.7 0.8 copy-done.3
  28.4 1.4 %fusion.25 = bf16[512,256]{0,1:T(8,128)(2,1)S(1)} fusion(f32[512,256]{0,1:T(8,128)S(1)} %fusion.62, bf16[512,512]{1,0:T(8,128)(2,1)} %copy-done.3, bf16[2,512,256]{2,1,0:T(8,128)(2,1)S(1)} %bitcast.135, s32[]{:T(128)S(6)} %select_n.141), kind=kOutput, calls=%fused_computation.29 | convolution fusion | flops 134479872 | bytes 1572868 | tf_op jit(solution)/shard_map/dot_general | solution.py:166
  31.3 14.1 %all-to-all-start = ((f32[32,5,128]{2,1,0:T(8,128)}), f32[32,5,128]{2,1,0:T(8,128)S(1)}, u32[]{:S(2)}, u32[]{:S(2)}) async-start(f32[32,5,128]{2,1,0:T(8,128)} %reshape.309), calls=%async_computation | async-start | bytes 262144 | tf_op jit(solution)/shard_map/all_to_all | solution.py:51
  45.8 10.5 %all-to-all-done = f32[32,5,128]{2,1,0:T(8,128)S(1)} async-done(((f32[32,5,128]{2,1,0:T(8,128)}), f32[32,5,128]{2,1,0:T(8,128)S(1)}, u32[]{:S(2)}, u32[]{:S(2)}) %all-to-all-start) | async-done | bytes 81952 | tf_op jit(solution)/shard_map/all_to_all | solution.py:51
  57.0 3.9 %all-to-all-start.1 = ((f32[32,5,128]{2,1,0:T(8,128)}), f32[32,5,128]{2,1,0:T(8,128)S(1)}, u32[]{:S(2)}, u32[]{:S(2)}) async-start(f32[32,5,128]{2,1,0:T(8,128)} %broadcast_in_dim.89), calls=%async_computation.1 | async-start | bytes 262144 | tf_op jit(solution)/shard_map/all_to_all | solution.py:64
  61.4 10.1 %all-to-all-done.1 = f32[32,5,128]{2,1,0:T(8,128)S(1)} async-done(((f32[32,5,128]{2,1,0:T(8,128)}), f32[32,5,128]{2,1,0:T(8,128)S(1)}, u32[]{:S(2)}, u32[]{:S(2)}) %all-to-all-start.1) | async-done | bytes 81952 | tf_op jit(solution)/shard_map/all_to_all | solution.py:64
  72.6 1.9 %collective-permute-start.5 = (f32[512,256]{0,1:T(8,128)S(1)}, f32[512,256]{0,1:T(8,128)S(1)}, u32[]{:S(2)}, u32[]{:S(2)}) collective-permute-start(f32[512,256]{0,1:T(8,128)S(1)} %bitcast.132), channel_id=1, source_target_pairs={{0,256},{256,0},{1,257},{257,1},{2,258},{258,2},{3,259},{259,3},{4... | collective-permute-start | bytes 1572872 | tf_op jit(solution)/shard_map/ppermute | solution.py:32
  74.7 1.0 bitcast_select_fusion.1
  75.7 0.7 collective-permute-done.5
  77.8 2.0 %collective-permute-start.6 = (f32[512,256]{0,1:T(8,128)S(1)}, f32[512,256]{0,1:T(8,128)S(1)}, u32[]{:S(2)}, u32[]{:S(2)}) collective-permute-start(f32[512,256]{0,1:T(8,128)S(1)} %fusion.102), channel_id=1, source_target_pairs={{0,256},{256,0},{1,257},{257,1},{2,258},{258,2},{3,259},{259,3},{4... | collective-permute-start | bytes 1572872 | tf_op jit(solution)/shard_map/ppermute | solution.py:32
  79.9 0.9 broadcast_select_fusion.3
  80.8 0.9 collective-permute-done.6
  81.8 1.5 %fusion.38 = (f32[]{:T(128)}, f32[512,256]{0,1:T(8,128)S(1)}) fusion(s32[512]{0:T(512)S(1)} %bitcast.141, f32[512]{0:T(512)S(1)} %fusion.89, bf16[128,256]{1,0:T(8,128)(2,1)S(1)} %get-tuple-element.26, bf16[128,256]{1,0:T(8,128)(2,1)S(1)} %get-tuple-element.25, f32[512,256]{0,1:T(8,128)S(1)} %get-tuple-element.10, f32[512]{0:T(512)S(1)} %add_rsqrt_fusion), kind=kOutput, calls=%fused_computation.49 | convolution fusion | flops 404881408 | bytes 1185796 | tf_op jit(solution)/shard_map/dot_general | solution.py:115
  83.2 0.7 multiply_reduce_fusion.1
  85.6 0.9 reshape.317
  86.5 3.9 %all-to-all-start.2 = ((f32[32,33,128]{2,1,0:T(8,128)}), f32[32,33,128]{2,1,0:T(8,128)S(1)}, u32[]{:S(2)}, u32[]{:S(2)}) async-start(f32[32,33,128]{2,1,0:T(8,128)} %reshape.317), calls=%async_computation.2 | async-start | bytes 1310720 | tf_op jit(solution)/shard_map/all_to_all | solution.py:51
  90.5 20.7 %all-to-all-done.2 = f32[32,33,128]{2,1,0:T(8,128)S(1)} async-done(((f32[32,33,128]{2,1,0:T(8,128)}), f32[32,33,128]{2,1,0:T(8,128)S(1)}, u32[]{:S(2)}, u32[]{:S(2)}) %all-to-all-start.2) | async-done | bytes 540704 | tf_op jit(solution)/shard_map/all_to_all | solution.py:51
  113.2 18.0 %all_to_all.20 = bf16[32,33,128]{2,1,0:T(8,128)(2,1)S(1)} all-to-all(bf16[32,33,128]{2,1,0:T(8,128)(2,1)S(1)} %broadcast_in_dim.92), channel_id=1, replica_groups=mesh['sec'=2,'atoms'=32,'batch'=8] {'atoms'}, dimensions={0} | all-to-all | bytes 540672 | tf_op jit(solution)/shard_map/all_to_all | solution.py:64
  132.0 0.9 broadcast_in_dim_reshape.3
  (83 shorter events, 10.6 us)
Async XLA Ops:
  0.6 24.6 %copy-start = (bf16[1024,256]{1,0:T(8,128)(2,1)S(1)}, bf16[1024,256]{1,0:T(8,128)(2,1)}, u32[]{:S(2)}) copy-start(bf16[1024,256]{1,0:T(8,128)(2,1)} %param.20) | copy-start | bytes 1572868
  0.6 14.3 %copy-start.1 = (bf16[1,512,512]{2,1,0:T(8,128)(2,1)S(1)}, bf16[1,512,512]{2,1,0:T(8,128)(2,1)}, u32[]{:S(2)}) copy-start(bf16[1,512,512]{2,1,0:T(8,128)(2,1)} %param.12) | copy-start | bytes 1572868
  0.7 12.5 %copy-start.10 = (s32[1,2,16]{2,1,0:T(2,128)S(1)}, s32[1,2,16]{2,1,0:T(2,128)}, u32[]{:S(2)}) copy-start(s32[1,2,16]{2,1,0:T(2,128)} %param.13) | copy-start | bytes 388
  0.7 13.2 %copy-start.9 = (bf16[512]{0:T(512)(128)(2,1)S(1)}, bf16[512]{0:T(512)(128)(2,1)}, u32[]{:S(2)}) copy-start(bf16[512]{0:T(512)(128)(2,1)} %param.18) | copy-start | bytes 3076
  1.8 12.1 %collective-permute-start = (bf16[256,512]{1,0:T(8,128)(2,1)S(1)}, bf16[256,512]{1,0:T(8,128)(2,1)S(1)}, u32[]{:S(2)}, u32[]{:S(2)}) collective-permute-start(bf16[256,512]{1,0:T(8,128)(2,1)S(1)} %get-tuple-element.23), channel_id=1, source_target_pairs={{0,8},{8,16},{16,24},{24,32},{32,40},{40,48},{48,56},{56,64},{64,7... | collective-permute-start | bytes 786440 | tf_op jit(solution)/shard_map/ppermute | solution.py:25
  5.3 9.7 %collective-permute-start.1 = (bf16[256,512]{1,0:T(8,128)(2,1)S(1)}, bf16[256,512]{1,0:T(8,128)(2,1)S(1)}, u32[]{:S(2)}, u32[]{:S(2)}) collective-permute-start(bf16[256,512]{1,0:T(8,128)(2,1)S(1)} %get-tuple-element.24), channel_id=1, source_target_pairs={{8,0},{16,8},{24,16},{32,24},{40,32},{48,40},{56,48},{64,56},{72,6... | collective-permute-start | bytes 786440 | tf_op jit(solution)/shard_map/ppermute | solution.py:26
  8.8 37.0 %collective-permute-start.4 = (bf16[256,512]{1,0:T(8,128)(2,1)}, bf16[256,512]{1,0:T(8,128)(2,1)}, u32[]{:S(2)}, u32[]{:S(2)}) collective-permute-start(bf16[256,512]{1,0:T(8,128)(2,1)} %bitcast.26), channel_id=1, source_target_pairs={{0,256},{256,0},{1,257},{257,1},{2,258},{258,2},{3,259},{259,3},{4... | collective-permute-start | bytes 786440 | tf_op jit(solution)/shard_map/ppermute | solution.py:32
  10.7 35.1 %collective-permute-start.3 = (bf16[128,256]{1,0:T(8,128)(2,1)}, bf16[128,256]{1,0:T(8,128)(2,1)}, u32[]{:S(2)}, u32[]{:S(2)}) collective-permute-start(bf16[128,256]{1,0:T(8,128)(2,1)} %bitcast.24), channel_id=1, source_target_pairs={{0,256},{256,0},{1,257},{257,1},{2,258},{258,2},{3,259},{259,3},{4... | collective-permute-start | bytes 196616 | tf_op jit(solution)/shard_map/ppermute | solution.py:32
  15.1 2.0 %copy-start.11 = (bf16[1,16,128,128]{3,2,1,0:T(8,128)(2,1)S(1)}, bf16[1,16,128,128]{3,2,1,0:T(8,128)(2,1)}, u32[]{:S(2)}) copy-start(bf16[1,16,128,128]{3,2,1,0:T(8,128)(2,1)} %param.14) | copy-start | bytes 1572868
  22.7 2.9 %copy-start.5 = (bf16[1024,256]{1,0:T(8,128)(2,1)S(1)}, bf16[1024,256]{1,0:T(8,128)(2,1)}, u32[]{:S(2)}) copy-start(bf16[1024,256]{1,0:T(8,128)(2,1)} %param.21) | copy-start | bytes 1572868
  22.9 3.8 %collective-permute-start.2 = (bf16[512,512]{1,0:T(8,128)(2,1)S(1)}, bf16[512,512]{1,0:T(8,128)(2,1)S(1)}, u32[]{:S(2)}, u32[]{:S(2)}) collective-permute-start(bf16[512,512]{1,0:T(8,128)(2,1)S(1)} %fusion.30), channel_id=1, source_target_pairs={{0,256},{256,0},{1,257},{257,1},{2,258},{258,2},{3,259},{259,3},{4... | collective-permute-start | bytes 1572872 | tf_op jit(solution)/shard_map/ppermute | solution.py:32
  25.2 3.2 %copy-start.6 = (bf16[1024,256]{1,0:T(8,128)(2,1)S(1)}, bf16[1024,256]{1,0:T(8,128)(2,1)}, u32[]{:S(2)}) copy-start(bf16[1024,256]{1,0:T(8,128)(2,1)} %param.21) | copy-start | bytes 1572868
  26.7 0.8 copy-start.3
  29.8 15.6 %copy-start.7 = (bf16[1024,256]{1,0:T(8,128)(2,1)S(1)}, bf16[1024,256]{1,0:T(8,128)(2,1)}, u32[]{:S(2)}) copy-start(bf16[1024,256]{1,0:T(8,128)(2,1)} %param.19) | copy-start | bytes 1572868
  29.8 31.0 %copy-start.4 = (bf16[512,512]{1,0:T(8,128)(2,1)S(1)}, bf16[512,512]{1,0:T(8,128)(2,1)}, u32[]{:S(2)}) copy-start(bf16[512,512]{1,0:T(8,128)(2,1)} %copy-done.3) | copy-start | bytes 1572868
  31.3 25.0 %all-to-all-start = ((f32[32,5,128]{2,1,0:T(8,128)}), f32[32,5,128]{2,1,0:T(8,128)S(1)}, u32[]{:S(2)}, u32[]{:S(2)}) async-start(f32[32,5,128]{2,1,0:T(8,128)} %reshape.309), calls=%async_computation | async-start | bytes 262144 | tf_op jit(solution)/shard_map/all_to_all | solution.py:51
  57.0 14.5 %all-to-all-start.1 = ((f32[32,5,128]{2,1,0:T(8,128)}), f32[32,5,128]{2,1,0:T(8,128)S(1)}, u32[]{:S(2)}, u32[]{:S(2)}) async-start(f32[32,5,128]{2,1,0:T(8,128)} %broadcast_in_dim.89), calls=%async_computation.1 | async-start | bytes 262144 | tf_op jit(solution)/shard_map/all_to_all | solution.py:64
  72.6 3.8 %collective-permute-start.5 = (f32[512,256]{0,1:T(8,128)S(1)}, f32[512,256]{0,1:T(8,128)S(1)}, u32[]{:S(2)}, u32[]{:S(2)}) collective-permute-start(f32[512,256]{0,1:T(8,128)S(1)} %bitcast.132), channel_id=1, source_target_pairs={{0,256},{256,0},{1,257},{257,1},{2,258},{258,2},{3,259},{259,3},{4... | collective-permute-start | bytes 1572872 | tf_op jit(solution)/shard_map/ppermute | solution.py:32
  76.5 1.0 copy-start.8
  77.5 6.5 %copy-start.2 = (bf16[512,512]{1,0:T(8,128)(2,1)}, bf16[512,512]{1,0:T(8,128)(2,1)S(1)}, u32[]{:S(2)}) copy-start(bf16[512,512]{1,0:T(8,128)(2,1)S(1)} %fusion.21) | copy-start | bytes 1572868
  77.5 4.3 %copy-start.12 = (s32[1,512]{1,0:T(1,128)S(1)}, s32[1,512]{1,0:T(1,128)}, u32[]{:S(2)}) copy-start(s32[1,512]{1,0:T(1,128)} %param.16) | copy-start | bytes 6148
  77.8 3.8 %collective-permute-start.6 = (f32[512,256]{0,1:T(8,128)S(1)}, f32[512,256]{0,1:T(8,128)S(1)}, u32[]{:S(2)}, u32[]{:S(2)}) collective-permute-start(f32[512,256]{0,1:T(8,128)S(1)} %fusion.102), channel_id=1, source_target_pairs={{0,256},{256,0},{1,257},{257,1},{2,258},{258,2},{3,259},{259,3},{4... | collective-permute-start | bytes 1572872 | tf_op jit(solution)/shard_map/ppermute | solution.py:32
  86.5 24.7 %all-to-all-start.2 = ((f32[32,33,128]{2,1,0:T(8,128)}), f32[32,33,128]{2,1,0:T(8,128)S(1)}, u32[]{:S(2)}, u32[]{:S(2)}) async-start(f32[32,33,128]{2,1,0:T(8,128)} %reshape.317), calls=%async_computation.2 | async-start | bytes 1310720 | tf_op jit(solution)/shard_map/all_to_all | solution.py:51

commit v13 on v12

--- a/solution.py
+++ b/solution.py
@@ -40,6 +40,23 @@
 
 def sum_sec(x):
     return x + swap_sec(x)
+
+
+def sum_atoms_grouped(x, riders):
+    peers = lax.axis_size("atoms")
+    inner = min(peers, 8)
+    rows = [[g * inner + k for k in range(inner)] for g in range(peers // inner)]
+    cols = [list(group) for group in zip(*rows)]
+    flat = x.reshape(-1)
+    lanes = -(-flat.shape[0] // 128) * 128
+    flat = jnp.pad(flat, (0, lanes - flat.shape[0])).reshape(1, lanes // 128, 128)
+    for groups in (rows, cols):
+        copies = jnp.broadcast_to(flat, (len(groups[0]),) + flat.shape[1:])
+        arrived = lax.all_to_all(copies, "atoms", 0, 0, tiled=True, axis_index_groups=groups)
+        if groups is rows:
+            arrived, riders = lax.optimization_barrier((arrived, riders))
+        flat = jnp.sum(arrived, axis=0, keepdims=True)
+    return flat.reshape(-1)[: x.size].reshape(x.shape), riders
 
 
 def sum_atoms(x, exact=None, riders=None):
@@ -174,7 +191,7 @@
         key_f.astype(jnp.bfloat16), value_f.astype(jnp.bfloat16), atom_mask, head_count
     )
     state_rows = jnp.concatenate([outer_state, key_total[:, None, :]], axis=1)
-    packed, partner = sum_atoms(state_rows, riders=partner)
+    packed, partner = sum_atoms_grouped(state_rows, partner)
     peak_all = join_sec(peak_part, partner[0], sec, 0)
     out_rows = join_sec(out_cols[:, sec, :], partner[1], sec, 0)
     outer_state, key_total = packed[:, :HEAD_DIM, :], packed[:, HEAD_DIM, :]

time: 137 us -> 141 us (1.029)
  starting transfers between devices: 37 us -> 33.6 us
  local copies, waits for them, and re-layouts: 12.2 us -> 14.7 us
  other arithmetic: 3.3 us -> 5.6 us
  waiting for transfers between devices: 44.8 us -> 46.8 us
    all_to_all x2 -> x1, starting transfers between devices: 18 us -> 3.9 us  [sum_atoms(): arrived = lax.all_to_all(pieces, 'atoms', 0, 0, tiled=True)]
    all_to_all x1 -> x2, starting transfers between devices: 3.86 us -> 14.5 us  [sum_atoms_grouped(): lax.all_to_all(copies, 'atoms', 0, 0, tiled=True, axis_index_groups=groups)]
    all_to_all x2 -> x1, waiting for transfers between devices: 31.2 us -> 20.7 us  [sum_atoms(): arrived = lax.all_to_all(pieces, 'atoms', 0, 0, tiled=True)]
    all_to_all x1 -> x2, waiting for transfers between devices: 10.1 us -> 16.4 us  [sum_atoms_grouped(): lax.all_to_all(copies, 'atoms', 0, 0, tiled=True, axis_index_groups=groups)]
    ppermute x1, waiting for transfers between devices: 1.09 us -> 4.13 us  [extended(): after = lax.ppermute(leading, axis, down)]
    ppermute x5, waiting for transfers between devices: 2.36 us -> 4.1 us  [swap_sec(): return lax.ppermute(x, 'sec', [(0, 1), (1, 0)])]
    broadcast_in_dim x0 -> x3, local copies, waits for them, and re-layouts: none -> 1.65 us  [sum_atoms_grouped(): copies = jnp.broadcast_to(flat, (len(groups[0]),) + flat.shape[1:])]
    unnamed x28 -> x30, local copies, waits for them, and re-layouts: 2.7 us -> 3.29 us
  transfers between devices with their start and end apart: 10 -> 10, of which waited for: 7 -> 9; matrix products, arithmetic and copies ran while one was open for 11% -> 7% of each run, Pallas kernels for 0% -> 0%
where the time goes in v13:
time: 141 us; the launch traced here: 140 us
  waiting for transfers between devices  46.8 us (33%)
  starting transfers between devices  33.6 us (24%)
  blocking collectives  20.5 us (15%)
  local copies, waits for them, and re-layouts  14.7 us (10%)
  matrix products  12.5 us (9%)
  between operations  6.11 us (4%)
  other arithmetic  5.6 us (4%)
    all_to_all x1, waiting for transfers between devices, sum_atoms(): arrived = lax.all_to_all(pieces, 'atoms', 0, 0, tiled=True)  20.7 us
    all_to_all x1, blocking collectives, sum_atoms(): lax.all_to_all(jnp.broadcast_to(owned, pieces.shape), 'atoms', 0, 0, tile...  18 us
    all_to_all x2, waiting for transfers between devices, sum_atoms_grouped(): lax.all_to_all(copies, 'atoms', 0, 0, tiled=True, axis_index_groups=groups)  16.4 us
    all_to_all x2, starting transfers between devices, sum_atoms_grouped(): lax.all_to_all(copies, 'atoms', 0, 0, tiled=True, axis_index_groups=groups)  14.5 us
    ppermute x5, starting transfers between devices, swap_sec(): return lax.ppermute(x, 'sec', [(0, 1), (1, 0)])  10.4 us
    ppermute x1, waiting for transfers between devices, extended(): after = lax.ppermute(leading, axis, down)  4.13 us
    ppermute x5, waiting for transfers between devices, swap_sec(): return lax.ppermute(x, 'sec', [(0, 1), (1, 0)])  4.1 us
    all_to_all x1, starting transfers between devices, sum_atoms(): arrived = lax.all_to_all(pieces, 'atoms', 0, 0, tiled=True)  3.9 us
  transfers between devices with their start and end apart: 10, of which 9 were waited for; matrix products, arithmetic and copies ran while one was open for 7% of the time, Pallas kernels for 0%

profile of v13, /device:TPU:6, one launch (start us, length us, event | category | flops | bytes accessed | tf_op | source)
XLA Modules:
  0.0 139.8 jit_solution(14165477723315808044)
XLA Ops:
  0.6 1.1 slice_bitcast_fusion.1
  1.8 3.5 %collective-permute-start = (bf16[256,512]{1,0:T(8,128)(2,1)S(1)}, bf16[256,512]{1,0:T(8,128)(2,1)S(1)}, u32[]{:S(2)}, u32[]{:S(2)}) collective-permute-start(bf16[256,512]{1,0:T(8,128)(2,1)S(1)} %get-tuple-element.23), channel_id=1, source_target_pairs={{0,8},{8,16},{16,24},{24,32},{32,40},{40,48},{48,56},{56,64},{64,7... | collective-permute-start | bytes 786440 | tf_op jit(solution)/shard_map/ppermute | solution.py:25
  5.3 1.3 collective-permute-start.1
  9.4 1.4 %collective-permute-done = bf16[256,512]{1,0:T(8,128)(2,1)S(1)} collective-permute-done((bf16[256,512]{1,0:T(8,128)(2,1)S(1)}, bf16[256,512]{1,0:T(8,128)(2,1)S(1)}, u32[]{:S(2)}, u32[]{:S(2)}) %collective-permute-start) | collective-permute-done | bytes 262176 | tf_op jit(solution)/shard_map/ppermute | solution.py:25
  10.8 4.1 %collective-permute-done.1 = bf16[256,512]{1,0:T(8,128)(2,1)S(1)} collective-permute-done((bf16[256,512]{1,0:T(8,128)(2,1)S(1)}, bf16[256,512]{1,0:T(8,128)(2,1)S(1)}, u32[]{:S(2)}, u32[]{:S(2)}) %collective-permute-start.1) | collective-permute-done | bytes 262176 | tf_op jit(solution)/shard_map/ppermute | solution.py:26
  14.9 1.1 pad_maximum_fusion
  16.0 2.0 %gather_fusion = bf16[16,128,512]{2,1,0:T(8,128)(2,1)} fusion(bf16[8,128,512]{2,1,0:T(8,128)(2,1)S(1)} %bitcast.123, s32[1024]{0:T(1024)S(1)} %pad_clamp_fusion), kind=kCustom, calls=%fused_computation | custom fusion | bytes 4194368 | tf_op jit(solution)/shard_map/jit(_take)/gather | solution.py:103
  18.1 3.1 %fusion.16 = f32[4,128,512]{2,1,0:T(8,128)S(1)} fusion(bf16[16,128,512]{2,1,0:T(8,128)(2,1)} %gather_fusion, pred[16]{0:T(512)(128)(4,1)S(1)} %get-tuple-element.13, pred[4,16]{1,0:T(4,128)(4,1)S(1)} %iota_compare_fusion.2, bf16[16,128,128]{2,1,0:T(8,128)(2,1)} %bitcast.142), kind=kOutput, calls=%fused_computation.17 | convolution fusion | flops 1076363264 | bytes 3670096 | tf_op jit(solution)/shard_map/btij,tjf->bif/dot_general | solution.py:106
  21.4 2.5 %psum.7 = f32[512]{0:T(512)S(1)} all-reduce(f32[512]{0:T(512)S(1)} %get-tuple-element.11), channel_id=1, replica_groups=mesh['sec'=2,'atoms'=32,'batch'=8] {'sec'}, use_global_device_ids=true, to_apply=%region_1.2 | all-reduce | flops 512 | bytes 4096 | tf_op jit(solution)/shard_map/psum | solution.py:170
  24.1 2.1 %collective-permute-start.2 = (bf16[512,512]{1,0:T(8,128)(2,1)S(1)}, bf16[512,512]{1,0:T(8,128)(2,1)S(1)}, u32[]{:S(2)}, u32[]{:S(2)}) collective-permute-start(bf16[512,512]{1,0:T(8,128)(2,1)S(1)} %fusion.30), channel_id=1, source_target_pairs={{0,256},{256,0},{1,257},{257,1},{2,258},{258,2},{3,259},{259,3},{4... | collective-permute-start | bytes 1572872 | tf_op jit(solution)/shard_map/ppermute | solution.py:32
  29.6 1.4 fusion.25
  31.8 0.8 broadcast_in_dim.97
  32.6 7.3 %all-to-all-start = ((f32[8,130,128]{2,1,0:T(8,128)}), f32[8,130,128]{2,1,0:T(8,128)S(1)}, u32[]{:S(2)}, u32[]{:S(2)}) async-start(f32[8,130,128]{2,1,0:T(8,128)} %broadcast_in_dim.97), calls=%async_computation | async-start | bytes 1114112 | tf_op jit(solution)/shard_map/all_to_all | solution.py:55
  39.9 1.2 copy.36
  41.9 1.9 %copy.37 = bf16[256,1,512]{2,0,1:T(8,128)(2,1)} copy(bf16[256,1,512]{0,2,1:T(8,128)(2,1)} %get-tuple-element.22) | data formatting | bytes 524288 | tf_op jit(solution)/shard_map/dynamic_slice | solution.py:178
  43.8 1.9 %collective-permute-start.4 = (bf16[256,512]{1,0:T(8,128)(2,1)}, bf16[256,512]{1,0:T(8,128)(2,1)}, u32[]{:S(2)}, u32[]{:S(2)}) collective-permute-start(bf16[256,512]{1,0:T(8,128)(2,1)} %bitcast.138), channel_id=1, source_target_pairs={{0,256},{256,0},{1,257},{257,1},{2,258},{258,2},{3,259},{259,3},{4... | collective-permute-start | bytes 786440 | tf_op jit(solution)/shard_map/ppermute | solution.py:32
  45.7 2.4 %collective-permute-start.3 = (bf16[128,256]{1,0:T(8,128)(2,1)S(1)}, bf16[128,256]{1,0:T(8,128)(2,1)S(1)}, u32[]{:S(2)}, u32[]{:S(2)}) collective-permute-start(bf16[128,256]{1,0:T(8,128)(2,1)S(1)} %bitcast.140), channel_id=1, source_target_pairs={{0,256},{256,0},{1,257},{257,1},{2,258},{258,2},{3,259},{259,3},{4... | collective-permute-start | bytes 196616 | tf_op jit(solution)/shard_map/ppermute | solution.py:32
  48.1 0.9 collective-permute-done.3
  49.6 8.8 %all-to-all-done = f32[8,130,128]{2,1,0:T(8,128)S(1)} async-done(((f32[8,130,128]{2,1,0:T(8,128)}), f32[8,130,128]{2,1,0:T(8,128)S(1)}, u32[]{:S(2)}, u32[]{:S(2)}) %all-to-all-start) | async-done | bytes 532512 | tf_op jit(solution)/shard_map/all_to_all | solution.py:55
  59.2 7.3 %all-to-all-start.1 = ((f32[4,130,128]{2,1,0:T(8,128)}), f32[4,130,128]{2,1,0:T(8,128)S(1)}, u32[]{:S(2)}, u32[]{:S(2)}) async-start(f32[4,130,128]{2,1,0:T(8,128)} %broadcast_in_dim.98), calls=%async_computation.1 | async-start | bytes 557056 | tf_op jit(solution)/shard_map/all_to_all | solution.py:55
  66.5 1.3 fusion.59
  68.3 7.6 %all-to-all-done.1 = f32[4,130,128]{2,1,0:T(8,128)S(1)} async-done(((f32[4,130,128]{2,1,0:T(8,128)}), f32[4,130,128]{2,1,0:T(8,128)S(1)}, u32[]{:S(2)}, u32[]{:S(2)}) %all-to-all-start.1) | async-done | bytes 266272 | tf_op jit(solution)/shard_map/all_to_all | solution.py:55
  77.0 1.9 %collective-permute-start.5 = (f32[512,256]{0,1:T(8,128)S(1)}, f32[512,256]{0,1:T(8,128)S(1)}, u32[]{:S(2)}, u32[]{:S(2)}) collective-permute-start(f32[512,256]{0,1:T(8,128)S(1)} %bitcast.132), channel_id=1, source_target_pairs={{0,256},{256,0},{1,257},{257,1},{2,258},{258,2},{3,259},{259,3},{4... | collective-permute-start | bytes 1572872 | tf_op jit(solution)/shard_map/ppermute | solution.py:32
  79.1 1.0 bitcast_select_fusion.1
  82.3 2.0 %collective-permute-start.6 = (f32[512,256]{0,1:T(8,128)S(1)}, f32[512,256]{0,1:T(8,128)S(1)}, u32[]{:S(2)}, u32[]{:S(2)}) collective-permute-start(f32[512,256]{0,1:T(8,128)S(1)} %fusion.102), channel_id=1, source_target_pairs={{0,256},{256,0},{1,257},{257,1},{2,258},{258,2},{3,259},{259,3},{4... | collective-permute-start | bytes 1572872 | tf_op jit(solution)/shard_map/ppermute | solution.py:32
  84.4 1.7 %collective-permute-done.6 = f32[512,256]{0,1:T(8,128)S(1)} collective-permute-done((f32[512,256]{0,1:T(8,128)S(1)}, f32[512,256]{0,1:T(8,128)S(1)}, u32[]{:S(2)}, u32[]{:S(2)}) %collective-permute-start.6) | collective-permute-done | bytes 524320 | tf_op jit(solution)/shard_map/ppermute | solution.py:32
  86.2 1.5 %fusion.38 = (f32[]{:T(128)}, f32[512,256]{0,1:T(8,128)S(1)}) fusion(s32[512]{0:T(512)S(1)} %bitcast.143, f32[512]{0:T(512)S(1)} %fusion.89, bf16[128,256]{1,0:T(8,128)(2,1)S(1)} %get-tuple-element.26, bf16[128,256]{1,0:T(8,128)(2,1)S(1)} %get-tuple-element.25, f32[512,256]{0,1:T(8,128)S(1)} %get-tuple-element.10, f32[512]{0:T(512)S(1)} %add_rsqrt_fusion), kind=kOutput, calls=%fused_computation.49 | convolution fusion | flops 404881408 | bytes 1185796 | tf_op jit(solution)/shard_map/dot_general | solution.py:132
  90.1 0.9 reshape.306
  91.0 3.9 %all-to-all-start.2 = ((f32[32,33,128]{2,1,0:T(8,128)}), f32[32,33,128]{2,1,0:T(8,128)S(1)}, u32[]{:S(2)}, u32[]{:S(2)}) async-start(f32[32,33,128]{2,1,0:T(8,128)} %reshape.306), calls=%async_computation.2 | async-start | bytes 1310720 | tf_op jit(solution)/shard_map/all_to_all | solution.py:68
  94.9 20.7 %all-to-all-done.2 = f32[32,33,128]{2,1,0:T(8,128)S(1)} async-done(((f32[32,33,128]{2,1,0:T(8,128)}), f32[32,33,128]{2,1,0:T(8,128)S(1)}, u32[]{:S(2)}, u32[]{:S(2)}) %all-to-all-start.2) | async-done | bytes 540704 | tf_op jit(solution)/shard_map/all_to_all | solution.py:68
  117.7 18.0 %all_to_all.20 = bf16[32,33,128]{2,1,0:T(8,128)(2,1)S(1)} all-to-all(bf16[32,33,128]{2,1,0:T(8,128)(2,1)S(1)} %broadcast_in_dim.101), channel_id=1, replica_groups=mesh['sec'=2,'atoms'=32,'batch'=8] {'atoms'}, dimensions={0} | all-to-all | bytes 540672 | tf_op jit(solution)/shard_map/all_to_all | solution.py:81
  136.4 0.9 broadcast_in_dim_reshape.3
  (84 shorter events, 16.0 us)
Async XLA Ops:
  0.6 25.8 %copy-start = (bf16[1024,256]{1,0:T(8,128)(2,1)S(1)}, bf16[1024,256]{1,0:T(8,128)(2,1)}, u32[]{:S(2)}) copy-start(bf16[1024,256]{1,0:T(8,128)(2,1)} %param.20) | copy-start | bytes 1572868
  1.8 9.0 %collective-permute-start = (bf16[256,512]{1,0:T(8,128)(2,1)S(1)}, bf16[256,512]{1,0:T(8,128)(2,1)S(1)}, u32[]{:S(2)}, u32[]{:S(2)}) collective-permute-start(bf16[256,512]{1,0:T(8,128)(2,1)S(1)} %get-tuple-element.23), channel_id=1, source_target_pairs={{0,8},{8,16},{16,24},{24,32},{32,40},{40,48},{48,56},{56,64},{64,7... | collective-permute-start | bytes 786440 | tf_op jit(solution)/shard_map/ppermute | solution.py:25
  5.3 9.7 %collective-permute-start.1 = (bf16[256,512]{1,0:T(8,128)(2,1)S(1)}, bf16[256,512]{1,0:T(8,128)(2,1)S(1)}, u32[]{:S(2)}, u32[]{:S(2)}) collective-permute-start(bf16[256,512]{1,0:T(8,128)(2,1)S(1)} %get-tuple-element.24), channel_id=1, source_target_pairs={{8,0},{16,8},{24,16},{32,24},{40,32},{48,40},{56,48},{64,56},{72,6... | collective-permute-start | bytes 786440 | tf_op jit(solution)/shard_map/ppermute | solution.py:26
  18.1 3.1 %copy-start.1 = (bf16[1,512,512]{2,1,0:T(8,128)(2,1)S(1)}, bf16[1,512,512]{2,1,0:T(8,128)(2,1)}, u32[]{:S(2)}) copy-start(bf16[1,512,512]{2,1,0:T(8,128)(2,1)} %param.12) | copy-start | bytes 1572868
  23.9 2.9 %copy-start.5 = (bf16[1024,256]{1,0:T(8,128)(2,1)S(1)}, bf16[1024,256]{1,0:T(8,128)(2,1)}, u32[]{:S(2)}) copy-start(bf16[1024,256]{1,0:T(8,128)(2,1)} %param.21) | copy-start | bytes 1572868
  24.1 3.8 %collective-permute-start.2 = (bf16[512,512]{1,0:T(8,128)(2,1)S(1)}, bf16[512,512]{1,0:T(8,128)(2,1)S(1)}, u32[]{:S(2)}, u32[]{:S(2)}) collective-permute-start(bf16[512,512]{1,0:T(8,128)(2,1)S(1)} %fusion.30), channel_id=1, source_target_pairs={{0,256},{256,0},{1,257},{257,1},{2,258},{258,2},{3,259},{259,3},{4... | collective-permute-start | bytes 1572872 | tf_op jit(solution)/shard_map/ppermute | solution.py:32
  26.4 3.2 %copy-start.6 = (bf16[1024,256]{1,0:T(8,128)(2,1)S(1)}, bf16[1024,256]{1,0:T(8,128)(2,1)}, u32[]{:S(2)}) copy-start(bf16[1024,256]{1,0:T(8,128)(2,1)} %param.21) | copy-start | bytes 1572868
  27.9 0.8 copy-start.3
  31.8 13.9 %copy-start.9 = (bf16[1,128,256]{2,1,0:T(8,128)(2,1)S(1)}, bf16[1,128,256]{2,1,0:T(8,128)(2,1)}, u32[]{:S(2)}) copy-start(bf16[1,128,256]{2,1,0:T(8,128)(2,1)} %param.17) | copy-start | bytes 196612
  32.6 25.8 %all-to-all-start = ((f32[8,130,128]{2,1,0:T(8,128)}), f32[8,130,128]{2,1,0:T(8,128)S(1)}, u32[]{:S(2)}, u32[]{:S(2)}) async-start(f32[8,130,128]{2,1,0:T(8,128)} %broadcast_in_dim.97), calls=%async_computation | async-start | bytes 1114112 | tf_op jit(solution)/shard_map/all_to_all | solution.py:55
  41.1 26.6 %copy-start.4 = (bf16[512,512]{1,0:T(8,128)(2,1)S(1)}, bf16[512,512]{1,0:T(8,128)(2,1)}, u32[]{:S(2)}) copy-start(bf16[512,512]{1,0:T(8,128)(2,1)} %copy-done.3) | copy-start | bytes 1572868
  41.9 25.9 %copy-start.7 = (bf16[1024,256]{1,0:T(8,128)(2,1)S(1)}, bf16[1024,256]{1,0:T(8,128)(2,1)}, u32[]{:S(2)}) copy-start(bf16[1024,256]{1,0:T(8,128)(2,1)} %param.19) | copy-start | bytes 1572868
  43.8 5.8 %collective-permute-start.4 = (bf16[256,512]{1,0:T(8,128)(2,1)}, bf16[256,512]{1,0:T(8,128)(2,1)}, u32[]{:S(2)}, u32[]{:S(2)}) collective-permute-start(bf16[256,512]{1,0:T(8,128)(2,1)} %bitcast.138), channel_id=1, source_target_pairs={{0,256},{256,0},{1,257},{257,1},{2,258},{258,2},{3,259},{259,3},{4... | collective-permute-start | bytes 786440 | tf_op jit(solution)/shard_map/ppermute | solution.py:32
  45.7 3.3 %collective-permute-start.3 = (bf16[128,256]{1,0:T(8,128)(2,1)S(1)}, bf16[128,256]{1,0:T(8,128)(2,1)S(1)}, u32[]{:S(2)}, u32[]{:S(2)}) collective-permute-start(bf16[128,256]{1,0:T(8,128)(2,1)S(1)} %bitcast.140), channel_id=1, source_target_pairs={{0,256},{256,0},{1,257},{257,1},{2,258},{258,2},{3,259},{259,3},{4... | collective-permute-start | bytes 196616 | tf_op jit(solution)/shard_map/ppermute | solution.py:32
  49.0 0.6 copy-start.11
  59.2 16.7 %all-to-all-start.1 = ((f32[4,130,128]{2,1,0:T(8,128)}), f32[4,130,128]{2,1,0:T(8,128)S(1)}, u32[]{:S(2)}, u32[]{:S(2)}) async-start(f32[4,130,128]{2,1,0:T(8,128)} %broadcast_in_dim.98), calls=%async_computation.1 | async-start | bytes 557056 | tf_op jit(solution)/shard_map/all_to_all | solution.py:55
  77.0 3.8 %collective-permute-start.5 = (f32[512,256]{0,1:T(8,128)S(1)}, f32[512,256]{0,1:T(8,128)S(1)}, u32[]{:S(2)}, u32[]{:S(2)}) collective-permute-start(f32[512,256]{0,1:T(8,128)S(1)} %bitcast.132), channel_id=1, source_target_pairs={{0,256},{256,0},{1,257},{257,1},{2,258},{258,2},{3,259},{259,3},{4... | collective-permute-start | bytes 1572872 | tf_op jit(solution)/shard_map/ppermute | solution.py:32
  81.0 1.0 copy-start.8
  81.1 3.2 %copy-start.10 = (bf16[1,128,256]{2,1,0:T(8,128)(2,1)S(1)}, bf16[1,128,256]{2,1,0:T(8,128)(2,1)}, u32[]{:S(2)}) copy-start(bf16[1,128,256]{2,1,0:T(8,128)(2,1)} %param.17) | copy-start | bytes 196612
  81.1 3.2 %copy-start.12 = (bf16[128,256]{1,0:T(8,128)(2,1)S(1)}, bf16[128,256]{1,0:T(8,128)(2,1)}, u32[]{:S(2)}) copy-start(bf16[128,256]{1,0:T(8,128)(2,1)} %copy-done.11) | copy-start | bytes 196612
  81.9 6.5 %copy-start.2 = (bf16[512,512]{1,0:T(8,128)(2,1)}, bf16[512,512]{1,0:T(8,128)(2,1)S(1)}, u32[]{:S(2)}) copy-start(bf16[512,512]{1,0:T(8,128)(2,1)S(1)} %fusion.21) | copy-start | bytes 1572868
  81.9 4.3 %copy-start.13 = (s32[1,512]{1,0:T(1,128)S(1)}, s32[1,512]{1,0:T(1,128)}, u32[]{:S(2)}) copy-start(s32[1,512]{1,0:T(1,128)} %param.16) | copy-start | bytes 6148
  82.3 3.8 %collective-permute-start.6 = (f32[512,256]{0,1:T(8,128)S(1)}, f32[512,256]{0,1:T(8,128)S(1)}, u32[]{:S(2)}, u32[]{:S(2)}) collective-permute-start(f32[512,256]{0,1:T(8,128)S(1)} %fusion.102), channel_id=1, source_target_pairs={{0,256},{256,0},{1,257},{257,1},{2,258},{258,2},{3,259},{259,3},{4... | collective-permute-start | bytes 1572872 | tf_op jit(solution)/shard_map/ppermute | solution.py:32
  91.0 24.7 %all-to-all-start.2 = ((f32[32,33,128]{2,1,0:T(8,128)}), f32[32,33,128]{2,1,0:T(8,128)S(1)}, u32[]{:S(2)}, u32[]{:S(2)}) async-start(f32[32,33,128]{2,1,0:T(8,128)} %reshape.306), calls=%async_computation.2 | async-start | bytes 1310720 | tf_op jit(solution)/shard_map/all_to_all | solution.py:68

commit v14 on v12

--- a/solution.py
+++ b/solution.py
@@ -12,7 +12,7 @@
 
 
 EPSILON = 1e-06
-HIGHEST = lax.Precision.HIGHEST
+PRECISION = lax.Precision.HIGH
 
 
 def extended(x, sides, width):
@@ -97,28 +97,28 @@
         * atom_mask[:, None, None]
     )
     value_f = value_rows.astype(jnp.float32).reshape(count_rows, head_count, -1)
-    outer_state = jnp.einsum("nhd,nhe->hde", feat_keys, value_f, precision=HIGHEST)
+    outer_state = jnp.einsum("nhd,nhe->hde", feat_keys, value_f, precision=PRECISION)
     return (outer_state, jnp.sum(feat_keys, axis=0))
 
 
 def read_summary(query_rows, outer_state, key_total, head_count):
     count_rows = query_rows.shape[0]
     feat_query = feature_map(query_rows.astype(jnp.float32)).reshape(count_rows, head_count, -1)
-    numerator = jnp.einsum("nhd,hde->nhe", feat_query, outer_state, precision=HIGHEST)
-    denominator = jnp.einsum("nhd,hd->nh", feat_query, key_total, precision=HIGHEST)
+    numerator = jnp.einsum("nhd,hde->nhe", feat_query, outer_state, precision=PRECISION)
+    denominator = jnp.einsum("nhd,hd->nh", feat_query, key_total, precision=PRECISION)
     return (numerator / denominator[..., None]).reshape(count_rows, -1)
 
 
 def contrast(unit_rows, peak_rows, label_part, mask_part, peak_start):
     logit_scale = 2.0 / math.sqrt(unit_rows.shape[-1])
     peak_f = peak_rows.astype(jnp.float32)
-    logits = logit_scale * jnp.dot(unit_rows, peak_f.T, precision=HIGHEST)
+    logits = logit_scale * jnp.dot(unit_rows, peak_f.T, precision=PRECISION)
     peak_index = peak_start + jnp.arange(peak_rows.shape[0], dtype=jnp.int32)
     target = (label_part[:, None] == peak_index[None, :]).astype(jnp.float32)
     sign_rows = 2.0 * target - 1.0
     loss_part = jnp.sum(mask_part[:, None] * jax.nn.softplus(-sign_rows * logits)) / PEAKS
     slopes = mask_part[:, None] * (jax.nn.sigmoid(logits) - target) * (1.0 / math.sqrt(PEAKS))
-    unit_grad = logit_scale * jnp.dot(slopes, peak_f, precision=HIGHEST)
+    unit_grad = logit_scale * jnp.dot(slopes, peak_f, precision=PRECISION)
     return (loss_part, unit_grad)
 
 

time: 137 us -> 136 us (level)
  no operation moved by 1% of the time
where the time goes in v14:
time: 136 us; the launch traced here: 135 us
  waiting for transfers between devices  44.8 us (33%)
  starting transfers between devices  37 us (27%)
  blocking collectives  20.5 us (15%)
  local copies, waits for them, and re-layouts  12.2 us (9%)
  matrix products  10.6 us (8%)
  between operations  6.18 us (5%)
  other arithmetic  3.31 us (2%)
    all_to_all x2, waiting for transfers between devices, sum_atoms(): arrived = lax.all_to_all(pieces, 'atoms', 0, 0, tiled=True)  31.3 us
    all_to_all x2, starting transfers between devices, sum_atoms(): arrived = lax.all_to_all(pieces, 'atoms', 0, 0, tiled=True)  18 us
    all_to_all x1, blocking collectives, sum_atoms(): lax.all_to_all(jnp.broadcast_to(owned, pieces.shape), 'atoms', 0, 0, tile...  18 us
    ppermute x5, starting transfers between devices, swap_sec(): return lax.ppermute(x, 'sec', [(0, 1), (1, 0)])  10.4 us
    all_to_all x1, waiting for transfers between devices, sum_atoms(): lax.all_to_all(jnp.broadcast_to(owned, pieces.shape), 'atoms', 0, 0, tile...  10.1 us
    all_to_all x1, starting transfers between devices, sum_atoms(): lax.all_to_all(jnp.broadcast_to(owned, pieces.shape), 'atoms', 0, 0, tile...  3.86 us
    ppermute x1, starting transfers between devices, extended(): before = lax.ppermute(last, axis, up)  3.5 us
    dot_general x1, matrix products, message_pass(): jnp.einsum('btij,tjf->bif', masked, panels, preferred_element_type=jnp.fl...  2.92 us
  transfers between devices with their start and end apart: 10, of which 7 were waited for; matrix products, arithmetic and copies ran while one was open for 11% of the time, Pallas kernels for 0%

profile of v14, /device:TPU:6, one launch (start us, length us, event | category | flops | bytes accessed | tf_op | source)
XLA Modules:
  0.0 134.6 jit_solution(10803052366177387725)
XLA Ops:
  0.7 1.1 slice_bitcast_fusion.1
  1.8 3.5 %collective-permute-start = (bf16[256,512]{1,0:T(8,128)(2,1)S(1)}, bf16[256,512]{1,0:T(8,128)(2,1)S(1)}, u32[]{:S(2)}, u32[]{:S(2)}) collective-permute-start(bf16[256,512]{1,0:T(8,128)(2,1)S(1)} %get-tuple-element.23), channel_id=1, source_target_pairs={{0,8},{8,16},{16,24},{24,32},{32,40},{40,48},{48,56},{56,64},{64,7... | collective-permute-start | bytes 786440 | tf_op jit(solution)/shard_map/ppermute | solution.py:25
  5.3 1.3 collective-permute-start.1
  6.6 1.2 copy.22
  7.9 0.8 copy.23
  8.8 1.9 %collective-permute-start.4 = (bf16[256,512]{1,0:T(8,128)(2,1)}, bf16[256,512]{1,0:T(8,128)(2,1)}, u32[]{:S(2)}, u32[]{:S(2)}) collective-permute-start(bf16[256,512]{1,0:T(8,128)(2,1)} %bitcast.26), channel_id=1, source_target_pairs={{0,256},{256,0},{1,257},{257,1},{2,258},{258,2},{3,259},{259,3},{4... | collective-permute-start | bytes 786440 | tf_op jit(solution)/shard_map/ppermute | solution.py:32
  10.7 2.4 %collective-permute-start.3 = (bf16[128,256]{1,0:T(8,128)(2,1)}, bf16[128,256]{1,0:T(8,128)(2,1)}, u32[]{:S(2)}, u32[]{:S(2)}) collective-permute-start(bf16[128,256]{1,0:T(8,128)(2,1)} %bitcast.24), channel_id=1, source_target_pairs={{0,256},{256,0},{1,257},{257,1},{2,258},{258,2},{3,259},{259,3},{4... | collective-permute-start | bytes 196616 | tf_op jit(solution)/shard_map/ppermute | solution.py:32
  13.9 1.1 collective-permute-done.1
  15.1 2.0 %gather_fusion = bf16[16,128,512]{2,1,0:T(8,128)(2,1)} fusion(bf16[8,128,512]{2,1,0:T(8,128)(2,1)S(1)} %bitcast.123, s32[1024]{0:T(1024)S(1)} %pad_clamp_fusion), kind=kCustom, calls=%fused_computation | custom fusion | bytes 4194368 | tf_op jit(solution)/shard_map/jit(_take)/gather | solution.py:86
  17.1 2.9 %fusion.16 = f32[4,128,512]{2,1,0:T(8,128)S(1)} fusion(bf16[16,128,512]{2,1,0:T(8,128)(2,1)} %gather_fusion, pred[16]{0:T(512)(128)(4,1)S(1)} %get-tuple-element.13, pred[4,16]{1,0:T(4,128)(4,1)S(1)} %iota_compare_fusion.2, bf16[16,128,128]{2,1,0:T(8,128)(2,1)S(1)} %bitcast.140), kind=kOutput, calls=%fused_computation.17 | convolution fusion | flops 1076363264 | bytes 3670096 | tf_op jit(solution)/shard_map/btij,tjf->bif/dot_general | solution.py:89
  20.2 2.5 %psum.7 = f32[512]{0:T(512)S(1)} all-reduce(f32[512]{0:T(512)S(1)} %get-tuple-element.11), channel_id=1, replica_groups=mesh['sec'=2,'atoms'=32,'batch'=8] {'sec'}, use_global_device_ids=true, to_apply=%region_1.2 | all-reduce | flops 512 | bytes 4096 | tf_op jit(solution)/shard_map/psum | solution.py:153
  22.9 2.1 %collective-permute-start.2 = (bf16[512,512]{1,0:T(8,128)(2,1)S(1)}, bf16[512,512]{1,0:T(8,128)(2,1)S(1)}, u32[]{:S(2)}, u32[]{:S(2)}) collective-permute-start(bf16[512,512]{1,0:T(8,128)(2,1)S(1)} %fusion.30), channel_id=1, source_target_pairs={{0,256},{256,0},{1,257},{257,1},{2,258},{258,2},{3,259},{259,3},{4... | collective-permute-start | bytes 1572872 | tf_op jit(solution)/shard_map/ppermute | solution.py:32
  26.0 0.8 collective-permute-done.2
  26.7 0.8 copy-done.3
  28.4 1.4 %fusion.25 = bf16[512,256]{0,1:T(8,128)(2,1)S(1)} fusion(f32[512,256]{0,1:T(8,128)S(1)} %fusion.62, bf16[512,512]{1,0:T(8,128)(2,1)} %copy-done.3, bf16[2,512,256]{2,1,0:T(8,128)(2,1)S(1)} %bitcast.135, s32[]{:T(128)S(6)} %select_n.141), kind=kOutput, calls=%fused_computation.29 | convolution fusion | flops 134479872 | bytes 1572868 | tf_op jit(solution)/shard_map/dot_general | solution.py:166
  31.1 14.1 %all-to-all-start = ((f32[32,5,128]{2,1,0:T(8,128)}), f32[32,5,128]{2,1,0:T(8,128)S(1)}, u32[]{:S(2)}, u32[]{:S(2)}) async-start(f32[32,5,128]{2,1,0:T(8,128)} %reshape.309), calls=%async_computation | async-start | bytes 262144 | tf_op jit(solution)/shard_map/all_to_all | solution.py:51
  45.6 10.5 %all-to-all-done = f32[32,5,128]{2,1,0:T(8,128)S(1)} async-done(((f32[32,5,128]{2,1,0:T(8,128)}), f32[32,5,128]{2,1,0:T(8,128)S(1)}, u32[]{:S(2)}, u32[]{:S(2)}) %all-to-all-start) | async-done | bytes 81952 | tf_op jit(solution)/shard_map/all_to_all | solution.py:51
  56.2 0.7 broadcast_in_dim.89
  56.8 3.9 %all-to-all-start.1 = ((f32[32,5,128]{2,1,0:T(8,128)}), f32[32,5,128]{2,1,0:T(8,128)S(1)}, u32[]{:S(2)}, u32[]{:S(2)}) async-start(f32[32,5,128]{2,1,0:T(8,128)} %broadcast_in_dim.89), calls=%async_computation.1 | async-start | bytes 262144 | tf_op jit(solution)/shard_map/all_to_all | solution.py:64
  61.2 10.1 %all-to-all-done.1 = f32[32,5,128]{2,1,0:T(8,128)S(1)} async-done(((f32[32,5,128]{2,1,0:T(8,128)}), f32[32,5,128]{2,1,0:T(8,128)S(1)}, u32[]{:S(2)}, u32[]{:S(2)}) %all-to-all-start.1) | async-done | bytes 81952 | tf_op jit(solution)/shard_map/all_to_all | solution.py:64
  72.2 1.9 %collective-permute-start.5 = (f32[512,256]{0,1:T(8,128)S(1)}, f32[512,256]{0,1:T(8,128)S(1)}, u32[]{:S(2)}, u32[]{:S(2)}) collective-permute-start(f32[512,256]{0,1:T(8,128)S(1)} %bitcast.132), channel_id=1, source_target_pairs={{0,256},{256,0},{1,257},{257,1},{2,258},{258,2},{3,259},{259,3},{4... | collective-permute-start | bytes 1572872 | tf_op jit(solution)/shard_map/ppermute | solution.py:32
  74.3 1.0 bitcast_select_fusion.1
  75.3 0.7 collective-permute-done.5
  77.4 2.0 %collective-permute-start.6 = (f32[512,256]{0,1:T(8,128)S(1)}, f32[512,256]{0,1:T(8,128)S(1)}, u32[]{:S(2)}, u32[]{:S(2)}) collective-permute-start(f32[512,256]{0,1:T(8,128)S(1)} %fusion.102), channel_id=1, source_target_pairs={{0,256},{256,0},{1,257},{257,1},{2,258},{258,2},{3,259},{259,3},{4... | collective-permute-start | bytes 1572872 | tf_op jit(solution)/shard_map/ppermute | solution.py:32
  79.4 0.9 broadcast_select_fusion.3
  80.3 0.9 collective-permute-done.6
  81.3 1.4 %fusion.38 = (f32[]{:T(128)}, f32[512,256]{0,1:T(8,128)S(1)}) fusion(s32[512]{0:T(512)S(1)} %bitcast.141, f32[512]{0:T(512)S(1)} %fusion.89, bf16[128,256]{1,0:T(8,128)(2,1)S(1)} %get-tuple-element.26, bf16[128,256]{1,0:T(8,128)(2,1)S(1)} %get-tuple-element.25, f32[512,256]{0,1:T(8,128)S(1)} %get-tuple-element.10, f32[512]{0:T(512)S(1)} %add_rsqrt_fusion), kind=kOutput, calls=%fused_computation.49 | convolution fusion | flops 203554816 | bytes 1185796 | tf_op jit(solution)/shard_map/dot_general | solution.py:115
  84.9 0.9 reshape.317
  85.8 3.9 %all-to-all-start.2 = ((f32[32,33,128]{2,1,0:T(8,128)}), f32[32,33,128]{2,1,0:T(8,128)S(1)}, u32[]{:S(2)}, u32[]{:S(2)}) async-start(f32[32,33,128]{2,1,0:T(8,128)} %reshape.317), calls=%async_computation.2 | async-start | bytes 1310720 | tf_op jit(solution)/shard_map/all_to_all | solution.py:51
  89.8 20.7 %all-to-all-done.2 = f32[32,33,128]{2,1,0:T(8,128)S(1)} async-done(((f32[32,33,128]{2,1,0:T(8,128)}), f32[32,33,128]{2,1,0:T(8,128)S(1)}, u32[]{:S(2)}, u32[]{:S(2)}) %all-to-all-start.2) | async-done | bytes 540704 | tf_op jit(solution)/shard_map/all_to_all | solution.py:51
  112.5 18.0 %all_to_all.20 = bf16[32,33,128]{2,1,0:T(8,128)(2,1)S(1)} all-to-all(bf16[32,33,128]{2,1,0:T(8,128)(2,1)S(1)} %broadcast_in_dim.92), channel_id=1, replica_groups=mesh['sec'=2,'atoms'=32,'batch'=8] {'atoms'}, dimensions={0} | all-to-all | bytes 540672 | tf_op jit(solution)/shard_map/all_to_all | solution.py:64
  131.3 0.9 broadcast_in_dim_reshape.3
  (83 shorter events, 10.0 us)
Async XLA Ops:
  0.6 24.6 %copy-start = (bf16[1024,256]{1,0:T(8,128)(2,1)S(1)}, bf16[1024,256]{1,0:T(8,128)(2,1)}, u32[]{:S(2)}) copy-start(bf16[1024,256]{1,0:T(8,128)(2,1)} %param.20) | copy-start | bytes 1572868
  0.6 14.3 %copy-start.1 = (bf16[1,512,512]{2,1,0:T(8,128)(2,1)S(1)}, bf16[1,512,512]{2,1,0:T(8,128)(2,1)}, u32[]{:S(2)}) copy-start(bf16[1,512,512]{2,1,0:T(8,128)(2,1)} %param.12) | copy-start | bytes 1572868
  0.7 12.5 %copy-start.10 = (s32[1,2,16]{2,1,0:T(2,128)S(1)}, s32[1,2,16]{2,1,0:T(2,128)}, u32[]{:S(2)}) copy-start(s32[1,2,16]{2,1,0:T(2,128)} %param.13) | copy-start | bytes 388
  0.7 13.2 %copy-start.9 = (bf16[512]{0:T(512)(128)(2,1)S(1)}, bf16[512]{0:T(512)(128)(2,1)}, u32[]{:S(2)}) copy-start(bf16[512]{0:T(512)(128)(2,1)} %param.18) | copy-start | bytes 3076
  1.8 12.1 %collective-permute-start = (bf16[256,512]{1,0:T(8,128)(2,1)S(1)}, bf16[256,512]{1,0:T(8,128)(2,1)S(1)}, u32[]{:S(2)}, u32[]{:S(2)}) collective-permute-start(bf16[256,512]{1,0:T(8,128)(2,1)S(1)} %get-tuple-element.23), channel_id=1, source_target_pairs={{0,8},{8,16},{16,24},{24,32},{32,40},{40,48},{48,56},{56,64},{64,7... | collective-permute-start | bytes 786440 | tf_op jit(solution)/shard_map/ppermute | solution.py:25
  5.3 9.7 %collective-permute-start.1 = (bf16[256,512]{1,0:T(8,128)(2,1)S(1)}, bf16[256,512]{1,0:T(8,128)(2,1)S(1)}, u32[]{:S(2)}, u32[]{:S(2)}) collective-permute-start(bf16[256,512]{1,0:T(8,128)(2,1)S(1)} %get-tuple-element.24), channel_id=1, source_target_pairs={{8,0},{16,8},{24,16},{32,24},{40,32},{48,40},{56,48},{64,56},{72,6... | collective-permute-start | bytes 786440 | tf_op jit(solution)/shard_map/ppermute | solution.py:26
  8.8 36.8 %collective-permute-start.4 = (bf16[256,512]{1,0:T(8,128)(2,1)}, bf16[256,512]{1,0:T(8,128)(2,1)}, u32[]{:S(2)}, u32[]{:S(2)}) collective-permute-start(bf16[256,512]{1,0:T(8,128)(2,1)} %bitcast.26), channel_id=1, source_target_pairs={{0,256},{256,0},{1,257},{257,1},{2,258},{258,2},{3,259},{259,3},{4... | collective-permute-start | bytes 786440 | tf_op jit(solution)/shard_map/ppermute | solution.py:32
  10.7 34.9 %collective-permute-start.3 = (bf16[128,256]{1,0:T(8,128)(2,1)}, bf16[128,256]{1,0:T(8,128)(2,1)}, u32[]{:S(2)}, u32[]{:S(2)}) collective-permute-start(bf16[128,256]{1,0:T(8,128)(2,1)} %bitcast.24), channel_id=1, source_target_pairs={{0,256},{256,0},{1,257},{257,1},{2,258},{258,2},{3,259},{259,3},{4... | collective-permute-start | bytes 196616 | tf_op jit(solution)/shard_map/ppermute | solution.py:32
  15.1 2.0 %copy-start.11 = (bf16[1,16,128,128]{3,2,1,0:T(8,128)(2,1)S(1)}, bf16[1,16,128,128]{3,2,1,0:T(8,128)(2,1)}, u32[]{:S(2)}) copy-start(bf16[1,16,128,128]{3,2,1,0:T(8,128)(2,1)} %param.14) | copy-start | bytes 1572868
  22.7 2.9 %copy-start.5 = (bf16[1024,256]{1,0:T(8,128)(2,1)S(1)}, bf16[1024,256]{1,0:T(8,128)(2,1)}, u32[]{:S(2)}) copy-start(bf16[1024,256]{1,0:T(8,128)(2,1)} %param.21) | copy-start | bytes 1572868
  22.9 3.8 %collective-permute-start.2 = (bf16[512,512]{1,0:T(8,128)(2,1)S(1)}, bf16[512,512]{1,0:T(8,128)(2,1)S(1)}, u32[]{:S(2)}, u32[]{:S(2)}) collective-permute-start(bf16[512,512]{1,0:T(8,128)(2,1)S(1)} %fusion.30), channel_id=1, source_target_pairs={{0,256},{256,0},{1,257},{257,1},{2,258},{258,2},{3,259},{259,3},{4... | collective-permute-start | bytes 1572872 | tf_op jit(solution)/shard_map/ppermute | solution.py:32
  25.2 3.2 %copy-start.6 = (bf16[1024,256]{1,0:T(8,128)(2,1)S(1)}, bf16[1024,256]{1,0:T(8,128)(2,1)}, u32[]{:S(2)}) copy-start(bf16[1024,256]{1,0:T(8,128)(2,1)} %param.21) | copy-start | bytes 1572868
  26.7 0.8 copy-start.3
  29.8 15.5 %copy-start.7 = (bf16[1024,256]{1,0:T(8,128)(2,1)S(1)}, bf16[1024,256]{1,0:T(8,128)(2,1)}, u32[]{:S(2)}) copy-start(bf16[1024,256]{1,0:T(8,128)(2,1)} %param.19) | copy-start | bytes 1572868
  29.8 30.9 %copy-start.4 = (bf16[512,512]{1,0:T(8,128)(2,1)S(1)}, bf16[512,512]{1,0:T(8,128)(2,1)}, u32[]{:S(2)}) copy-start(bf16[512,512]{1,0:T(8,128)(2,1)} %copy-done.3) | copy-start | bytes 1572868
  31.1 25.0 %all-to-all-start = ((f32[32,5,128]{2,1,0:T(8,128)}), f32[32,5,128]{2,1,0:T(8,128)S(1)}, u32[]{:S(2)}, u32[]{:S(2)}) async-start(f32[32,5,128]{2,1,0:T(8,128)} %reshape.309), calls=%async_computation | async-start | bytes 262144 | tf_op jit(solution)/shard_map/all_to_all | solution.py:51
  56.8 14.5 %all-to-all-start.1 = ((f32[32,5,128]{2,1,0:T(8,128)}), f32[32,5,128]{2,1,0:T(8,128)S(1)}, u32[]{:S(2)}, u32[]{:S(2)}) async-start(f32[32,5,128]{2,1,0:T(8,128)} %broadcast_in_dim.89), calls=%async_computation.1 | async-start | bytes 262144 | tf_op jit(solution)/shard_map/all_to_all | solution.py:64
  72.2 3.8 %collective-permute-start.5 = (f32[512,256]{0,1:T(8,128)S(1)}, f32[512,256]{0,1:T(8,128)S(1)}, u32[]{:S(2)}, u32[]{:S(2)}) collective-permute-start(f32[512,256]{0,1:T(8,128)S(1)} %bitcast.132), channel_id=1, source_target_pairs={{0,256},{256,0},{1,257},{257,1},{2,258},{258,2},{3,259},{259,3},{4... | collective-permute-start | bytes 1572872 | tf_op jit(solution)/shard_map/ppermute | solution.py:32
  76.1 1.0 copy-start.8
  77.0 6.2 %copy-start.2 = (bf16[512,512]{1,0:T(8,128)(2,1)}, bf16[512,512]{1,0:T(8,128)(2,1)S(1)}, u32[]{:S(2)}) copy-start(bf16[512,512]{1,0:T(8,128)(2,1)S(1)} %fusion.21) | copy-start | bytes 1572868
  77.0 4.3 %copy-start.12 = (s32[1,512]{1,0:T(1,128)S(1)}, s32[1,512]{1,0:T(1,128)}, u32[]{:S(2)}) copy-start(s32[1,512]{1,0:T(1,128)} %param.16) | copy-start | bytes 6148
  77.4 3.8 %collective-permute-start.6 = (f32[512,256]{0,1:T(8,128)S(1)}, f32[512,256]{0,1:T(8,128)S(1)}, u32[]{:S(2)}, u32[]{:S(2)}) collective-permute-start(f32[512,256]{0,1:T(8,128)S(1)} %fusion.102), channel_id=1, source_target_pairs={{0,256},{256,0},{1,257},{257,1},{2,258},{258,2},{3,259},{259,3},{4... | collective-permute-start | bytes 1572872 | tf_op jit(solution)/shard_map/ppermute | solution.py:32
  85.8 24.7 %all-to-all-start.2 = ((f32[32,33,128]{2,1,0:T(8,128)}), f32[32,33,128]{2,1,0:T(8,128)S(1)}, u32[]{:S(2)}, u32[]{:S(2)}) async-start(f32[32,33,128]{2,1,0:T(8,128)} %reshape.317), calls=%async_computation.2 | async-start | bytes 1310720 | tf_op jit(solution)/shard_map/all_to_all | solution.py:51

commit v15 on v12

--- a/solution.py
+++ b/solution.py
@@ -150,7 +150,8 @@
     label_row = pair_labels[0]
     peak_part = peak_embed[0]
     hidden_f = hidden_one.astype(jnp.float32)
-    square_sum = lax.psum(jnp.sum(hidden_f * hidden_f, axis=-1), "sec")
+    square_part = jnp.sum(hidden_f * hidden_f, axis=-1)
+    square_sum = square_part + swap_sec(square_part)
     row_scale = lax.rsqrt(square_sum[:, None] / D + EPSILON)
     normed = (hidden_f * row_scale * norm_gain.astype(jnp.float32)).astype(jnp.bfloat16)
     head_cols = w_query.shape[1]

time: 137 us -> 136 us (level)
  blocking collectives: 20.5 us -> 18 us
  starting transfers between devices: 37 us -> 38.9 us
    psum x1 -> x0, blocking collectives: 2.46 us -> none  [shards(): square_sum = lax.psum(jnp.sum(hidden_f * hidden_f, axis=-1), 'sec')]
    ppermute x5 -> x6, starting transfers between devices: 10.4 us -> 12.3 us  [swap_sec(): return lax.ppermute(x, 'sec', [(0, 1), (1, 0)])]
    ppermute x5 -> x6, waiting for transfers between devices: 2.36 us -> 3.45 us  [swap_sec(): return lax.ppermute(x, 'sec', [(0, 1), (1, 0)])]
  transfers between devices with their start and end apart: 10 -> 11, of which waited for: 7 -> 8; matrix products, arithmetic and copies ran while one was open for 11% -> 11% of each run, Pallas kernels for 0% -> 0%
where the time goes in v15:
time: 136 us; the launch traced here: 135 us
  waiting for transfers between devices  46 us (34%)
  starting transfers between devices  38.9 us (29%)
  blocking collectives  18 us (13%)
  local copies, waits for them, and re-layouts  11.4 us (8%)
  matrix products  11.2 us (8%)
  between operations  6.18 us (5%)
  other arithmetic  3.34 us (2%)
    all_to_all x2, waiting for transfers between devices, sum_atoms(): arrived = lax.all_to_all(pieces, 'atoms', 0, 0, tiled=True)  31.2 us
    all_to_all x1, blocking collectives, sum_atoms(): lax.all_to_all(jnp.broadcast_to(owned, pieces.shape), 'atoms', 0, 0, tile...  18 us
    all_to_all x2, starting transfers between devices, sum_atoms(): arrived = lax.all_to_all(pieces, 'atoms', 0, 0, tiled=True)  18 us
    ppermute x6, starting transfers between devices, swap_sec(): return lax.ppermute(x, 'sec', [(0, 1), (1, 0)])  12.3 us
    all_to_all x1, waiting for transfers between devices, sum_atoms(): lax.all_to_all(jnp.broadcast_to(owned, pieces.shape), 'atoms', 0, 0, tile...  10.1 us
    all_to_all x1, starting transfers between devices, sum_atoms(): lax.all_to_all(jnp.broadcast_to(owned, pieces.shape), 'atoms', 0, 0, tile...  3.86 us
    ppermute x1, starting transfers between devices, extended(): before = lax.ppermute(last, axis, up)  3.5 us
    ppermute x6, waiting for transfers between devices, swap_sec(): return lax.ppermute(x, 'sec', [(0, 1), (1, 0)])  3.45 us
  transfers between devices with their start and end apart: 11, of which 8 were waited for; matrix products, arithmetic and copies ran while one was open for 11% of the time, Pallas kernels for 0%

profile of v15, /device:TPU:6, one launch (start us, length us, event | category | flops | bytes accessed | tf_op | source)
XLA Modules:
  0.0 135.0 jit_solution(7767347347055264337)
XLA Ops:
  0.7 1.2 slice_bitcast_fusion.1
  1.8 3.5 %collective-permute-start = (bf16[256,512]{1,0:T(8,128)(2,1)S(1)}, bf16[256,512]{1,0:T(8,128)(2,1)S(1)}, u32[]{:S(2)}, u32[]{:S(2)}) collective-permute-start(bf16[256,512]{1,0:T(8,128)(2,1)S(1)} %get-tuple-element.23), channel_id=1, source_target_pairs={{0,8},{8,16},{16,24},{24,32},{32,40},{40,48},{48,56},{56,64},{64,7... | collective-permute-start | bytes 786440 | tf_op jit(solution)/shard_map/ppermute | solution.py:25
  5.3 1.3 collective-permute-start.1
  6.6 1.2 copy.22
  7.9 0.8 copy.23
  8.8 1.9 %collective-permute-start.5 = (bf16[256,512]{1,0:T(8,128)(2,1)}, bf16[256,512]{1,0:T(8,128)(2,1)}, u32[]{:S(2)}, u32[]{:S(2)}) collective-permute-start(bf16[256,512]{1,0:T(8,128)(2,1)} %bitcast.26), channel_id=1, source_target_pairs={{0,256},{256,0},{1,257},{257,1},{2,258},{258,2},{3,259},{259,3},{4... | collective-permute-start | bytes 786440 | tf_op jit(solution)/shard_map/ppermute | solution.py:32
  10.7 2.4 %collective-permute-start.4 = (bf16[128,256]{1,0:T(8,128)(2,1)}, bf16[128,256]{1,0:T(8,128)(2,1)}, u32[]{:S(2)}, u32[]{:S(2)}) collective-permute-start(bf16[128,256]{1,0:T(8,128)(2,1)} %bitcast.24), channel_id=1, source_target_pairs={{0,256},{256,0},{1,257},{257,1},{2,258},{258,2},{3,259},{259,3},{4... | collective-permute-start | bytes 196616 | tf_op jit(solution)/shard_map/ppermute | solution.py:32
  13.9 1.1 collective-permute-done.1
  15.1 2.0 %gather_fusion = bf16[16,128,512]{2,1,0:T(8,128)(2,1)} fusion(bf16[8,128,512]{2,1,0:T(8,128)(2,1)S(1)} %bitcast.123, s32[1024]{0:T(1024)S(1)} %pad_clamp_fusion), kind=kCustom, calls=%fused_computation | custom fusion | bytes 4194368 | tf_op jit(solution)/shard_map/jit(_take)/gather | solution.py:86
  17.1 2.9 %fusion.16 = f32[4,128,512]{2,1,0:T(8,128)S(1)} fusion(bf16[16,128,512]{2,1,0:T(8,128)(2,1)} %gather_fusion, pred[16]{0:T(512)(128)(4,1)S(1)} %get-tuple-element.13, pred[4,16]{1,0:T(4,128)(4,1)S(1)} %iota_compare_fusion.2, bf16[16,128,128]{2,1,0:T(8,128)(2,1)S(1)} %bitcast.140), kind=kOutput, calls=%fused_computation.17 | convolution fusion | flops 1076363264 | bytes 3670096 | tf_op jit(solution)/shard_map/btij,tjf->bif/dot_general | solution.py:89
  20.3 1.9 %collective-permute-start.2 = (f32[512]{0:T(512)S(1)}, f32[512]{0:T(512)S(1)}, u32[]{:S(2)}, u32[]{:S(2)}) collective-permute-start(f32[512]{0:T(512)S(1)} %get-tuple-element.11), channel_id=1, source_target_pairs={{0,256},{256,0},{1,257},{257,1},{2,258},{258,2},{3,259},{259,3},{4... | collective-permute-start | bytes 6152 | tf_op jit(solution)/shard_map/ppermute | solution.py:32
  22.2 1.1 collective-permute-done.2
  23.5 2.1 %collective-permute-start.3 = (bf16[512,512]{1,0:T(8,128)(2,1)S(1)}, bf16[512,512]{1,0:T(8,128)(2,1)S(1)}, u32[]{:S(2)}, u32[]{:S(2)}) collective-permute-start(bf16[512,512]{1,0:T(8,128)(2,1)S(1)} %fusion.30), channel_id=1, source_target_pairs={{0,256},{256,0},{1,257},{257,1},{2,258},{258,2},{3,259},{259,3},{4... | collective-permute-start | bytes 1572872 | tf_op jit(solution)/shard_map/ppermute | solution.py:32
  26.5 0.8 collective-permute-done.3
  28.2 1.3 fusion.25
  31.0 14.1 %all-to-all-start = ((f32[32,5,128]{2,1,0:T(8,128)}), f32[32,5,128]{2,1,0:T(8,128)S(1)}, u32[]{:S(2)}, u32[]{:S(2)}) async-start(f32[32,5,128]{2,1,0:T(8,128)} %reshape.309), calls=%async_computation | async-start | bytes 262144 | tf_op jit(solution)/shard_map/all_to_all | solution.py:51
  45.4 10.5 %all-to-all-done = f32[32,5,128]{2,1,0:T(8,128)S(1)} async-done(((f32[32,5,128]{2,1,0:T(8,128)}), f32[32,5,128]{2,1,0:T(8,128)S(1)}, u32[]{:S(2)}, u32[]{:S(2)}) %all-to-all-start) | async-done | bytes 81952 | tf_op jit(solution)/shard_map/all_to_all | solution.py:51
  56.6 3.9 %all-to-all-start.1 = ((f32[32,5,128]{2,1,0:T(8,128)}), f32[32,5,128]{2,1,0:T(8,128)S(1)}, u32[]{:S(2)}, u32[]{:S(2)}) async-start(f32[32,5,128]{2,1,0:T(8,128)} %broadcast_in_dim.89), calls=%async_computation.1 | async-start | bytes 262144 | tf_op jit(solution)/shard_map/all_to_all | solution.py:64
  61.0 10.1 %all-to-all-done.1 = f32[32,5,128]{2,1,0:T(8,128)S(1)} async-done(((f32[32,5,128]{2,1,0:T(8,128)}), f32[32,5,128]{2,1,0:T(8,128)S(1)}, u32[]{:S(2)}, u32[]{:S(2)}) %all-to-all-start.1) | async-done | bytes 81952 | tf_op jit(solution)/shard_map/all_to_all | solution.py:64
  72.3 1.9 %collective-permute-start.6 = (f32[512,256]{0,1:T(8,128)S(1)}, f32[512,256]{0,1:T(8,128)S(1)}, u32[]{:S(2)}, u32[]{:S(2)}) collective-permute-start(f32[512,256]{0,1:T(8,128)S(1)} %bitcast.132), channel_id=1, source_target_pairs={{0,256},{256,0},{1,257},{257,1},{2,258},{258,2},{3,259},{259,3},{4... | collective-permute-start | bytes 1572872 | tf_op jit(solution)/shard_map/ppermute | solution.py:32
  74.4 1.0 bitcast_select_fusion.1
  75.4 0.7 collective-permute-done.6
  77.5 2.0 %collective-permute-start.7 = (f32[512,256]{0,1:T(8,128)S(1)}, f32[512,256]{0,1:T(8,128)S(1)}, u32[]{:S(2)}, u32[]{:S(2)}) collective-permute-start(f32[512,256]{0,1:T(8,128)S(1)} %fusion.102), channel_id=1, source_target_pairs={{0,256},{256,0},{1,257},{257,1},{2,258},{258,2},{3,259},{259,3},{4... | collective-permute-start | bytes 1572872 | tf_op jit(solution)/shard_map/ppermute | solution.py:32
  79.6 0.9 broadcast_select_fusion.3
  80.5 0.9 collective-permute-done.7
  81.5 1.5 %fusion.38 = (f32[]{:T(128)}, f32[512,256]{0,1:T(8,128)S(1)}) fusion(s32[512]{0:T(512)S(1)} %bitcast.141, f32[512]{0:T(512)S(1)} %fusion.89, bf16[128,256]{1,0:T(8,128)(2,1)S(1)} %get-tuple-element.26, bf16[128,256]{1,0:T(8,128)(2,1)S(1)} %get-tuple-element.25, f32[512,256]{0,1:T(8,128)S(1)} %get-tuple-element.10, f32[512]{0:T(512)S(1)} %add_rsqrt_fusion), kind=kOutput, calls=%fused_computation.49 | convolution fusion | flops 404881408 | bytes 1185796 | tf_op jit(solution)/shard_map/dot_general | solution.py:115
  83.0 0.7 multiply_reduce_fusion.1
  85.3 0.9 reshape.317
  86.2 3.9 %all-to-all-start.2 = ((f32[32,33,128]{2,1,0:T(8,128)}), f32[32,33,128]{2,1,0:T(8,128)S(1)}, u32[]{:S(2)}, u32[]{:S(2)}) async-start(f32[32,33,128]{2,1,0:T(8,128)} %reshape.317), calls=%async_computation.2 | async-start | bytes 1310720 | tf_op jit(solution)/shard_map/all_to_all | solution.py:51
  90.2 20.7 %all-to-all-done.2 = f32[32,33,128]{2,1,0:T(8,128)S(1)} async-done(((f32[32,33,128]{2,1,0:T(8,128)}), f32[32,33,128]{2,1,0:T(8,128)S(1)}, u32[]{:S(2)}, u32[]{:S(2)}) %all-to-all-start.2) | async-done | bytes 540704 | tf_op jit(solution)/shard_map/all_to_all | solution.py:51
  112.9 18.0 %all_to_all.20 = bf16[32,33,128]{2,1,0:T(8,128)(2,1)S(1)} all-to-all(bf16[32,33,128]{2,1,0:T(8,128)(2,1)S(1)} %broadcast_in_dim.92), channel_id=1, replica_groups=mesh['sec'=2,'atoms'=32,'batch'=8] {'atoms'}, dimensions={0} | all-to-all | bytes 540672 | tf_op jit(solution)/shard_map/all_to_all | solution.py:64
  131.7 0.9 broadcast_in_dim_reshape.3
  (78 shorter events, 10.7 us)
Async XLA Ops:
  0.6 25.2 %copy-start = (bf16[1024,256]{1,0:T(8,128)(2,1)S(1)}, bf16[1024,256]{1,0:T(8,128)(2,1)}, u32[]{:S(2)}) copy-start(bf16[1024,256]{1,0:T(8,128)(2,1)} %param.20) | copy-start | bytes 1572868
  0.6 14.3 %copy-start.1 = (bf16[1,512,512]{2,1,0:T(8,128)(2,1)S(1)}, bf16[1,512,512]{2,1,0:T(8,128)(2,1)}, u32[]{:S(2)}) copy-start(bf16[1,512,512]{2,1,0:T(8,128)(2,1)} %param.12) | copy-start | bytes 1572868
  0.7 12.5 %copy-start.7 = (s32[1,2,16]{2,1,0:T(2,128)S(1)}, s32[1,2,16]{2,1,0:T(2,128)}, u32[]{:S(2)}) copy-start(s32[1,2,16]{2,1,0:T(2,128)} %param.13) | copy-start | bytes 388
  1.8 12.0 %collective-permute-start = (bf16[256,512]{1,0:T(8,128)(2,1)S(1)}, bf16[256,512]{1,0:T(8,128)(2,1)S(1)}, u32[]{:S(2)}, u32[]{:S(2)}) collective-permute-start(bf16[256,512]{1,0:T(8,128)(2,1)S(1)} %get-tuple-element.23), channel_id=1, source_target_pairs={{0,8},{8,16},{16,24},{24,32},{32,40},{40,48},{48,56},{56,64},{64,7... | collective-permute-start | bytes 786440 | tf_op jit(solution)/shard_map/ppermute | solution.py:25
  5.3 9.7 %collective-permute-start.1 = (bf16[256,512]{1,0:T(8,128)(2,1)S(1)}, bf16[256,512]{1,0:T(8,128)(2,1)S(1)}, u32[]{:S(2)}, u32[]{:S(2)}) collective-permute-start(bf16[256,512]{1,0:T(8,128)(2,1)S(1)} %get-tuple-element.24), channel_id=1, source_target_pairs={{8,0},{16,8},{24,16},{32,24},{40,32},{48,40},{56,48},{64,56},{72,6... | collective-permute-start | bytes 786440 | tf_op jit(solution)/shard_map/ppermute | solution.py:26
  8.8 36.6 %collective-permute-start.5 = (bf16[256,512]{1,0:T(8,128)(2,1)}, bf16[256,512]{1,0:T(8,128)(2,1)}, u32[]{:S(2)}, u32[]{:S(2)}) collective-permute-start(bf16[256,512]{1,0:T(8,128)(2,1)} %bitcast.26), channel_id=1, source_target_pairs={{0,256},{256,0},{1,257},{257,1},{2,258},{258,2},{3,259},{259,3},{4... | collective-permute-start | bytes 786440 | tf_op jit(solution)/shard_map/ppermute | solution.py:32
  10.7 34.7 %collective-permute-start.4 = (bf16[128,256]{1,0:T(8,128)(2,1)}, bf16[128,256]{1,0:T(8,128)(2,1)}, u32[]{:S(2)}, u32[]{:S(2)}) collective-permute-start(bf16[128,256]{1,0:T(8,128)(2,1)} %bitcast.24), channel_id=1, source_target_pairs={{0,256},{256,0},{1,257},{257,1},{2,258},{258,2},{3,259},{259,3},{4... | collective-permute-start | bytes 196616 | tf_op jit(solution)/shard_map/ppermute | solution.py:32
  15.1 2.0 %copy-start.8 = (bf16[1,16,128,128]{3,2,1,0:T(8,128)(2,1)S(1)}, bf16[1,16,128,128]{3,2,1,0:T(8,128)(2,1)}, u32[]{:S(2)}) copy-start(bf16[1,16,128,128]{3,2,1,0:T(8,128)(2,1)} %param.14) | copy-start | bytes 1572868
  20.0 2.2 %copy-start.6 = (bf16[512]{0:T(512)(128)(2,1)S(1)}, bf16[512]{0:T(512)(128)(2,1)}, u32[]{:S(2)}) copy-start(bf16[512]{0:T(512)(128)(2,1)} %param.18) | copy-start | bytes 3076
  20.3 3.0 %collective-permute-start.2 = (f32[512]{0:T(512)S(1)}, f32[512]{0:T(512)S(1)}, u32[]{:S(2)}, u32[]{:S(2)}) collective-permute-start(f32[512]{0:T(512)S(1)} %get-tuple-element.11), channel_id=1, source_target_pairs={{0,256},{256,0},{1,257},{257,1},{2,258},{258,2},{3,259},{259,3},{4... | collective-permute-start | bytes 6152 | tf_op jit(solution)/shard_map/ppermute | solution.py:32
  23.3 2.9 %copy-start.3 = (bf16[1024,256]{1,0:T(8,128)(2,1)S(1)}, bf16[1024,256]{1,0:T(8,128)(2,1)}, u32[]{:S(2)}) copy-start(bf16[1024,256]{1,0:T(8,128)(2,1)} %param.21) | copy-start | bytes 1572868
  23.5 3.8 %collective-permute-start.3 = (bf16[512,512]{1,0:T(8,128)(2,1)S(1)}, bf16[512,512]{1,0:T(8,128)(2,1)S(1)}, u32[]{:S(2)}, u32[]{:S(2)}) collective-permute-start(bf16[512,512]{1,0:T(8,128)(2,1)S(1)} %fusion.30), channel_id=1, source_target_pairs={{0,256},{256,0},{1,257},{257,1},{2,258},{258,2},{3,259},{259,3},{4... | collective-permute-start | bytes 1572872 | tf_op jit(solution)/shard_map/ppermute | solution.py:32
  29.5 15.6 %copy-start.4 = (bf16[1024,256]{1,0:T(8,128)(2,1)S(1)}, bf16[1024,256]{1,0:T(8,128)(2,1)}, u32[]{:S(2)}) copy-start(bf16[1024,256]{1,0:T(8,128)(2,1)} %param.19) | copy-start | bytes 1572868
  31.0 25.0 %all-to-all-start = ((f32[32,5,128]{2,1,0:T(8,128)}), f32[32,5,128]{2,1,0:T(8,128)S(1)}, u32[]{:S(2)}, u32[]{:S(2)}) async-start(f32[32,5,128]{2,1,0:T(8,128)} %reshape.309), calls=%async_computation | async-start | bytes 262144 | tf_op jit(solution)/shard_map/all_to_all | solution.py:51
  56.6 14.5 %all-to-all-start.1 = ((f32[32,5,128]{2,1,0:T(8,128)}), f32[32,5,128]{2,1,0:T(8,128)S(1)}, u32[]{:S(2)}, u32[]{:S(2)}) async-start(f32[32,5,128]{2,1,0:T(8,128)} %broadcast_in_dim.89), calls=%async_computation.1 | async-start | bytes 262144 | tf_op jit(solution)/shard_map/all_to_all | solution.py:64
  72.3 3.8 %collective-permute-start.6 = (f32[512,256]{0,1:T(8,128)S(1)}, f32[512,256]{0,1:T(8,128)S(1)}, u32[]{:S(2)}, u32[]{:S(2)}) collective-permute-start(f32[512,256]{0,1:T(8,128)S(1)} %bitcast.132), channel_id=1, source_target_pairs={{0,256},{256,0},{1,257},{257,1},{2,258},{258,2},{3,259},{259,3},{4... | collective-permute-start | bytes 1572872 | tf_op jit(solution)/shard_map/ppermute | solution.py:32
  76.2 1.0 copy-start.5
  77.2 6.5 %copy-start.2 = (bf16[512,512]{1,0:T(8,128)(2,1)}, bf16[512,512]{1,0:T(8,128)(2,1)S(1)}, u32[]{:S(2)}) copy-start(bf16[512,512]{1,0:T(8,128)(2,1)S(1)} %fusion.21) | copy-start | bytes 1572868
  77.2 4.3 %copy-start.9 = (s32[1,512]{1,0:T(1,128)S(1)}, s32[1,512]{1,0:T(1,128)}, u32[]{:S(2)}) copy-start(s32[1,512]{1,0:T(1,128)} %param.16) | copy-start | bytes 6148
  77.5 3.8 %collective-permute-start.7 = (f32[512,256]{0,1:T(8,128)S(1)}, f32[512,256]{0,1:T(8,128)S(1)}, u32[]{:S(2)}, u32[]{:S(2)}) collective-permute-start(f32[512,256]{0,1:T(8,128)S(1)} %fusion.102), channel_id=1, source_target_pairs={{0,256},{256,0},{1,257},{257,1},{2,258},{258,2},{3,259},{259,3},{4... | collective-permute-start | bytes 1572872 | tf_op jit(solution)/shard_map/ppermute | solution.py:32
  86.2 24.7 %all-to-all-start.2 = ((f32[32,33,128]{2,1,0:T(8,128)}), f32[32,33,128]{2,1,0:T(8,128)S(1)}, u32[]{:S(2)}, u32[]{:S(2)}) async-start(f32[32,33,128]{2,1,0:T(8,128)} %reshape.317), calls=%async_computation.2 | async-start | bytes 1310720 | tf_op jit(solution)/shard_map/all_to_all | solution.py:51

commit v16 on v15

--- a/solution.py
+++ b/solution.py
@@ -62,7 +62,7 @@
         target = here & (row == spare[0]) & (lane == spare[1])
         owned = jnp.where(target, rest[0, slot // 128, slot % 128], owned).astype(jnp.bfloat16)
     spread = lax.all_to_all(jnp.broadcast_to(owned, pieces.shape), "atoms", 0, 0, tiled=True)
-    total = spread.reshape(-1)[: x.size].reshape(x.shape).astype(jnp.float32)
+    total = spread.reshape(-1)[: x.size].reshape(x.shape)
     return total if riders is None else (total, riders)
 
 
@@ -196,8 +196,10 @@
     zero = jnp.zeros((1,), jnp.float32)
     payload = jnp.concatenate([proj_part.reshape(-1), loss_part.reshape(1), zero])
     packed = sum_atoms(payload, exact=proj_part.size)
-    proj_total = packed[: proj_part.size].reshape(proj_part.shape)
-    loss_sum = packed[proj_part.size] + packed[proj_part.size + 1]
+    proj_total = packed[: proj_part.size].reshape(proj_part.shape).astype(jnp.float32)
+    loss_sum = packed[proj_part.size].astype(jnp.float32) + packed[proj_part.size + 1].astype(
+        jnp.float32
+    )
     loss_total = loss_sum / (local_rows * lax.axis_size("atoms"))
     return (hidden_two[None], loss_total.reshape(1), proj_total[None])
 

time: 136 us -> 136 us (level)
  no operation moved by 1% of the time
where the time goes in v16:
time: 136 us; the launch traced here: 135 us
  waiting for transfers between devices  46 us (34%)
  starting transfers between devices  38.9 us (29%)
  blocking collectives  18 us (13%)
  matrix products  11.2 us (8%)
  local copies, waits for them, and re-layouts  10.6 us (8%)
  between operations  6.17 us (5%)
  other arithmetic  4.14 us (3%)
    all_to_all x2, waiting for transfers between devices, sum_atoms(): arrived = lax.all_to_all(pieces, 'atoms', 0, 0, tiled=True)  31.2 us
    all_to_all x1, blocking collectives, sum_atoms(): lax.all_to_all(jnp.broadcast_to(owned, pieces.shape), 'atoms', 0, 0, tile...  18 us
    all_to_all x2, starting transfers between devices, sum_atoms(): arrived = lax.all_to_all(pieces, 'atoms', 0, 0, tiled=True)  18 us
    ppermute x6, starting transfers between devices, swap_sec(): return lax.ppermute(x, 'sec', [(0, 1), (1, 0)])  12.3 us
    all_to_all x1, waiting for transfers between devices, sum_atoms(): lax.all_to_all(jnp.broadcast_to(owned, pieces.shape), 'atoms', 0, 0, tile...  10.1 us
    all_to_all x1, starting transfers between devices, sum_atoms(): lax.all_to_all(jnp.broadcast_to(owned, pieces.shape), 'atoms', 0, 0, tile...  3.86 us
    ppermute x1, starting transfers between devices, extended(): before = lax.ppermute(last, axis, up)  3.5 us
    ppermute x6, waiting for transfers between devices, swap_sec(): return lax.ppermute(x, 'sec', [(0, 1), (1, 0)])  3.45 us
  transfers between devices with their start and end apart: 11, of which 8 were waited for; matrix products, arithmetic and copies ran while one was open for 11% of the time, Pallas kernels for 0%

profile of v16, /device:TPU:6, one launch (start us, length us, event | category | flops | bytes accessed | tf_op | source)
XLA Modules:
  0.0 135.0 jit_solution(12461056944913362175)
XLA Ops:
  0.7 1.2 slice_bitcast_fusion.2
  1.8 3.5 %collective-permute-start = (bf16[256,512]{1,0:T(8,128)(2,1)S(1)}, bf16[256,512]{1,0:T(8,128)(2,1)S(1)}, u32[]{:S(2)}, u32[]{:S(2)}) collective-permute-start(bf16[256,512]{1,0:T(8,128)(2,1)S(1)} %get-tuple-element.21), channel_id=1, source_target_pairs={{0,8},{8,16},{16,24},{24,32},{32,40},{40,48},{48,56},{56,64},{64,7... | collective-permute-start | bytes 786440 | tf_op jit(solution)/shard_map/ppermute | solution.py:25
  5.3 1.3 collective-permute-start.1
  6.6 1.2 copy.22
  7.9 0.8 copy.23
  8.8 1.9 %collective-permute-start.5 = (bf16[256,512]{1,0:T(8,128)(2,1)}, bf16[256,512]{1,0:T(8,128)(2,1)}, u32[]{:S(2)}, u32[]{:S(2)}) collective-permute-start(bf16[256,512]{1,0:T(8,128)(2,1)} %bitcast.26), channel_id=1, source_target_pairs={{0,256},{256,0},{1,257},{257,1},{2,258},{258,2},{3,259},{259,3},{4... | collective-permute-start | bytes 786440 | tf_op jit(solution)/shard_map/ppermute | solution.py:32
  10.7 2.4 %collective-permute-start.4 = (bf16[128,256]{1,0:T(8,128)(2,1)}, bf16[128,256]{1,0:T(8,128)(2,1)}, u32[]{:S(2)}, u32[]{:S(2)}) collective-permute-start(bf16[128,256]{1,0:T(8,128)(2,1)} %bitcast.24), channel_id=1, source_target_pairs={{0,256},{256,0},{1,257},{257,1},{2,258},{258,2},{3,259},{259,3},{4... | collective-permute-start | bytes 196616 | tf_op jit(solution)/shard_map/ppermute | solution.py:32
  13.9 1.1 collective-permute-done.1
  15.1 2.0 %gather_fusion = bf16[16,128,512]{2,1,0:T(8,128)(2,1)} fusion(bf16[8,128,512]{2,1,0:T(8,128)(2,1)S(1)} %bitcast.128, s32[1024]{0:T(1024)S(1)} %pad_clamp_fusion), kind=kCustom, calls=%fused_computation | custom fusion | bytes 4194368 | tf_op jit(solution)/shard_map/jit(_take)/gather | solution.py:86
  17.1 2.9 %fusion.16 = f32[4,128,512]{2,1,0:T(8,128)S(1)} fusion(bf16[16,128,512]{2,1,0:T(8,128)(2,1)} %gather_fusion, pred[16]{0:T(512)(128)(4,1)S(1)} %get-tuple-element.13, pred[4,16]{1,0:T(4,128)(4,1)S(1)} %iota_compare_fusion.2, bf16[16,128,128]{2,1,0:T(8,128)(2,1)S(1)} %bitcast.145), kind=kOutput, calls=%fused_computation.17 | convolution fusion | flops 1076363264 | bytes 3670096 | tf_op jit(solution)/shard_map/btij,tjf->bif/dot_general | solution.py:89
  20.3 1.9 %collective-permute-start.2 = (f32[512]{0:T(512)S(1)}, f32[512]{0:T(512)S(1)}, u32[]{:S(2)}, u32[]{:S(2)}) collective-permute-start(f32[512]{0:T(512)S(1)} %get-tuple-element.11), channel_id=1, source_target_pairs={{0,256},{256,0},{1,257},{257,1},{2,258},{258,2},{3,259},{259,3},{4... | collective-permute-start | bytes 6152 | tf_op jit(solution)/shard_map/ppermute | solution.py:32
  22.2 1.1 collective-permute-done.2
  23.5 2.1 %collective-permute-start.3 = (bf16[512,512]{1,0:T(8,128)(2,1)S(1)}, bf16[512,512]{1,0:T(8,128)(2,1)S(1)}, u32[]{:S(2)}, u32[]{:S(2)}) collective-permute-start(bf16[512,512]{1,0:T(8,128)(2,1)S(1)} %fusion.30), channel_id=1, source_target_pairs={{0,256},{256,0},{1,257},{257,1},{2,258},{258,2},{3,259},{259,3},{4... | collective-permute-start | bytes 1572872 | tf_op jit(solution)/shard_map/ppermute | solution.py:32
  26.5 0.8 collective-permute-done.3
  28.2 1.3 fusion.25
  31.0 14.1 %all-to-all-start = ((f32[32,5,128]{2,1,0:T(8,128)}), f32[32,5,128]{2,1,0:T(8,128)S(1)}, u32[]{:S(2)}, u32[]{:S(2)}) async-start(f32[32,5,128]{2,1,0:T(8,128)} %reshape.314), calls=%async_computation | async-start | bytes 262144 | tf_op jit(solution)/shard_map/all_to_all | solution.py:51
  45.4 10.5 %all-to-all-done = f32[32,5,128]{2,1,0:T(8,128)S(1)} async-done(((f32[32,5,128]{2,1,0:T(8,128)}), f32[32,5,128]{2,1,0:T(8,128)S(1)}, u32[]{:S(2)}, u32[]{:S(2)}) %all-to-all-start) | async-done | bytes 81952 | tf_op jit(solution)/shard_map/all_to_all | solution.py:51
  56.6 3.9 %all-to-all-start.1 = ((f32[32,5,128]{2,1,0:T(8,128)}), f32[32,5,128]{2,1,0:T(8,128)S(1)}, u32[]{:S(2)}, u32[]{:S(2)}) async-start(f32[32,5,128]{2,1,0:T(8,128)} %broadcast_in_dim.95), calls=%async_computation.1 | async-start | bytes 262144 | tf_op jit(solution)/shard_map/all_to_all | solution.py:64
  61.0 10.1 %all-to-all-done.1 = f32[32,5,128]{2,1,0:T(8,128)S(1)} async-done(((f32[32,5,128]{2,1,0:T(8,128)}), f32[32,5,128]{2,1,0:T(8,128)S(1)}, u32[]{:S(2)}, u32[]{:S(2)}) %all-to-all-start.1) | async-done | bytes 81952 | tf_op jit(solution)/shard_map/all_to_all | solution.py:64
  72.3 1.9 %collective-permute-start.6 = (f32[512,256]{0,1:T(8,128)S(1)}, f32[512,256]{0,1:T(8,128)S(1)}, u32[]{:S(2)}, u32[]{:S(2)}) collective-permute-start(f32[512,256]{0,1:T(8,128)S(1)} %bitcast.137), channel_id=1, source_target_pairs={{0,256},{256,0},{1,257},{257,1},{2,258},{258,2},{3,259},{259,3},{4... | collective-permute-start | bytes 1572872 | tf_op jit(solution)/shard_map/ppermute | solution.py:32
  74.4 1.0 bitcast_select_fusion.1
  75.4 0.7 collective-permute-done.6
  77.5 2.0 %collective-permute-start.7 = (f32[512,256]{0,1:T(8,128)S(1)}, f32[512,256]{0,1:T(8,128)S(1)}, u32[]{:S(2)}, u32[]{:S(2)}) collective-permute-start(f32[512,256]{0,1:T(8,128)S(1)} %fusion.103), channel_id=1, source_target_pairs={{0,256},{256,0},{1,257},{257,1},{2,258},{258,2},{3,259},{259,3},{4... | collective-permute-start | bytes 1572872 | tf_op jit(solution)/shard_map/ppermute | solution.py:32
  79.6 0.9 broadcast_select_fusion.3
  80.5 0.9 collective-permute-done.7
  81.5 1.5 %fusion.38 = (f32[]{:T(128)}, f32[512,256]{0,1:T(8,128)S(1)}) fusion(s32[512]{0:T(512)S(1)} %bitcast.146, f32[512]{0:T(512)S(1)} %fusion.90, bf16[128,256]{1,0:T(8,128)(2,1)S(1)} %get-tuple-element.26, bf16[128,256]{1,0:T(8,128)(2,1)S(1)} %get-tuple-element.25, f32[512,256]{0,1:T(8,128)S(1)} %get-tuple-element.10, f32[512]{0:T(512)S(1)} %add_rsqrt_fusion), kind=kOutput, calls=%fused_computation.49 | convolution fusion | flops 404881408 | bytes 1185796 | tf_op jit(solution)/shard_map/dot_general | solution.py:115
  83.0 0.7 multiply_reduce_fusion.1
  85.3 0.9 reshape.322
  86.2 3.9 %all-to-all-start.2 = ((f32[32,33,128]{2,1,0:T(8,128)}), f32[32,33,128]{2,1,0:T(8,128)S(1)}, u32[]{:S(2)}, u32[]{:S(2)}) async-start(f32[32,33,128]{2,1,0:T(8,128)} %reshape.322), calls=%async_computation.2 | async-start | bytes 1310720 | tf_op jit(solution)/shard_map/all_to_all | solution.py:51
  90.2 20.7 %all-to-all-done.2 = f32[32,33,128]{2,1,0:T(8,128)S(1)} async-done(((f32[32,33,128]{2,1,0:T(8,128)}), f32[32,33,128]{2,1,0:T(8,128)S(1)}, u32[]{:S(2)}, u32[]{:S(2)}) %all-to-all-start.2) | async-done | bytes 540704 | tf_op jit(solution)/shard_map/all_to_all | solution.py:51
  112.9 18.0 %all_to_all.20 = bf16[32,33,128]{2,1,0:T(8,128)(2,1)S(1)} all-to-all(bf16[32,33,128]{2,1,0:T(8,128)(2,1)S(1)} %broadcast_in_dim.98), channel_id=1, replica_groups=mesh['sec'=2,'atoms'=32,'batch'=8] {'atoms'}, dimensions={0} | all-to-all | bytes 540672 | tf_op jit(solution)/shard_map/all_to_all | solution.py:64
  131.1 0.8 fusion.58
  (77 shorter events, 10.7 us)
Async XLA Ops:
  0.6 25.2 %copy-start = (bf16[1024,256]{1,0:T(8,128)(2,1)S(1)}, bf16[1024,256]{1,0:T(8,128)(2,1)}, u32[]{:S(2)}) copy-start(bf16[1024,256]{1,0:T(8,128)(2,1)} %param.20) | copy-start | bytes 1572868
  0.6 14.3 %copy-start.1 = (bf16[1,512,512]{2,1,0:T(8,128)(2,1)S(1)}, bf16[1,512,512]{2,1,0:T(8,128)(2,1)}, u32[]{:S(2)}) copy-start(bf16[1,512,512]{2,1,0:T(8,128)(2,1)} %param.12) | copy-start | bytes 1572868
  0.7 12.5 %copy-start.7 = (s32[1,2,16]{2,1,0:T(2,128)S(1)}, s32[1,2,16]{2,1,0:T(2,128)}, u32[]{:S(2)}) copy-start(s32[1,2,16]{2,1,0:T(2,128)} %param.13) | copy-start | bytes 388
  1.8 12.0 %collective-permute-start = (bf16[256,512]{1,0:T(8,128)(2,1)S(1)}, bf16[256,512]{1,0:T(8,128)(2,1)S(1)}, u32[]{:S(2)}, u32[]{:S(2)}) collective-permute-start(bf16[256,512]{1,0:T(8,128)(2,1)S(1)} %get-tuple-element.21), channel_id=1, source_target_pairs={{0,8},{8,16},{16,24},{24,32},{32,40},{40,48},{48,56},{56,64},{64,7... | collective-permute-start | bytes 786440 | tf_op jit(solution)/shard_map/ppermute | solution.py:25
  5.3 9.7 %collective-permute-start.1 = (bf16[256,512]{1,0:T(8,128)(2,1)S(1)}, bf16[256,512]{1,0:T(8,128)(2,1)S(1)}, u32[]{:S(2)}, u32[]{:S(2)}) collective-permute-start(bf16[256,512]{1,0:T(8,128)(2,1)S(1)} %get-tuple-element.22), channel_id=1, source_target_pairs={{8,0},{16,8},{24,16},{32,24},{40,32},{48,40},{56,48},{64,56},{72,6... | collective-permute-start | bytes 786440 | tf_op jit(solution)/shard_map/ppermute | solution.py:26
  8.8 36.6 %collective-permute-start.5 = (bf16[256,512]{1,0:T(8,128)(2,1)}, bf16[256,512]{1,0:T(8,128)(2,1)}, u32[]{:S(2)}, u32[]{:S(2)}) collective-permute-start(bf16[256,512]{1,0:T(8,128)(2,1)} %bitcast.26), channel_id=1, source_target_pairs={{0,256},{256,0},{1,257},{257,1},{2,258},{258,2},{3,259},{259,3},{4... | collective-permute-start | bytes 786440 | tf_op jit(solution)/shard_map/ppermute | solution.py:32
  10.7 34.7 %collective-permute-start.4 = (bf16[128,256]{1,0:T(8,128)(2,1)}, bf16[128,256]{1,0:T(8,128)(2,1)}, u32[]{:S(2)}, u32[]{:S(2)}) collective-permute-start(bf16[128,256]{1,0:T(8,128)(2,1)} %bitcast.24), channel_id=1, source_target_pairs={{0,256},{256,0},{1,257},{257,1},{2,258},{258,2},{3,259},{259,3},{4... | collective-permute-start | bytes 196616 | tf_op jit(solution)/shard_map/ppermute | solution.py:32
  15.1 2.0 %copy-start.8 = (bf16[1,16,128,128]{3,2,1,0:T(8,128)(2,1)S(1)}, bf16[1,16,128,128]{3,2,1,0:T(8,128)(2,1)}, u32[]{:S(2)}) copy-start(bf16[1,16,128,128]{3,2,1,0:T(8,128)(2,1)} %param.14) | copy-start | bytes 1572868
  20.0 2.2 %copy-start.6 = (bf16[512]{0:T(512)(128)(2,1)S(1)}, bf16[512]{0:T(512)(128)(2,1)}, u32[]{:S(2)}) copy-start(bf16[512]{0:T(512)(128)(2,1)} %param.18) | copy-start | bytes 3076
  20.3 3.0 %collective-permute-start.2 = (f32[512]{0:T(512)S(1)}, f32[512]{0:T(512)S(1)}, u32[]{:S(2)}, u32[]{:S(2)}) collective-permute-start(f32[512]{0:T(512)S(1)} %get-tuple-element.11), channel_id=1, source_target_pairs={{0,256},{256,0},{1,257},{257,1},{2,258},{258,2},{3,259},{259,3},{4... | collective-permute-start | bytes 6152 | tf_op jit(solution)/shard_map/ppermute | solution.py:32
  23.3 2.9 %copy-start.3 = (bf16[1024,256]{1,0:T(8,128)(2,1)S(1)}, bf16[1024,256]{1,0:T(8,128)(2,1)}, u32[]{:S(2)}) copy-start(bf16[1024,256]{1,0:T(8,128)(2,1)} %param.21) | copy-start | bytes 1572868
  23.5 3.8 %collective-permute-start.3 = (bf16[512,512]{1,0:T(8,128)(2,1)S(1)}, bf16[512,512]{1,0:T(8,128)(2,1)S(1)}, u32[]{:S(2)}, u32[]{:S(2)}) collective-permute-start(bf16[512,512]{1,0:T(8,128)(2,1)S(1)} %fusion.30), channel_id=1, source_target_pairs={{0,256},{256,0},{1,257},{257,1},{2,258},{258,2},{3,259},{259,3},{4... | collective-permute-start | bytes 1572872 | tf_op jit(solution)/shard_map/ppermute | solution.py:32
  29.5 15.6 %copy-start.4 = (bf16[1024,256]{1,0:T(8,128)(2,1)S(1)}, bf16[1024,256]{1,0:T(8,128)(2,1)}, u32[]{:S(2)}) copy-start(bf16[1024,256]{1,0:T(8,128)(2,1)} %param.19) | copy-start | bytes 1572868
  31.0 25.0 %all-to-all-start = ((f32[32,5,128]{2,1,0:T(8,128)}), f32[32,5,128]{2,1,0:T(8,128)S(1)}, u32[]{:S(2)}, u32[]{:S(2)}) async-start(f32[32,5,128]{2,1,0:T(8,128)} %reshape.314), calls=%async_computation | async-start | bytes 262144 | tf_op jit(solution)/shard_map/all_to_all | solution.py:51
  56.6 14.5 %all-to-all-start.1 = ((f32[32,5,128]{2,1,0:T(8,128)}), f32[32,5,128]{2,1,0:T(8,128)S(1)}, u32[]{:S(2)}, u32[]{:S(2)}) async-start(f32[32,5,128]{2,1,0:T(8,128)} %broadcast_in_dim.95), calls=%async_computation.1 | async-start | bytes 262144 | tf_op jit(solution)/shard_map/all_to_all | solution.py:64
  72.3 3.8 %collective-permute-start.6 = (f32[512,256]{0,1:T(8,128)S(1)}, f32[512,256]{0,1:T(8,128)S(1)}, u32[]{:S(2)}, u32[]{:S(2)}) collective-permute-start(f32[512,256]{0,1:T(8,128)S(1)} %bitcast.137), channel_id=1, source_target_pairs={{0,256},{256,0},{1,257},{257,1},{2,258},{258,2},{3,259},{259,3},{4... | collective-permute-start | bytes 1572872 | tf_op jit(solution)/shard_map/ppermute | solution.py:32
  76.2 1.0 copy-start.5
  77.2 6.5 %copy-start.2 = (bf16[512,512]{1,0:T(8,128)(2,1)}, bf16[512,512]{1,0:T(8,128)(2,1)S(1)}, u32[]{:S(2)}) copy-start(bf16[512,512]{1,0:T(8,128)(2,1)S(1)} %fusion.21) | copy-start | bytes 1572868
  77.2 4.3 %copy-start.9 = (s32[1,512]{1,0:T(1,128)S(1)}, s32[1,512]{1,0:T(1,128)}, u32[]{:S(2)}) copy-start(s32[1,512]{1,0:T(1,128)} %param.16) | copy-start | bytes 6148
  77.5 3.8 %collective-permute-start.7 = (f32[512,256]{0,1:T(8,128)S(1)}, f32[512,256]{0,1:T(8,128)S(1)}, u32[]{:S(2)}, u32[]{:S(2)}) collective-permute-start(f32[512,256]{0,1:T(8,128)S(1)} %fusion.103), channel_id=1, source_target_pairs={{0,256},{256,0},{1,257},{257,1},{2,258},{258,2},{3,259},{259,3},{4... | collective-permute-start | bytes 1572872 | tf_op jit(solution)/shard_map/ppermute | solution.py:32
  86.2 24.7 %all-to-all-start.2 = ((f32[32,33,128]{2,1,0:T(8,128)}), f32[32,33,128]{2,1,0:T(8,128)S(1)}, u32[]{:S(2)}, u32[]{:S(2)}) async-start(f32[32,33,128]{2,1,0:T(8,128)} %reshape.322), calls=%async_computation.2 | async-start | bytes 1310720 | tf_op jit(solution)/shard_map/all_to_all | solution.py:51

commit v17 on v15

--- a/solution.py
+++ b/solution.py
@@ -158,8 +158,9 @@
     sec = lax.axis_index("sec")
     width = normed.shape[1]
     other_rows = swap_sec(normed)
-    out_cols = w_out.reshape(w_out.shape[0], 2, width)
-    partner = (swap_sec(peak_part), swap_sec(out_cols[:, 1 - sec, :]))
+    out_mine = lax.dynamic_slice_in_dim(w_out, sec * width, width, axis=1)
+    out_sent = lax.dynamic_slice_in_dim(w_out, (1 - sec) * width, width, axis=1)
+    partner = (swap_sec(peak_part), swap_sec(out_sent))
 
     def project(weight):
         halves = weight.reshape(2, width, weight.shape[1])
@@ -177,7 +178,7 @@
     state_rows = jnp.concatenate([outer_state, key_total[:, None, :]], axis=1)
     packed, partner = sum_atoms(state_rows, riders=partner)
     peak_all = join_sec(peak_part, partner[0], sec, 0)
-    out_rows = join_sec(out_cols[:, sec, :], partner[1], sec, 0)
+    out_rows = join_sec(out_mine, partner[1], sec, 0)
     outer_state, key_total = packed[:, :HEAD_DIM, :], packed[:, HEAD_DIM, :]
     attended = read_summary(query_f.astype(jnp.bfloat16), outer_state, key_total, head_count)
     attended_all = join_sec(attended, swap_sec(attended), sec, 1)

time: 136 us -> 139 us (1.022)
  other arithmetic: 3.34 us -> 4.87 us
  transfers between devices with their start and end apart: 11 -> 11, of which waited for: 8 -> 8; matrix products, arithmetic and copies ran while one was open for 11% -> 12% of each run, Pallas kernels for 0% -> 0%
where the time goes in v17:
time: 139 us; the launch traced here: 138 us
  waiting for transfers between devices  45 us (32%)
  starting transfers between devices  39.8 us (29%)
  blocking collectives  18 us (13%)
  matrix products  12.4 us (9%)
  local copies, waits for them, and re-layouts  11.6 us (8%)
  between operations  6.17 us (4%)
  other arithmetic  4.87 us (4%)
    all_to_all x2, waiting for transfers between devices, sum_atoms(): arrived = lax.all_to_all(pieces, 'atoms', 0, 0, tiled=True)  31.2 us
    all_to_all x2, starting transfers between devices, sum_atoms(): arrived = lax.all_to_all(pieces, 'atoms', 0, 0, tiled=True)  18.9 us
    all_to_all x1, blocking collectives, sum_atoms(): lax.all_to_all(jnp.broadcast_to(owned, pieces.shape), 'atoms', 0, 0, tile...  18 us
    ppermute x6, starting transfers between devices, swap_sec(): return lax.ppermute(x, 'sec', [(0, 1), (1, 0)])  12.3 us
    all_to_all x1, waiting for transfers between devices, sum_atoms(): lax.all_to_all(jnp.broadcast_to(owned, pieces.shape), 'atoms', 0, 0, tile...  9.11 us
    ppermute x6, waiting for transfers between devices, swap_sec(): return lax.ppermute(x, 'sec', [(0, 1), (1, 0)])  4.46 us
    all_to_all x1, starting transfers between devices, sum_atoms(): lax.all_to_all(jnp.broadcast_to(owned, pieces.shape), 'atoms', 0, 0, tile...  3.86 us
    dot_general x3, matrix products, project(): jnp.dot(other_rows, halves[1 - sec], preferred_element_type=jnp.float32)  3.56 us
  transfers between devices with their start and end apart: 11, of which 8 were waited for; matrix products, arithmetic and copies ran while one was open for 12% of the time, Pallas kernels for 0%

profile of v17, /device:TPU:6, one launch (start us, length us, event | category | flops | bytes accessed | tf_op | source)
XLA Modules:
  0.0 137.9 jit_solution(11857889610469891873)
XLA Ops:
  0.6 1.1 slice_bitcast_fusion.1
  1.8 3.5 %collective-permute-start = (bf16[256,512]{1,0:T(8,128)(2,1)S(1)}, bf16[256,512]{1,0:T(8,128)(2,1)S(1)}, u32[]{:S(2)}, u32[]{:S(2)}) collective-permute-start(bf16[256,512]{1,0:T(8,128)(2,1)S(1)} %get-tuple-element.21), channel_id=1, source_target_pairs={{0,8},{8,16},{16,24},{24,32},{32,40},{40,48},{48,56},{56,64},{64,7... | collective-permute-start | bytes 786440 | tf_op jit(solution)/shard_map/ppermute | solution.py:25
  5.3 1.3 collective-permute-start.1
  6.6 1.7 %constant_dynamic-slice_fusion = bf16[256,512]{1,0:T(8,128)(2,1)} fusion(bf16[256,1024]{1,0:T(8,128)(2,1)} %param.22, s32[]{:T(128)S(6)} %select_n.148), kind=kLoop, calls=%fused_computation.123 | loop fusion | bytes 524292 | tf_op jit(solution)/shard_map/dynamic_slice | solution.py:162
  8.3 1.9 %collective-permute-start.5 = (bf16[256,512]{1,0:T(8,128)(2,1)}, bf16[256,512]{1,0:T(8,128)(2,1)S(1)}, u32[]{:S(2)}, u32[]{:S(2)}) collective-permute-start(bf16[256,512]{1,0:T(8,128)(2,1)} %constant_dynamic-slice_fusion), channel_id=1, source_target_pairs={{0,256},{256,0},{1,257},{257,1},{2,258},{258,2},{3,259},{259,3},{4... | collective-permute-start | bytes 786440 | tf_op jit(solution)/shard_map/ppermute | solution.py:32
  10.2 2.4 %collective-permute-start.4 = (bf16[128,256]{1,0:T(8,128)(2,1)}, bf16[128,256]{1,0:T(8,128)(2,1)}, u32[]{:S(2)}, u32[]{:S(2)}) collective-permute-start(bf16[128,256]{1,0:T(8,128)(2,1)} %bitcast.133), channel_id=1, source_target_pairs={{0,256},{256,0},{1,257},{257,1},{2,258},{258,2},{3,259},{259,3},{4... | collective-permute-start | bytes 196616 | tf_op jit(solution)/shard_map/ppermute | solution.py:32
  12.6 0.8 compare_and_fusion.1
  14.9 1.1 pad_maximum_fusion
  16.1 2.0 %gather_fusion = bf16[16,128,512]{2,1,0:T(8,128)(2,1)} fusion(bf16[8,128,512]{2,1,0:T(8,128)(2,1)S(1)} %bitcast.118, s32[1024]{0:T(1024)S(1)} %pad_clamp_fusion), kind=kCustom, calls=%fused_computation | custom fusion | bytes 4194368 | tf_op jit(solution)/shard_map/jit(_take)/gather | solution.py:86
  18.1 3.0 %fusion.16 = f32[4,128,512]{2,1,0:T(8,128)S(1)} fusion(bf16[16,128,512]{2,1,0:T(8,128)(2,1)} %gather_fusion, pred[16]{0:T(512)(128)(4,1)S(1)} %get-tuple-element.13, pred[4,16]{1,0:T(4,128)(4,1)S(1)} %iota_compare_fusion.2, bf16[16,128,128]{2,1,0:T(8,128)(2,1)S(1)} %bitcast.135), kind=kOutput, calls=%fused_computation.17 | convolution fusion | flops 1076363264 | bytes 3670096 | tf_op jit(solution)/shard_map/btij,tjf->bif/dot_general | solution.py:89
  21.3 1.9 %collective-permute-start.2 = (f32[512]{0:T(512)S(1)}, f32[512]{0:T(512)S(1)}, u32[]{:S(2)}, u32[]{:S(2)}) collective-permute-start(f32[512]{0:T(512)S(1)} %get-tuple-element.11), channel_id=1, source_target_pairs={{0,256},{256,0},{1,257},{257,1},{2,258},{258,2},{3,259},{259,3},{4... | collective-permute-start | bytes 6152 | tf_op jit(solution)/shard_map/ppermute | solution.py:32
  23.3 1.1 collective-permute-done.2
  24.6 2.1 %collective-permute-start.3 = (bf16[512,512]{1,0:T(8,128)(2,1)S(1)}, bf16[512,512]{1,0:T(8,128)(2,1)S(1)}, u32[]{:S(2)}, u32[]{:S(2)}) collective-permute-start(bf16[512,512]{1,0:T(8,128)(2,1)S(1)} %fusion.30), channel_id=1, source_target_pairs={{0,256},{256,0},{1,257},{257,1},{2,258},{258,2},{3,259},{259,3},{4... | collective-permute-start | bytes 1572872 | tf_op jit(solution)/shard_map/ppermute | solution.py:32
  27.6 0.8 collective-permute-done.3
  28.4 0.8 copy-done.3
  30.0 1.4 %fusion.25 = bf16[512,256]{0,1:T(8,128)(2,1)S(1)} fusion(f32[512,256]{0,1:T(8,128)S(1)} %fusion.62, bf16[512,512]{1,0:T(8,128)(2,1)} %copy-done.3, bf16[2,512,256]{2,1,0:T(8,128)(2,1)S(1)} %bitcast.129, s32[]{:T(128)S(6)} %select_n.145), kind=kOutput, calls=%fused_computation.29 | convolution fusion | flops 134479872 | bytes 1572868 | tf_op jit(solution)/shard_map/dot_general | solution.py:168
  32.9 15.0 %all-to-all-start = ((f32[32,5,128]{2,1,0:T(8,128)}), f32[32,5,128]{2,1,0:T(8,128)S(1)}, u32[]{:S(2)}, u32[]{:S(2)}) async-start(f32[32,5,128]{2,1,0:T(8,128)} %reshape.306), calls=%async_computation | async-start | bytes 262144 | tf_op jit(solution)/shard_map/all_to_all | solution.py:51
  48.3 10.5 %all-to-all-done = f32[32,5,128]{2,1,0:T(8,128)S(1)} async-done(((f32[32,5,128]{2,1,0:T(8,128)}), f32[32,5,128]{2,1,0:T(8,128)S(1)}, u32[]{:S(2)}, u32[]{:S(2)}) %all-to-all-start) | async-done | bytes 81952 | tf_op jit(solution)/shard_map/all_to_all | solution.py:51
  59.5 3.9 %all-to-all-start.1 = ((f32[32,5,128]{2,1,0:T(8,128)}), f32[32,5,128]{2,1,0:T(8,128)S(1)}, u32[]{:S(2)}, u32[]{:S(2)}) async-start(f32[32,5,128]{2,1,0:T(8,128)} %broadcast_in_dim.89), calls=%async_computation.1 | async-start | bytes 262144 | tf_op jit(solution)/shard_map/all_to_all | solution.py:64
  63.4 1.5 %fusion.42 = f32[512,256]{0,1:T(8,128)S(1)} fusion(f32[512,256]{0,1:T(8,128)S(1)} %fusion.59, bf16[512,512]{1,0:T(8,128)(2,1)S(1)} %copy-done.4, bf16[2,512,256]{2,1,0:T(8,128)(2,1)} %bitcast.130, s32[]{:T(128)S(6)} %select_n.145), kind=kOutput, calls=%fused_computation.53 | convolution fusion | flops 135135232 | bytes 1835012 | tf_op jit(solution)/shard_map/dot_general | solution.py:168
  64.9 9.1 %all-to-all-done.1 = f32[32,5,128]{2,1,0:T(8,128)S(1)} async-done(((f32[32,5,128]{2,1,0:T(8,128)}), f32[32,5,128]{2,1,0:T(8,128)S(1)}, u32[]{:S(2)}, u32[]{:S(2)}) %all-to-all-start.1) | async-done | bytes 81952 | tf_op jit(solution)/shard_map/all_to_all | solution.py:64
  75.2 1.9 %collective-permute-start.6 = (f32[512,256]{0,1:T(8,128)S(1)}, f32[512,256]{0,1:T(8,128)S(1)}, u32[]{:S(2)}, u32[]{:S(2)}) collective-permute-start(f32[512,256]{0,1:T(8,128)S(1)} %bitcast.126), channel_id=1, source_target_pairs={{0,256},{256,0},{1,257},{257,1},{2,258},{258,2},{3,259},{259,3},{4... | collective-permute-start | bytes 1572872 | tf_op jit(solution)/shard_map/ppermute | solution.py:32
  77.2 1.7 %collective-permute-done.6 = f32[512,256]{0,1:T(8,128)S(1)} collective-permute-done((f32[512,256]{0,1:T(8,128)S(1)}, f32[512,256]{0,1:T(8,128)S(1)}, u32[]{:S(2)}, u32[]{:S(2)}) %collective-permute-start.6) | collective-permute-done | bytes 524320 | tf_op jit(solution)/shard_map/ppermute | solution.py:32
  80.4 2.0 %collective-permute-start.7 = (f32[512,256]{0,1:T(8,128)S(1)}, f32[512,256]{0,1:T(8,128)S(1)}, u32[]{:S(2)}, u32[]{:S(2)}) collective-permute-start(f32[512,256]{0,1:T(8,128)S(1)} %fusion.102), channel_id=1, source_target_pairs={{0,256},{256,0},{1,257},{257,1},{2,258},{258,2},{3,259},{259,3},{4... | collective-permute-start | bytes 1572872 | tf_op jit(solution)/shard_map/ppermute | solution.py:32
  82.4 0.9 broadcast_select_fusion.5
  83.3 0.9 collective-permute-done.7
  84.3 1.5 %fusion.38 = (f32[]{:T(128)}, f32[512,256]{0,1:T(8,128)S(1)}) fusion(s32[512]{0:T(512)S(1)} %bitcast.136, f32[512]{0:T(512)S(1)} %fusion.89, bf16[128,256]{1,0:T(8,128)(2,1)S(1)} %get-tuple-element.24, bf16[128,256]{1,0:T(8,128)(2,1)S(1)} %get-tuple-element.23, f32[512,256]{0,1:T(8,128)S(1)} %get-tuple-element.10, f32[512]{0:T(512)S(1)} %add_rsqrt_fusion), kind=kOutput, calls=%fused_computation.49 | convolution fusion | flops 404881408 | bytes 1185796 | tf_op jit(solution)/shard_map/dot_general | solution.py:115
  88.2 0.9 reshape.313
  89.1 3.9 %all-to-all-start.2 = ((f32[32,33,128]{2,1,0:T(8,128)}), f32[32,33,128]{2,1,0:T(8,128)S(1)}, u32[]{:S(2)}, u32[]{:S(2)}) async-start(f32[32,33,128]{2,1,0:T(8,128)} %reshape.313), calls=%async_computation.2 | async-start | bytes 1310720 | tf_op jit(solution)/shard_map/all_to_all | solution.py:51
  93.0 20.7 %all-to-all-done.2 = f32[32,33,128]{2,1,0:T(8,128)S(1)} async-done(((f32[32,33,128]{2,1,0:T(8,128)}), f32[32,33,128]{2,1,0:T(8,128)S(1)}, u32[]{:S(2)}, u32[]{:S(2)}) %all-to-all-start.2) | async-done | bytes 540704 | tf_op jit(solution)/shard_map/all_to_all | solution.py:51
  115.7 18.0 %all_to_all.20 = bf16[32,33,128]{2,1,0:T(8,128)(2,1)S(1)} all-to-all(bf16[32,33,128]{2,1,0:T(8,128)(2,1)S(1)} %broadcast_in_dim.92), channel_id=1, replica_groups=mesh['sec'=2,'atoms'=32,'batch'=8] {'atoms'}, dimensions={0} | all-to-all | bytes 540672 | tf_op jit(solution)/shard_map/all_to_all | solution.py:64
  134.5 0.9 broadcast_in_dim_reshape.3
  (83 shorter events, 11.5 us)
Async XLA Ops:
  0.6 26.2 %copy-start = (bf16[1024,256]{1,0:T(8,128)(2,1)S(1)}, bf16[1024,256]{1,0:T(8,128)(2,1)}, u32[]{:S(2)}) copy-start(bf16[1024,256]{1,0:T(8,128)(2,1)} %param.20) | copy-start | bytes 1572868
  1.8 13.0 %collective-permute-start = (bf16[256,512]{1,0:T(8,128)(2,1)S(1)}, bf16[256,512]{1,0:T(8,128)(2,1)S(1)}, u32[]{:S(2)}, u32[]{:S(2)}) collective-permute-start(bf16[256,512]{1,0:T(8,128)(2,1)S(1)} %get-tuple-element.21), channel_id=1, source_target_pairs={{0,8},{8,16},{16,24},{24,32},{32,40},{40,48},{48,56},{56,64},{64,7... | collective-permute-start | bytes 786440 | tf_op jit(solution)/shard_map/ppermute | solution.py:25
  5.3 9.7 %collective-permute-start.1 = (bf16[256,512]{1,0:T(8,128)(2,1)S(1)}, bf16[256,512]{1,0:T(8,128)(2,1)S(1)}, u32[]{:S(2)}, u32[]{:S(2)}) collective-permute-start(bf16[256,512]{1,0:T(8,128)(2,1)S(1)} %get-tuple-element.22), channel_id=1, source_target_pairs={{8,0},{16,8},{24,16},{32,24},{40,32},{48,40},{56,48},{64,56},{72,6... | collective-permute-start | bytes 786440 | tf_op jit(solution)/shard_map/ppermute | solution.py:26
  8.3 40.1 %collective-permute-start.5 = (bf16[256,512]{1,0:T(8,128)(2,1)}, bf16[256,512]{1,0:T(8,128)(2,1)S(1)}, u32[]{:S(2)}, u32[]{:S(2)}) collective-permute-start(bf16[256,512]{1,0:T(8,128)(2,1)} %constant_dynamic-slice_fusion), channel_id=1, source_target_pairs={{0,256},{256,0},{1,257},{257,1},{2,258},{258,2},{3,259},{259,3},{4... | collective-permute-start | bytes 786440 | tf_op jit(solution)/shard_map/ppermute | solution.py:32
  10.2 38.1 %collective-permute-start.4 = (bf16[128,256]{1,0:T(8,128)(2,1)}, bf16[128,256]{1,0:T(8,128)(2,1)}, u32[]{:S(2)}, u32[]{:S(2)}) collective-permute-start(bf16[128,256]{1,0:T(8,128)(2,1)} %bitcast.133), channel_id=1, source_target_pairs={{0,256},{256,0},{1,257},{257,1},{2,258},{258,2},{3,259},{259,3},{4... | collective-permute-start | bytes 196616 | tf_op jit(solution)/shard_map/ppermute | solution.py:32
  16.0 2.0 %copy-start.12 = (bf16[1,16,128,128]{3,2,1,0:T(8,128)(2,1)S(1)}, bf16[1,16,128,128]{3,2,1,0:T(8,128)(2,1)}, u32[]{:S(2)}) copy-start(bf16[1,16,128,128]{3,2,1,0:T(8,128)(2,1)} %param.14) | copy-start | bytes 1572868
  18.1 3.0 %copy-start.1 = (bf16[1,512,512]{2,1,0:T(8,128)(2,1)S(1)}, bf16[1,512,512]{2,1,0:T(8,128)(2,1)}, u32[]{:S(2)}) copy-start(bf16[1,512,512]{2,1,0:T(8,128)(2,1)} %param.12) | copy-start | bytes 1572868
  21.1 2.2 %copy-start.11 = (bf16[512]{0:T(512)(128)(2,1)S(1)}, bf16[512]{0:T(512)(128)(2,1)}, u32[]{:S(2)}) copy-start(bf16[512]{0:T(512)(128)(2,1)} %param.18) | copy-start | bytes 3076
  21.3 3.0 %collective-permute-start.2 = (f32[512]{0:T(512)S(1)}, f32[512]{0:T(512)S(1)}, u32[]{:S(2)}, u32[]{:S(2)}) collective-permute-start(f32[512]{0:T(512)S(1)} %get-tuple-element.11), channel_id=1, source_target_pairs={{0,256},{256,0},{1,257},{257,1},{2,258},{258,2},{3,259},{259,3},{4... | collective-permute-start | bytes 6152 | tf_op jit(solution)/shard_map/ppermute | solution.py:32
  24.4 2.9 %copy-start.6 = (bf16[1024,256]{1,0:T(8,128)(2,1)S(1)}, bf16[1024,256]{1,0:T(8,128)(2,1)}, u32[]{:S(2)}) copy-start(bf16[1024,256]{1,0:T(8,128)(2,1)} %param.21) | copy-start | bytes 1572868
  24.6 3.8 %collective-permute-start.3 = (bf16[512,512]{1,0:T(8,128)(2,1)S(1)}, bf16[512,512]{1,0:T(8,128)(2,1)S(1)}, u32[]{:S(2)}, u32[]{:S(2)}) collective-permute-start(bf16[512,512]{1,0:T(8,128)(2,1)S(1)} %fusion.30), channel_id=1, source_target_pairs={{0,256},{256,0},{1,257},{257,1},{2,258},{258,2},{3,259},{259,3},{4... | collective-permute-start | bytes 1572872 | tf_op jit(solution)/shard_map/ppermute | solution.py:32
  26.9 3.2 %copy-start.7 = (bf16[1024,256]{1,0:T(8,128)(2,1)S(1)}, bf16[1024,256]{1,0:T(8,128)(2,1)}, u32[]{:S(2)}) copy-start(bf16[1024,256]{1,0:T(8,128)(2,1)} %param.21) | copy-start | bytes 1572868
  28.4 0.8 copy-start.3
  31.4 16.5 %copy-start.8 = (bf16[1024,256]{1,0:T(8,128)(2,1)S(1)}, bf16[1024,256]{1,0:T(8,128)(2,1)}, u32[]{:S(2)}) copy-start(bf16[1024,256]{1,0:T(8,128)(2,1)} %param.19) | copy-start | bytes 1572868
  31.4 31.9 %copy-start.4 = (bf16[512,512]{1,0:T(8,128)(2,1)S(1)}, bf16[512,512]{1,0:T(8,128)(2,1)}, u32[]{:S(2)}) copy-start(bf16[512,512]{1,0:T(8,128)(2,1)} %copy-done.3) | copy-start | bytes 1572868
  32.9 25.9 %all-to-all-start = ((f32[32,5,128]{2,1,0:T(8,128)}), f32[32,5,128]{2,1,0:T(8,128)S(1)}, u32[]{:S(2)}, u32[]{:S(2)}) async-start(f32[32,5,128]{2,1,0:T(8,128)} %reshape.306), calls=%async_computation | async-start | bytes 262144 | tf_op jit(solution)/shard_map/all_to_all | solution.py:51
  59.5 14.5 %all-to-all-start.1 = ((f32[32,5,128]{2,1,0:T(8,128)}), f32[32,5,128]{2,1,0:T(8,128)S(1)}, u32[]{:S(2)}, u32[]{:S(2)}) async-start(f32[32,5,128]{2,1,0:T(8,128)} %broadcast_in_dim.89), calls=%async_computation.1 | async-start | bytes 262144 | tf_op jit(solution)/shard_map/all_to_all | solution.py:64
  63.4 13.7 %copy-start.5 = (bf16[256,1024]{1,0:T(8,128)(2,1)S(1)}, bf16[256,1024]{1,0:T(8,128)(2,1)}, u32[]{:S(2)}) copy-start(bf16[256,1024]{1,0:T(8,128)(2,1)} %param.22) | copy-start | bytes 1572868
  75.2 3.8 %collective-permute-start.6 = (f32[512,256]{0,1:T(8,128)S(1)}, f32[512,256]{0,1:T(8,128)S(1)}, u32[]{:S(2)}, u32[]{:S(2)}) collective-permute-start(f32[512,256]{0,1:T(8,128)S(1)} %bitcast.126), channel_id=1, source_target_pairs={{0,256},{256,0},{1,257},{257,1},{2,258},{258,2},{3,259},{259,3},{4... | collective-permute-start | bytes 1572872 | tf_op jit(solution)/shard_map/ppermute | solution.py:32
  79.1 1.0 copy-start.9
  79.2 3.2 %copy-start.10 = (bf16[1,128,256]{2,1,0:T(8,128)(2,1)S(1)}, bf16[1,128,256]{2,1,0:T(8,128)(2,1)}, u32[]{:S(2)}) copy-start(bf16[1,128,256]{2,1,0:T(8,128)(2,1)} %param.17) | copy-start | bytes 196612
  80.0 6.5 %copy-start.2 = (bf16[512,512]{1,0:T(8,128)(2,1)}, bf16[512,512]{1,0:T(8,128)(2,1)S(1)}, u32[]{:S(2)}) copy-start(bf16[512,512]{1,0:T(8,128)(2,1)S(1)} %fusion.21) | copy-start | bytes 1572868
  80.0 4.3 %copy-start.13 = (s32[1,512]{1,0:T(1,128)S(1)}, s32[1,512]{1,0:T(1,128)}, u32[]{:S(2)}) copy-start(s32[1,512]{1,0:T(1,128)} %param.16) | copy-start | bytes 6148
  80.4 3.8 %collective-permute-start.7 = (f32[512,256]{0,1:T(8,128)S(1)}, f32[512,256]{0,1:T(8,128)S(1)}, u32[]{:S(2)}, u32[]{:S(2)}) collective-permute-start(f32[512,256]{0,1:T(8,128)S(1)} %fusion.102), channel_id=1, source_target_pairs={{0,256},{256,0},{1,257},{257,1},{2,258},{258,2},{3,259},{259,3},{4... | collective-permute-start | bytes 1572872 | tf_op jit(solution)/shard_map/ppermute | solution.py:32
  89.1 24.7 %all-to-all-start.2 = ((f32[32,33,128]{2,1,0:T(8,128)}), f32[32,33,128]{2,1,0:T(8,128)S(1)}, u32[]{:S(2)}, u32[]{:S(2)}) async-start(f32[32,33,128]{2,1,0:T(8,128)} %reshape.313), calls=%async_computation.2 | async-start | bytes 1310720 | tf_op jit(solution)/shard_map/all_to_all | solution.py:51
